TPU v7x, 32 devices: a whole 2x2x4 slice. The times are simulated.
32 devices in a mesh: seq: 16 (over z, y, x), head: 2 (over core).
Axes of the slice: x: 2, y: 2, z: 4, core: 2. Of those that a mesh axis runs over, the one named last changes fastest.
Arguments:
- query_raw: bfloat16 [2048, 1024], P('seq', 'head'), may hold values from -448 to 448
- key_raw: bfloat16 [2048, 1024], P('seq', 'head'), may hold values from -448 to 448
- value_raw: bfloat16 [2048, 2048], P('seq', 'head'), may hold values from -448 to 448
- query_scale: float32 [2048, 8], P('seq', 'head'), may hold values from 0.004 to 0.04
- key_block_scale: float32 [2048, 8], P('seq', 'head'), may hold values from 0.004 to 0.04
- value_scale: float32 [2048, 16], P('seq', 'head'), may hold values from 0.004 to 0.04
- conv_query: bfloat16 [4, 1024], P(None, 'head'), may hold values from -3 to 3
- key_filter_taps: bfloat16 [4, 1024], P(None, 'head'), may hold values from -3 to 3
- conv_value: bfloat16 [4, 2048], P(None, 'head'), may hold values from -3 to 3
- gate_input: float32 [2048, 16], P('seq', 'head'), may hold values from -7 to 28672
- beta_logit: float32 [2048, 16], P('seq', 'head'), may hold values from -12 to 5
- decay_base: float32 [16], replicated, may hold values from -16 to 0
- step_bias: float32 [16], replicated, may hold values from -3 to 3
- output_gate: bfloat16 [2048, 2048], P('seq', 'head'), may hold values from -6 to 6
- norm_gain: float32 [128], replicated, may hold values from 0.5 to 1.5
Outputs:
- output: bfloat16 [2048, 2048], P('seq', 'head')
All inputs are finite; a program needn't handle non-finite values.
Results may differ from a plain program's by a relative error of at most 0.0048.
Values may be sent and summed in bfloat16 or wider, within the bound.
No kernel may reach another device: no remote copies, remote signals or barrier semaphores. Data moves between devices by JAX's collectives and lax.ppermute only.
A program may use at most 512 MiB of HBM per device.

v0:
```python
import jax
import jax.numpy as jnp
from jax import lax
from jax.sharding import PartitionSpec as P

CH = 64


HIGHEST = lax.Precision.HIGHEST
EPSILON = 1e-06


def from_behind(value, axis, steps):
    count = lax.axis_size(axis)
    first, last = (max(0, -steps), min(count, count - steps))
    return lax.ppermute(value, axis, [(source, source + steps) for source in range(first, last)])


def prefix_2(shard, axis, combine, identity):
    devices, mine = (lax.axis_size(axis), lax.axis_index(axis))
    everything = jax.tree.map(lambda part: lax.all_gather(part, axis), shard)
    start = jax.tree.map(
        lambda part, zero: jnp.broadcast_to(jnp.asarray(zero, part.dtype), part.shape),
        shard,
        identity,
    )

    def hop(k, before):
        reached = k < mine
        new = combine(before, jax.tree.map(lambda part: part[k], everything))
        return jax.tree.map(lambda a, b: jnp.where(reached, a, b), new, before)

    return lax.fori_loop(0, devices, hop, start)


def expand_quantized(raw_rows, scales):
    row_count = raw_rows.shape[0]
    head_count = scales.shape[1]
    shaped = raw_rows.astype(jnp.float32).reshape(row_count, head_count, -1) * scales[:, :, None]
    return shaped.reshape(row_count, -1)


def causal_filter(window, weights):
    kernel_span = weights.shape[0]
    row_count = window.shape[0] - kernel_span + 1
    summed = jnp.zeros((row_count, window.shape[1]), jnp.float32)
    for offset_tap in range(kernel_span):
        summed = summed + window[offset_tap : offset_tap + row_count] * weights[offset_tap].astype(
            jnp.float32
        )
    return lax.optimization_barrier(jax.nn.silu(summed).astype(jnp.bfloat16))


def unit_heads(conv_rows, head_width):
    row_count = conv_rows.shape[0]
    shaped = conv_rows.astype(jnp.float32).reshape(row_count, -1, head_width)
    return shaped * lax.rsqrt(jnp.sum(shaped * shaped, axis=-1, keepdims=True) + EPSILON)


def head_inputs(
    query_conv,
    key_filtered,
    value_conv,
    gate_rows,
    beta_rows,
    decay_base,
    step_bias,
    head_width,
    block,
):
    row_count = query_conv.shape[0]
    queries = unit_heads(query_conv, head_width) * head_width ** (-0.5)
    key_units = unit_heads(key_filtered, head_width)
    value_units = value_conv.astype(jnp.float32).reshape(row_count, -1, head_width)
    repeats = value_units.shape[1] // key_units.shape[1]
    queries = jnp.repeat(queries, repeats, axis=1)
    key_units = jnp.repeat(key_units, repeats, axis=1)
    logdec = -jnp.exp(decay_base)[None, :] * jax.nn.softplus(gate_rows + step_bias[None, :])
    betas_all = jax.nn.sigmoid(beta_rows)
    block_count = row_count // block

    def to_blocks(array):
        return array.reshape(block_count, block, array.shape[1], -1).transpose(0, 2, 1, 3)

    def to_block_rows(array):
        return array.reshape(block_count, block, -1).transpose(0, 2, 1)

    return (
        to_blocks(queries),
        to_blocks(key_units),
        to_blocks(value_units),
        to_block_rows(logdec),
        to_block_rows(betas_all),
    )


def unit_lower_inverse(strict_part):
    length = strict_part.shape[-1]
    negated = -strict_part
    inverse = jnp.eye(length, dtype=jnp.float32) + negated
    power = negated
    span = 2
    while span < length:
        power = jnp.einsum("bhij,bhjk->bhik", power, power, precision=HIGHEST)
        inverse = inverse + jnp.einsum("bhij,bhjk->bhik", inverse, power, precision=HIGHEST)
        span = span * 2
    return inverse


def block_terms(queries, key_units, value_units, logdec, beta_units):
    length = logdec.shape[-1]
    positions = jnp.arange(length)
    lower_incl = positions[:, None] >= positions[None, :]
    lower_strict = positions[:, None] > positions[None, :]
    cumulative = jnp.cumsum(logdec, axis=-1)
    differ = cumulative[..., :, None] - cumulative[..., None, :]
    decay_incl = jnp.where(lower_incl, jnp.exp(jnp.where(lower_incl, differ, 0.0)), 0.0)
    decay_strict = jnp.where(lower_strict, decay_incl, 0.0)
    key_gram = jnp.einsum("bhid,bhjd->bhij", key_units, key_units, precision=HIGHEST)
    inverse = unit_lower_inverse(beta_units[..., :, None] * key_gram * decay_strict)
    growth = jnp.exp(cumulative)
    stacked = jnp.concatenate(
        [beta_units[..., None] * value_units, (beta_units * growth)[..., None] * key_units], axis=-1
    )
    solved = jnp.einsum("bhij,bhjd->bhid", inverse, stacked, precision=HIGHEST)
    value_width = value_units.shape[-1]
    weight_values = solved[..., :value_width]
    weight_keys = solved[..., value_width:]
    mixing = decay_incl * jnp.einsum("bhid,bhjd->bhij", queries, key_units, precision=HIGHEST)
    zero_out = jnp.einsum("bhij,bhjd->bhid", mixing, weight_values, precision=HIGHEST)
    readout = growth[..., None] * queries - jnp.einsum(
        "bhij,bhjd->bhid", mixing, weight_keys, precision=HIGHEST
    )
    fading = jnp.exp(cumulative[..., -1:] - cumulative)[..., None] * key_units
    eye_key = jnp.eye(key_units.shape[-1], dtype=jnp.float32)
    transition = growth[..., -1][..., None, None] * eye_key - jnp.einsum(
        "bhjd,bhje->bhde", fading, weight_keys, precision=HIGHEST
    )
    offset = jnp.einsum("bhjd,bhje->bhde", fading, weight_values, precision=HIGHEST)
    return (zero_out, readout, transition, offset)


def product(left, right):
    return jnp.einsum("hde,hef->hdf", left, right, precision=HIGHEST)


def chain_blocks(transition, offset):
    head_count = offset.shape[1]
    key_width = offset.shape[2]
    value_width = offset.shape[3]
    initial = (
        jnp.zeros((head_count, key_width, value_width), jnp.float32),
        jnp.broadcast_to(jnp.eye(key_width, dtype=jnp.float32), (head_count, key_width, key_width)),
    )

    def chain_advance(carried, block_items):
        state_now, map_now = carried
        trans_now, offset_now = block_items
        following = (product(trans_now, state_now) + offset_now, product(trans_now, map_now))
        return (following, ())

    return lax.scan(chain_advance, initial, (transition, offset))


def replay_blocks(transition, offset, incoming):

    def replay_advance(state_now, block_items):
        trans_now, offset_now = block_items
        return (product(trans_now, state_now) + offset_now, state_now)

    _, starts = lax.scan(replay_advance, incoming, (transition, offset))
    return starts


def combine_maps(earlier, later):
    trans_early, offset_early = earlier
    trans_late, offset_late = later
    return (product(trans_late, trans_early), product(trans_late, offset_early) + offset_late)


def to_rows(blocks):
    return blocks.transpose(0, 2, 1, 3).reshape(-1, blocks.shape[1], blocks.shape[3])


def gated_norm(delta_rows, gate_raw, norm_gain):
    meansq = jnp.mean(delta_rows * delta_rows, axis=-1, keepdims=True)
    normed = delta_rows * lax.rsqrt(meansq + EPSILON) * norm_gain
    gate_float = gate_raw.astype(jnp.float32).reshape(delta_rows.shape)
    return (normed * jax.nn.silu(gate_float)).reshape(delta_rows.shape[0], -1).astype(jnp.bfloat16)


def identity_of(trans_like, offset_like):
    return (
        jnp.broadcast_to(jnp.eye(trans_like.shape[1], dtype=jnp.float32), trans_like.shape),
        jnp.zeros_like(offset_like),
    )


def shards(
    query_raw,
    key_raw,
    value_raw,
    query_scale,
    key_block_scale,
    value_scale,
    conv_query,
    key_filter_taps,
    conv_value,
    gate_input,
    beta_logit,
    decay_base,
    step_bias,
    output_gate,
    norm_gain,
):
    head_width = norm_gain.shape[0]
    margin = conv_query.shape[0] - 1
    query_deq = expand_quantized(query_raw, query_scale)
    key_deq = expand_quantized(key_raw, key_block_scale)
    value_deq = expand_quantized(value_raw, value_scale)
    tail_rows = from_behind((query_deq[-margin:], key_deq[-margin:], value_deq[-margin:]), "seq", 1)
    query_conv = causal_filter(jnp.concatenate([tail_rows[0], query_deq], axis=0), conv_query)
    key_filtered = causal_filter(jnp.concatenate([tail_rows[1], key_deq], axis=0), key_filter_taps)
    value_conv = causal_filter(jnp.concatenate([tail_rows[2], value_deq], axis=0), conv_value)
    local_heads = gate_input.shape[1]
    first_head = lax.axis_index("head") * local_heads
    base_part = lax.dynamic_slice_in_dim(decay_base, first_head, local_heads)
    bias_part = lax.dynamic_slice_in_dim(step_bias, first_head, local_heads)
    zero_out, readout, transition, offset = block_terms(
        *head_inputs(
            query_conv,
            key_filtered,
            value_conv,
            gate_input,
            beta_logit,
            base_part,
            bias_part,
            head_width,
            CH,
        )
    )
    finals, emitted = chain_blocks(transition, offset)
    dev_offset, dev_trans = finals
    prefix = prefix_2(
        (dev_trans, dev_offset), "seq", combine_maps, identity_of(dev_trans, dev_offset)
    )
    incoming = prefix[1]
    starts = replay_blocks(transition, offset, incoming)
    outputs = zero_out + jnp.einsum("bhid,bhde->bhie", readout, starts, precision=HIGHEST)
    gated_rows = gated_norm(to_rows(outputs), output_gate, norm_gain)
    return gated_rows


def solution(mesh):
    placed = (
        P("seq", "head"),
        P("seq", "head"),
        P("seq", "head"),
        P("seq", "head"),
        P("seq", "head"),
        P("seq", "head"),
        P(None, "head"),
        P(None, "head"),
        P(None, "head"),
        P("seq", "head"),
        P("seq", "head"),
        P(),
        P(),
        P("seq", "head"),
        P(),
    )
    return jax.shard_map(
        shards, mesh=mesh, in_specs=placed, out_specs=P("seq", "head"), check_vma=False
    )
```

profile of v0, /device:TPU:28, one launch (start us, length us, event | category | flops | bytes accessed | tf_op | source)
XLA Modules:
  0.0 314.2 jit_solution(9955817574548314963)
XLA Ops:
  8.4 3.4 %collective-permute-start.1 = (f32[3,512]{1,0:T(4,128)S(1)}, f32[3,512]{1,0:T(4,128)S(1)}, u32[]{:S(2)}, u32[]{:S(2)}) collective-permute-start(f32[3,512]{1,0:T(4,128)S(1)} %bitcast.188), channel_id=1, source_target_pairs={{0,2},{2,4},{4,6},{6,8},{8,10},{10,12},{12,14},{14,16},{16,18},{18... | collective-permute-start | bytes 18440 | tf_op jit(solution)/shard_map/ppermute | solution.py:16
  13.8 1.9 collective-permute-start.2
  34.2 2.2 fusion.50
  36.4 2.0 convolution_subtract_fusion
  38.6 2.9 while.40
  43.3 1.9 collective-permute-start
  45.6 4.2 %collective-permute-done = f32[3,512]{1,0:T(4,128)S(1)} collective-permute-done((f32[3,512]{1,0:T(4,128)S(1)}, f32[3,512]{1,0:T(4,128)S(1)}, u32[]{:S(2)}, u32[]{:S(2)}) %collective-permute-start) | collective-permute-done | bytes 6176 | tf_op jit(solution)/shard_map/ppermute | solution.py:16
  50.5 2.0 convolution_multiply_fusion.1
  54.3 2.5 convolution_subtract_fusion.1
  56.8 98.0 %all-gather.5.cloned.1.call-done = f32[128,128,128]{2,1,0:T(8,128)} async-done(((f32[8,128,128]{2,1,0:T(8,128)}), f32[128,128,128]{2,1,0:T(8,128)}) %all-gather.5.cloned.1.call-update) | async-done | bytes 8388624 | tf_op jit(solution)/shard_map/all_gather | solution.py:21
  154.8 113.8 %all-gather.7.cloned.1.call-done = f32[128,128,128]{2,1,0:T(8,128)} async-done(((f32[8,128,128]{2,1,0:T(8,128)}), f32[128,128,128]{2,1,0:T(8,128)}) %all-gather.7.cloned.1.call-update) | async-done | bytes 8388624 | tf_op jit(solution)/shard_map/all_gather | solution.py:21
  268.6 31.5 %while.41 = (s32[]{:T(128)}, f32[8,128,128]{2,1,0:T(8,128)S(1)}, s32[]{:T(128)}, f32[16,8,128,128]{3,2,1,0:T(8,128)}, f32[16,8,128,128]{3,2,1,0:T(8,128)}, /*index=5*/s32[]{:T(128)}, s32[]{:T(128)}) while((s32[]{:T(128)}, f32[8,128,128]{2,1,0:T(8,128)S(1)}, s32[]{:T(128)}, f32[16,8,128,128]{3,2,1,0:T(8,128)}, ...), condition=%wide.region_6.7_spmd.clone, body=%wide.region_5.6_spmd.clone.sunk | while | flops 201850880 | bytes 3672679 | solution.py:33
  268.7 1.9 fusion.135
  270.6 1.9 fusion.135
  272.6 1.9 fusion.135
  276.6 1.9 fusion.135
  278.5 1.9 fusion.135
  282.5 1.9 fusion.135
  286.4 1.9 fusion.135
  288.4 1.9 fusion.135
  294.3 1.9 fusion.135
  296.2 1.9 fusion.135
  300.1 3.1 while.39
  303.2 2.5 multiply_reduce_fusion
  (142 shorter events, 46.0 us)
Async XLA Ops:
  6.5 39.0 %copy-start = (f32[128]{0:T(128)S(1)}, f32[128]{0:T(128)}, u32[]{:S(2)}) copy-start(f32[128]{0:T(128)} %param.35) | copy-start | bytes 1540
  6.5 148.3 %all-gather.5.cloned.1.call-start = ((), (), s32[]{:S(2)}) async-start(), calls=%async_computation | async-start | bytes 8912896 | tf_op jit(solution)/shard_map/all_gather | solution.py:21
  8.4 15.4 %collective-permute-start.1 = (f32[3,512]{1,0:T(4,128)S(1)}, f32[3,512]{1,0:T(4,128)S(1)}, u32[]{:S(2)}, u32[]{:S(2)}) collective-permute-start(f32[3,512]{1,0:T(4,128)S(1)} %bitcast.188), channel_id=1, source_target_pairs={{0,2},{2,4},{4,6},{6,8},{8,10},{10,12},{12,14},{14,16},{16,18},{18... | collective-permute-start | bytes 18440 | tf_op jit(solution)/shard_map/ppermute | solution.py:16
  13.8 18.6 %collective-permute-start.2 = (f32[3,1024]{1,0:T(4,128)S(1)}, f32[3,1024]{1,0:T(4,128)S(1)}, u32[]{:S(2)}, u32[]{:S(2)}) collective-permute-start(f32[3,1024]{1,0:T(4,128)S(1)} %bitcast.179), channel_id=1, source_target_pairs={{0,2},{2,4},{4,6},{6,8},{8,10},{10,12},{12,14},{14,16},{16,18},{18... | collective-permute-start | bytes 36872 | tf_op jit(solution)/shard_map/ppermute | solution.py:16
  24.7 11.8 %copy-start.3 = (f32[128,4,2,128]{3,0,2,1:T(8,128)}, f32[128,4,2,128]{3,0,2,1:T(8,128)S(1)}, u32[]{:S(2)}) copy-start(f32[128,4,2,128]{3,0,2,1:T(8,128)S(1)} %broadcast_in_dim.28) | copy-start | bytes 1572868
  34.2 4.3 %copy-start.4 = (f32[2,8,64,256]{3,2,1,0:T(8,128)}, f32[2,8,64,256]{3,2,1,0:T(8,128)S(1)}, u32[]{:S(2)}) copy-start(f32[2,8,64,256]{3,2,1,0:T(8,128)S(1)} %fusion.25) | copy-start | bytes 3145732
  38.5 4.5 %copy-start.8 = (f32[128,4]{0,1:T(4,128)S(1)}, f32[128,4]{0,1:T(4,128)}, u32[]{:S(2)}) copy-start(f32[128,4]{0,1:T(4,128)} %param.24) | copy-start | bytes 6148
  38.6 4.6 %copy-start.5 = (bf16[128,512]{1,0:T(8,128)(2,1)S(1)}, bf16[128,512]{1,0:T(8,128)(2,1)}, u32[]{:S(2)}) copy-start(bf16[128,512]{1,0:T(8,128)(2,1)} %param.21) | copy-start | bytes 393220
  38.6 6.7 %copy-start.7 = (bf16[4,512]{1,0:T(4,128)(2,1)S(1)}, bf16[4,512]{1,0:T(4,128)(2,1)}, u32[]{:S(2)}) copy-start(bf16[4,512]{1,0:T(4,128)(2,1)} %param.27) | copy-start | bytes 12292
  41.4 0.8 copy-start.1
  41.5 1.0 copy-start.2
  42.3 226.4 %all-gather.7.cloned.1.call-start = ((), (), s32[]{:S(2)}) async-start(), calls=%async_computation.1 | async-start | bytes 8912896 | tf_op jit(solution)/shard_map/all_gather | solution.py:21
  43.3 6.4 %collective-permute-start = (f32[3,512]{1,0:T(4,128)S(1)}, f32[3,512]{1,0:T(4,128)S(1)}, u32[]{:S(2)}, u32[]{:S(2)}) collective-permute-start(f32[3,512]{1,0:T(4,128)S(1)} %bitcast.189), channel_id=1, source_target_pairs={{0,2},{2,4},{4,6},{6,8},{8,10},{10,12},{12,14},{14,16},{16,18},{18... | collective-permute-start | bytes 18440 | tf_op jit(solution)/shard_map/ppermute | solution.py:16
  300.1 6.3 %copy-start.6 = (bf16[128,1024]{1,0:T(8,128)(2,1)S(1)}, bf16[128,1024]{1,0:T(8,128)(2,1)}, u32[]{:S(2)}) copy-start(bf16[128,1024]{1,0:T(8,128)(2,1)} %param.34) | copy-start | bytes 786436
Sparse Core Ops, SparseCore 0:
  42.4 112.3 all-gather.4
  157.6 111.0 all-gather.6
where the time goes:
time: 319 us; the launch traced here: 314 us
  waiting for transfers between devices  217 us (68%)
  matrix products  55.8 us (17%)
  between operations  14 us (4%)
  other arithmetic  10.7 us (3%)
  local copies, waits for them, and re-layouts  9.13 us (3%)
  starting transfers between devices  7.25 us (2%)
    all_gather x2, waiting for transfers between devices, prefix_2(): everything = jax.tree.map(lambda part: lax.all_gather(part, axis), shard)  212 us
    dot_general x22, matrix products, product(): return jnp.einsum('hde,hef->hdf', left, right, precision=HIGHEST)  34.2 us
    ppermute x3, starting transfers between devices, from_behind(): lax.ppermute(value, axis, [(source, source + steps) for source in range(f...  7.21 us
  transfers between devices with their start and end apart: 5, of which 3 were waited for; matrix products, arithmetic and copies ran while one was open for 8% of the time, Pallas kernels for 0%

commit v1 on v0

--- a/solution.py
+++ b/solution.py
@@ -16,21 +16,20 @@
     return lax.ppermute(value, axis, [(source, source + steps) for source in range(first, last)])
 
 
-def prefix_2(shard, axis, combine, identity):
+def scan_states(trans, offset, axis):
     devices, mine = (lax.axis_size(axis), lax.axis_index(axis))
-    everything = jax.tree.map(lambda part: lax.all_gather(part, axis), shard)
-    start = jax.tree.map(
-        lambda part, zero: jnp.broadcast_to(jnp.asarray(zero, part.dtype), part.shape),
-        shard,
-        identity,
-    )
-
-    def hop(k, before):
-        reached = k < mine
-        new = combine(before, jax.tree.map(lambda part: part[k], everything))
-        return jax.tree.map(lambda a, b: jnp.where(reached, a, b), new, before)
-
-    return lax.fori_loop(0, devices, hop, start)
+    span = 1
+    while span < devices:
+        pairs = [(source, source + span) for source in range(devices - span)]
+        if 2 * span < devices:
+            trans_in, offset_in = lax.ppermute((trans, offset), axis, pairs)
+            offset = product(trans, offset_in) + offset
+            trans = jnp.where(mine >= span, product(trans, trans_in), trans)
+        else:
+            offset_in = lax.ppermute(offset, axis, pairs)
+            offset = product(trans, offset_in) + offset
+        span = span * 2
+    return from_behind(offset, axis, 1)
 
 
 def expand_quantized(raw_rows, scales):
@@ -218,7 +217,17 @@
     query_deq = expand_quantized(query_raw, query_scale)
     key_deq = expand_quantized(key_raw, key_block_scale)
     value_deq = expand_quantized(value_raw, value_scale)
-    tail_rows = from_behind((query_deq[-margin:], key_deq[-margin:], value_deq[-margin:]), "seq", 1)
+    query_width, key_width = (query_deq.shape[1], key_deq.shape[1])
+    tails = from_behind(
+        jnp.concatenate([query_deq[-margin:], key_deq[-margin:], value_deq[-margin:]], axis=1),
+        "seq",
+        1,
+    )
+    tail_rows = (
+        tails[:, :query_width],
+        tails[:, query_width : query_width + key_width],
+        tails[:, query_width + key_width :],
+    )
     query_conv = causal_filter(jnp.concatenate([tail_rows[0], query_deq], axis=0), conv_query)
     key_filtered = causal_filter(jnp.concatenate([tail_rows[1], key_deq], axis=0), key_filter_taps)
     value_conv = causal_filter(jnp.concatenate([tail_rows[2], value_deq], axis=0), conv_value)
@@ -241,10 +250,7 @@
     )
     finals, emitted = chain_blocks(transition, offset)
     dev_offset, dev_trans = finals
-    prefix = prefix_2(
-        (dev_trans, dev_offset), "seq", combine_maps, identity_of(dev_trans, dev_offset)
-    )
-    incoming = prefix[1]
+    incoming = scan_states(dev_trans, dev_offset, "seq")
     starts = replay_blocks(transition, offset, incoming)
     outputs = zero_out + jnp.einsum("bhid,bhde->bhie", readout, starts, precision=HIGHEST)
     gated_rows = gated_norm(to_rows(outputs), output_gate, norm_gain)

time: 319 us -> 151 us (0.47); the launches traced: 314 us -> 150 us
  waiting for transfers between devices: 217 us -> 81.7 us
  matrix products: 55.8 us -> 31.1 us
  between operations: 14 us -> 0.72 us
  starting transfers between devices: 7.25 us -> 17.6 us
  other arithmetic: 10.7 us -> 4.19 us
  local copies, waits for them, and re-layouts: 9.13 us -> 14.3 us
    all_gather x2 -> x0, waiting for transfers between devices: 212 us -> none  [prefix_2(): everything = jax.tree.map(lambda part: lax.all_gather(part, axis), shard)]
    ppermute x0 -> x7, waiting for transfers between devices: none -> 73.3 us  [the longest x6 52.4 us: scan_states(): trans_in, offset_in = lax.ppermute((trans, offset), axis, pairs)]
    dot_general x22 -> x13, matrix products: 34.2 us -> 12.6 us  [product(): return jnp.einsum('hde,hef->hdf', left, right, precision=HIGHEST)]
    ppermute x0 -> x7, starting transfers between devices: none -> 10.4 us  [the longest x6 9 us: scan_states(): trans_in, offset_in = lax.ppermute((trans, offset), axis, pairs)]
    unnamed x26 -> x40, local copies, waits for them, and re-layouts: 2.86 us -> 8.74 us
    ppermute x3 -> x2, waiting for transfers between devices: 4.2 us -> 8.39 us  [from_behind(): lax.ppermute(value, axis, [(source, source + steps) for source in range(f...]
    ppermute x3 -> x2, starting transfers between devices: 7.21 us -> 7.17 us  [from_behind(): lax.ppermute(value, axis, [(source, source + steps) for source in range(f...]
  transfers between devices with their start and end apart: 5 -> 9, of which waited for: 3 -> 8; matrix products, arithmetic and copies ran while one was open for 8% -> 9% of each run, Pallas kernels for 0% -> 0%
where the time goes in v1:
time: 151 us; the launch traced here: 150 us
  waiting for transfers between devices  81.7 us (54%)
  matrix products  31.1 us (21%)
  starting transfers between devices  17.6 us (12%)
  local copies, waits for them, and re-layouts  14.3 us (9%)
  other arithmetic  4.19 us (3%)
    ppermute x6, waiting for transfers between devices, scan_states(): trans_in, offset_in = lax.ppermute((trans, offset), axis, pairs)  52.4 us
    ppermute x1, waiting for transfers between devices, scan_states(): offset_in = lax.ppermute(offset, axis, pairs)  20.9 us
    dot_general x13, matrix products, product(): return jnp.einsum('hde,hef->hdf', left, right, precision=HIGHEST)  12.6 us
    ppermute x6, starting transfers between devices, scan_states(): trans_in, offset_in = lax.ppermute((trans, offset), axis, pairs)  9 us
    unnamed x40, local copies, waits for them, and re-layouts  8.74 us
    ppermute x2, waiting for transfers between devices, from_behind(): lax.ppermute(value, axis, [(source, source + steps) for source in range(f...  8.39 us
    ppermute x2, starting transfers between devices, from_behind(): lax.ppermute(value, axis, [(source, source + steps) for source in range(f...  7.17 us
    dot_general x5, matrix products, unit_lower_inverse(): jnp.einsum('bhij,bhjk->bhik', inverse, power, precision=HIGHEST)  3.33 us
  transfers between devices with their start and end apart: 9, of which 8 were waited for; matrix products, arithmetic and copies ran while one was open for 9% of the time, Pallas kernels for 0%

profile of v1, /device:TPU:28, one launch (start us, length us, event | category | flops | bytes accessed | tf_op | source)
XLA Modules:
  0.0 149.7 jit_solution(10359839021422668549)
XLA Ops:
  4.7 3.4 %collective-permute-start = (f32[3,2048]{1,0:T(4,128)S(1)}, f32[3,2048]{1,0:T(4,128)S(1)}, u32[]{:S(2)}, u32[]{:S(2)}) collective-permute-start(f32[3,2048]{1,0:T(4,128)S(1)} %pad_maximum_fusion.3), channel_id=1, source_target_pairs={{0,2},{2,4},{4,6},{6,8},{8,10},{10,12},{12,14},{14,16},{16,18},{18... | collective-permute-start | bytes 73736 | tf_op jit(solution)/shard_map/ppermute | solution.py:16
  23.5 2.2 %fusion.42 = f32[2,8,128,128]{3,2,1,0:T(8,128)S(1)} fusion(f32[2,8,64,256]{3,2,1,0:T(8,128)S(1)} %fusion.17, f32[2,64,8,128]{3,1,0,2:T(8,128)S(1)} %bitcast.158, f32[2,8,64]{2,1,0:T(8,128)S(1)} %get-tuple-element.103), kind=kOutput, calls=%fused_computation.79 | convolution fusion | flops 201457664 | bytes 2105344 | tf_op jit(solution)/shard_map/bhjd,bhje->bhde/dot_general | solution.py:138
  25.7 2.1 %convolution_subtract_fusion = f32[2,8,128,128]{3,2,1,0:T(8,128)S(1)} fusion(f32[128,128]{1,0:T(8,128)S(1)} %fusion.69, f32[2,8]{1,0:T(2,128)S(1)} %slice_reduce_fusion.1, f32[2,64,8,128]{3,1,0,2:T(8,128)S(1)} %bitcast.159, f32[2,8,64]{2,1,0:T(8,128)S(1)} %get-tuple-element.103, f32[2,8,64,256]{3,2,1,0:T(8,128)S(1)} %fusion.17), kind=kOutput, calls=%fused_computation.17 | convolution fusion | flops 201981952 | bytes 2171904 | tf_op jit(solution)/shard_map/bhjd,bhje->bhde/dot_general | solution.py:135
  27.8 2.9 %while.26 = (s32[]{:T(128)}, f32[8,128,128]{2,1,0:T(8,128)S(1)}, f32[8,128,128]{2,1,0:T(8,128)S(1)}, f32[2,8,128,128]{3,2,1,0:T(8,128)S(1)}, f32[2,8,128,128]{3,2,1,0:T(8,128)S(1)}, /*index=5*/s32[]{:T(128)}, s32[]{:T(128)}) while((s32[]{:T(128)}, f32[8,128,128]{2,1,0:T(8,128)S(1)}, f32[8,128,128]{2,1,0:T(8,128)S(1)}, ...), condition=%wide.region_4.5_spmd.clone, body=%wide.region_3.4_spmd.clone.sunk | while | flops 402915328 | bytes 5768802 | solution.py:161
  30.7 1.9 %collective-permute-start.4 = (f32[8,128,128]{2,1,0:T(8,128)S(1)}, f32[8,128,128]{2,1,0:T(8,128)}, u32[]{:S(2)}, u32[]{:S(2)}) collective-permute-start(f32[8,128,128]{2,1,0:T(8,128)S(1)} %get-tuple-element.61), channel_id=1, source_target_pairs={{0,2},{2,4},{4,6},{6,8},{8,10},{10,12},{12,14},{14,16},{16,18},{18... | collective-permute-start | bytes 1572872 | tf_op jit(solution)/shard_map/ppermute | solution.py:25
  33.6 1.9 %collective-permute-start.1 = (f32[8,128,128]{2,1,0:T(8,128)S(1)}, f32[8,128,128]{2,1,0:T(8,128)}, u32[]{:S(2)}, u32[]{:S(2)}) collective-permute-start(f32[8,128,128]{2,1,0:T(8,128)S(1)} %get-tuple-element.60), channel_id=1, source_target_pairs={{0,2},{2,4},{4,6},{6,8},{8,10},{10,12},{12,14},{14,16},{16,18},{18... | collective-permute-start | bytes 1572872 | tf_op jit(solution)/shard_map/ppermute | solution.py:25
  35.5 12.9 %collective-permute-done.4 = f32[8,128,128]{2,1,0:T(8,128)} collective-permute-done((f32[8,128,128]{2,1,0:T(8,128)S(1)}, f32[8,128,128]{2,1,0:T(8,128)}, u32[]{:S(2)}, u32[]{:S(2)}) %collective-permute-start.4) | collective-permute-done | bytes 524320 | tf_op jit(solution)/shard_map/ppermute | solution.py:25
  48.4 2.5 %convolution_add_fusion.11 = f32[8,128,128]{2,1,0:T(8,128)} fusion(f32[8,128,128]{2,1,0:T(8,128)S(1)} %get-tuple-element.61, f32[8,128,128]{2,1,0:T(8,128)S(1)} %get-tuple-element.60, f32[8,128,128]{2,1,0:T(8,128)} %collective-permute-done.4), kind=kOutput, calls=%fused_computation.31 | convolution fusion | flops 201457664 | bytes 2097152 | tf_op jit(solution)/shard_map/hde,hef->hdf/dot_general | solution.py:143
  52.7 5.6 %collective-permute-done.1 = f32[8,128,128]{2,1,0:T(8,128)} collective-permute-done((f32[8,128,128]{2,1,0:T(8,128)S(1)}, f32[8,128,128]{2,1,0:T(8,128)}, u32[]{:S(2)}, u32[]{:S(2)}) %collective-permute-start.1) | collective-permute-done | bytes 524320 | tf_op jit(solution)/shard_map/ppermute | solution.py:25
  58.3 1.7 %convolution_select_fusion.2 = f32[8,128,128]{2,1,0:T(8,128)S(1)} fusion(f32[8,128,128]{2,1,0:T(8,128)S(1)} %get-tuple-element.60, f32[8,128,128]{2,1,0:T(8,128)} %collective-permute-done.1, pred[]{:T(512)S(6)} %ge.39), kind=kOutput, calls=%fused_computation.20 | convolution fusion | flops 201457664 | bytes 1572865 | tf_op jit(solution)/shard_map/hde,hef->hdf/dot_general | solution.py:143
  60.0 1.3 collective-permute-start.2
  61.3 8.2 %collective-permute-done.5 = f32[8,128,128]{2,1,0:T(8,128)} collective-permute-done((f32[8,128,128]{2,1,0:T(8,128)}, f32[8,128,128]{2,1,0:T(8,128)}, u32[]{:S(2)}, u32[]{:S(2)}) %collective-permute-start.5) | collective-permute-done | bytes 524320 | tf_op jit(solution)/shard_map/ppermute | solution.py:25
  69.5 1.9 %convolution_add_fusion.10 = f32[8,128,128]{2,1,0:T(8,128)S(1)} fusion(f32[8,128,128]{2,1,0:T(8,128)} %convolution_add_fusion.11, f32[8,128,128]{2,1,0:T(8,128)S(1)} %convolution_select_fusion.2, f32[8,128,128]{2,1,0:T(8,128)} %collective-permute-done.5), kind=kOutput, calls=%fused_computation.30 | convolution fusion | flops 201457664 | bytes 2097152 | tf_op jit(solution)/shard_map/hde,hef->hdf/dot_general | solution.py:143
  71.4 1.3 collective-permute-start.6
  73.0 7.6 %collective-permute-done.2 = f32[8,128,128]{2,1,0:T(8,128)S(1)} collective-permute-done((f32[8,128,128]{2,1,0:T(8,128)S(1)}, f32[8,128,128]{2,1,0:T(8,128)S(1)}, u32[]{:S(2)}, u32[]{:S(2)}) %collective-permute-start.2) | collective-permute-done | bytes 524320 | tf_op jit(solution)/shard_map/ppermute | solution.py:25
  82.5 11.6 %collective-permute-done.6 = f32[8,128,128]{2,1,0:T(8,128)S(1)} collective-permute-done((f32[8,128,128]{2,1,0:T(8,128)S(1)}, f32[8,128,128]{2,1,0:T(8,128)S(1)}, u32[]{:S(2)}, u32[]{:S(2)}) %collective-permute-start.6) | collective-permute-done | bytes 524320 | tf_op jit(solution)/shard_map/ppermute | solution.py:25
  94.8 1.4 collective-permute-start.7
  97.2 6.5 %collective-permute-done.3 = f32[8,128,128]{2,1,0:T(8,128)S(1)} collective-permute-done((f32[8,128,128]{2,1,0:T(8,128)S(1)}, f32[8,128,128]{2,1,0:T(8,128)S(1)}, u32[]{:S(2)}, u32[]{:S(2)}) %collective-permute-start.3) | collective-permute-done | bytes 524320 | tf_op jit(solution)/shard_map/ppermute | solution.py:25
  104.4 20.9 %collective-permute-done.7 = f32[8,128,128]{2,1,0:T(8,128)S(1)} collective-permute-done((f32[8,128,128]{2,1,0:T(8,128)S(1)}, f32[8,128,128]{2,1,0:T(8,128)S(1)}, u32[]{:S(2)}, u32[]{:S(2)}) %collective-permute-start.7) | collective-permute-done | bytes 524320 | tf_op jit(solution)/shard_map/ppermute | solution.py:29
  126.0 3.8 %collective-permute-start.8 = (f32[8,128,128]{2,1,0:T(8,128)S(1)}, f32[8,128,128]{2,1,0:T(8,128)S(1)}, u32[]{:S(2)}, u32[]{:S(2)}) collective-permute-start(f32[8,128,128]{2,1,0:T(8,128)S(1)} %convolution_add_fusion.8), channel_id=1, source_target_pairs={{0,2},{2,4},{4,6},{6,8},{8,10},{10,12},{12,14},{14,16},{16,18},{18... | collective-permute-start | bytes 1572872 | tf_op jit(solution)/shard_map/ppermute | solution.py:16
  130.4 1.5 convolution_subtract_fusion.1
  131.9 8.4 %collective-permute-done.8 = f32[8,128,128]{2,1,0:T(8,128)S(1)} collective-permute-done((f32[8,128,128]{2,1,0:T(8,128)S(1)}, f32[8,128,128]{2,1,0:T(8,128)S(1)}, u32[]{:S(2)}, u32[]{:S(2)}) %collective-permute-start.8) | collective-permute-done | bytes 524320 | tf_op jit(solution)/shard_map/ppermute | solution.py:16
  140.3 4.5 %while.25 = (s32[]{:T(128)}, f32[8,128,128]{2,1,0:T(8,128)S(1)}, f32[2,8,128,128]{3,2,1,0:T(8,128)}, f32[2,8,128,128]{3,2,1,0:T(8,128)S(1)}, f32[2,8,128,128]{3,2,1,0:T(8,128)S(1)}, /*index=5*/s32[]{:T(128)}) while((s32[]{:T(128)}, f32[8,128,128]{2,1,0:T(8,128)S(1)}, f32[2,8,128,128]{3,2,1,0:T(8,128)}, f32[2,8,128,128]{3,2,1,0:T(8,128)S(1)}, ...), condition=%wide.region_6.7_spmd, body=%wide.region_5.6_spmd.sunk | while | flops 201457664 | bytes 12584073 | solution.py:170
  144.8 2.5 %multiply_reduce_fusion = (f32[2,64,8]{1,2,0:T(8,128)S(1)}, f32[2,64,8,128]{3,1,2,0:T(8,128)S(1)}) fusion(f32[2,8,64,128]{3,2,1,0:T(8,128)S(1)} %fusion.44, f32[2,8,128,128]{3,2,1,0:T(8,128)} %get-tuple-element.62, f32[2,8,64,128]{3,2,0,1:T(8,128)} %convolution_subtract_fusion.1), kind=kOutput, calls=%fused_computation.74 | convolution fusion | flops 201718784 | bytes 2625536 | tf_op jit(solution)/shard_map/bhid,bhde->bhie/dot_general | solution.py:255
  (148 shorter events, 37.9 us)
Async XLA Ops:
  0.0 32.6 %copy-start = (f32[128]{0:T(128)S(1)}, f32[128]{0:T(128)}, u32[]{:S(2)}) copy-start(f32[128]{0:T(128)} %param.33) | copy-start | bytes 1540
  0.0 2.4 %copy-start.9 = (bf16[128,512]{1,0:T(8,128)(2,1)S(1)}, bf16[128,512]{1,0:T(8,128)(2,1)}, u32[]{:S(2)}) copy-start(bf16[128,512]{1,0:T(8,128)(2,1)} %param.19) | copy-start | bytes 393220
  2.4 0.9 copy-start.8
  3.3 0.9 copy-start.5
  4.7 8.4 %collective-permute-start = (f32[3,2048]{1,0:T(4,128)S(1)}, f32[3,2048]{1,0:T(4,128)S(1)}, u32[]{:S(2)}, u32[]{:S(2)}) collective-permute-start(f32[3,2048]{1,0:T(4,128)S(1)} %pad_maximum_fusion.3), channel_id=1, source_target_pairs={{0,2},{2,4},{4,6},{6,8},{8,10},{10,12},{12,14},{14,16},{16,18},{18... | collective-permute-start | bytes 73736 | tf_op jit(solution)/shard_map/ppermute | solution.py:16
  8.2 1.4 copy-start.15
  11.5 0.7 copy-start.11
  14.6 11.1 %copy-start.1 = (f32[128,4,2,128]{3,0,2,1:T(8,128)}, f32[128,4,2,128]{3,0,2,1:T(8,128)S(1)}, u32[]{:S(2)}) copy-start(f32[128,4,2,128]{3,0,2,1:T(8,128)S(1)} %broadcast_in_dim.30) | copy-start | bytes 1572868
  23.5 2.2 %copy-start.3 = (f32[2,8,64,256]{3,2,1,0:T(8,128)}, f32[2,8,64,256]{3,2,1,0:T(8,128)S(1)}, u32[]{:S(2)}) copy-start(f32[2,8,64,256]{3,2,1,0:T(8,128)S(1)} %fusion.17) | copy-start | bytes 3145732
  30.7 17.7 %collective-permute-start.4 = (f32[8,128,128]{2,1,0:T(8,128)S(1)}, f32[8,128,128]{2,1,0:T(8,128)}, u32[]{:S(2)}, u32[]{:S(2)}) collective-permute-start(f32[8,128,128]{2,1,0:T(8,128)S(1)} %get-tuple-element.61), channel_id=1, source_target_pairs={{0,2},{2,4},{4,6},{6,8},{8,10},{10,12},{12,14},{14,16},{16,18},{18... | collective-permute-start | bytes 1572872 | tf_op jit(solution)/shard_map/ppermute | solution.py:25
  33.6 24.7 %collective-permute-start.1 = (f32[8,128,128]{2,1,0:T(8,128)S(1)}, f32[8,128,128]{2,1,0:T(8,128)}, u32[]{:S(2)}, u32[]{:S(2)}) collective-permute-start(f32[8,128,128]{2,1,0:T(8,128)S(1)} %get-tuple-element.60), channel_id=1, source_target_pairs={{0,2},{2,4},{4,6},{6,8},{8,10},{10,12},{12,14},{14,16},{16,18},{18... | collective-permute-start | bytes 1572872 | tf_op jit(solution)/shard_map/ppermute | solution.py:25
  50.9 18.6 %collective-permute-start.5 = (f32[8,128,128]{2,1,0:T(8,128)}, f32[8,128,128]{2,1,0:T(8,128)}, u32[]{:S(2)}, u32[]{:S(2)}) collective-permute-start(f32[8,128,128]{2,1,0:T(8,128)} %convolution_add_fusion.11), channel_id=1, source_target_pairs={{0,4},{2,6},{4,8},{6,10},{8,12},{10,14},{12,16},{14,18},{16,20},{1... | collective-permute-start | bytes 1572872 | tf_op jit(solution)/shard_map/ppermute | solution.py:25
  60.0 20.6 %collective-permute-start.2 = (f32[8,128,128]{2,1,0:T(8,128)S(1)}, f32[8,128,128]{2,1,0:T(8,128)S(1)}, u32[]{:S(2)}, u32[]{:S(2)}) collective-permute-start(f32[8,128,128]{2,1,0:T(8,128)S(1)} %convolution_select_fusion.2), channel_id=1, source_target_pairs={{0,4},{2,6},{4,8},{6,10},{8,12},{10,14},{12,16},{14,18},{16,20},{1... | collective-permute-start | bytes 1572872 | tf_op jit(solution)/shard_map/ppermute | solution.py:25
  71.4 22.7 %collective-permute-start.6 = (f32[8,128,128]{2,1,0:T(8,128)S(1)}, f32[8,128,128]{2,1,0:T(8,128)S(1)}, u32[]{:S(2)}, u32[]{:S(2)}) collective-permute-start(f32[8,128,128]{2,1,0:T(8,128)S(1)} %convolution_add_fusion.10), channel_id=1, source_target_pairs={{0,8},{2,10},{4,12},{6,14},{8,16},{10,18},{12,20},{14,22},{16,24},... | collective-permute-start | bytes 1572872 | tf_op jit(solution)/shard_map/ppermute | solution.py:25
  81.2 22.5 %collective-permute-start.3 = (f32[8,128,128]{2,1,0:T(8,128)S(1)}, f32[8,128,128]{2,1,0:T(8,128)S(1)}, u32[]{:S(2)}, u32[]{:S(2)}) collective-permute-start(f32[8,128,128]{2,1,0:T(8,128)S(1)} %convolution_select_fusion.1), channel_id=1, source_target_pairs={{0,8},{2,10},{4,12},{6,14},{8,16},{10,18},{12,20},{14,22},{16,24},... | collective-permute-start | bytes 1572872 | tf_op jit(solution)/shard_map/ppermute | solution.py:25
  94.8 1.5 copy-start.2
  94.8 30.5 %collective-permute-start.7 = (f32[8,128,128]{2,1,0:T(8,128)S(1)}, f32[8,128,128]{2,1,0:T(8,128)S(1)}, u32[]{:S(2)}, u32[]{:S(2)}) collective-permute-start(f32[8,128,128]{2,1,0:T(8,128)S(1)} %convolution_add_fusion.9), channel_id=1, source_target_pairs={{0,16},{2,18},{4,20},{6,22},{8,24},{10,26},{12,28},{14,30},{1,17},... | collective-permute-start | bytes 1572872 | tf_op jit(solution)/shard_map/ppermute | solution.py:29
  104.4 25.3 %copy-start.4 = (f32[2,8,64,256]{3,2,1,0:T(8,128)S(1)}, f32[2,8,64,256]{3,2,1,0:T(8,128)}, u32[]{:S(2)}) copy-start(f32[2,8,64,256]{3,2,1,0:T(8,128)} %copy-done.3) | copy-start | bytes 3145732
  126.0 14.3 %collective-permute-start.8 = (f32[8,128,128]{2,1,0:T(8,128)S(1)}, f32[8,128,128]{2,1,0:T(8,128)S(1)}, u32[]{:S(2)}, u32[]{:S(2)}) collective-permute-start(f32[8,128,128]{2,1,0:T(8,128)S(1)} %convolution_add_fusion.8), channel_id=1, source_target_pairs={{0,2},{2,4},{4,6},{6,8},{8,10},{10,12},{12,14},{14,16},{16,18},{18... | collective-permute-start | bytes 1572872 | tf_op jit(solution)/shard_map/ppermute | solution.py:16
  140.3 1.2 copy-start.6
  141.6 1.0 copy-start.7
  142.5 1.2 copy-start.6
  143.8 1.0 copy-start.7
  147.7 1.0 copy-start.10
  (6 other events, 4.1 us)

commit v2 on v1

--- a/solution.py
+++ b/solution.py
@@ -16,20 +16,36 @@
     return lax.ppermute(value, axis, [(source, source + steps) for source in range(first, last)])
 
 
+def compose(later, earlier, width):
+    merged = jnp.einsum("hde,hef->hdf", later[..., :width], earlier, precision=HIGHEST)
+    return merged.at[..., width:].add(later[..., width:])
+
+
 def scan_states(trans, offset, axis):
     devices, mine = (lax.axis_size(axis), lax.axis_index(axis))
+    width = trans.shape[-1]
+    inclusive = jnp.concatenate([trans, offset], axis=-1)
+    exclusive = None
+    state = jnp.zeros_like(offset)
     span = 1
     while span < devices:
         pairs = [(source, source + span) for source in range(devices - span)]
-        if 2 * span < devices:
-            trans_in, offset_in = lax.ppermute((trans, offset), axis, pairs)
-            offset = product(trans, offset_in) + offset
-            trans = jnp.where(mine >= span, product(trans, trans_in), trans)
+        if 2 * span >= devices:
+            earlier_state = lax.ppermute(inclusive[..., width:], axis, pairs)
+            if exclusive is None:
+                state = earlier_state
+            else:
+                state = state + product(exclusive[..., :width], earlier_state)
+            break
+        earlier = lax.ppermute(inclusive, axis, pairs)
+        exclusive = earlier if exclusive is None else compose(exclusive, earlier, width)
+        state = exclusive[..., width:]
+        if 4 * span < devices:
+            inclusive = jnp.where(mine >= span, compose(inclusive, earlier, width), inclusive)
         else:
-            offset_in = lax.ppermute(offset, axis, pairs)
-            offset = product(trans, offset_in) + offset
+            inclusive = inclusive.at[..., width:].add(product(inclusive[..., :width], earlier[..., width:]))
         span = span * 2
-    return from_behind(offset, axis, 1)
+    return state
 
 
 def expand_quantized(raw_rows, scales):

time: 151 us -> 156 us (1.033)
  starting transfers between devices: 17.6 us -> 9.41 us
  waiting for transfers between devices: 81.7 us -> 86.6 us
  local copies, waits for them, and re-layouts: 14.3 us -> 18.8 us
  matrix products: 31.1 us -> 32.8 us
    ppermute x7 -> x4, waiting for transfers between devices: 73.3 us -> 86.6 us  [the longest x3 67 us: scan_states(): earlier = lax.ppermute(inclusive, axis, pairs)]
    ppermute x2 -> x1, waiting for transfers between devices: 8.39 us -> 0.01 us  [from_behind(): lax.ppermute(value, axis, [(source, source + steps) for source in range(f...]
    dot_general x0 -> x4, matrix products: none -> 7.9 us  [compose(): jnp.einsum('hde,hef->hdf', later[..., :width], earlier, precision=HIGHEST)]
    dot_general x13 -> x8, matrix products: 12.6 us -> 6.36 us  [product(): return jnp.einsum('hde,hef->hdf', left, right, precision=HIGHEST)]
    ppermute x7 -> x4, starting transfers between devices: 10.4 us -> 6.01 us  [the longest x3 4.49 us: scan_states(): earlier = lax.ppermute(inclusive, axis, pairs)]
    ppermute x2 -> x1, starting transfers between devices: 7.17 us -> 3.4 us  [from_behind(): lax.ppermute(value, axis, [(source, source + steps) for source in range(f...]
    unnamed x40 -> x51, local copies, waits for them, and re-layouts: 8.74 us -> 8.97 us
  transfers between devices with their start and end apart: 9 -> 5, of which waited for: 8 -> 4; matrix products, arithmetic and copies ran while one was open for 9% -> 7% of each run, Pallas kernels for 0% -> 0%
where the time goes in v2:
time: 156 us; the launch traced here: 153 us
  waiting for transfers between devices  86.6 us (56%)
  matrix products  32.8 us (21%)
  local copies, waits for them, and re-layouts  18.8 us (12%)
  starting transfers between devices  9.41 us (6%)
  other arithmetic  4.78 us (3%)
    ppermute x3, waiting for transfers between devices, scan_states(): earlier = lax.ppermute(inclusive, axis, pairs)  67 us
    ppermute x1, waiting for transfers between devices, scan_states(): earlier_state = lax.ppermute(inclusive[..., width:], axis, pairs)  19.6 us
    unnamed x51, local copies, waits for them, and re-layouts  8.97 us
    dot_general x4, matrix products, compose(): jnp.einsum('hde,hef->hdf', later[..., :width], earlier, precision=HIGHEST)  7.9 us
    dot_general x8, matrix products, product(): return jnp.einsum('hde,hef->hdf', left, right, precision=HIGHEST)  6.36 us
    while x14, local copies, waits for them, and re-layouts  4.5 us
    ppermute x3, starting transfers between devices, scan_states(): earlier = lax.ppermute(inclusive, axis, pairs)  4.49 us
    ppermute x1, starting transfers between devices, from_behind(): lax.ppermute(value, axis, [(source, source + steps) for source in range(f...  3.4 us
  transfers between devices with their start and end apart: 5, of which 4 were waited for; matrix products, arithmetic and copies ran while one was open for 7% of the time, Pallas kernels for 0%

profile of v2, /device:TPU:28, one launch (start us, length us, event | category | flops | bytes accessed | tf_op | source)
XLA Modules:
  0.0 153.3 jit_solution(5990257870311468419)
XLA Ops:
  0.8 1.0 reshape.253
  3.2 3.4 %collective-permute-start = (f32[3,2048]{1,0:T(4,128)S(1)}, f32[3,2048]{1,0:T(4,128)S(1)}, u32[]{:S(2)}, u32[]{:S(2)}) collective-permute-start(f32[3,2048]{1,0:T(4,128)S(1)} %pad_maximum_fusion.3), channel_id=1, source_target_pairs={{0,2},{2,4},{4,6},{6,8},{8,10},{10,12},{12,14},{14,16},{16,18},{18... | collective-permute-start | bytes 73736 | tf_op jit(solution)/shard_map/ppermute | solution.py:16
  22.4 1.0 fusion.17
  23.4 2.2 %fusion.57 = f32[2,8,128,128]{3,2,1,0:T(8,128)S(1)} fusion(f32[2,8,64,256]{3,2,1,0:T(8,128)S(1)} %fusion.17, f32[2,64,8,128]{3,1,0,2:T(8,128)S(1)} %bitcast.150, f32[2,8,64]{2,1,0:T(8,128)S(1)} %get-tuple-element.163), kind=kOutput, calls=%fused_computation.93 | convolution fusion | flops 201457664 | bytes 2105344 | tf_op jit(solution)/shard_map/bhjd,bhje->bhde/dot_general | solution.py:154
  25.6 2.1 %convolution_subtract_fusion = f32[2,8,128,128]{3,2,1,0:T(8,128)S(1)} fusion(f32[128,128]{1,0:T(8,128)S(1)} %fusion.84, f32[2,8]{1,0:T(2,128)S(1)} %slice_reduce_fusion.1, f32[2,64,8,128]{3,1,0,2:T(8,128)S(1)} %bitcast.151, f32[2,8,64]{2,1,0:T(8,128)S(1)} %get-tuple-element.163, f32[2,8,64,256]{3,2,1,0:T(8,128)S(1)} %fusion.17), kind=kOutput, calls=%fused_computation.17 | convolution fusion | flops 201981952 | bytes 2171904 | tf_op jit(solution)/shard_map/bhjd,bhje->bhde/dot_general | solution.py:151
  27.7 2.9 %while.31 = (s32[]{:T(128)}, f32[8,128,128]{2,1,0:T(8,128)S(1)}, f32[8,128,128]{2,1,0:T(8,128)S(1)}, f32[2,8,128,128]{3,2,1,0:T(8,128)S(1)}, f32[2,8,128,128]{3,2,1,0:T(8,128)S(1)}, /*index=5*/s32[]{:T(128)}, s32[]{:T(128)}) while((s32[]{:T(128)}, f32[8,128,128]{2,1,0:T(8,128)S(1)}, f32[8,128,128]{2,1,0:T(8,128)S(1)}, ...), condition=%wide.region_4.5_spmd.clone, body=%wide.region_3.4_spmd.clone.sunk | while | flops 402915328 | bytes 5768283 | solution.py:177
  32.3 1.9 %collective-permute-start.1 = (f32[8,128,256]{2,1,0:T(8,128)}, f32[8,128,256]{2,1,0:T(8,128)}, u32[]{:S(2)}, u32[]{:S(2)}) collective-permute-start(f32[8,128,256]{2,1,0:T(8,128)} %constant_dynamic-update-slice_fusion), channel_id=1, source_target_pairs={{0,2},{2,4},{4,6},{6,8},{8,10},{10,12},{12,14},{14,16},{16,18},{18... | collective-permute-start | bytes 3145736 | tf_op jit(solution)/shard_map/ppermute | solution.py:40
  34.8 25.2 %collective-permute-done.1 = f32[8,128,256]{2,1,0:T(8,128)} collective-permute-done((f32[8,128,256]{2,1,0:T(8,128)}, f32[8,128,256]{2,1,0:T(8,128)}, u32[]{:S(2)}, u32[]{:S(2)}) %collective-permute-start.1) | collective-permute-done | bytes 1048608 | tf_op jit(solution)/shard_map/ppermute | solution.py:40
  60.0 2.2 %fusion.99 = f32[8,128,256]{2,1,0:T(8,128)S(1)} fusion(f32[8,128,128]{2,1,0:T(8,128)S(1)} %get-tuple-element.120, f32[8,128,256]{2,1,0:T(8,128)} %collective-permute-done.1), kind=kOutput, calls=%fused_computation.190 | convolution fusion | flops 402653184 | bytes 2621440 | tf_op jit(solution)/shard_map/hde,hef->hdf/dot_general | solution.py:20
  62.6 1.3 collective-permute-start.2
  65.4 22.9 %collective-permute-done.2 = f32[8,128,256]{2,1,0:T(8,128)} collective-permute-done((f32[8,128,256]{2,1,0:T(8,128)S(1)}, f32[8,128,256]{2,1,0:T(8,128)}, u32[]{:S(2)}, u32[]{:S(2)}) %collective-permute-start.2) | collective-permute-done | bytes 1048608 | tf_op jit(solution)/shard_map/ppermute | solution.py:40
  88.4 2.2 %fusion.41 = f32[8,128,256]{2,1,0:T(8,128)S(1)} fusion(f32[8,128,256]{2,1,0:T(8,128)} %collective-permute-done.2, f32[8,128,256]{2,1,0:T(8,128)S(1)} %broadcast_select_fusion.1), kind=kOutput, calls=%fused_computation.66 | convolution fusion | flops 402653184 | bytes 2621440 | tf_op jit(solution)/shard_map/hde,hef->hdf/dot_general | solution.py:20
  90.9 1.3 collective-permute-start.3
  95.2 1.5 convolution_subtract_fusion.1
  96.7 18.9 %collective-permute-done.3 = f32[8,128,256]{2,1,0:T(8,128)S(1)} collective-permute-done((f32[8,128,256]{2,1,0:T(8,128)S(1)}, f32[8,128,256]{2,1,0:T(8,128)S(1)}, u32[]{:S(2)}, u32[]{:S(2)}) %collective-permute-start.3) | collective-permute-done | bytes 1048608 | tf_op jit(solution)/shard_map/ppermute | solution.py:40
  116.2 1.5 collective-permute-start.4
  117.8 2.4 %fusion.46 = f32[8,128,256]{2,1,0:T(8,128)S(1)} fusion(f32[8,128,256]{2,1,0:T(8,128)} %collective-permute-done.2, f32[8,128,256]{2,1,0:T(8,128)} %collective-permute-done.1), kind=kOutput, calls=%fused_computation.72 | convolution fusion | flops 402653184 | bytes 2621440 | tf_op jit(solution)/shard_map/hde,hef->hdf/dot_general | solution.py:20
  120.2 1.0 fusion.43
  121.2 19.6 %collective-permute-done.4 = f32[8,128,128]{2,1,0:T(8,128)S(1)} collective-permute-done((f32[8,128,128]{2,1,0:T(8,128)S(1)}, f32[8,128,128]{2,1,0:T(8,128)S(1)}, u32[]{:S(2)}, u32[]{:S(2)}) %collective-permute-start.4) | collective-permute-done | bytes 524320 | tf_op jit(solution)/shard_map/ppermute | solution.py:34
  140.8 1.8 %fusion.39 = f32[8,128,128]{2,1,0:T(8,128)S(1)} fusion(f32[8,128,256]{2,1,0:T(8,128)} %collective-permute-done.1, f32[8,128,256]{2,1,0:T(8,128)S(1)} %fusion.46, f32[8,128,256]{2,1,0:T(8,128)S(1)} %fusion.43, f32[8,128,128]{2,1,0:T(8,128)S(1)} %collective-permute-done.4), kind=kOutput, calls=%fused_computation.63 | convolution fusion | flops 201719808 | bytes 3145728 | tf_op jit(solution)/shard_map/hde,hef->hdf/dot_general | solution.py:159
  142.5 5.8 %while.30 = (s32[]{:T(128)}, f32[8,128,128]{2,1,0:T(8,128)S(1)}, f32[2,8,128,128]{3,2,1,0:T(8,128)}, f32[2,8,128,128]{3,2,1,0:T(8,128)S(1)}, f32[2,8,128,128]{3,2,1,0:T(8,128)S(1)}, /*index=5*/s32[]{:T(128)}) while((s32[]{:T(128)}, f32[8,128,128]{2,1,0:T(8,128)S(1)}, f32[2,8,128,128]{3,2,1,0:T(8,128)}, f32[2,8,128,128]{3,2,1,0:T(8,128)S(1)}, ...), condition=%wide.region_6.7_spmd, body=%wide.region_5.6_spmd.sunk | while | flops 201457664 | bytes 12584065 | solution.py:186
  142.6 1.2 copy-done.6
  145.5 1.2 copy-done.6
  148.4 2.5 %multiply_reduce_fusion = (f32[2,64,8]{1,2,0:T(8,128)S(1)}, f32[2,64,8,128]{3,1,2,0:T(8,128)S(1)}) fusion(f32[2,8,64,128]{3,2,1,0:T(8,128)S(1)} %fusion.59, f32[2,8,128,128]{3,2,1,0:T(8,128)} %get-tuple-element.122, f32[2,8,64,128]{3,2,0,1:T(8,128)} %convolution_subtract_fusion.1), kind=kOutput, calls=%fused_computation.86 | convolution fusion | flops 201718784 | bytes 2625536 | tf_op jit(solution)/shard_map/bhid,bhde->bhie/dot_general | solution.py:271
  (155 shorter events, 34.0 us)
Async XLA Ops:
  0.0 63.9 %copy-start = (f32[128]{0:T(128)S(1)}, f32[128]{0:T(128)}, u32[]{:S(2)}) copy-start(f32[128]{0:T(128)} %param.43) | copy-start | bytes 1540
  0.8 1.1 copy-start.21
  0.8 1.2 copy-start.9
  1.9 1.0 copy-start.5
  3.2 9.1 %collective-permute-start = (f32[3,2048]{1,0:T(4,128)S(1)}, f32[3,2048]{1,0:T(4,128)S(1)}, u32[]{:S(2)}, u32[]{:S(2)}) collective-permute-start(f32[3,2048]{1,0:T(4,128)S(1)} %pad_maximum_fusion.3), channel_id=1, source_target_pairs={{0,2},{2,4},{4,6},{6,8},{8,10},{10,12},{12,14},{14,16},{16,18},{18... | collective-permute-start | bytes 73736 | tf_op jit(solution)/shard_map/ppermute | solution.py:16
  6.7 7.1 %copy-start.11 = (pred[64,64]{1,0:T(8,128)(4,1)}, pred[64,64]{1,0:T(8,128)(4,1)S(1)}, u32[]{:S(2)}) copy-start(pred[64,64]{1,0:T(8,128)(4,1)S(1)} %get-tuple-element.183) | copy-start | bytes 12292
  7.4 0.9 copy-start.8
  8.3 1.4 copy-start.19
  9.8 0.7 copy-start.20
  11.1 0.7 copy-start.14
  13.8 11.8 %copy-start.1 = (f32[128,4,2,128]{3,0,2,1:T(8,128)}, f32[128,4,2,128]{3,0,2,1:T(8,128)S(1)}, u32[]{:S(2)}) copy-start(f32[128,4,2,128]{3,0,2,1:T(8,128)S(1)} %broadcast_in_dim.30) | copy-start | bytes 1572868
  23.4 2.2 %copy-start.3 = (f32[2,8,64,256]{3,2,1,0:T(8,128)}, f32[2,8,64,256]{3,2,1,0:T(8,128)S(1)}, u32[]{:S(2)}) copy-start(f32[2,8,64,256]{3,2,1,0:T(8,128)S(1)} %fusion.17) | copy-start | bytes 3145732
  32.3 27.7 %collective-permute-start.1 = (f32[8,128,256]{2,1,0:T(8,128)}, f32[8,128,256]{2,1,0:T(8,128)}, u32[]{:S(2)}, u32[]{:S(2)}) collective-permute-start(f32[8,128,256]{2,1,0:T(8,128)} %constant_dynamic-update-slice_fusion), channel_id=1, source_target_pairs={{0,2},{2,4},{4,6},{6,8},{8,10},{10,12},{12,14},{14,16},{16,18},{18... | collective-permute-start | bytes 3145736 | tf_op jit(solution)/shard_map/ppermute | solution.py:40
  62.6 1.3 copy-start.17
  62.6 25.7 %collective-permute-start.2 = (f32[8,128,256]{2,1,0:T(8,128)S(1)}, f32[8,128,256]{2,1,0:T(8,128)}, u32[]{:S(2)}, u32[]{:S(2)}) collective-permute-start(f32[8,128,256]{2,1,0:T(8,128)S(1)} %broadcast_select_fusion.1), channel_id=1, source_target_pairs={{0,4},{2,6},{4,8},{6,10},{8,12},{10,14},{12,16},{14,18},{16,20},{1... | collective-permute-start | bytes 3145736 | tf_op jit(solution)/shard_map/ppermute | solution.py:40
  90.9 24.7 %collective-permute-start.3 = (f32[8,128,256]{2,1,0:T(8,128)S(1)}, f32[8,128,256]{2,1,0:T(8,128)S(1)}, u32[]{:S(2)}, u32[]{:S(2)}) collective-permute-start(f32[8,128,256]{2,1,0:T(8,128)S(1)} %broadcast_select_fusion), channel_id=1, source_target_pairs={{0,8},{2,10},{4,12},{6,14},{8,16},{10,18},{12,20},{14,22},{16,24},... | collective-permute-start | bytes 3145736 | tf_op jit(solution)/shard_map/ppermute | solution.py:40
  92.4 1.0 copy-start.2
  92.5 2.0 %copy-start.4 = (f32[2,8,64,256]{3,2,1,0:T(8,128)S(1)}, f32[2,8,64,256]{3,2,1,0:T(8,128)}, u32[]{:S(2)}) copy-start(f32[2,8,64,256]{3,2,1,0:T(8,128)} %copy-done.3) | copy-start | bytes 3145732
  116.2 24.5 %collective-permute-start.4 = (f32[8,128,128]{2,1,0:T(8,128)S(1)}, f32[8,128,128]{2,1,0:T(8,128)S(1)}, u32[]{:S(2)}, u32[]{:S(2)}) collective-permute-start(f32[8,128,128]{2,1,0:T(8,128)S(1)} %slice_add_fusion), channel_id=1, source_target_pairs={{0,16},{2,18},{4,20},{6,22},{8,24},{10,26},{12,28},{14,30},{1,17},... | collective-permute-start | bytes 1572872 | tf_op jit(solution)/shard_map/ppermute | solution.py:34
  142.6 1.2 copy-start.6
  143.8 1.0 copy-start.7
  145.5 1.2 copy-start.6
  146.8 1.0 copy-start.7
  151.4 1.0 copy-start.10
  (7 other events, 4.8 us)

commit v3 on v1

--- a/solution.py
+++ b/solution.py
@@ -18,18 +18,31 @@
 
 def scan_states(trans, offset, axis):
     devices, mine = (lax.axis_size(axis), lax.axis_index(axis))
+    spans = []
     span = 1
     while span < devices:
+        spans.append(span)
+        span = span * 2
+    inclusive_maps, exclusive_maps = ([], [None])
+    inclusive = trans
+    for span in spans[:-1]:
         pairs = [(source, source + span) for source in range(devices - span)]
-        if 2 * span < devices:
-            trans_in, offset_in = lax.ppermute((trans, offset), axis, pairs)
-            offset = product(trans, offset_in) + offset
-            trans = jnp.where(mine >= span, product(trans, trans_in), trans)
-        else:
-            offset_in = lax.ppermute(offset, axis, pairs)
-            offset = product(trans, offset_in) + offset
-        span = span * 2
-    return from_behind(offset, axis, 1)
+        inclusive_maps.append(inclusive)
+        earlier = lax.ppermute(inclusive, axis, pairs)
+        last_map = exclusive_maps[-1]
+        exclusive_maps.append(earlier if last_map is None else product(last_map, earlier))
+        if 4 * span < devices:
+            inclusive = jnp.where(mine >= span, product(inclusive, earlier), inclusive)
+    state = jnp.zeros_like(offset)
+    carried = offset
+    for step, span in enumerate(spans):
+        pairs = [(source, source + span) for source in range(devices - span)]
+        earlier = lax.ppermute(carried, axis, pairs)
+        last_map = exclusive_maps[step]
+        state = earlier if last_map is None else state + product(last_map, earlier)
+        if step + 1 < len(spans):
+            carried = product(inclusive_maps[step], earlier) + carried
+    return state
 
 
 def expand_quantized(raw_rows, scales):
@@ -143,40 +156,6 @@
     return jnp.einsum("hde,hef->hdf", left, right, precision=HIGHEST)
 
 
-def chain_blocks(transition, offset):
-    head_count = offset.shape[1]
-    key_width = offset.shape[2]
-    value_width = offset.shape[3]
-    initial = (
-        jnp.zeros((head_count, key_width, value_width), jnp.float32),
-        jnp.broadcast_to(jnp.eye(key_width, dtype=jnp.float32), (head_count, key_width, key_width)),
-    )
-
-    def chain_advance(carried, block_items):
-        state_now, map_now = carried
-        trans_now, offset_now = block_items
-        following = (product(trans_now, state_now) + offset_now, product(trans_now, map_now))
-        return (following, ())
-
-    return lax.scan(chain_advance, initial, (transition, offset))
-
-
-def replay_blocks(transition, offset, incoming):
-
-    def replay_advance(state_now, block_items):
-        trans_now, offset_now = block_items
-        return (product(trans_now, state_now) + offset_now, state_now)
-
-    _, starts = lax.scan(replay_advance, incoming, (transition, offset))
-    return starts
-
-
-def combine_maps(earlier, later):
-    trans_early, offset_early = earlier
-    trans_late, offset_late = later
-    return (product(trans_late, trans_early), product(trans_late, offset_early) + offset_late)
-
-
 def to_rows(blocks):
     return blocks.transpose(0, 2, 1, 3).reshape(-1, blocks.shape[1], blocks.shape[3])
 
@@ -186,13 +165,6 @@
     normed = delta_rows * lax.rsqrt(meansq + EPSILON) * norm_gain
     gate_float = gate_raw.astype(jnp.float32).reshape(delta_rows.shape)
     return (normed * jax.nn.silu(gate_float)).reshape(delta_rows.shape[0], -1).astype(jnp.bfloat16)
-
-
-def identity_of(trans_like, offset_like):
-    return (
-        jnp.broadcast_to(jnp.eye(trans_like.shape[1], dtype=jnp.float32), trans_like.shape),
-        jnp.zeros_like(offset_like),
-    )
 
 
 def shards(
@@ -248,11 +220,20 @@
             CH,
         )
     )
-    finals, emitted = chain_blocks(transition, offset)
-    dev_offset, dev_trans = finals
+    dev_trans, dev_offset = (transition[0], offset[0])
+    local_outs, read_maps = ([zero_out[0]], [readout[0]])
+    for block in range(1, transition.shape[0]):
+        read_maps.append(jnp.einsum("hid,hde->hie", readout[block], dev_trans, precision=HIGHEST))
+        local_outs.append(
+            zero_out[block]
+            + jnp.einsum("hid,hde->hie", readout[block], dev_offset, precision=HIGHEST)
+        )
+        dev_offset = product(transition[block], dev_offset) + offset[block]
+        dev_trans = product(transition[block], dev_trans)
     incoming = scan_states(dev_trans, dev_offset, "seq")
-    starts = replay_blocks(transition, offset, incoming)
-    outputs = zero_out + jnp.einsum("bhid,bhde->bhie", readout, starts, precision=HIGHEST)
+    outputs = jnp.stack(local_outs) + jnp.einsum(
+        "bhid,hde->bhie", jnp.stack(read_maps), incoming, precision=HIGHEST
+    )
     gated_rows = gated_norm(to_rows(outputs), output_gate, norm_gain)
     return gated_rows
 

time: 151 us -> 133 us (0.88)
  matrix products: 31.1 us -> 24.7 us
  waiting for transfers between devices: 81.7 us -> 76.2 us
  starting transfers between devices: 17.6 us -> 13.9 us
  local copies, waits for them, and re-layouts: 14.3 us -> 10.7 us
    ppermute x2 -> x1, waiting for transfers between devices: 8.39 us -> 0.01 us  [from_behind(): lax.ppermute(value, axis, [(source, source + steps) for source in range(f...]
    dot_general x13 -> x12, matrix products: 12.6 us -> 7.79 us  [product(): return jnp.einsum('hde,hef->hdf', left, right, precision=HIGHEST)]
    ppermute x2 -> x1, starting transfers between devices: 7.17 us -> 3.4 us  [from_behind(): lax.ppermute(value, axis, [(source, source + steps) for source in range(f...]
    while x14 -> x0, local copies, waits for them, and re-layouts: 3.19 us -> none
    ppermute x7, waiting for transfers between devices: 73.3 us -> 76.2 us  [the longest x4 52.1 us: scan_states(): earlier = lax.ppermute(carried, axis, pairs)]
    unnamed x40 -> x36, local copies, waits for them, and re-layouts: 8.74 us -> 8.12 us
  transfers between devices with their start and end apart: 9 -> 8, of which waited for: 8 -> 7; matrix products, arithmetic and copies ran while one was open for 9% -> 7% of each run, Pallas kernels for 0% -> 0%
where the time goes in v3:
time: 133 us; the launch traced here: 130 us
  waiting for transfers between devices  76.2 us (57%)
  matrix products  24.7 us (19%)
  starting transfers between devices  13.9 us (10%)
  local copies, waits for them, and re-layouts  10.7 us (8%)
  other arithmetic  4.18 us (3%)
    ppermute x4, waiting for transfers between devices, scan_states(): earlier = lax.ppermute(carried, axis, pairs)  52.1 us
    ppermute x3, waiting for transfers between devices, scan_states(): earlier = lax.ppermute(inclusive, axis, pairs)  24.1 us
    unnamed x36, local copies, waits for them, and re-layouts  8.12 us
    dot_general x12, matrix products, product(): return jnp.einsum('hde,hef->hdf', left, right, precision=HIGHEST)  7.79 us
    ppermute x4, starting transfers between devices, scan_states(): earlier = lax.ppermute(carried, axis, pairs)  5.8 us
    ppermute x3, starting transfers between devices, scan_states(): earlier = lax.ppermute(inclusive, axis, pairs)  4.73 us
    ppermute x1, starting transfers between devices, from_behind(): lax.ppermute(value, axis, [(source, source + steps) for source in range(f...  3.4 us
    dot_general x5, matrix products, unit_lower_inverse(): jnp.einsum('bhij,bhjk->bhik', inverse, power, precision=HIGHEST)  3.24 us
  transfers between devices with their start and end apart: 8, of which 7 were waited for; matrix products, arithmetic and copies ran while one was open for 7% of the time, Pallas kernels for 0%

profile of v3, /device:TPU:28, one launch (start us, length us, event | category | flops | bytes accessed | tf_op | source)
XLA Modules:
  0.0 130.4 jit_solution(6386586529135678160)
XLA Ops:
  0.0 0.8 copy.47
  2.5 0.8 copy-done.4
  3.4 0.9 copy-done.3
  4.7 3.4 %collective-permute-start = (f32[3,2048]{1,0:T(4,128)S(1)}, f32[3,2048]{1,0:T(4,128)S(1)}, u32[]{:S(2)}, u32[]{:S(2)}) collective-permute-start(f32[3,2048]{1,0:T(4,128)S(1)} %pad_maximum_fusion.3), channel_id=1, source_target_pairs={{0,2},{2,4},{4,6},{6,8},{8,10},{10,12},{12,14},{14,16},{16,18},{18... | collective-permute-start | bytes 73736 | tf_op jit(solution)/shard_map/ppermute | solution.py:16
  15.7 1.0 fusion.4
  16.7 1.0 convolution_multiply_fusion.1
  24.4 1.2 fusion.8
  26.3 2.0 %fusion.33 = f32[2,8,128,128]{3,2,1,0:T(8,128)S(1)} fusion(f32[2,8,64,256]{3,2,1,0:T(8,128)S(1)} %fusion.8, f32[2,64,8,128]{3,1,0,2:T(8,128)S(1)} %bitcast.174, f32[2,8,64]{2,1,0:T(8,128)S(1)} %get-tuple-element.7), kind=kOutput, calls=%fused_computation.74 | convolution fusion | flops 201457664 | bytes 2105344 | tf_op jit(solution)/shard_map/bhjd,bhje->bhde/dot_general | solution.py:151
  28.3 2.0 %convolution_subtract_fusion = f32[2,8,128,128]{3,2,1,0:T(8,128)S(1)} fusion(f32[128,128]{1,0:T(8,128)S(1)} %fusion.64, f32[2,8]{1,0:T(2,128)S(1)} %slice_reduce_fusion, f32[2,8,64,256]{3,2,1,0:T(8,128)S(1)} %fusion.8, f32[2,64,8,128]{3,1,0,2:T(8,128)S(1)} %bitcast.175, f32[2,8,64]{2,1,0:T(8,128)S(1)} %get-tuple-element.7), kind=kOutput, calls=%fused_computation | convolution fusion | flops 201981952 | bytes 2171904 | tf_op jit(solution)/shard_map/bhjd,bhje->bhde/dot_general | solution.py:148
  31.0 1.9 %collective-permute-start.1 = (f32[8,128,128]{2,1,0:T(8,128)S(1)}, f32[8,128,128]{2,1,0:T(8,128)S(1)}, u32[]{:S(2)}, u32[]{:S(2)}) collective-permute-start(f32[8,128,128]{2,1,0:T(8,128)S(1)} %convolution_add_fusion.9), channel_id=1, source_target_pairs={{0,2},{2,4},{4,6},{6,8},{8,10},{10,12},{12,14},{14,16},{16,18},{18... | collective-permute-start | bytes 1572872 | tf_op jit(solution)/shard_map/ppermute | solution.py:40
  33.5 1.9 %collective-permute-start.2 = (f32[8,128,128]{2,1,0:T(8,128)S(1)}, f32[8,128,128]{2,1,0:T(8,128)S(1)}, u32[]{:S(2)}, u32[]{:S(2)}) collective-permute-start(f32[8,128,128]{2,1,0:T(8,128)S(1)} %fusion.34), channel_id=1, source_target_pairs={{0,2},{2,4},{4,6},{6,8},{8,10},{10,12},{12,14},{14,16},{16,18},{18... | collective-permute-start | bytes 1572872 | tf_op jit(solution)/shard_map/ppermute | solution.py:31
  36.1 12.4 %collective-permute-done.1 = f32[8,128,128]{2,1,0:T(8,128)S(1)} collective-permute-done((f32[8,128,128]{2,1,0:T(8,128)S(1)}, f32[8,128,128]{2,1,0:T(8,128)S(1)}, u32[]{:S(2)}, u32[]{:S(2)}) %collective-permute-start.1) | collective-permute-done | bytes 524320 | tf_op jit(solution)/shard_map/ppermute | solution.py:40
  49.3 1.3 collective-permute-start.3
  50.6 7.9 %collective-permute-done.2 = f32[8,128,128]{2,1,0:T(8,128)S(1)} collective-permute-done((f32[8,128,128]{2,1,0:T(8,128)S(1)}, f32[8,128,128]{2,1,0:T(8,128)S(1)}, u32[]{:S(2)}, u32[]{:S(2)}) %collective-permute-start.2) | collective-permute-done | bytes 524320 | tf_op jit(solution)/shard_map/ppermute | solution.py:31
  59.1 1.3 collective-permute-start.4
  61.6 8.1 %collective-permute-done.3 = f32[8,128,128]{2,1,0:T(8,128)S(1)} collective-permute-done((f32[8,128,128]{2,1,0:T(8,128)S(1)}, f32[8,128,128]{2,1,0:T(8,128)S(1)}, u32[]{:S(2)}, u32[]{:S(2)}) %collective-permute-start.3) | collective-permute-done | bytes 524320 | tf_op jit(solution)/shard_map/ppermute | solution.py:40
  70.3 1.3 collective-permute-start.5
  71.6 9.2 %collective-permute-done.4 = f32[8,128,128]{2,1,0:T(8,128)S(1)} collective-permute-done((f32[8,128,128]{2,1,0:T(8,128)S(1)}, f32[8,128,128]{2,1,0:T(8,128)S(1)}, u32[]{:S(2)}, u32[]{:S(2)}) %collective-permute-start.4) | collective-permute-done | bytes 524320 | tf_op jit(solution)/shard_map/ppermute | solution.py:31
  81.5 1.5 %collective-permute-start.6 = (f32[8,128,128]{2,1,0:T(8,128)S(1)}, f32[8,128,128]{2,1,0:T(8,128)S(1)}, u32[]{:S(2)}, u32[]{:S(2)}) collective-permute-start(f32[8,128,128]{2,1,0:T(8,128)S(1)} %convolution_select_fusion), channel_id=1, source_target_pairs={{0,8},{2,10},{4,12},{6,14},{8,16},{10,18},{12,20},{14,22},{16,24},... | collective-permute-start | bytes 1572872 | tf_op jit(solution)/shard_map/ppermute | solution.py:31
  83.7 10.7 %collective-permute-done.5 = f32[8,128,128]{2,1,0:T(8,128)S(1)} collective-permute-done((f32[8,128,128]{2,1,0:T(8,128)S(1)}, f32[8,128,128]{2,1,0:T(8,128)S(1)}, u32[]{:S(2)}, u32[]{:S(2)}) %collective-permute-start.5) | collective-permute-done | bytes 524320 | tf_op jit(solution)/shard_map/ppermute | solution.py:40
  95.0 1.3 collective-permute-start.7
  97.0 7.0 %collective-permute-done.6 = f32[8,128,128]{2,1,0:T(8,128)S(1)} collective-permute-done((f32[8,128,128]{2,1,0:T(8,128)S(1)}, f32[8,128,128]{2,1,0:T(8,128)S(1)}, u32[]{:S(2)}, u32[]{:S(2)}) %collective-permute-start.6) | collective-permute-done | bytes 524320 | tf_op jit(solution)/shard_map/ppermute | solution.py:31
  104.7 20.9 %collective-permute-done.7 = f32[8,128,128]{2,1,0:T(8,128)S(1)} collective-permute-done((f32[8,128,128]{2,1,0:T(8,128)S(1)}, f32[8,128,128]{2,1,0:T(8,128)S(1)}, u32[]{:S(2)}, u32[]{:S(2)}) %collective-permute-start.7) | collective-permute-done | bytes 524320 | tf_op jit(solution)/shard_map/ppermute | solution.py:40
  129.4 1.0 fusion.32
  (125 shorter events, 28.9 us)
Async XLA Ops:
  0.0 10.9 %copy-start = (f32[128]{0:T(128)S(1)}, f32[128]{0:T(128)}, u32[]{:S(2)}) copy-start(f32[128]{0:T(128)} %param.29) | copy-start | bytes 1540
  0.0 2.4 %copy-start.5 = (bf16[128,512]{1,0:T(8,128)(2,1)S(1)}, bf16[128,512]{1,0:T(8,128)(2,1)}, u32[]{:S(2)}) copy-start(bf16[128,512]{1,0:T(8,128)(2,1)} %param.15) | copy-start | bytes 393220
  1.6 0.7 copy-start.10
  2.4 0.9 copy-start.4
  3.3 0.9 copy-start.3
  4.7 8.7 %collective-permute-start = (f32[3,2048]{1,0:T(4,128)S(1)}, f32[3,2048]{1,0:T(4,128)S(1)}, u32[]{:S(2)}, u32[]{:S(2)}) collective-permute-start(f32[3,2048]{1,0:T(4,128)S(1)} %pad_maximum_fusion.3), channel_id=1, source_target_pairs={{0,2},{2,4},{4,6},{6,8},{8,10},{10,12},{12,14},{14,16},{16,18},{18... | collective-permute-start | bytes 73736 | tf_op jit(solution)/shard_map/ppermute | solution.py:16
  8.1 0.7 copy-start.13
  8.2 1.4 %copy-start.11 = (f32[128,8]{0,1:T(8,128)S(1)}, f32[128,8]{0,1:T(8,128)}, u32[]{:S(2)}) copy-start(f32[128,8]{0,1:T(8,128)} %param.24) | copy-start | bytes 12292
  10.1 0.7 copy-start.12
  10.8 0.8 copy-start.9
  10.9 0.7 copy-start.8
  11.6 0.7 copy-start.7
  26.3 34.8 %copy-start.2 = (f32[2,8,64,128]{3,2,1,0:T(8,128)}, f32[2,8,64,128]{3,2,1,0:T(8,128)S(1)}, u32[]{:S(2)}) copy-start(f32[2,8,64,128]{3,2,1,0:T(8,128)S(1)} %fusion.38) | copy-start | bytes 1572868
  31.0 17.6 %collective-permute-start.1 = (f32[8,128,128]{2,1,0:T(8,128)S(1)}, f32[8,128,128]{2,1,0:T(8,128)S(1)}, u32[]{:S(2)}, u32[]{:S(2)}) collective-permute-start(f32[8,128,128]{2,1,0:T(8,128)S(1)} %convolution_add_fusion.9), channel_id=1, source_target_pairs={{0,2},{2,4},{4,6},{6,8},{8,10},{10,12},{12,14},{14,16},{16,18},{18... | collective-permute-start | bytes 1572872 | tf_op jit(solution)/shard_map/ppermute | solution.py:40
  33.5 24.9 %collective-permute-start.2 = (f32[8,128,128]{2,1,0:T(8,128)S(1)}, f32[8,128,128]{2,1,0:T(8,128)S(1)}, u32[]{:S(2)}, u32[]{:S(2)}) collective-permute-start(f32[8,128,128]{2,1,0:T(8,128)S(1)} %fusion.34), channel_id=1, source_target_pairs={{0,2},{2,4},{4,6},{6,8},{8,10},{10,12},{12,14},{14,16},{16,18},{18... | collective-permute-start | bytes 1572872 | tf_op jit(solution)/shard_map/ppermute | solution.py:31
  36.1 24.9 %copy-start.1 = (f32[2,8,64,128]{3,2,1,0:T(8,128)}, f32[2,8,64,128]{3,2,1,0:T(8,128)S(1)}, u32[]{:S(2)}) copy-start(f32[2,8,64,128]{3,2,1,0:T(8,128)S(1)} %convolution_subtract_fusion.1) | copy-start | bytes 1572868
  49.3 20.4 %collective-permute-start.3 = (f32[8,128,128]{2,1,0:T(8,128)S(1)}, f32[8,128,128]{2,1,0:T(8,128)S(1)}, u32[]{:S(2)}, u32[]{:S(2)}) collective-permute-start(f32[8,128,128]{2,1,0:T(8,128)S(1)} %convolution_add_fusion.8), channel_id=1, source_target_pairs={{0,4},{2,6},{4,8},{6,10},{8,12},{10,14},{12,16},{14,18},{16,20},{1... | collective-permute-start | bytes 1572872 | tf_op jit(solution)/shard_map/ppermute | solution.py:40
  59.1 21.7 %collective-permute-start.4 = (f32[8,128,128]{2,1,0:T(8,128)S(1)}, f32[8,128,128]{2,1,0:T(8,128)S(1)}, u32[]{:S(2)}, u32[]{:S(2)}) collective-permute-start(f32[8,128,128]{2,1,0:T(8,128)S(1)} %convolution_select_fusion.1), channel_id=1, source_target_pairs={{0,4},{2,6},{4,8},{6,10},{8,12},{10,14},{12,16},{14,18},{16,20},{1... | collective-permute-start | bytes 1572872 | tf_op jit(solution)/shard_map/ppermute | solution.py:31
  70.3 24.0 %collective-permute-start.5 = (f32[8,128,128]{2,1,0:T(8,128)S(1)}, f32[8,128,128]{2,1,0:T(8,128)S(1)}, u32[]{:S(2)}, u32[]{:S(2)}) collective-permute-start(f32[8,128,128]{2,1,0:T(8,128)S(1)} %convolution_add_fusion.6), channel_id=1, source_target_pairs={{0,8},{2,10},{4,12},{6,14},{8,16},{10,18},{12,20},{14,22},{16,24},... | collective-permute-start | bytes 1572872 | tf_op jit(solution)/shard_map/ppermute | solution.py:40
  81.5 22.5 %collective-permute-start.6 = (f32[8,128,128]{2,1,0:T(8,128)S(1)}, f32[8,128,128]{2,1,0:T(8,128)S(1)}, u32[]{:S(2)}, u32[]{:S(2)}) collective-permute-start(f32[8,128,128]{2,1,0:T(8,128)S(1)} %convolution_select_fusion), channel_id=1, source_target_pairs={{0,8},{2,10},{4,12},{6,14},{8,16},{10,18},{12,20},{14,22},{16,24},... | collective-permute-start | bytes 1572872 | tf_op jit(solution)/shard_map/ppermute | solution.py:31
  95.0 30.5 %collective-permute-start.7 = (f32[8,128,128]{2,1,0:T(8,128)S(1)}, f32[8,128,128]{2,1,0:T(8,128)S(1)}, u32[]{:S(2)}, u32[]{:S(2)}) collective-permute-start(f32[8,128,128]{2,1,0:T(8,128)S(1)} %convolution_add_fusion.5), channel_id=1, source_target_pairs={{0,16},{2,18},{4,20},{6,22},{8,24},{10,26},{12,28},{14,30},{1,17},... | collective-permute-start | bytes 1572872 | tf_op jit(solution)/shard_map/ppermute | solution.py:40
  126.2 1.0 slice-start
  126.2 1.0 slice-start.1
  128.5 1.0 copy-start.6
  (1 other events, 0.7 us)

commit v4 on v3

--- a/solution.py
+++ b/solution.py
@@ -69,41 +69,14 @@
     return shaped * lax.rsqrt(jnp.sum(shaped * shaped, axis=-1, keepdims=True) + EPSILON)
 
 
-def head_inputs(
-    query_conv,
-    key_filtered,
-    value_conv,
-    gate_rows,
-    beta_rows,
-    decay_base,
-    step_bias,
-    head_width,
-    block,
-):
-    row_count = query_conv.shape[0]
-    queries = unit_heads(query_conv, head_width) * head_width ** (-0.5)
-    key_units = unit_heads(key_filtered, head_width)
-    value_units = value_conv.astype(jnp.float32).reshape(row_count, -1, head_width)
-    repeats = value_units.shape[1] // key_units.shape[1]
-    queries = jnp.repeat(queries, repeats, axis=1)
-    key_units = jnp.repeat(key_units, repeats, axis=1)
-    logdec = -jnp.exp(decay_base)[None, :] * jax.nn.softplus(gate_rows + step_bias[None, :])
-    betas_all = jax.nn.sigmoid(beta_rows)
-    block_count = row_count // block
-
-    def to_blocks(array):
-        return array.reshape(block_count, block, array.shape[1], -1).transpose(0, 2, 1, 3)
-
-    def to_block_rows(array):
-        return array.reshape(block_count, block, -1).transpose(0, 2, 1)
-
-    return (
-        to_blocks(queries),
-        to_blocks(key_units),
-        to_blocks(value_units),
-        to_block_rows(logdec),
-        to_block_rows(betas_all),
-    )
+def to_blocks(array, block):
+    block_count = array.shape[0] // block
+    return array.reshape(block_count, block, array.shape[1], -1).transpose(0, 2, 1, 3)
+
+
+def to_block_rows(array, block):
+    block_count = array.shape[0] // block
+    return array.reshape(block_count, block, -1).transpose(0, 2, 1)
 
 
 def unit_lower_inverse(strict_part):
@@ -119,7 +92,7 @@
     return inverse
 
 
-def block_terms(queries, key_units, value_units, logdec, beta_units):
+def key_terms(key_units, logdec, beta_units):
     length = logdec.shape[-1]
     positions = jnp.arange(length)
     lower_incl = positions[:, None] >= positions[None, :]
@@ -131,25 +104,35 @@
     key_gram = jnp.einsum("bhid,bhjd->bhij", key_units, key_units, precision=HIGHEST)
     inverse = unit_lower_inverse(beta_units[..., :, None] * key_gram * decay_strict)
     growth = jnp.exp(cumulative)
-    stacked = jnp.concatenate(
-        [beta_units[..., None] * value_units, (beta_units * growth)[..., None] * key_units], axis=-1
-    )
-    solved = jnp.einsum("bhij,bhjd->bhid", inverse, stacked, precision=HIGHEST)
-    value_width = value_units.shape[-1]
-    weight_values = solved[..., :value_width]
-    weight_keys = solved[..., value_width:]
+    weight_keys = jnp.einsum(
+        "bhij,bhjd->bhid",
+        inverse,
+        (beta_units * growth)[..., None] * key_units,
+        precision=HIGHEST,
+    )
+    fading = jnp.exp(cumulative[..., -1:] - cumulative)[..., None] * key_units
+    eye_key = jnp.eye(key_units.shape[-1], dtype=jnp.float32)
+    transition = growth[..., -1][..., None, None] * eye_key - jnp.einsum(
+        "bhjd,bhje->bhde", fading, weight_keys, precision=HIGHEST
+    )
+    return (inverse, weight_keys, fading, transition, decay_incl, growth)
+
+
+def value_terms(inverse, fading, value_units, beta_units):
+    weight_values = jnp.einsum(
+        "bhij,bhjd->bhid", inverse, beta_units[..., None] * value_units, precision=HIGHEST
+    )
+    offset = jnp.einsum("bhjd,bhje->bhde", fading, weight_values, precision=HIGHEST)
+    return (weight_values, offset)
+
+
+def query_terms(queries, key_units, decay_incl, growth, weight_values, weight_keys):
     mixing = decay_incl * jnp.einsum("bhid,bhjd->bhij", queries, key_units, precision=HIGHEST)
     zero_out = jnp.einsum("bhij,bhjd->bhid", mixing, weight_values, precision=HIGHEST)
     readout = growth[..., None] * queries - jnp.einsum(
         "bhij,bhjd->bhid", mixing, weight_keys, precision=HIGHEST
     )
-    fading = jnp.exp(cumulative[..., -1:] - cumulative)[..., None] * key_units
-    eye_key = jnp.eye(key_units.shape[-1], dtype=jnp.float32)
-    transition = growth[..., -1][..., None, None] * eye_key - jnp.einsum(
-        "bhjd,bhje->bhde", fading, weight_keys, precision=HIGHEST
-    )
-    offset = jnp.einsum("bhjd,bhje->bhde", fading, weight_values, precision=HIGHEST)
-    return (zero_out, readout, transition, offset)
+    return (zero_out, readout)
 
 
 def product(left, right):
@@ -200,36 +183,55 @@
         tails[:, query_width : query_width + key_width],
         tails[:, query_width + key_width :],
     )
-    query_conv = causal_filter(jnp.concatenate([tail_rows[0], query_deq], axis=0), conv_query)
-    key_filtered = causal_filter(jnp.concatenate([tail_rows[1], key_deq], axis=0), key_filter_taps)
-    value_conv = causal_filter(jnp.concatenate([tail_rows[2], value_deq], axis=0), conv_value)
     local_heads = gate_input.shape[1]
     first_head = lax.axis_index("head") * local_heads
     base_part = lax.dynamic_slice_in_dim(decay_base, first_head, local_heads)
     bias_part = lax.dynamic_slice_in_dim(step_bias, first_head, local_heads)
-    zero_out, readout, transition, offset = block_terms(
-        *head_inputs(
-            query_conv,
-            key_filtered,
-            value_conv,
-            gate_input,
-            beta_logit,
-            base_part,
-            bias_part,
-            head_width,
-            CH,
-        )
-    )
-    dev_trans, dev_offset = (transition[0], offset[0])
+    key_filtered = causal_filter(jnp.concatenate([tail_rows[1], key_deq], axis=0), key_filter_taps)
+    row_count = key_filtered.shape[0]
+    key_rows = unit_heads(key_filtered, head_width)
+    repeats = local_heads // key_rows.shape[1]
+    key_units = to_blocks(jnp.repeat(key_rows, repeats, axis=1), CH)
+    logdec = -jnp.exp(base_part)[None, :] * jax.nn.softplus(gate_input + bias_part[None, :])
+    logdec = to_block_rows(logdec, CH)
+    beta_units = to_block_rows(jax.nn.sigmoid(beta_logit), CH)
+    inverse, weight_keys, fading, transition, decay_incl, growth = key_terms(
+        key_units, logdec, beta_units
+    )
+    dev_trans = transition[0]
+    trans_before = [None]
+    for block in range(1, transition.shape[0]):
+        trans_before.append(dev_trans)
+        dev_trans = product(transition[block], dev_trans)
+    value_window, _ = lax.optimization_barrier(
+        (jnp.concatenate([tail_rows[2], value_deq], axis=0), dev_trans)
+    )
+    value_conv = causal_filter(value_window, conv_value)
+    value_units = to_blocks(value_conv.astype(jnp.float32).reshape(row_count, -1, head_width), CH)
+    weight_values, offset = value_terms(inverse, fading, value_units, beta_units)
+    dev_offset = offset[0]
+    offset_before = [None]
+    for block in range(1, transition.shape[0]):
+        offset_before.append(dev_offset)
+        dev_offset = product(transition[block], dev_offset) + offset[block]
+    query_window, _ = lax.optimization_barrier(
+        (jnp.concatenate([tail_rows[0], query_deq], axis=0), dev_offset)
+    )
+    query_conv = causal_filter(query_window, conv_query)
+    query_rows = unit_heads(query_conv, head_width) * head_width ** (-0.5)
+    queries = to_blocks(jnp.repeat(query_rows, repeats, axis=1), CH)
+    zero_out, readout = query_terms(
+        queries, key_units, decay_incl, growth, weight_values, weight_keys
+    )
     local_outs, read_maps = ([zero_out[0]], [readout[0]])
     for block in range(1, transition.shape[0]):
-        read_maps.append(jnp.einsum("hid,hde->hie", readout[block], dev_trans, precision=HIGHEST))
+        read_maps.append(
+            jnp.einsum("hid,hde->hie", readout[block], trans_before[block], precision=HIGHEST)
+        )
         local_outs.append(
             zero_out[block]
-            + jnp.einsum("hid,hde->hie", readout[block], dev_offset, precision=HIGHEST)
+            + jnp.einsum("hid,hde->hie", readout[block], offset_before[block], precision=HIGHEST)
         )
-        dev_offset = product(transition[block], dev_offset) + offset[block]
-        dev_trans = product(transition[block], dev_trans)
     incoming = scan_states(dev_trans, dev_offset, "seq")
     outputs = jnp.stack(local_outs) + jnp.einsum(
         "bhid,hde->bhie", jnp.stack(read_maps), incoming, precision=HIGHEST

time: 133 us -> 134 us (level); the launches traced: 130 us -> 133 us
  matrix products: 24.7 us -> 28.1 us
  waiting for transfers between devices: 76.2 us -> 73.1 us
  local copies, waits for them, and re-layouts: 10.7 us -> 12.2 us
    ppermute x3, waiting for transfers between devices: 24.1 us -> 13.9 us  [scan_states(): earlier = lax.ppermute(inclusive, axis, pairs)]
    ppermute x4, waiting for transfers between devices: 52.1 us -> 59.2 us  [scan_states(): earlier = lax.ppermute(carried, axis, pairs)]
    dot_general x12, matrix products: 7.79 us -> 11.2 us  [product(): return jnp.einsum('hde,hef->hdf', left, right, precision=HIGHEST)]
    unnamed x36 -> x60, local copies, waits for them, and re-layouts: 8.12 us -> 9.98 us
    dot_general x9 -> x10, matrix products: 9.64 us -> 9.6 us  [the longest x1 1.89 us: key_terms(): jnp.einsum('bhjd,bhje->bhde', fading, weight_keys, precision=HIGHEST)]
  transfers between devices with their start and end apart: 8 -> 8, of which waited for: 7 -> 6; matrix products, arithmetic and copies ran while one was open for 7% -> 13% of each run, Pallas kernels for 0% -> 0%
where the time goes in v4:
time: 134 us; the launch traced here: 133 us
  waiting for transfers between devices  73.1 us (55%)
  matrix products  28.1 us (21%)
  starting transfers between devices  14 us (10%)
  local copies, waits for them, and re-layouts  12.2 us (9%)
  other arithmetic  4.78 us (4%)
    ppermute x4, waiting for transfers between devices, scan_states(): earlier = lax.ppermute(carried, axis, pairs)  59.2 us
    ppermute x3, waiting for transfers between devices, scan_states(): earlier = lax.ppermute(inclusive, axis, pairs)  13.9 us
    dot_general x12, matrix products, product(): return jnp.einsum('hde,hef->hdf', left, right, precision=HIGHEST)  11.2 us
    unnamed x60, local copies, waits for them, and re-layouts  9.98 us
    ppermute x4, starting transfers between devices, scan_states(): earlier = lax.ppermute(carried, axis, pairs)  5.92 us
    ppermute x3, starting transfers between devices, scan_states(): earlier = lax.ppermute(inclusive, axis, pairs)  4.73 us
    ppermute x1, starting transfers between devices, from_behind(): lax.ppermute(value, axis, [(source, source + steps) for source in range(f...  3.4 us
    dot_general x5, matrix products, unit_lower_inverse(): jnp.einsum('bhij,bhjk->bhik', inverse, power, precision=HIGHEST)  3.29 us
  transfers between devices with their start and end apart: 8, of which 6 were waited for; matrix products, arithmetic and copies ran while one was open for 13% of the time, Pallas kernels for 0%

profile of v4, /device:TPU:28, one launch (start us, length us, event | category | flops | bytes accessed | tf_op | source)
XLA Modules:
  0.0 133.1 jit_solution(3924521909781034531)
XLA Ops:
  3.4 0.9 copy-done.7
  4.7 3.4 %collective-permute-start = (f32[3,2048]{1,0:T(4,128)S(1)}, f32[3,2048]{1,0:T(4,128)S(1)}, u32[]{:S(2)}, u32[]{:S(2)}) collective-permute-start(f32[3,2048]{1,0:T(4,128)S(1)} %pad_maximum_fusion.3), channel_id=1, source_target_pairs={{0,2},{2,4},{4,6},{6,8},{8,10},{10,12},{12,14},{14,16},{16,18},{18... | collective-permute-start | bytes 73736 | tf_op jit(solution)/shard_map/ppermute | solution.py:16
  15.3 1.0 fusion.4
  23.9 1.9 %convolution_subtract_fusion = f32[2,8,128,128]{3,2,1,0:T(8,128)S(1)} fusion(f32[2,8,64,128]{3,2,1,0:T(8,128)S(1)} %fusion.19, f32[128,128]{1,0:T(8,128)S(1)} %fusion.40, f32[2,8]{1,0:T(2,128)S(1)} %slice_reduce_fusion.1, f32[2,8,64,128]{3,2,0,1:T(8,128)S(1)} %get-tuple-element.9), kind=kOutput, calls=%fused_computation | convolution fusion | flops 201850880 | bytes 2162752 | tf_op jit(solution)/shard_map/bhjd,bhje->bhde/dot_general | solution.py:115
  25.8 0.8 fusion.23
  26.6 1.9 %collective-permute-start.2 = (f32[8,128,128]{2,1,0:T(8,128)S(1)}, f32[8,128,128]{2,1,0:T(8,128)S(1)}, u32[]{:S(2)}, u32[]{:S(2)}) collective-permute-start(f32[8,128,128]{2,1,0:T(8,128)S(1)} %fusion.23), channel_id=1, source_target_pairs={{0,2},{2,4},{4,6},{6,8},{8,10},{10,12},{12,14},{14,16},{16,18},{18... | collective-permute-start | bytes 1572872 | tf_op jit(solution)/shard_map/ppermute | solution.py:31
  29.9 1.8 %fusion.25 = f32[2,8,128,128]{3,2,1,0:T(8,128)S(1)} fusion(f32[2,8,64,128]{3,2,1,0:T(8,128)S(1)} %fusion.17, f32[2,8,64,128]{3,2,0,1:T(8,128)S(1)} %get-tuple-element.9), kind=kOutput, calls=%fused_computation.60 | convolution fusion | flops 201326592 | bytes 2097152 | tf_op jit(solution)/shard_map/bhjd,bhje->bhde/dot_general | solution.py:125
  31.7 1.5 %convolution_add_fusion.9 = f32[8,128,128]{2,1,0:T(8,128)} fusion(f32[2,8,128,128]{3,2,1,0:T(8,128)S(1)} %fusion.25, f32[2,8,128,128]{3,2,1,0:T(8,128)S(1)} %convolution_subtract_fusion), kind=kOutput, calls=%fused_computation.17 | convolution fusion | flops 201457664 | bytes 2097152 | tf_op jit(solution)/shard_map/hde,hef->hdf/dot_general | solution.py:139
  33.2 1.9 %collective-permute-start.1 = (f32[8,128,128]{2,1,0:T(8,128)}, f32[8,128,128]{2,1,0:T(8,128)}, u32[]{:S(2)}, u32[]{:S(2)}) collective-permute-start(f32[8,128,128]{2,1,0:T(8,128)} %convolution_add_fusion.9), channel_id=1, source_target_pairs={{0,2},{2,4},{4,6},{6,8},{8,10},{10,12},{12,14},{14,16},{16,18},{18... | collective-permute-start | bytes 1572872 | tf_op jit(solution)/shard_map/ppermute | solution.py:40
  37.3 1.0 convolution_multiply_fusion
  39.7 14.5 %collective-permute-done.1 = f32[8,128,128]{2,1,0:T(8,128)} collective-permute-done((f32[8,128,128]{2,1,0:T(8,128)}, f32[8,128,128]{2,1,0:T(8,128)}, u32[]{:S(2)}, u32[]{:S(2)}) %collective-permute-start.1) | collective-permute-done | bytes 524320 | tf_op jit(solution)/shard_map/ppermute | solution.py:40
  54.2 1.8 %convolution_add_fusion.8 = f32[8,128,128]{2,1,0:T(8,128)S(1)} fusion(f32[8,128,128]{2,1,0:T(8,128)} %convolution_add_fusion.9, f32[8,128,128]{2,1,0:T(8,128)S(1)} %fusion.23, f32[8,128,128]{2,1,0:T(8,128)} %collective-permute-done.1), kind=kOutput, calls=%fused_computation.14 | convolution fusion | flops 201457664 | bytes 2097152 | tf_op jit(solution)/shard_map/hde,hef->hdf/dot_general | solution.py:139
  56.0 1.4 %collective-permute-start.3 = (f32[8,128,128]{2,1,0:T(8,128)S(1)}, f32[8,128,128]{2,1,0:T(8,128)S(1)}, u32[]{:S(2)}, u32[]{:S(2)}) collective-permute-start(f32[8,128,128]{2,1,0:T(8,128)S(1)} %convolution_add_fusion.8), channel_id=1, source_target_pairs={{0,4},{2,6},{4,8},{6,10},{8,12},{10,14},{12,16},{14,18},{16,20},{1... | collective-permute-start | bytes 1572872 | tf_op jit(solution)/shard_map/ppermute | solution.py:40
  58.1 1.3 collective-permute-start.4
  60.7 12.2 %collective-permute-done.3 = f32[8,128,128]{2,1,0:T(8,128)S(1)} collective-permute-done((f32[8,128,128]{2,1,0:T(8,128)S(1)}, f32[8,128,128]{2,1,0:T(8,128)S(1)}, u32[]{:S(2)}, u32[]{:S(2)}) %collective-permute-start.3) | collective-permute-done | bytes 524320 | tf_op jit(solution)/shard_map/ppermute | solution.py:40
  73.6 1.3 collective-permute-start.5
  74.9 6.9 %collective-permute-done.4 = f32[8,128,128]{2,1,0:T(8,128)S(1)} collective-permute-done((f32[8,128,128]{2,1,0:T(8,128)S(1)}, f32[8,128,128]{2,1,0:T(8,128)S(1)}, u32[]{:S(2)}, u32[]{:S(2)}) %collective-permute-start.4) | collective-permute-done | bytes 524320 | tf_op jit(solution)/shard_map/ppermute | solution.py:31
  82.4 1.5 %collective-permute-start.6 = (f32[8,128,128]{2,1,0:T(8,128)S(1)}, f32[8,128,128]{2,1,0:T(8,128)S(1)}, u32[]{:S(2)}, u32[]{:S(2)}) collective-permute-start(f32[8,128,128]{2,1,0:T(8,128)S(1)} %convolution_select_fusion), channel_id=1, source_target_pairs={{0,8},{2,10},{4,12},{6,14},{8,16},{10,18},{12,20},{14,22},{16,24},... | collective-permute-start | bytes 1572872 | tf_op jit(solution)/shard_map/ppermute | solution.py:31
  84.6 11.6 %collective-permute-done.5 = f32[8,128,128]{2,1,0:T(8,128)S(1)} collective-permute-done((f32[8,128,128]{2,1,0:T(8,128)S(1)}, f32[8,128,128]{2,1,0:T(8,128)S(1)}, u32[]{:S(2)}, u32[]{:S(2)}) %collective-permute-start.5) | collective-permute-done | bytes 524320 | tf_op jit(solution)/shard_map/ppermute | solution.py:40
  96.9 1.3 collective-permute-start.7
  98.9 7.0 %collective-permute-done.6 = f32[8,128,128]{2,1,0:T(8,128)S(1)} collective-permute-done((f32[8,128,128]{2,1,0:T(8,128)S(1)}, f32[8,128,128]{2,1,0:T(8,128)S(1)}, u32[]{:S(2)}, u32[]{:S(2)}) %collective-permute-start.6) | collective-permute-done | bytes 524320 | tf_op jit(solution)/shard_map/ppermute | solution.py:31
  106.5 20.9 %collective-permute-done.7 = f32[8,128,128]{2,1,0:T(8,128)S(1)} collective-permute-done((f32[8,128,128]{2,1,0:T(8,128)S(1)}, f32[8,128,128]{2,1,0:T(8,128)S(1)}, u32[]{:S(2)}, u32[]{:S(2)}) %collective-permute-start.7) | collective-permute-done | bytes 524320 | tf_op jit(solution)/shard_map/ppermute | solution.py:40
  128.1 1.8 %fusion.2 = f32[8,128,128,1]{2,1,0,3:T(8,128)S(1)} fusion(f32[8,128,128]{2,1,0:T(8,128)S(1)} %fusion.58, f32[8,128,128]{2,1,0:T(8,128)S(1)} %fusion.56, f32[8,128,128]{2,1,0:T(8,128)} %collective-permute-done.1, f32[8,128,128]{2,1,0:T(8,128)S(1)} %collective-permute-done.2, f32[8,128,128]{2,1,0:T(8,128)S(1)} %collective-permute-done.3), kind=kOutput, calls=%fused_computation.13 | convolution fusion | flops 201719808 | bytes 3145728 | tf_op jit(solution)/shard_map/hde,hef->hdf/dot_general | solution.py:139
  132.1 1.0 fusion.22
  (153 shorter events, 31.7 us)
Async XLA Ops:
  0.0 10.9 %copy-start = (f32[128]{0:T(128)S(1)}, f32[128]{0:T(128)}, u32[]{:S(2)}) copy-start(f32[128]{0:T(128)} %param.29) | copy-start | bytes 1540
  0.0 2.4 %copy-start.9 = (bf16[128,512]{1,0:T(8,128)(2,1)S(1)}, bf16[128,512]{1,0:T(8,128)(2,1)}, u32[]{:S(2)}) copy-start(bf16[128,512]{1,0:T(8,128)(2,1)} %param.15) | copy-start | bytes 393220
  3.3 0.9 copy-start.7
  4.7 9.8 %collective-permute-start = (f32[3,2048]{1,0:T(4,128)S(1)}, f32[3,2048]{1,0:T(4,128)S(1)}, u32[]{:S(2)}, u32[]{:S(2)}) collective-permute-start(f32[3,2048]{1,0:T(4,128)S(1)} %pad_maximum_fusion.3), channel_id=1, source_target_pairs={{0,2},{2,4},{4,6},{6,8},{8,10},{10,12},{12,14},{14,16},{16,18},{18... | collective-permute-start | bytes 73736 | tf_op jit(solution)/shard_map/ppermute | solution.py:16
  8.1 7.1 %copy-start.13 = (pred[64,64]{1,0:T(8,128)(4,1)}, pred[64,64]{1,0:T(8,128)(4,1)S(1)}, u32[]{:S(2)}) copy-start(pred[64,64]{1,0:T(8,128)(4,1)S(1)} %get-tuple-element.33) | copy-start | bytes 12292
  8.2 1.4 %copy-start.23 = (f32[128,8]{0,1:T(8,128)S(1)}, f32[128,8]{0,1:T(8,128)}, u32[]{:S(2)}) copy-start(f32[128,8]{0,1:T(8,128)} %param.24) | copy-start | bytes 12292
  10.9 1.4 %copy-start.17 = (bf16[4,512]{1,0:T(4,128)(2,1)S(1)}, bf16[4,512]{1,0:T(4,128)(2,1)}, u32[]{:S(2)}) copy-start(bf16[4,512]{1,0:T(4,128)(2,1)} %param.22) | copy-start | bytes 12292
  23.9 1.9 %copy-start.1 = (f32[2,8,64,128]{3,2,1,0:T(8,128)}, f32[2,8,64,128]{3,2,1,0:T(8,128)S(1)}, u32[]{:S(2)}) copy-start(f32[2,8,64,128]{3,2,1,0:T(8,128)S(1)} %fusion.19) | copy-start | bytes 1572868
  26.6 30.8 %collective-permute-start.2 = (f32[8,128,128]{2,1,0:T(8,128)S(1)}, f32[8,128,128]{2,1,0:T(8,128)S(1)}, u32[]{:S(2)}, u32[]{:S(2)}) collective-permute-start(f32[8,128,128]{2,1,0:T(8,128)S(1)} %fusion.23), channel_id=1, source_target_pairs={{0,2},{2,4},{4,6},{6,8},{8,10},{10,12},{12,14},{14,16},{16,18},{18... | collective-permute-start | bytes 1572872 | tf_op jit(solution)/shard_map/ppermute | solution.py:31
  31.7 3.4 %copy-start.3 = (f32[2,8,128,128]{3,2,1,0:T(8,128)}, f32[2,8,128,128]{3,2,1,0:T(8,128)S(1)}, u32[]{:S(2)}) copy-start(f32[2,8,128,128]{3,2,1,0:T(8,128)S(1)} %fusion.25) | copy-start | bytes 3145732
  33.2 21.0 %collective-permute-start.1 = (f32[8,128,128]{2,1,0:T(8,128)}, f32[8,128,128]{2,1,0:T(8,128)}, u32[]{:S(2)}, u32[]{:S(2)}) collective-permute-start(f32[8,128,128]{2,1,0:T(8,128)} %convolution_add_fusion.9), channel_id=1, source_target_pairs={{0,2},{2,4},{4,6},{6,8},{8,10},{10,12},{12,14},{14,16},{16,18},{18... | collective-permute-start | bytes 1572872 | tf_op jit(solution)/shard_map/ppermute | solution.py:40
  37.3 1.0 copy-start.2
  37.3 1.0 copy-start.12
  39.0 21.1 %copy-start.5 = (f32[2,8,64,128]{3,2,1,0:T(8,128)}, f32[2,8,64,128]{3,2,1,0:T(8,128)S(1)}, u32[]{:S(2)}) copy-start(f32[2,8,64,128]{3,2,1,0:T(8,128)S(1)} %convolution_subtract_fusion.1) | copy-start | bytes 1572868
  39.7 20.4 %copy-start.6 = (f32[2,8,64,128]{3,2,1,0:T(8,128)}, f32[2,8,64,128]{3,2,1,0:T(8,128)S(1)}, u32[]{:S(2)}) copy-start(f32[2,8,64,128]{3,2,1,0:T(8,128)S(1)} %fusion.54) | copy-start | bytes 1572868
  56.0 4.1 %copy-start.4 = (f32[2,8,128,128]{3,2,1,0:T(8,128)S(1)}, f32[2,8,128,128]{3,2,1,0:T(8,128)}, u32[]{:S(2)}) copy-start(f32[2,8,128,128]{3,2,1,0:T(8,128)} %copy-done.3) | copy-start | bytes 3145732
  56.0 16.9 %collective-permute-start.3 = (f32[8,128,128]{2,1,0:T(8,128)S(1)}, f32[8,128,128]{2,1,0:T(8,128)S(1)}, u32[]{:S(2)}, u32[]{:S(2)}) collective-permute-start(f32[8,128,128]{2,1,0:T(8,128)S(1)} %convolution_add_fusion.8), channel_id=1, source_target_pairs={{0,4},{2,6},{4,8},{6,10},{8,12},{10,14},{12,16},{14,18},{16,20},{1... | collective-permute-start | bytes 1572872 | tf_op jit(solution)/shard_map/ppermute | solution.py:40
  58.1 23.6 %collective-permute-start.4 = (f32[8,128,128]{2,1,0:T(8,128)S(1)}, f32[8,128,128]{2,1,0:T(8,128)S(1)}, u32[]{:S(2)}, u32[]{:S(2)}) collective-permute-start(f32[8,128,128]{2,1,0:T(8,128)S(1)} %convolution_select_fusion.1), channel_id=1, source_target_pairs={{0,4},{2,6},{4,8},{6,10},{8,12},{10,14},{12,16},{14,18},{16,20},{1... | collective-permute-start | bytes 1572872 | tf_op jit(solution)/shard_map/ppermute | solution.py:31
  73.6 22.6 %collective-permute-start.5 = (f32[8,128,128]{2,1,0:T(8,128)S(1)}, f32[8,128,128]{2,1,0:T(8,128)S(1)}, u32[]{:S(2)}, u32[]{:S(2)}) collective-permute-start(f32[8,128,128]{2,1,0:T(8,128)S(1)} %convolution_add_fusion.6), channel_id=1, source_target_pairs={{0,8},{2,10},{4,12},{6,14},{8,16},{10,18},{12,20},{14,22},{16,24},... | collective-permute-start | bytes 1572872 | tf_op jit(solution)/shard_map/ppermute | solution.py:40
  82.4 23.4 %collective-permute-start.6 = (f32[8,128,128]{2,1,0:T(8,128)S(1)}, f32[8,128,128]{2,1,0:T(8,128)S(1)}, u32[]{:S(2)}, u32[]{:S(2)}) collective-permute-start(f32[8,128,128]{2,1,0:T(8,128)S(1)} %convolution_select_fusion), channel_id=1, source_target_pairs={{0,8},{2,10},{4,12},{6,14},{8,16},{10,18},{12,20},{14,22},{16,24},... | collective-permute-start | bytes 1572872 | tf_op jit(solution)/shard_map/ppermute | solution.py:31
  96.9 30.5 %collective-permute-start.7 = (f32[8,128,128]{2,1,0:T(8,128)S(1)}, f32[8,128,128]{2,1,0:T(8,128)S(1)}, u32[]{:S(2)}, u32[]{:S(2)}) collective-permute-start(f32[8,128,128]{2,1,0:T(8,128)S(1)} %convolution_add_fusion.5), channel_id=1, source_target_pairs={{0,16},{2,18},{4,20},{6,22},{8,24},{10,26},{12,28},{14,30},{1,17},... | collective-permute-start | bytes 1572872 | tf_op jit(solution)/shard_map/ppermute | solution.py:40
  128.1 1.8 %slice-start = ((f32[2,8,64,128]{3,2,1,0:T(8,128)}), f32[1,8,64,128]{3,2,1,0:T(8,128)S(1)}, s32[]{:S(2)}) async-start(f32[2,8,64,128]{3,2,1,0:T(8,128)} %copy-done.5), calls=%async_computation | async-start | bytes 524288 | tf_op jit(solution)/shard_map/slice | solution.py:226
  128.1 1.8 %slice-start.1 = ((f32[2,8,64,128]{3,2,1,0:T(8,128)}), f32[1,8,64,128]{3,2,1,0:T(8,128)S(1)}, s32[]{:S(2)}) async-start(f32[2,8,64,128]{3,2,1,0:T(8,128)} %copy-done.6), calls=%async_computation.1 | async-start | bytes 524288 | tf_op jit(solution)/shard_map/slice | solution.py:226
  131.1 1.0 copy-start.10
  (13 other events, 9.0 us)

commit v5 on v4

--- a/solution.py
+++ b/solution.py
@@ -18,30 +18,40 @@
 
 def scan_states(trans, offset, axis):
     devices, mine = (lax.axis_size(axis), lax.axis_index(axis))
+    width = trans.shape[-1]
+    eye = jnp.eye(width, dtype=jnp.float32)
     spans = []
     span = 1
     while span < devices:
         spans.append(span)
         span = span * 2
-    inclusive_maps, exclusive_maps = ([], [None])
-    inclusive = trans
-    for span in spans[:-1]:
-        pairs = [(source, source + span) for source in range(devices - span)]
-        inclusive_maps.append(inclusive)
-        earlier = lax.ppermute(inclusive, axis, pairs)
-        last_map = exclusive_maps[-1]
-        exclusive_maps.append(earlier if last_map is None else product(last_map, earlier))
-        if 4 * span < devices:
-            inclusive = jnp.where(mine >= span, product(inclusive, earlier), inclusive)
-    state = jnp.zeros_like(offset)
-    carried = offset
+    inclusive_map, carried = (trans, offset)
+    exclusive_map, state = (None, jnp.zeros_like(offset))
     for step, span in enumerate(spans):
         pairs = [(source, source + span) for source in range(devices - span)]
-        earlier = lax.ppermute(carried, axis, pairs)
-        last_map = exclusive_maps[step]
-        state = earlier if last_map is None else state + product(last_map, earlier)
-        if step + 1 < len(spans):
-            carried = product(inclusive_maps[step], earlier) + carried
+        reached = jnp.where(mine >= span, 1.0, 0.0)
+        if step + 1 == len(spans):
+            earlier = lax.ppermute(carried.astype(jnp.bfloat16), axis, pairs)
+            earlier_state = earlier.astype(jnp.float32)
+            if exclusive_map is None:
+                state = earlier_state
+            else:
+                state = state + product(exclusive_map, earlier_state)
+            break
+        sent = jnp.concatenate([inclusive_map - eye, carried], axis=-1).astype(jnp.bfloat16)
+        earlier = lax.ppermute(sent, axis, pairs).astype(jnp.float32)
+        earlier_map = earlier[..., :width] + reached * eye
+        earlier_state = earlier[..., width:]
+        if exclusive_map is None:
+            exclusive_map, state = (earlier_map, earlier_state)
+        else:
+            state = state + product(exclusive_map, earlier_state)
+            exclusive_map = product(exclusive_map, earlier_map)
+        carried = product(inclusive_map, earlier_state) + carried
+        if step + 2 < len(spans):
+            inclusive_map = jnp.where(
+                mine >= span, product(inclusive_map, earlier_map), inclusive_map
+            )
     return state
 
 

time: 134 us -> 110 us (0.82)
  the two profiles are of different devices: /device:TPU:28 before, /device:TPU:24 now
where the time goes in v5:
time: 110 us; the launch traced here: 109 us
  waiting for transfers between devices  41.2 us (37%)
  matrix products  28.5 us (26%)
  local copies, waits for them, and re-layouts  18.7 us (17%)
  starting transfers between devices  12.3 us (11%)
  other arithmetic  7.18 us (7%)
    ppermute x3, waiting for transfers between devices, scan_states(): earlier = lax.ppermute(sent, axis, pairs).astype(jnp.float32)  31.1 us
    unnamed x78, local copies, waits for them, and re-layouts  13.4 us
    dot_general x12, matrix products, product(): return jnp.einsum('hde,hef->hdf', left, right, precision=HIGHEST)  10.3 us
    ppermute x1, waiting for transfers between devices, scan_states(): earlier = lax.ppermute(carried.astype(jnp.bfloat16), axis, pairs)  10.1 us
    ppermute x3, starting transfers between devices, scan_states(): earlier = lax.ppermute(sent, axis, pairs).astype(jnp.float32)  7.44 us
    ppermute x1, starting transfers between devices, from_behind(): lax.ppermute(value, axis, [(source, source + steps) for source in range(f...  3.4 us
    dot_general x5, matrix products, unit_lower_inverse(): jnp.einsum('bhij,bhjk->bhik', inverse, power, precision=HIGHEST)  3.29 us
    dot_general x5, matrix products, unit_lower_inverse(): power = jnp.einsum('bhij,bhjk->bhik', power, power, precision=HIGHEST)  3.22 us
  transfers between devices with their start and end apart: 5, of which 4 were waited for; matrix products, arithmetic and copies ran while one was open for 12% of the time, Pallas kernels for 0%

profile of v5, /device:TPU:24, one launch (start us, length us, event | category | flops | bytes accessed | tf_op | source)
XLA Modules:
  0.0 108.8 jit_solution(17104813605802306172)
XLA Ops:
  3.4 0.9 copy-done.6
  4.7 3.4 %collective-permute-start = (f32[3,2048]{1,0:T(4,128)S(1)}, f32[3,2048]{1,0:T(4,128)S(1)}, u32[]{:S(2)}, u32[]{:S(2)}) collective-permute-start(f32[3,2048]{1,0:T(4,128)S(1)} %pad_maximum_fusion.6), channel_id=1, source_target_pairs={{0,2},{2,4},{4,6},{6,8},{8,10},{10,12},{12,14},{14,16},{16,18},{18... | collective-permute-start | bytes 73736 | tf_op jit(solution)/shard_map/ppermute | solution.py:16
  18.2 1.0 fusion.1
  26.8 2.1 %convolution_subtract_fusion = f32[2,8,128,128]{3,2,1,0:T(8,128)S(1)} fusion(f32[2,8,64,128]{3,2,1,0:T(8,128)S(1)} %fusion.21, f32[128,128]{1,0:T(8,128)S(1)} %fusion.65, f32[2,8]{1,0:T(2,128)S(1)} %slice_reduce_fusion.1, f32[2,8,64,128]{3,2,0,1:T(8,128)S(1)} %get-tuple-element.9), kind=kOutput, calls=%fused_computation | convolution fusion | flops 201850880 | bytes 2162752 | tf_op jit(solution)/shard_map/bhjd,bhje->bhde/dot_general | solution.py:125
  28.9 1.7 %subtract_convert_fusion.2 = (bf16[8,128,128]{1,2,0:T(8,128)(2,1)}, f32[8,128,128]{1,2,0:T(8,128)S(1)}) fusion(f32[128,128]{0,1:T(8,128)S(1)} %copy.130, f32[2,8,128,128]{3,2,1,0:T(8,128)S(1)} %convolution_subtract_fusion), kind=kOutput, calls=%fused_computation.66 | convolution fusion | flops 201588736 | bytes 1900544 | tf_op jit(solution)/shard_map/hde,hef->hdf/dot_general | solution.py:149
  33.1 1.8 %fusion.31 = f32[2,8,128,128]{2,3,1,0:T(8,128)S(1)} fusion(f32[2,8,64,128]{3,2,1,0:T(8,128)S(1)} %fusion.19, f32[2,8,64,128]{3,2,0,1:T(8,128)S(1)} %get-tuple-element.9), kind=kOutput, calls=%fused_computation.73 | convolution fusion | flops 201326592 | bytes 2097152 | tf_op jit(solution)/shard_map/bhjd,bhje->bhde/dot_general | solution.py:135
  35.0 2.1 %fusion.74 = (bf16[8,128,128]{1,2,0:T(8,128)(2,1)}, f32[8,128,128]{1,2,0:T(8,128)}) fusion(f32[2,8,128,128]{2,3,1,0:T(8,128)S(1)} %fusion.31, f32[2,8,128,128]{3,2,1,0:T(8,128)S(1)} %convolution_subtract_fusion), kind=kOutput, calls=%fused_computation.169 | convolution fusion | flops 201588736 | bytes 2359296 | tf_op jit(solution)/shard_map/hde,hef->hdf/dot_general | solution.py:149
  37.8 0.8 multiply_convert_fusion.1
  38.6 1.0 reshape.156
  40.6 1.0 pad_maximum_fusion.1
  41.6 3.4 %collective-permute-start.1 = (bf16[8,128,256]{1,2,0:T(8,128)(2,1)S(1)}, bf16[8,128,256]{1,2,0:T(8,128)(2,1)S(1)}, u32[]{:S(2)}, u32[]{:S(2)}) collective-permute-start(bf16[8,128,256]{1,2,0:T(8,128)(2,1)S(1)} %pad_maximum_fusion.1), channel_id=1, source_target_pairs={{0,2},{2,4},{4,6},{6,8},{8,10},{10,12},{12,14},{14,16},{16,18},{18... | collective-permute-start | bytes 1572872 | tf_op jit(solution)/shard_map/ppermute | solution.py:42
  45.9 1.0 convolution_multiply_fusion
  46.9 11.7 %collective-permute-done.1 = bf16[8,128,256]{1,2,0:T(8,128)(2,1)S(1)} collective-permute-done((bf16[8,128,256]{1,2,0:T(8,128)(2,1)S(1)}, bf16[8,128,256]{1,2,0:T(8,128)(2,1)S(1)}, u32[]{:S(2)}, u32[]{:S(2)}) %collective-permute-start.1) | collective-permute-done | bytes 524320 | tf_op jit(solution)/shard_map/ppermute | solution.py:42
  60.2 2.5 %collective-permute-start.2 = (bf16[8,128,256]{1,2,0:T(8,128)(2,1)S(1)}, bf16[8,128,256]{1,2,0:T(8,128)(2,1)S(1)}, u32[]{:S(2)}, u32[]{:S(2)}) collective-permute-start(bf16[8,128,256]{1,2,0:T(8,128)(2,1)S(1)} %pad_maximum_fusion.2), channel_id=1, source_target_pairs={{0,4},{2,6},{4,8},{6,10},{8,12},{10,14},{12,16},{14,18},{16,20},{1... | collective-permute-start | bytes 1572872 | tf_op jit(solution)/shard_map/ppermute | solution.py:42
  64.9 1.1 %fusion.5 = f32[1,8,64,128]{3,2,1,0:T(8,128)S(1)} fusion(f32[2,8,128,128]{2,3,1,0:T(8,128)S(1)} %copy-done.2, f32[2,8,64,128]{3,2,1,0:T(8,128)S(1)} %fusion.82, f32[2,8,64,128]{3,2,1,0:T(8,128)S(1)} %convolution_subtract_fusion.1), kind=kOutput, calls=%fused_computation.23 | convolution fusion | flops 100728832 | bytes 1310720 | tf_op jit(solution)/shard_map/hid,hde->hie/dot_general | solution.py:243
  66.0 9.5 %collective-permute-done.2 = bf16[8,128,256]{1,2,0:T(8,128)(2,1)S(1)} collective-permute-done((bf16[8,128,256]{1,2,0:T(8,128)(2,1)S(1)}, bf16[8,128,256]{1,2,0:T(8,128)(2,1)S(1)}, u32[]{:S(2)}, u32[]{:S(2)}) %collective-permute-start.2) | collective-permute-done | bytes 524320 | tf_op jit(solution)/shard_map/ppermute | solution.py:42
  77.0 1.5 %collective-permute-start.3 = (bf16[8,128,256]{1,2,0:T(8,128)(2,1)S(1)}, bf16[8,128,256]{1,2,0:T(8,128)(2,1)S(1)}, u32[]{:S(2)}, u32[]{:S(2)}) collective-permute-start(bf16[8,128,256]{1,2,0:T(8,128)(2,1)S(1)} %pad_maximum_fusion.3), channel_id=1, source_target_pairs={{0,8},{2,10},{4,12},{6,14},{8,16},{10,18},{12,20},{14,22},{16,24},... | collective-permute-start | bytes 1572872 | tf_op jit(solution)/shard_map/ppermute | solution.py:42
  79.6 1.0 fusion.26
  80.7 9.8 %collective-permute-done.3 = bf16[8,128,256]{1,2,0:T(8,128)(2,1)S(1)} collective-permute-done((bf16[8,128,256]{1,2,0:T(8,128)(2,1)S(1)}, bf16[8,128,256]{1,2,0:T(8,128)(2,1)S(1)}, u32[]{:S(2)}, u32[]{:S(2)}) %collective-permute-start.3) | collective-permute-done | bytes 524320 | tf_op jit(solution)/shard_map/ppermute | solution.py:42
  90.9 1.4 %collective-permute-start.4 = (bf16[8,128,128]{1,2,0:T(8,128)(2,1)S(1)}, bf16[8,128,128]{1,2,0:T(8,128)(2,1)S(1)}, u32[]{:S(2)}, u32[]{:S(2)}) collective-permute-start(bf16[8,128,128]{1,2,0:T(8,128)(2,1)S(1)} %fusion.4), channel_id=1, source_target_pairs={{0,16},{2,18},{4,20},{6,22},{8,24},{10,26},{12,28},{14,30},{1,17},... | collective-permute-start | bytes 786440 | tf_op jit(solution)/shard_map/ppermute | solution.py:34
  93.0 1.2 %fusion.23 = f32[8,128,128]{2,1,0:T(8,128)S(1)} fusion(f32[8,128,128]{2,1,0:T(8,128)S(1)} %fusion.26, bf16[8,128,256]{1,2,0:T(8,128)(2,1)S(1)} %collective-permute-done.3, f32[128,128]{0,1:T(8,128)S(1)} %copy-done.12), kind=kOutput, calls=%fused_computation.59 | convolution fusion | flops 201588736 | bytes 1376256 | tf_op jit(solution)/shard_map/hde,hef->hdf/dot_general | solution.py:149
  94.2 10.1 %collective-permute-done.4 = bf16[8,128,128]{1,2,0:T(8,128)(2,1)S(1)} collective-permute-done((bf16[8,128,128]{1,2,0:T(8,128)(2,1)S(1)}, bf16[8,128,128]{1,2,0:T(8,128)(2,1)S(1)}, u32[]{:S(2)}, u32[]{:S(2)}) %collective-permute-start.4) | collective-permute-done | bytes 262176 | tf_op jit(solution)/shard_map/ppermute | solution.py:34
  105.0 1.3 %multiply_reduce_fusion = (f32[2,64,8]{1,2,0:T(8,128)S(1)}, f32[2,64,8,128]{3,1,2,0:T(8,128)S(1)}) fusion(f32[1,8,64,128]{3,2,1,0:T(8,128)S(1)} %convolution_bitcast_fusion.1, f32[1,8,64,128]{3,2,1,0:T(8,128)S(1)} %slice-done, f32[8,128,128]{1,2,0:T(8,128)S(1)} %fusion.83, f32[8,128,128]{1,2,0:T(8,128)S(1)} %fusion.56, f32[8,128,128]{1,2,0:T(8,128)S(1)} %fusion.36, ...), kind=kOutput, calls=%fused_computation.58 | convolution fusion | flops 202374144 | bytes 3674112 | tf_op jit(solution)/shard_map/bhid,hde->bhie/dot_general | solution.py:246
  107.8 1.0 fusion.28
  (176 shorter events, 35.5 us)
Async XLA Ops:
  0.0 10.9 %copy-start = (f32[128]{0:T(128)S(1)}, f32[128]{0:T(128)}, u32[]{:S(2)}) copy-start(f32[128]{0:T(128)} %param.29) | copy-start | bytes 1540
  0.0 2.4 %copy-start.10 = (bf16[128,512]{1,0:T(8,128)(2,1)S(1)}, bf16[128,512]{1,0:T(8,128)(2,1)}, u32[]{:S(2)}) copy-start(bf16[128,512]{1,0:T(8,128)(2,1)} %param.15) | copy-start | bytes 393220
  4.7 12.1 %collective-permute-start = (f32[3,2048]{1,0:T(4,128)S(1)}, f32[3,2048]{1,0:T(4,128)S(1)}, u32[]{:S(2)}, u32[]{:S(2)}) collective-permute-start(f32[3,2048]{1,0:T(4,128)S(1)} %pad_maximum_fusion.6), channel_id=1, source_target_pairs={{0,2},{2,4},{4,6},{6,8},{8,10},{10,12},{12,14},{14,16},{16,18},{18... | collective-permute-start | bytes 73736 | tf_op jit(solution)/shard_map/ppermute | solution.py:16
  8.1 10.0 %copy-start.15 = (pred[64,64]{1,0:T(8,128)(4,1)}, pred[64,64]{1,0:T(8,128)(4,1)S(1)}, u32[]{:S(2)}) copy-start(pred[64,64]{1,0:T(8,128)(4,1)S(1)} %get-tuple-element.45) | copy-start | bytes 12292
  8.2 1.3 %copy-start.32 = (f32[128,8]{0,1:T(8,128)S(1)}, f32[128,8]{0,1:T(8,128)}, u32[]{:S(2)}) copy-start(f32[128,8]{0,1:T(8,128)} %param.24) | copy-start | bytes 12292
  10.9 1.4 %copy-start.26 = (bf16[4,512]{1,0:T(4,128)(2,1)S(1)}, bf16[4,512]{1,0:T(4,128)(2,1)}, u32[]{:S(2)}) copy-start(bf16[4,512]{1,0:T(4,128)(2,1)} %param.22) | copy-start | bytes 12292
  15.1 3.1 %copy-start.17 = (f32[2,64,8]{1,2,0:T(8,128)}, f32[2,64,8]{1,2,0:T(8,128)S(1)}, u32[]{:S(2)}) copy-start(f32[2,64,8]{1,2,0:T(8,128)S(1)} %copy.224) | copy-start | bytes 12292
  28.9 1.7 %copy-start.24 = (f32[1,1024]{1,0:T(1,128)S(1)}, f32[1,1024]{1,0:T(1,128)}, u32[]{:S(2)}) copy-start(f32[1,1024]{1,0:T(1,128)} %get-tuple-element.16) | copy-start | bytes 12292
  35.0 2.1 %copy-start.1 = (f32[2,8,128,128]{2,3,1,0:T(8,128)}, f32[2,8,128,128]{2,3,1,0:T(8,128)S(1)}, u32[]{:S(2)}) copy-start(f32[2,8,128,128]{2,3,1,0:T(8,128)S(1)} %fusion.31) | copy-start | bytes 3145732
  35.0 2.1 %copy-start.19 = (f32[3,512]{1,0:T(4,128)S(1)}, f32[3,512]{1,0:T(4,128)}, u32[]{:S(2)}) copy-start(f32[3,512]{1,0:T(4,128)} %get-tuple-element.11) | copy-start | bytes 18436
  39.6 1.0 copy-start.7
  41.6 17.1 %collective-permute-start.1 = (bf16[8,128,256]{1,2,0:T(8,128)(2,1)S(1)}, bf16[8,128,256]{1,2,0:T(8,128)(2,1)S(1)}, u32[]{:S(2)}, u32[]{:S(2)}) collective-permute-start(bf16[8,128,256]{1,2,0:T(8,128)(2,1)S(1)} %pad_maximum_fusion.1), channel_id=1, source_target_pairs={{0,2},{2,4},{4,6},{6,8},{8,10},{10,12},{12,14},{14,16},{16,18},{18... | collective-permute-start | bytes 1572872 | tf_op jit(solution)/shard_map/ppermute | solution.py:42
  58.7 1.0 copy-start.5
  60.2 3.2 %copy-start.14 = (f32[2,8,64]{2,1,0:T(8,128)S(1)}, f32[2,8,64]{2,1,0:T(8,128)}, u32[]{:S(2)}) copy-start(f32[2,8,64]{2,1,0:T(8,128)} %copy-done.13) | copy-start | bytes 12292
  60.2 15.3 %collective-permute-start.2 = (bf16[8,128,256]{1,2,0:T(8,128)(2,1)S(1)}, bf16[8,128,256]{1,2,0:T(8,128)(2,1)S(1)}, u32[]{:S(2)}, u32[]{:S(2)}) collective-permute-start(bf16[8,128,256]{1,2,0:T(8,128)(2,1)S(1)} %pad_maximum_fusion.2), channel_id=1, source_target_pairs={{0,4},{2,6},{4,8},{6,10},{8,12},{10,14},{12,16},{14,18},{16,20},{1... | collective-permute-start | bytes 1572872 | tf_op jit(solution)/shard_map/ppermute | solution.py:42
  63.4 15.8 %copy-start.4 = (f32[2,8,64,128]{3,2,1,0:T(8,128)}, f32[2,8,64,128]{3,2,1,0:T(8,128)S(1)}, u32[]{:S(2)}) copy-start(f32[2,8,64,128]{3,2,1,0:T(8,128)S(1)} %fusion.82) | copy-start | bytes 1572868
  63.5 1.4 %copy-start.2 = (f32[2,8,128,128]{2,3,1,0:T(8,128)S(1)}, f32[2,8,128,128]{2,3,1,0:T(8,128)}, u32[]{:S(2)}) copy-start(f32[2,8,128,128]{2,3,1,0:T(8,128)} %copy-done.1) | copy-start | bytes 3145732
  64.9 14.3 %copy-start.3 = (f32[2,8,64,128]{3,2,1,0:T(8,128)}, f32[2,8,64,128]{3,2,1,0:T(8,128)S(1)}, u32[]{:S(2)}) copy-start(f32[2,8,64,128]{3,2,1,0:T(8,128)S(1)} %convolution_subtract_fusion.1) | copy-start | bytes 1572868
  77.0 13.4 %collective-permute-start.3 = (bf16[8,128,256]{1,2,0:T(8,128)(2,1)S(1)}, bf16[8,128,256]{1,2,0:T(8,128)(2,1)S(1)}, u32[]{:S(2)}, u32[]{:S(2)}) collective-permute-start(bf16[8,128,256]{1,2,0:T(8,128)(2,1)S(1)} %pad_maximum_fusion.3), channel_id=1, source_target_pairs={{0,8},{2,10},{4,12},{6,14},{8,16},{10,18},{12,20},{14,22},{16,24},... | collective-permute-start | bytes 1572872 | tf_op jit(solution)/shard_map/ppermute | solution.py:42
  90.9 2.1 %copy-start.12 = (f32[128,128]{0,1:T(8,128)S(1)}, f32[128,128]{0,1:T(8,128)}, u32[]{:S(2)}) copy-start(f32[128,128]{0,1:T(8,128)} %copy.144) | copy-start | bytes 196612
  90.9 13.4 %collective-permute-start.4 = (bf16[8,128,128]{1,2,0:T(8,128)(2,1)S(1)}, bf16[8,128,128]{1,2,0:T(8,128)(2,1)S(1)}, u32[]{:S(2)}, u32[]{:S(2)}) collective-permute-start(bf16[8,128,128]{1,2,0:T(8,128)(2,1)S(1)} %fusion.4), channel_id=1, source_target_pairs={{0,16},{2,18},{4,20},{6,22},{8,24},{10,26},{12,28},{14,30},{1,17},... | collective-permute-start | bytes 786440 | tf_op jit(solution)/shard_map/ppermute | solution.py:34
  94.2 10.8 %slice-start = ((f32[2,8,64,128]{3,2,1,0:T(8,128)}), f32[1,8,64,128]{3,2,1,0:T(8,128)S(1)}, s32[]{:S(2)}) async-start(f32[2,8,64,128]{3,2,1,0:T(8,128)} %copy-done.3), calls=%async_computation | async-start | bytes 524288 | tf_op jit(solution)/shard_map/slice | solution.py:236
  94.2 10.8 %slice-start.1 = ((f32[2,8,64,128]{3,2,1,0:T(8,128)}), f32[1,8,64,128]{3,2,1,0:T(8,128)S(1)}, s32[]{:S(2)}) async-start(f32[2,8,64,128]{3,2,1,0:T(8,128)} %copy-done.4), calls=%async_computation.1 | async-start | bytes 524288 | tf_op jit(solution)/shard_map/slice | solution.py:236
  106.8 1.0 copy-start.11
  (19 other events, 13.5 us)

commit v6 on v5

--- a/solution.py
+++ b/solution.py
@@ -16,7 +16,7 @@
     return lax.ppermute(value, axis, [(source, source + steps) for source in range(first, last)])
 
 
-def scan_states(trans, offset, axis):
+def scan_states(trans, offset, axis, rider, side_work):
     devices, mine = (lax.axis_size(axis), lax.axis_index(axis))
     width = trans.shape[-1]
     eye = jnp.eye(width, dtype=jnp.float32)
@@ -31,7 +31,13 @@
         pairs = [(source, source + span) for source in range(devices - span)]
         reached = jnp.where(mine >= span, 1.0, 0.0)
         if step + 1 == len(spans):
-            earlier = lax.ppermute(carried.astype(jnp.bfloat16), axis, pairs)
+            sent = carried.astype(jnp.bfloat16)
+            if step == 0:
+                rider, sent = lax.optimization_barrier((rider, sent))
+            earlier = lax.ppermute(sent, axis, pairs)
+            if step == 0:
+                rider = side_work(rider)
+                rider, earlier = lax.optimization_barrier((rider, earlier))
             earlier_state = earlier.astype(jnp.float32)
             if exclusive_map is None:
                 state = earlier_state
@@ -39,7 +45,13 @@
                 state = state + product(exclusive_map, earlier_state)
             break
         sent = jnp.concatenate([inclusive_map - eye, carried], axis=-1).astype(jnp.bfloat16)
-        earlier = lax.ppermute(sent, axis, pairs).astype(jnp.float32)
+        if step == 0:
+            rider, sent = lax.optimization_barrier((rider, sent))
+        earlier = lax.ppermute(sent, axis, pairs)
+        if step == 0:
+            rider = side_work(rider)
+            rider, earlier = lax.optimization_barrier((rider, earlier))
+        earlier = earlier.astype(jnp.float32)
         earlier_map = earlier[..., :width] + reached * eye
         earlier_state = earlier[..., width:]
         if exclusive_map is None:
@@ -52,7 +64,7 @@
             inclusive_map = jnp.where(
                 mine >= span, product(inclusive_map, earlier_map), inclusive_map
             )
-    return state
+    return (state, rider)
 
 
 def expand_quantized(raw_rows, scales):
@@ -224,25 +236,34 @@
     for block in range(1, transition.shape[0]):
         offset_before.append(dev_offset)
         dev_offset = product(transition[block], dev_offset) + offset[block]
-    query_window, _ = lax.optimization_barrier(
-        (jnp.concatenate([tail_rows[0], query_deq], axis=0), dev_offset)
-    )
-    query_conv = causal_filter(query_window, conv_query)
-    query_rows = unit_heads(query_conv, head_width) * head_width ** (-0.5)
-    queries = to_blocks(jnp.repeat(query_rows, repeats, axis=1), CH)
-    zero_out, readout = query_terms(
-        queries, key_units, decay_incl, growth, weight_values, weight_keys
-    )
-    local_outs, read_maps = ([zero_out[0]], [readout[0]])
-    for block in range(1, transition.shape[0]):
-        read_maps.append(
-            jnp.einsum("hid,hde->hie", readout[block], trans_before[block], precision=HIGHEST)
+
+    def query_side(query_window):
+        query_conv = causal_filter(query_window, conv_query)
+        query_rows = unit_heads(query_conv, head_width) * head_width ** (-0.5)
+        queries = to_blocks(jnp.repeat(query_rows, repeats, axis=1), CH)
+        zero_out, readout = query_terms(
+            queries, key_units, decay_incl, growth, weight_values, weight_keys
         )
-        local_outs.append(
-            zero_out[block]
-            + jnp.einsum("hid,hde->hie", readout[block], offset_before[block], precision=HIGHEST)
-        )
-    incoming = scan_states(dev_trans, dev_offset, "seq")
+        local_outs, read_maps = ([zero_out[0]], [readout[0]])
+        for block in range(1, transition.shape[0]):
+            read_maps.append(
+                jnp.einsum("hid,hde->hie", readout[block], trans_before[block], precision=HIGHEST)
+            )
+            local_outs.append(
+                zero_out[block]
+                + jnp.einsum(
+                    "hid,hde->hie", readout[block], offset_before[block], precision=HIGHEST
+                )
+            )
+        return (local_outs, read_maps)
+
+    incoming, (local_outs, read_maps) = scan_states(
+        dev_trans,
+        dev_offset,
+        "seq",
+        jnp.concatenate([tail_rows[0], query_deq], axis=0),
+        query_side,
+    )
     outputs = jnp.stack(local_outs) + jnp.einsum(
         "bhid,hde->bhie", jnp.stack(read_maps), incoming, precision=HIGHEST
     )

time: 110 us -> 114 us (1.036)
  waiting for transfers between devices: 41.2 us -> 42.9 us
  other arithmetic: 7.18 us -> 8.64 us
    unnamed x78 -> x86, local copies, waits for them, and re-layouts: 13.4 us -> 10.9 us
    ppermute x4, waiting for transfers between devices: 41.2 us -> 42.9 us  [scan_states(): earlier = lax.ppermute(sent, axis, pairs)]
    concatenate x3, other arithmetic: 1.06 us -> 2.53 us  [scan_states(): jnp.concatenate([inclusive_map - eye, carried], axis=-1)]
    squeeze x0 -> x2, local copies, waits for them, and re-layouts: none -> 1.43 us  [query_side(): local_outs, read_maps = ([zero_out[0]], [readout[0]])]
  transfers between devices with their start and end apart: 5 -> 5, of which waited for: 4 -> 4; matrix products, arithmetic and copies ran while one was open for 12% -> 10% of each run, Pallas kernels for 0% -> 0%
where the time goes in v6:
time: 114 us; the launch traced here: 113 us
  waiting for transfers between devices  42.9 us (38%)
  matrix products  29.3 us (26%)
  local copies, waits for them, and re-layouts  18.7 us (16%)
  starting transfers between devices  12.2 us (11%)
  other arithmetic  8.64 us (8%)
    ppermute x4, waiting for transfers between devices, scan_states(): earlier = lax.ppermute(sent, axis, pairs)  42.9 us
    unnamed x86, local copies, waits for them, and re-layouts  10.9 us
    dot_general x12, matrix products, product(): return jnp.einsum('hde,hef->hdf', left, right, precision=HIGHEST)  10.5 us
    ppermute x4, starting transfers between devices, scan_states(): earlier = lax.ppermute(sent, axis, pairs)  8.82 us
    ppermute x1, starting transfers between devices, from_behind(): lax.ppermute(value, axis, [(source, source + steps) for source in range(f...  3.4 us
    dot_general x5, matrix products, unit_lower_inverse(): jnp.einsum('bhij,bhjk->bhik', inverse, power, precision=HIGHEST)  3.29 us
    dot_general x5, matrix products, unit_lower_inverse(): power = jnp.einsum('bhij,bhjk->bhik', power, power, precision=HIGHEST)  3.22 us
    concatenate x3, other arithmetic, scan_states(): jnp.concatenate([inclusive_map - eye, carried], axis=-1)  2.53 us
  transfers between devices with their start and end apart: 5, of which 4 were waited for; matrix products, arithmetic and copies ran while one was open for 10% of the time, Pallas kernels for 0%

profile of v6, /device:TPU:24, one launch (start us, length us, event | category | flops | bytes accessed | tf_op | source)
XLA Modules:
  0.0 112.7 jit_solution(9297042461298153152)
XLA Ops:
  0.8 1.0 reshape.133
  3.2 3.4 %collective-permute-start = (f32[3,2048]{1,0:T(4,128)S(1)}, f32[3,2048]{1,0:T(4,128)S(1)}, u32[]{:S(2)}, u32[]{:S(2)}) collective-permute-start(f32[3,2048]{1,0:T(4,128)S(1)} %pad_maximum_fusion.6), channel_id=1, source_target_pairs={{0,2},{2,4},{4,6},{6,8},{8,10},{10,12},{12,14},{14,16},{16,18},{18... | collective-permute-start | bytes 73736 | tf_op jit(solution)/shard_map/ppermute | solution.py:16
  16.6 1.0 fusion.1
  25.2 1.9 %convolution_subtract_fusion = f32[2,8,128,128]{3,2,1,0:T(8,128)S(1)} fusion(f32[2,8,64,128]{3,2,1,0:T(8,128)S(1)} %fusion.20, f32[128,128]{1,0:T(8,128)S(1)} %fusion.65, f32[2,8]{1,0:T(2,128)S(1)} %slice_reduce_fusion.1, f32[2,8,64,128]{3,2,0,1:T(8,128)S(1)} %get-tuple-element.21), kind=kOutput, calls=%fused_computation | convolution fusion | flops 201850880 | bytes 2162752 | tf_op jit(solution)/shard_map/bhjd,bhje->bhde/dot_general | solution.py:137
  27.1 1.2 %subtract_convert_fusion.2 = (bf16[8,128,128]{1,2,0:T(8,128)(2,1)S(1)}, f32[8,128,128]{1,2,0:T(8,128)S(1)}) fusion(f32[128,128]{0,1:T(8,128)S(1)} %copy.124, f32[2,8,128,128]{3,2,1,0:T(8,128)S(1)} %convolution_subtract_fusion), kind=kOutput, calls=%fused_computation.65 | convolution fusion | flops 201588736 | bytes 1900544 | tf_op jit(solution)/shard_map/hde,hef->hdf/dot_general | solution.py:161
  31.6 1.8 %fusion.31 = f32[2,8,128,128]{2,3,1,0:T(8,128)S(1)} fusion(f32[2,8,64,128]{3,2,1,0:T(8,128)S(1)} %fusion.18, f32[2,8,64,128]{3,2,0,1:T(8,128)S(1)} %get-tuple-element.21), kind=kOutput, calls=%fused_computation.72 | convolution fusion | flops 201326592 | bytes 2097152 | tf_op jit(solution)/shard_map/bhjd,bhje->bhde/dot_general | solution.py:147
  33.4 2.0 %fusion.74 = (bf16[8,128,128]{1,2,0:T(8,128)(2,1)S(1)}, f32[8,128,128]{1,2,0:T(8,128)}) fusion(f32[2,8,128,128]{2,3,1,0:T(8,128)S(1)} %fusion.31, f32[2,8,128,128]{3,2,1,0:T(8,128)S(1)} %convolution_subtract_fusion), kind=kOutput, calls=%fused_computation.170 | convolution fusion | flops 201588736 | bytes 2359296 | tf_op jit(solution)/shard_map/hde,hef->hdf/dot_general | solution.py:161
  37.8 1.0 reshape.156
  40.0 1.0 convolution_multiply_fusion
  43.1 3.4 %collective-permute-start.1 = (bf16[8,128,256]{1,2,0:T(8,128)(2,1)S(1)}, bf16[8,128,256]{1,2,0:T(8,128)(2,1)S(1)}, u32[]{:S(2)}, u32[]{:S(2)}) collective-permute-start(bf16[8,128,256]{1,2,0:T(8,128)(2,1)S(1)} %copy-done.13), channel_id=1, source_target_pairs={{0,2},{2,4},{4,6},{6,8},{8,10},{10,12},{12,14},{14,16},{16,18},{18... | collective-permute-start | bytes 1572872 | tf_op jit(solution)/shard_map/ppermute | solution.py:50
  47.2 1.3 %fusion.29 = f32[8,64,128]{2,1,0:T(8,128)} fusion(f32[2,8,128,128]{3,2,1,0:T(8,128)S(1)} %convolution_subtract_fusion, f32[2,8,64,128]{3,2,1,0:T(8,128)S(1)} %convolution_subtract_fusion.1), kind=kOutput, calls=%fused_computation.70 | convolution fusion | flops 100663296 | bytes 1048576 | tf_op jit(solution)/shard_map/hid,hde->hie/dot_general | solution.py:250
  48.5 1.1 convolution_add_fusion.9
  49.7 10.5 %collective-permute-done.1 = bf16[8,128,256]{1,2,0:T(8,128)(2,1)S(1)} collective-permute-done((bf16[8,128,256]{1,2,0:T(8,128)(2,1)S(1)}, bf16[8,128,256]{1,2,0:T(8,128)(2,1)S(1)}, u32[]{:S(2)}, u32[]{:S(2)}) %collective-permute-start.1) | collective-permute-done | bytes 524320 | tf_op jit(solution)/shard_map/ppermute | solution.py:50
  60.3 1.2 %fusion.75 = (bf16[8,128,128]{1,2,0:T(8,128)(2,1)S(1)}, f32[8,128,128]{1,2,0:T(8,128)}) fusion(f32[8,128,128]{1,2,0:T(8,128)S(1)} %copy-done.3, f32[8,128,128]{1,2,0:T(8,128)S(1)} %get-tuple-element.43, bf16[8,128,256]{1,2,0:T(8,128)(2,1)S(1)} %collective-permute-done.1), kind=kOutput, calls=%fused_computation.171 | convolution fusion | flops 201588736 | bytes 2097152 | tf_op jit(solution)/shard_map/hde,hef->hdf/dot_general | solution.py:161
  63.0 2.7 %collective-permute-start.2 = (bf16[8,128,256]{1,2,0:T(8,128)(2,1)}, bf16[8,128,256]{1,2,0:T(8,128)(2,1)S(1)}, u32[]{:S(2)}, u32[]{:S(2)}) collective-permute-start(bf16[8,128,256]{1,2,0:T(8,128)(2,1)} %pad_maximum_fusion.2), channel_id=1, source_target_pairs={{0,4},{2,6},{4,8},{6,10},{8,12},{10,14},{12,16},{14,18},{16,20},{1... | collective-permute-start | bytes 1572872 | tf_op jit(solution)/shard_map/ppermute | solution.py:50
  65.9 12.6 %collective-permute-done.2 = bf16[8,128,256]{1,2,0:T(8,128)(2,1)S(1)} collective-permute-done((bf16[8,128,256]{1,2,0:T(8,128)(2,1)}, bf16[8,128,256]{1,2,0:T(8,128)(2,1)S(1)}, u32[]{:S(2)}, u32[]{:S(2)}) %collective-permute-start.2) | collective-permute-done | bytes 524320 | tf_op jit(solution)/shard_map/ppermute | solution.py:50
  80.8 1.3 %collective-permute-start.3 = (bf16[8,128,256]{1,2,0:T(8,128)(2,1)}, bf16[8,128,256]{1,2,0:T(8,128)(2,1)S(1)}, u32[]{:S(2)}, u32[]{:S(2)}) collective-permute-start(bf16[8,128,256]{1,2,0:T(8,128)(2,1)} %pad_maximum_fusion.3), channel_id=1, source_target_pairs={{0,8},{2,10},{4,12},{6,14},{8,16},{10,18},{12,20},{14,22},{16,24},... | collective-permute-start | bytes 1572872 | tf_op jit(solution)/shard_map/ppermute | solution.py:50
  83.6 1.0 fusion.25
  84.6 9.7 %collective-permute-done.3 = bf16[8,128,256]{1,2,0:T(8,128)(2,1)S(1)} collective-permute-done((bf16[8,128,256]{1,2,0:T(8,128)(2,1)}, bf16[8,128,256]{1,2,0:T(8,128)(2,1)S(1)}, u32[]{:S(2)}, u32[]{:S(2)}) %collective-permute-start.3) | collective-permute-done | bytes 524320 | tf_op jit(solution)/shard_map/ppermute | solution.py:50
  94.8 1.4 %collective-permute-start.4 = (bf16[8,128,128]{1,2,0:T(8,128)(2,1)S(1)}, bf16[8,128,128]{1,2,0:T(8,128)(2,1)S(1)}, u32[]{:S(2)}, u32[]{:S(2)}) collective-permute-start(bf16[8,128,128]{1,2,0:T(8,128)(2,1)S(1)} %fusion.4), channel_id=1, source_target_pairs={{0,16},{2,18},{4,20},{6,22},{8,24},{10,26},{12,28},{14,30},{1,17},... | collective-permute-start | bytes 786440 | tf_op jit(solution)/shard_map/ppermute | solution.py:37
  96.9 1.2 %fusion.22 = f32[8,128,128]{2,1,0:T(8,128)S(1)} fusion(f32[8,128,128]{2,1,0:T(8,128)S(1)} %fusion.25, bf16[8,128,256]{1,2,0:T(8,128)(2,1)S(1)} %collective-permute-done.3, f32[128,128]{0,1:T(8,128)S(1)} %copy-done.15), kind=kOutput, calls=%fused_computation.57 | convolution fusion | flops 201588736 | bytes 1376256 | tf_op jit(solution)/shard_map/hde,hef->hdf/dot_general | solution.py:161
  98.2 10.1 %collective-permute-done.4 = bf16[8,128,128]{1,2,0:T(8,128)(2,1)S(1)} collective-permute-done((bf16[8,128,128]{1,2,0:T(8,128)(2,1)S(1)}, bf16[8,128,128]{1,2,0:T(8,128)(2,1)S(1)}, u32[]{:S(2)}, u32[]{:S(2)}) %collective-permute-start.4) | collective-permute-done | bytes 262176 | tf_op jit(solution)/shard_map/ppermute | solution.py:37
  109.0 1.3 %multiply_reduce_fusion = (f32[2,64,8]{1,2,0:T(8,128)S(1)}, f32[2,64,8,128]{3,1,2,0:T(8,128)S(1)}) fusion(f32[1,8,64,128]{3,2,1,0:T(8,128)S(1)} %bitcast.185, f32[1,8,64,128]{3,2,1,0:T(8,128)S(1)} %bitcast.183, f32[8,128,128]{1,2,0:T(8,128)S(1)} %fusion.83, f32[8,128,128]{1,2,0:T(8,128)S(1)} %fusion.56, f32[8,128,128]{1,2,0:T(8,128)S(1)} %fusion.36, ...), kind=kOutput, calls=%fused_computation.56 | convolution fusion | flops 202374144 | bytes 3674112 | tf_op jit(solution)/shard_map/bhid,hde->bhie/dot_general | solution.py:267
  111.7 1.0 fusion.27
  (183 shorter events, 37.5 us)
Async XLA Ops:
  0.0 65.9 %copy-start = (f32[128]{0:T(128)S(1)}, f32[128]{0:T(128)}, u32[]{:S(2)}) copy-start(f32[128]{0:T(128)} %param.29) | copy-start | bytes 1540
  0.8 1.1 copy-start.37
  0.8 1.2 %copy-start.12 = (bf16[128,512]{1,0:T(8,128)(2,1)S(1)}, bf16[128,512]{1,0:T(8,128)(2,1)}, u32[]{:S(2)}) copy-start(bf16[128,512]{1,0:T(8,128)(2,1)} %param.15) | copy-start | bytes 393220
  1.9 1.0 copy-start.8
  3.2 11.9 %collective-permute-start = (f32[3,2048]{1,0:T(4,128)S(1)}, f32[3,2048]{1,0:T(4,128)S(1)}, u32[]{:S(2)}, u32[]{:S(2)}) collective-permute-start(f32[3,2048]{1,0:T(4,128)S(1)} %pad_maximum_fusion.6), channel_id=1, source_target_pairs={{0,2},{2,4},{4,6},{6,8},{8,10},{10,12},{12,14},{14,16},{16,18},{18... | collective-permute-start | bytes 73736 | tf_op jit(solution)/shard_map/ppermute | solution.py:16
  6.7 9.9 %copy-start.19 = (pred[64,64]{1,0:T(8,128)(4,1)}, pred[64,64]{1,0:T(8,128)(4,1)S(1)}, u32[]{:S(2)}) copy-start(pred[64,64]{1,0:T(8,128)(4,1)S(1)} %get-tuple-element.57) | copy-start | bytes 12292
  8.3 1.4 %copy-start.35 = (f32[128,8]{0,1:T(8,128)S(1)}, f32[128,8]{0,1:T(8,128)}, u32[]{:S(2)}) copy-start(f32[128,8]{0,1:T(8,128)} %param.24) | copy-start | bytes 12292
  14.9 1.6 %copy-start.21 = (f32[2,64,8]{1,2,0:T(8,128)}, f32[2,64,8]{1,2,0:T(8,128)S(1)}, u32[]{:S(2)}) copy-start(f32[2,64,8]{1,2,0:T(8,128)S(1)} %copy.224) | copy-start | bytes 12292
  33.4 2.9 %copy-start.1 = (f32[2,8,128,128]{2,3,1,0:T(8,128)}, f32[2,8,128,128]{2,3,1,0:T(8,128)S(1)}, u32[]{:S(2)}) copy-start(f32[2,8,128,128]{2,3,1,0:T(8,128)S(1)} %fusion.31) | copy-start | bytes 3145732
  40.0 1.0 copy-start.17
  41.7 1.4 %copy-start.13 = (bf16[8,128,256]{1,2,0:T(8,128)(2,1)S(1)}, bf16[8,128,256]{1,2,0:T(8,128)(2,1)}, u32[]{:S(2)}) copy-start(bf16[8,128,256]{1,2,0:T(8,128)(2,1)} %pad_maximum_fusion.1) | copy-start | bytes 1572868
  42.4 6.2 %copy-start.2 = (f32[2,8,128,128]{2,3,1,0:T(8,128)S(1)}, f32[2,8,128,128]{2,3,1,0:T(8,128)}, u32[]{:S(2)}) copy-start(f32[2,8,128,128]{2,3,1,0:T(8,128)} %copy-done.1) | copy-start | bytes 3145732
  43.1 17.1 %collective-permute-start.1 = (bf16[8,128,256]{1,2,0:T(8,128)(2,1)S(1)}, bf16[8,128,256]{1,2,0:T(8,128)(2,1)S(1)}, u32[]{:S(2)}, u32[]{:S(2)}) collective-permute-start(bf16[8,128,256]{1,2,0:T(8,128)(2,1)S(1)} %copy-done.13), channel_id=1, source_target_pairs={{0,2},{2,4},{4,6},{6,8},{8,10},{10,12},{12,14},{14,16},{16,18},{18... | collective-permute-start | bytes 1572872 | tf_op jit(solution)/shard_map/ppermute | solution.py:50
  49.7 10.6 %copy-start.3 = (f32[8,128,128]{1,2,0:T(8,128)S(1)}, f32[8,128,128]{1,2,0:T(8,128)}, u32[]{:S(2)}) copy-start(f32[8,128,128]{1,2,0:T(8,128)} %get-tuple-element.41) | copy-start | bytes 1572868
  63.0 15.5 %collective-permute-start.2 = (bf16[8,128,256]{1,2,0:T(8,128)(2,1)}, bf16[8,128,256]{1,2,0:T(8,128)(2,1)S(1)}, u32[]{:S(2)}, u32[]{:S(2)}) collective-permute-start(bf16[8,128,256]{1,2,0:T(8,128)(2,1)} %pad_maximum_fusion.2), channel_id=1, source_target_pairs={{0,4},{2,6},{4,8},{6,10},{8,12},{10,14},{12,16},{14,18},{16,20},{1... | collective-permute-start | bytes 1572872 | tf_op jit(solution)/shard_map/ppermute | solution.py:50
  65.9 13.3 %copy-start.9 = (f32[128,128]{0,1:T(8,128)}, f32[128,128]{0,1:T(8,128)S(1)}, u32[]{:S(2)}) copy-start(f32[128,128]{0,1:T(8,128)S(1)} %copy.137) | copy-start | bytes 196612
  78.5 1.0 copy-start.4
  80.8 13.6 %collective-permute-start.3 = (bf16[8,128,256]{1,2,0:T(8,128)(2,1)}, bf16[8,128,256]{1,2,0:T(8,128)(2,1)S(1)}, u32[]{:S(2)}, u32[]{:S(2)}) collective-permute-start(bf16[8,128,256]{1,2,0:T(8,128)(2,1)} %pad_maximum_fusion.3), channel_id=1, source_target_pairs={{0,8},{2,10},{4,12},{6,14},{8,16},{10,18},{12,20},{14,22},{16,24},... | collective-permute-start | bytes 1572872 | tf_op jit(solution)/shard_map/ppermute | solution.py:50
  94.8 2.1 %copy-start.15 = (f32[128,128]{0,1:T(8,128)S(1)}, f32[128,128]{0,1:T(8,128)}, u32[]{:S(2)}) copy-start(f32[128,128]{0,1:T(8,128)} %copy.144) | copy-start | bytes 196612
  94.8 13.4 %collective-permute-start.4 = (bf16[8,128,128]{1,2,0:T(8,128)(2,1)S(1)}, bf16[8,128,128]{1,2,0:T(8,128)(2,1)S(1)}, u32[]{:S(2)}, u32[]{:S(2)}) collective-permute-start(bf16[8,128,128]{1,2,0:T(8,128)(2,1)S(1)} %fusion.4), channel_id=1, source_target_pairs={{0,16},{2,18},{4,20},{6,22},{8,24},{10,26},{12,28},{14,30},{1,17},... | collective-permute-start | bytes 786440 | tf_op jit(solution)/shard_map/ppermute | solution.py:37
  98.1 10.8 %copy-start.5 = (f32[8,64,128]{2,1,0:T(8,128)S(1)}, f32[8,64,128]{2,1,0:T(8,128)}, u32[]{:S(2)}) copy-start(f32[8,64,128]{2,1,0:T(8,128)} %slice_bitcast_fusion.10) | copy-start | bytes 786436
  98.2 10.8 %copy-start.6 = (f32[8,64,128]{2,1,0:T(8,128)S(1)}, f32[8,64,128]{2,1,0:T(8,128)}, u32[]{:S(2)}) copy-start(f32[8,64,128]{2,1,0:T(8,128)} %slice_bitcast_fusion.13) | copy-start | bytes 786436
  98.2 10.8 %copy-start.7 = (f32[8,64,128]{2,1,0:T(8,128)S(1)}, f32[8,64,128]{2,1,0:T(8,128)}, u32[]{:S(2)}) copy-start(f32[8,64,128]{2,1,0:T(8,128)} %fusion.29) | copy-start | bytes 786436
  110.8 1.0 copy-start.14
  (22 other events, 15.6 us)

commit v7 on v4

--- a/solution.py
+++ b/solution.py
@@ -23,12 +23,15 @@
     while span < devices:
         spans.append(span)
         span = span * 2
+    eye = jnp.eye(trans.shape[-1], dtype=jnp.float32)
     inclusive_maps, exclusive_maps = ([], [None])
     inclusive = trans
     for span in spans[:-1]:
         pairs = [(source, source + span) for source in range(devices - span)]
         inclusive_maps.append(inclusive)
-        earlier = lax.ppermute(inclusive, axis, pairs)
+        reached = jnp.where(mine >= span, 1.0, 0.0)
+        earlier = lax.ppermute((inclusive - eye).astype(jnp.bfloat16), axis, pairs)
+        earlier = earlier.astype(jnp.float32) + reached * eye
         last_map = exclusive_maps[-1]
         exclusive_maps.append(earlier if last_map is None else product(last_map, earlier))
         if 4 * span < devices:
@@ -37,7 +40,7 @@
     carried = offset
     for step, span in enumerate(spans):
         pairs = [(source, source + span) for source in range(devices - span)]
-        earlier = lax.ppermute(carried, axis, pairs)
+        earlier = lax.ppermute(carried.astype(jnp.bfloat16), axis, pairs).astype(jnp.float32)
         last_map = exclusive_maps[step]
         state = earlier if last_map is None else state + product(last_map, earlier)
         if step + 1 < len(spans):

time: 134 us -> 97.3 us (0.73)
  waiting for transfers between devices: 73.1 us -> 33.4 us
  other arithmetic: 4.78 us -> 8.78 us
  matrix products: 28.1 us -> 25.2 us
  local copies, waits for them, and re-layouts: 12.2 us -> 14 us
    ppermute x7, waiting for transfers between devices: 73.1 us -> 33.4 us  [the longest x4 27.1 us: scan_states(): lax.ppermute(carried.astype(jnp.bfloat16), axis, pairs).astype(jnp.float32)]
    dot_general x12, matrix products: 11.2 us -> 8.15 us  [product(): return jnp.einsum('hde,hef->hdf', left, right, precision=HIGHEST)]
    mul x3, other arithmetic: 0.19 us -> 1.7 us  [expand_quantized(): raw_rows.astype(jnp.float32).reshape(row_count, head_count, -1)]
    unnamed x60 -> x86, local copies, waits for them, and re-layouts: 9.98 us -> 9.32 us
  transfers between devices with their start and end apart: 8 -> 8, of which waited for: 6 -> 7; matrix products, arithmetic and copies ran while one was open for 13% -> 12% of each run, Pallas kernels for 0% -> 0%
where the time goes in v7:
time: 97.3 us; the launch traced here: 96.5 us
  waiting for transfers between devices  33.4 us (34%)
  matrix products  25.2 us (26%)
  starting transfers between devices  14.2 us (15%)
  local copies, waits for them, and re-layouts  14 us (14%)
  other arithmetic  8.78 us (9%)
    ppermute x4, waiting for transfers between devices, scan_states(): lax.ppermute(carried.astype(jnp.bfloat16), axis, pairs).astype(jnp.float32)  27.1 us
    unnamed x86, local copies, waits for them, and re-layouts  9.32 us
    dot_general x12, matrix products, product(): return jnp.einsum('hde,hef->hdf', left, right, precision=HIGHEST)  8.15 us
    ppermute x3, waiting for transfers between devices, scan_states(): earlier = lax.ppermute((inclusive - eye).astype(jnp.bfloat16), axis, pairs)  6.25 us
    ppermute x4, starting transfers between devices, scan_states(): lax.ppermute(carried.astype(jnp.bfloat16), axis, pairs).astype(jnp.float32)  6.05 us
    ppermute x3, starting transfers between devices, scan_states(): earlier = lax.ppermute((inclusive - eye).astype(jnp.bfloat16), axis, pairs)  4.73 us
    ppermute x1, starting transfers between devices, from_behind(): lax.ppermute(value, axis, [(source, source + steps) for source in range(f...  3.4 us
    dot_general x5, matrix products, unit_lower_inverse(): jnp.einsum('bhij,bhjk->bhik', inverse, power, precision=HIGHEST)  3.29 us
  transfers between devices with their start and end apart: 8, of which 7 were waited for; matrix products, arithmetic and copies ran while one was open for 12% of the time, Pallas kernels for 0%

profile of v7, /device:TPU:28, one launch (start us, length us, event | category | flops | bytes accessed | tf_op | source)
XLA Modules:
  0.0 96.5 jit_solution(3438177244152229145)
XLA Ops:
  0.8 1.0 %reshape.133 = f32[128,4,128]{2,1,0:T(4,128)S(1)} reshape(bf16[128,512]{1,0:T(8,128)(2,1)} %param.16) | data formatting | bytes 393216 | tf_op jit(solution)/shard_map/reshape | solution.py:54
  3.2 3.4 %collective-permute-start = (f32[3,2048]{1,0:T(4,128)S(1)}, f32[3,2048]{1,0:T(4,128)S(1)}, u32[]{:S(2)}, u32[]{:S(2)}) collective-permute-start(f32[3,2048]{1,0:T(4,128)S(1)} %pad_maximum_fusion.3), channel_id=1, source_target_pairs={{0,2},{2,4},{4,6},{6,8},{8,10},{10,12},{12,14},{14,16},{16,18},{18... | collective-permute-start | bytes 73736 | tf_op jit(solution)/shard_map/ppermute | solution.py:16
  17.9 1.0 %fusion.1 = f32[2,8,64,64]{3,2,1,0:T(8,128)S(1)} fusion(f32[2,8,64,128]{3,2,0,1:T(8,128)S(1)} %bitcast.174, f32[2,8,64]{2,1,0:T(8,128)S(1)} %bitcast.188, f32[2,8,64]{2,1,0:T(8,128)S(1)} %reduce_window_sum.11, pred[64,64]{1,0:T(8,128)(4,1)S(1)} %get-tuple-element.44, pred[64,64]{1,0:T(8,128)(4,1)S(1)} %get-tuple-element.45), kind=kOutput, calls=%fused_computation.13 | convolution fusion | flops 101122048 | bytes 802816 | tf_op jit(solution)/shard_map/bhid,bhjd->bhij/dot_general | solution.py:107
  26.5 1.9 %convolution_subtract_fusion = f32[2,8,128,128]{3,2,1,0:T(8,128)S(1)} fusion(f32[2,8,64,128]{3,2,1,0:T(8,128)S(1)} %fusion.18, f32[128,128]{1,0:T(8,128)S(1)} %fusion.57, f32[2,8]{1,0:T(2,128)S(1)} %slice_reduce_fusion.1, f32[2,8,64,128]{3,2,0,1:T(8,128)S(1)} %get-tuple-element.9), kind=kOutput, calls=%fused_computation | convolution fusion | flops 201850880 | bytes 2162752 | tf_op jit(solution)/shard_map/bhjd,bhje->bhde/dot_general | solution.py:118
  28.4 1.5 %subtract_convert_fusion.2 = (bf16[8,128,128]{2,1,0:T(8,128)(2,1)}, f32[8,128,128]{2,1,0:T(8,128)S(1)}) fusion(f32[128,128]{1,0:T(8,128)S(1)} %fusion.57, f32[2,8,128,128]{3,2,1,0:T(8,128)S(1)} %convolution_subtract_fusion), kind=kOutput, calls=%fused_computation.64 | convolution fusion | flops 201588736 | bytes 1900544 | tf_op jit(solution)/shard_map/hde,hef->hdf/dot_general | solution.py:142
  32.6 1.8 %fusion.33 = f32[2,8,128,128]{3,2,1,0:T(8,128)S(1)} fusion(f32[2,8,64,128]{3,2,1,0:T(8,128)S(1)} %fusion.16, f32[2,8,64,128]{3,2,0,1:T(8,128)S(1)} %get-tuple-element.9), kind=kOutput, calls=%fused_computation.72 | convolution fusion | flops 201326592 | bytes 2097152 | tf_op jit(solution)/shard_map/bhjd,bhje->bhde/dot_general | solution.py:128
  34.4 1.5 %fusion.66 = (bf16[8,128,128]{2,1,0:T(8,128)(2,1)}, f32[8,128,128]{2,1,0:T(8,128)}) fusion(f32[2,8,128,128]{3,2,1,0:T(8,128)S(1)} %fusion.33, f32[2,8,128,128]{3,2,1,0:T(8,128)S(1)} %convolution_subtract_fusion), kind=kOutput, calls=%fused_computation.158 | convolution fusion | flops 201588736 | bytes 2359296 | tf_op jit(solution)/shard_map/hde,hef->hdf/dot_general | solution.py:142
  37.5 1.0 %reshape.156 = f32[128,4,128]{2,1,0:T(4,128)S(1)} reshape(bf16[128,512]{1,0:T(8,128)(2,1)} %multiply_convert_fusion.1) | data formatting | bytes 393216 | tf_op jit(solution)/shard_map/reshape | solution.py:71
  39.7 1.0 convolution_multiply_fusion
  42.5 2.0 %collective-permute-start.1 = (bf16[8,128,128]{2,1,0:T(8,128)(2,1)S(1)}, bf16[8,128,128]{2,1,0:T(8,128)(2,1)S(1)}, u32[]{:S(2)}, u32[]{:S(2)}) collective-permute-start(bf16[8,128,128]{2,1,0:T(8,128)(2,1)S(1)} %copy-done.12), channel_id=1, source_target_pairs={{0,2},{2,4},{4,6},{6,8},{8,10},{10,12},{12,14},{14,16},{16,18},{18... | collective-permute-start | bytes 786440 | tf_op jit(solution)/shard_map/ppermute | solution.py:43
  44.6 1.9 %collective-permute-start.2 = (bf16[8,128,128]{2,1,0:T(8,128)(2,1)S(1)}, bf16[8,128,128]{2,1,0:T(8,128)(2,1)S(1)}, u32[]{:S(2)}, u32[]{:S(2)}) collective-permute-start(bf16[8,128,128]{2,1,0:T(8,128)(2,1)S(1)} %copy-done.14), channel_id=1, source_target_pairs={{0,2},{2,4},{4,6},{6,8},{8,10},{10,12},{12,14},{14,16},{16,18},{18... | collective-permute-start | bytes 786440 | tf_op jit(solution)/shard_map/ppermute | solution.py:33
  47.8 6.9 %collective-permute-done.1 = bf16[8,128,128]{2,1,0:T(8,128)(2,1)S(1)} collective-permute-done((bf16[8,128,128]{2,1,0:T(8,128)(2,1)S(1)}, bf16[8,128,128]{2,1,0:T(8,128)(2,1)S(1)}, u32[]{:S(2)}, u32[]{:S(2)}) %collective-permute-start.1) | collective-permute-done | bytes 262176 | tf_op jit(solution)/shard_map/ppermute | solution.py:43
  55.0 1.3 %collective-permute-start.3 = (bf16[8,128,128]{2,1,0:T(8,128)(2,1)S(1)}, bf16[8,128,128]{2,1,0:T(8,128)(2,1)S(1)}, u32[]{:S(2)}, u32[]{:S(2)}) collective-permute-start(bf16[8,128,128]{2,1,0:T(8,128)(2,1)S(1)} %get-tuple-element.36), channel_id=1, source_target_pairs={{0,4},{2,6},{4,8},{6,10},{8,12},{10,14},{12,16},{14,18},{16,20},{1... | collective-permute-start | bytes 786440 | tf_op jit(solution)/shard_map/ppermute | solution.py:43
  56.3 2.6 %collective-permute-done.2 = bf16[8,128,128]{2,1,0:T(8,128)(2,1)S(1)} collective-permute-done((bf16[8,128,128]{2,1,0:T(8,128)(2,1)S(1)}, bf16[8,128,128]{2,1,0:T(8,128)(2,1)S(1)}, u32[]{:S(2)}, u32[]{:S(2)}) %collective-permute-start.2) | collective-permute-done | bytes 262176 | tf_op jit(solution)/shard_map/ppermute | solution.py:33
  59.6 1.3 %collective-permute-start.4 = (bf16[8,128,128]{2,1,0:T(8,128)(2,1)S(1)}, bf16[8,128,128]{2,1,0:T(8,128)(2,1)S(1)}, u32[]{:S(2)}, u32[]{:S(2)}) collective-permute-start(bf16[8,128,128]{2,1,0:T(8,128)(2,1)S(1)} %get-tuple-element.30), channel_id=1, source_target_pairs={{0,4},{2,6},{4,8},{6,10},{8,12},{10,14},{12,16},{14,18},{16,20},{1... | collective-permute-start | bytes 786440 | tf_op jit(solution)/shard_map/ppermute | solution.py:33
  60.9 5.3 %collective-permute-done.3 = bf16[8,128,128]{2,1,0:T(8,128)(2,1)S(1)} collective-permute-done((bf16[8,128,128]{2,1,0:T(8,128)(2,1)S(1)}, bf16[8,128,128]{2,1,0:T(8,128)(2,1)S(1)}, u32[]{:S(2)}, u32[]{:S(2)}) %collective-permute-start.3) | collective-permute-done | bytes 262176 | tf_op jit(solution)/shard_map/ppermute | solution.py:43
  66.6 1.3 %collective-permute-start.5 = (bf16[8,128,128]{2,1,0:T(8,128)(2,1)S(1)}, bf16[8,128,128]{2,1,0:T(8,128)(2,1)S(1)}, u32[]{:S(2)}, u32[]{:S(2)}) collective-permute-start(bf16[8,128,128]{2,1,0:T(8,128)(2,1)S(1)} %get-tuple-element.38), channel_id=1, source_target_pairs={{0,8},{2,10},{4,12},{6,14},{8,16},{10,18},{12,20},{14,22},{16,24},... | collective-permute-start | bytes 786440 | tf_op jit(solution)/shard_map/ppermute | solution.py:43
  67.9 2.2 %collective-permute-done.4 = bf16[8,128,128]{2,1,0:T(8,128)(2,1)S(1)} collective-permute-done((bf16[8,128,128]{2,1,0:T(8,128)(2,1)S(1)}, bf16[8,128,128]{2,1,0:T(8,128)(2,1)S(1)}, u32[]{:S(2)}, u32[]{:S(2)}) %collective-permute-start.4) | collective-permute-done | bytes 262176 | tf_op jit(solution)/shard_map/ppermute | solution.py:33
  70.7 1.5 %collective-permute-start.6 = (bf16[8,128,128]{2,1,0:T(8,128)(2,1)S(1)}, bf16[8,128,128]{2,1,0:T(8,128)(2,1)S(1)}, u32[]{:S(2)}, u32[]{:S(2)}) collective-permute-start(bf16[8,128,128]{2,1,0:T(8,128)(2,1)S(1)} %get-tuple-element.32), channel_id=1, source_target_pairs={{0,8},{2,10},{4,12},{6,14},{8,16},{10,18},{12,20},{14,22},{16,24},... | collective-permute-start | bytes 786440 | tf_op jit(solution)/shard_map/ppermute | solution.py:33
  73.3 5.6 %collective-permute-done.5 = bf16[8,128,128]{2,1,0:T(8,128)(2,1)S(1)} collective-permute-done((bf16[8,128,128]{2,1,0:T(8,128)(2,1)S(1)}, bf16[8,128,128]{2,1,0:T(8,128)(2,1)S(1)}, u32[]{:S(2)}, u32[]{:S(2)}) %collective-permute-start.5) | collective-permute-done | bytes 262176 | tf_op jit(solution)/shard_map/ppermute | solution.py:43
  79.4 1.4 %collective-permute-start.7 = (bf16[8,128,128]{2,1,0:T(8,128)(2,1)S(1)}, bf16[8,128,128]{2,1,0:T(8,128)(2,1)S(1)}, u32[]{:S(2)}, u32[]{:S(2)}) collective-permute-start(bf16[8,128,128]{2,1,0:T(8,128)(2,1)S(1)} %fusion.4), channel_id=1, source_target_pairs={{0,16},{2,18},{4,20},{6,22},{8,24},{10,26},{12,28},{14,30},{1,17},... | collective-permute-start | bytes 786440 | tf_op jit(solution)/shard_map/ppermute | solution.py:43
  81.2 1.5 %collective-permute-done.6 = bf16[8,128,128]{2,1,0:T(8,128)(2,1)S(1)} collective-permute-done((bf16[8,128,128]{2,1,0:T(8,128)(2,1)S(1)}, bf16[8,128,128]{2,1,0:T(8,128)(2,1)S(1)}, u32[]{:S(2)}, u32[]{:S(2)}) %collective-permute-start.6) | collective-permute-done | bytes 262176 | tf_op jit(solution)/shard_map/ppermute | solution.py:33
  83.4 9.4 %collective-permute-done.7 = bf16[8,128,128]{2,1,0:T(8,128)(2,1)S(1)} collective-permute-done((bf16[8,128,128]{2,1,0:T(8,128)(2,1)S(1)}, bf16[8,128,128]{2,1,0:T(8,128)(2,1)S(1)}, u32[]{:S(2)}, u32[]{:S(2)}) %collective-permute-start.7) | collective-permute-done | bytes 262176 | tf_op jit(solution)/shard_map/ppermute | solution.py:43
  95.5 1.0 %fusion.30 = bf16[128,1024]{1,0:T(8,128)(2,1)} fusion(bf16[128,1024]{1,0:T(8,128)(2,1)S(1)} %copy-done.13, f32[16,8,8,128]{3,2,1,0:T(8,128)S(1)} %bitcast.181, f32[16,8,8,128]{3,2,1,0:T(8,128)S(1)} %bitcast.179, f32[1024]{0:T(1024)S(1)} %broadcast_bitcast_fusion), kind=kLoop, calls=%fused_computation.69 | loop fusion | flops 1179648 | bytes 1576960 | tf_op jit(solution)/shard_map/convert_element_type | solution.py:153
  (182 shorter events, 36.2 us)
Async XLA Ops:
  0.0 15.8 %copy-start = (f32[128]{0:T(128)S(1)}, f32[128]{0:T(128)}, u32[]{:S(2)}) copy-start(f32[128]{0:T(128)} %param.29) | copy-start | bytes 1540
  3.2 13.3 %collective-permute-start = (f32[3,2048]{1,0:T(4,128)S(1)}, f32[3,2048]{1,0:T(4,128)S(1)}, u32[]{:S(2)}, u32[]{:S(2)}) collective-permute-start(f32[3,2048]{1,0:T(4,128)S(1)} %pad_maximum_fusion.3), channel_id=1, source_target_pairs={{0,2},{2,4},{4,6},{6,8},{8,10},{10,12},{12,14},{14,16},{16,18},{18... | collective-permute-start | bytes 73736 | tf_op jit(solution)/shard_map/ppermute | solution.py:16
  6.7 11.2 %copy-start.18 = (pred[64,64]{1,0:T(8,128)(4,1)}, pred[64,64]{1,0:T(8,128)(4,1)S(1)}, u32[]{:S(2)}) copy-start(pred[64,64]{1,0:T(8,128)(4,1)S(1)} %get-tuple-element.45) | copy-start | bytes 12292
  16.5 1.4 %copy-start.20 = (f32[2,64,8]{1,2,0:T(8,128)}, f32[2,64,8]{1,2,0:T(8,128)S(1)}, u32[]{:S(2)}) copy-start(f32[2,64,8]{1,2,0:T(8,128)S(1)} %copy.129) | copy-start | bytes 12292
  28.4 1.6 %copy-start.5 = (f32[128,1024]{1,0:T(8,128)S(1)}, f32[128,1024]{1,0:T(8,128)}, u32[]{:S(2)}) copy-start(f32[128,1024]{1,0:T(8,128)} %convert_multiply_fusion.1) | copy-start | bytes 1572868
  34.4 1.6 %copy-start.1 = (f32[2,8,128,128]{3,2,1,0:T(8,128)}, f32[2,8,128,128]{3,2,1,0:T(8,128)S(1)}, u32[]{:S(2)}) copy-start(f32[2,8,128,128]{3,2,1,0:T(8,128)S(1)} %fusion.33) | copy-start | bytes 3145732
  34.4 1.6 %copy-start.8 = (f32[128,512]{1,0:T(8,128)S(1)}, f32[128,512]{1,0:T(8,128)}, u32[]{:S(2)}) copy-start(f32[128,512]{1,0:T(8,128)} %bitcast_multiply_fusion.5) | copy-start | bytes 786436
  34.4 1.6 %copy-start.22 = (f32[3,512]{1,0:T(4,128)S(1)}, f32[3,512]{1,0:T(4,128)}, u32[]{:S(2)}) copy-start(f32[3,512]{1,0:T(4,128)} %get-tuple-element.11) | copy-start | bytes 18436
  41.4 5.7 %copy-start.4 = (f32[2,8,64,128]{3,2,1,0:T(8,128)}, f32[2,8,64,128]{3,2,1,0:T(8,128)S(1)}, u32[]{:S(2)}) copy-start(f32[2,8,64,128]{3,2,1,0:T(8,128)S(1)} %fusion.74) | copy-start | bytes 1572868
  41.4 3.2 %copy-start.14 = (bf16[8,128,128]{2,1,0:T(8,128)(2,1)S(1)}, bf16[8,128,128]{2,1,0:T(8,128)(2,1)}, u32[]{:S(2)}) copy-start(bf16[8,128,128]{2,1,0:T(8,128)(2,1)} %get-tuple-element.28) | copy-start | bytes 786436
  42.1 5.0 %copy-start.3 = (f32[2,8,64,128]{3,2,1,0:T(8,128)}, f32[2,8,64,128]{3,2,1,0:T(8,128)S(1)}, u32[]{:S(2)}) copy-start(f32[2,8,64,128]{3,2,1,0:T(8,128)S(1)} %convolution_subtract_fusion.1) | copy-start | bytes 1572868
  42.1 5.0 %copy-start.2 = (f32[2,8,128,128]{3,2,1,0:T(8,128)S(1)}, f32[2,8,128,128]{3,2,1,0:T(8,128)}, u32[]{:S(2)}) copy-start(f32[2,8,128,128]{3,2,1,0:T(8,128)} %copy-done.1) | copy-start | bytes 3145732
  42.5 12.1 %collective-permute-start.1 = (bf16[8,128,128]{2,1,0:T(8,128)(2,1)S(1)}, bf16[8,128,128]{2,1,0:T(8,128)(2,1)S(1)}, u32[]{:S(2)}, u32[]{:S(2)}) collective-permute-start(bf16[8,128,128]{2,1,0:T(8,128)(2,1)S(1)} %copy-done.12), channel_id=1, source_target_pairs={{0,2},{2,4},{4,6},{6,8},{8,10},{10,12},{12,14},{14,16},{16,18},{18... | collective-permute-start | bytes 786440 | tf_op jit(solution)/shard_map/ppermute | solution.py:43
  44.6 14.3 %collective-permute-start.2 = (bf16[8,128,128]{2,1,0:T(8,128)(2,1)S(1)}, bf16[8,128,128]{2,1,0:T(8,128)(2,1)S(1)}, u32[]{:S(2)}, u32[]{:S(2)}) collective-permute-start(bf16[8,128,128]{2,1,0:T(8,128)(2,1)S(1)} %copy-done.14), channel_id=1, source_target_pairs={{0,2},{2,4},{4,6},{6,8},{8,10},{10,12},{12,14},{14,16},{16,18},{18... | collective-permute-start | bytes 786440 | tf_op jit(solution)/shard_map/ppermute | solution.py:33
  47.1 7.5 %copy-start.6 = (f32[8,128,128]{2,1,0:T(8,128)S(1)}, f32[8,128,128]{2,1,0:T(8,128)}, u32[]{:S(2)}) copy-start(f32[8,128,128]{2,1,0:T(8,128)} %get-tuple-element.35) | copy-start | bytes 1572868
  55.0 11.1 %collective-permute-start.3 = (bf16[8,128,128]{2,1,0:T(8,128)(2,1)S(1)}, bf16[8,128,128]{2,1,0:T(8,128)(2,1)S(1)}, u32[]{:S(2)}, u32[]{:S(2)}) collective-permute-start(bf16[8,128,128]{2,1,0:T(8,128)(2,1)S(1)} %get-tuple-element.36), channel_id=1, source_target_pairs={{0,4},{2,6},{4,8},{6,10},{8,12},{10,14},{12,16},{14,18},{16,20},{1... | collective-permute-start | bytes 786440 | tf_op jit(solution)/shard_map/ppermute | solution.py:43
  59.6 10.4 %collective-permute-start.4 = (bf16[8,128,128]{2,1,0:T(8,128)(2,1)S(1)}, bf16[8,128,128]{2,1,0:T(8,128)(2,1)S(1)}, u32[]{:S(2)}, u32[]{:S(2)}) collective-permute-start(bf16[8,128,128]{2,1,0:T(8,128)(2,1)S(1)} %get-tuple-element.30), channel_id=1, source_target_pairs={{0,4},{2,6},{4,8},{6,10},{8,12},{10,14},{12,16},{14,18},{16,20},{1... | collective-permute-start | bytes 786440 | tf_op jit(solution)/shard_map/ppermute | solution.py:33
  66.2 3.9 %copy-start.9 = (f32[128,128]{1,0:T(8,128)S(1)}, f32[128,128]{1,0:T(8,128)}, u32[]{:S(2)}) copy-start(f32[128,128]{1,0:T(8,128)} %fusion.55) | copy-start | bytes 196612
  66.6 12.4 %collective-permute-start.5 = (bf16[8,128,128]{2,1,0:T(8,128)(2,1)S(1)}, bf16[8,128,128]{2,1,0:T(8,128)(2,1)S(1)}, u32[]{:S(2)}, u32[]{:S(2)}) collective-permute-start(bf16[8,128,128]{2,1,0:T(8,128)(2,1)S(1)} %get-tuple-element.38), channel_id=1, source_target_pairs={{0,8},{2,10},{4,12},{6,14},{8,16},{10,18},{12,20},{14,22},{16,24},... | collective-permute-start | bytes 786440 | tf_op jit(solution)/shard_map/ppermute | solution.py:43
  70.7 12.0 %collective-permute-start.6 = (bf16[8,128,128]{2,1,0:T(8,128)(2,1)S(1)}, bf16[8,128,128]{2,1,0:T(8,128)(2,1)S(1)}, u32[]{:S(2)}, u32[]{:S(2)}) collective-permute-start(bf16[8,128,128]{2,1,0:T(8,128)(2,1)S(1)} %get-tuple-element.32), channel_id=1, source_target_pairs={{0,8},{2,10},{4,12},{6,14},{8,16},{10,18},{12,20},{14,22},{16,24},... | collective-permute-start | bytes 786440 | tf_op jit(solution)/shard_map/ppermute | solution.py:33
  79.4 3.4 %copy-start.15 = (f32[128,128]{1,0:T(8,128)S(1)}, f32[128,128]{1,0:T(8,128)}, u32[]{:S(2)}) copy-start(f32[128,128]{1,0:T(8,128)} %fusion.54) | copy-start | bytes 196612
  79.4 13.4 %collective-permute-start.7 = (bf16[8,128,128]{2,1,0:T(8,128)(2,1)S(1)}, bf16[8,128,128]{2,1,0:T(8,128)(2,1)S(1)}, u32[]{:S(2)}, u32[]{:S(2)}) collective-permute-start(bf16[8,128,128]{2,1,0:T(8,128)(2,1)S(1)} %fusion.4), channel_id=1, source_target_pairs={{0,16},{2,18},{4,20},{6,22},{8,24},{10,26},{12,28},{14,30},{1,17},... | collective-permute-start | bytes 786440 | tf_op jit(solution)/shard_map/ppermute | solution.py:43
  83.4 9.8 %slice-start = ((f32[2,8,64,128]{3,2,1,0:T(8,128)}), f32[1,8,64,128]{3,2,1,0:T(8,128)S(1)}, s32[]{:S(2)}) async-start(f32[2,8,64,128]{3,2,1,0:T(8,128)} %copy-done.3), calls=%async_computation | async-start | bytes 524288 | tf_op jit(solution)/shard_map/slice | solution.py:229
  83.4 9.8 %slice-start.1 = ((f32[2,8,64,128]{3,2,1,0:T(8,128)}), f32[1,8,64,128]{3,2,1,0:T(8,128)S(1)}, s32[]{:S(2)}) async-start(f32[2,8,64,128]{3,2,1,0:T(8,128)} %copy-done.4), calls=%async_computation.1 | async-start | bytes 524288 | tf_op jit(solution)/shard_map/slice | solution.py:229
  (26 other events, 20.7 us)

commit v8 on v7

--- a/solution.py
+++ b/solution.py
@@ -16,7 +16,7 @@
     return lax.ppermute(value, axis, [(source, source + steps) for source in range(first, last)])
 
 
-def scan_states(trans, offset, axis):
+def scan_states(trans, offset, axis, rider):
     devices, mine = (lax.axis_size(axis), lax.axis_index(axis))
     spans = []
     span = 1
@@ -31,6 +31,8 @@
         inclusive_maps.append(inclusive)
         reached = jnp.where(mine >= span, 1.0, 0.0)
         earlier = lax.ppermute((inclusive - eye).astype(jnp.bfloat16), axis, pairs)
+        if span == 1:
+            rider, earlier = lax.optimization_barrier((rider, earlier))
         earlier = earlier.astype(jnp.float32) + reached * eye
         last_map = exclusive_maps[-1]
         exclusive_maps.append(earlier if last_map is None else product(last_map, earlier))
@@ -40,12 +42,15 @@
     carried = offset
     for step, span in enumerate(spans):
         pairs = [(source, source + span) for source in range(devices - span)]
-        earlier = lax.ppermute(carried.astype(jnp.bfloat16), axis, pairs).astype(jnp.float32)
+        earlier = lax.ppermute(carried.astype(jnp.bfloat16), axis, pairs)
+        if devices == 2:
+            rider, earlier = lax.optimization_barrier((rider, earlier))
+        earlier = earlier.astype(jnp.float32)
         last_map = exclusive_maps[step]
         state = earlier if last_map is None else state + product(last_map, earlier)
         if step + 1 < len(spans):
             carried = product(inclusive_maps[step], earlier) + carried
-    return state
+    return (state, rider)
 
 
 def expand_quantized(raw_rows, scales):
@@ -217,8 +222,8 @@
     for block in range(1, transition.shape[0]):
         offset_before.append(dev_offset)
         dev_offset = product(transition[block], dev_offset) + offset[block]
-    query_window, _ = lax.optimization_barrier(
-        (jnp.concatenate([tail_rows[0], query_deq], axis=0), dev_offset)
+    incoming, query_window = scan_states(
+        dev_trans, dev_offset, "seq", jnp.concatenate([tail_rows[0], query_deq], axis=0)
     )
     query_conv = causal_filter(query_window, conv_query)
     query_rows = unit_heads(query_conv, head_width) * head_width ** (-0.5)
@@ -235,7 +240,6 @@
             zero_out[block]
             + jnp.einsum("hid,hde->hie", readout[block], offset_before[block], precision=HIGHEST)
         )
-    incoming = scan_states(dev_trans, dev_offset, "seq")
     outputs = jnp.stack(local_outs) + jnp.einsum(
         "bhid,hde->bhie", jnp.stack(read_maps), incoming, precision=HIGHEST
     )

time: 97.3 us -> 99.9 us (1.027)
  local copies, waits for them, and re-layouts: 14 us -> 16 us
  waiting for transfers between devices: 33.4 us -> 31.7 us
  matrix products: 25.2 us -> 26.4 us
  other arithmetic: 8.78 us -> 9.78 us
    ppermute x4, waiting for transfers between devices: 27.1 us -> 22.9 us  [scan_states(): earlier = lax.ppermute(carried.astype(jnp.bfloat16), axis, pairs)]
    ppermute x3, waiting for transfers between devices: 6.25 us -> 8.76 us  [scan_states(): earlier = lax.ppermute((inclusive - eye).astype(jnp.bfloat16), axis, pairs)]
    unnamed x86 -> x82, local copies, waits for them, and re-layouts: 9.32 us -> 11.5 us
    reduce_sum x2, other arithmetic: 0.41 us -> 1.43 us  [unit_heads(): jnp.sum(shaped * shaped, axis=-1, keepdims=True) + EPSILON]
  transfers between devices with their start and end apart: 8 -> 8, of which waited for: 7 -> 5; matrix products, arithmetic and copies ran while one was open for 12% -> 23% of each run, Pallas kernels for 0% -> 0%
where the time goes in v8:
time: 99.9 us; the launch traced here: 98.9 us
  waiting for transfers between devices  31.7 us (32%)
  matrix products  26.4 us (26%)
  local copies, waits for them, and re-layouts  16 us (16%)
  starting transfers between devices  14.2 us (14%)
  other arithmetic  9.78 us (10%)
    ppermute x4, waiting for transfers between devices, scan_states(): earlier = lax.ppermute(carried.astype(jnp.bfloat16), axis, pairs)  22.9 us
    unnamed x82, local copies, waits for them, and re-layouts  11.5 us
    ppermute x3, waiting for transfers between devices, scan_states(): earlier = lax.ppermute((inclusive - eye).astype(jnp.bfloat16), axis, pairs)  8.76 us
    dot_general x12, matrix products, product(): return jnp.einsum('hde,hef->hdf', left, right, precision=HIGHEST)  8.2 us
    ppermute x4, starting transfers between devices, scan_states(): earlier = lax.ppermute(carried.astype(jnp.bfloat16), axis, pairs)  6.27 us
    ppermute x3, starting transfers between devices, scan_states(): earlier = lax.ppermute((inclusive - eye).astype(jnp.bfloat16), axis, pairs)  4.5 us
    ppermute x1, starting transfers between devices, from_behind(): lax.ppermute(value, axis, [(source, source + steps) for source in range(f...  3.4 us
    dot_general x5, matrix products, unit_lower_inverse(): jnp.einsum('bhij,bhjk->bhik', inverse, power, precision=HIGHEST)  3.29 us
  transfers between devices with their start and end apart: 8, of which 5 were waited for; matrix products, arithmetic and copies ran while one was open for 23% of the time, Pallas kernels for 0%

profile of v8, /device:TPU:28, one launch (start us, length us, event | category | flops | bytes accessed | tf_op | source)
XLA Modules:
  0.0 98.9 jit_solution(10618563489195390287)
XLA Ops:
  4.7 3.4 %collective-permute-start = (f32[3,2048]{1,0:T(4,128)S(1)}, f32[3,2048]{1,0:T(4,128)S(1)}, u32[]{:S(2)}, u32[]{:S(2)}) collective-permute-start(f32[3,2048]{1,0:T(4,128)S(1)} %pad_maximum_fusion.3), channel_id=1, source_target_pairs={{0,2},{2,4},{4,6},{6,8},{8,10},{10,12},{12,14},{14,16},{16,18},{18... | collective-permute-start | bytes 73736 | tf_op jit(solution)/shard_map/ppermute | solution.py:16
  16.2 0.9 convert_multiply_fusion.1
  19.2 1.0 %fusion.1 = f32[2,8,64,64]{3,2,1,0:T(8,128)S(1)} fusion(f32[2,8,64,128]{3,2,0,1:T(8,128)S(1)} %bitcast.174, f32[2,8,64]{2,1,0:T(8,128)S(1)} %bitcast.188, f32[2,8,64]{2,1,0:T(8,128)S(1)} %reduce_window_sum.11, pred[64,64]{1,0:T(8,128)(4,1)S(1)} %get-tuple-element.46, pred[64,64]{1,0:T(8,128)(4,1)S(1)} %get-tuple-element.47), kind=kOutput, calls=%fused_computation.13 | convolution fusion | flops 101122048 | bytes 802816 | tf_op jit(solution)/shard_map/bhid,bhjd->bhij/dot_general | solution.py:112
  27.8 2.1 %convolution_subtract_fusion = f32[2,8,128,128]{3,2,1,0:T(8,128)S(1)} fusion(f32[2,8,64,128]{3,2,1,0:T(8,128)S(1)} %fusion.18, f32[128,128]{1,0:T(8,128)S(1)} %fusion.57, f32[2,8]{1,0:T(2,128)S(1)} %slice_reduce_fusion.1, f32[2,8,64,128]{3,2,0,1:T(8,128)S(1)} %get-tuple-element.11), kind=kOutput, calls=%fused_computation | convolution fusion | flops 201850880 | bytes 2162752 | tf_op jit(solution)/shard_map/bhjd,bhje->bhde/dot_general | solution.py:123
  33.5 1.9 %collective-permute-start.1 = (bf16[8,128,128]{2,1,0:T(8,128)(2,1)S(1)}, bf16[8,128,128]{2,1,0:T(8,128)(2,1)S(1)}, u32[]{:S(2)}, u32[]{:S(2)}) collective-permute-start(bf16[8,128,128]{2,1,0:T(8,128)(2,1)S(1)} %get-tuple-element.30), channel_id=1, source_target_pairs={{0,2},{2,4},{4,6},{6,8},{8,10},{10,12},{12,14},{14,16},{16,18},{18... | collective-permute-start | bytes 786440 | tf_op jit(solution)/shard_map/ppermute | solution.py:33
  35.4 1.8 %fusion.33 = f32[2,8,128,128]{3,2,1,0:T(8,128)S(1)} fusion(f32[2,8,64,128]{3,2,1,0:T(8,128)S(1)} %fusion.15, f32[2,8,64,128]{3,2,0,1:T(8,128)S(1)} %get-tuple-element.11), kind=kOutput, calls=%fused_computation.72 | convolution fusion | flops 201326592 | bytes 2097152 | tf_op jit(solution)/shard_map/bhjd,bhje->bhde/dot_general | solution.py:133
  37.3 1.5 %fusion.66 = (bf16[8,128,128]{2,1,0:T(8,128)(2,1)}, f32[8,128,128]{2,1,0:T(8,128)}) fusion(f32[2,8,128,128]{3,2,1,0:T(8,128)S(1)} %fusion.33, f32[2,8,128,128]{3,2,1,0:T(8,128)S(1)} %convolution_subtract_fusion), kind=kOutput, calls=%fused_computation.158 | convolution fusion | flops 201588736 | bytes 2359296 | tf_op jit(solution)/shard_map/hde,hef->hdf/dot_general | solution.py:147
  38.8 1.9 %collective-permute-start.2 = (bf16[8,128,128]{2,1,0:T(8,128)(2,1)}, bf16[8,128,128]{2,1,0:T(8,128)(2,1)}, u32[]{:S(2)}, u32[]{:S(2)}) collective-permute-start(bf16[8,128,128]{2,1,0:T(8,128)(2,1)} %get-tuple-element.36), channel_id=1, source_target_pairs={{0,2},{2,4},{4,6},{6,8},{8,10},{10,12},{12,14},{14,16},{16,18},{18... | collective-permute-start | bytes 786440 | tf_op jit(solution)/shard_map/ppermute | solution.py:45
  40.8 3.3 %collective-permute-done.1 = bf16[8,128,128]{2,1,0:T(8,128)(2,1)S(1)} collective-permute-done((bf16[8,128,128]{2,1,0:T(8,128)(2,1)S(1)}, bf16[8,128,128]{2,1,0:T(8,128)(2,1)S(1)}, u32[]{:S(2)}, u32[]{:S(2)}) %collective-permute-start.1) | collective-permute-done | bytes 262176 | tf_op jit(solution)/shard_map/ppermute | solution.py:33
  45.6 1.7 %reshape.152 = f32[128,4,128]{2,1,0:T(4,128)} reshape(bf16[128,512]{1,0:T(8,128)(2,1)} %multiply_convert_fusion.1) | data formatting | bytes 393216 | tf_op jit(solution)/shard_map/reshape | solution.py:76
  47.3 1.2 %multiply_reduce_fusion.1 = f32[128,4]{1,0:T(8,128)S(1)} fusion(f32[128,4,128]{2,1,0:T(4,128)} %reshape.152), kind=kLoop, calls=%fused_computation.103 | loop fusion | flops 130560 | bytes 264192 | tf_op jit(solution)/shard_map/reduce_sum | solution.py:77
  49.5 1.0 convolution_multiply_fusion
  52.6 1.3 %collective-permute-start.4 = (bf16[8,128,128]{2,1,0:T(8,128)(2,1)S(1)}, bf16[8,128,128]{2,1,0:T(8,128)(2,1)S(1)}, u32[]{:S(2)}, u32[]{:S(2)}) collective-permute-start(bf16[8,128,128]{2,1,0:T(8,128)(2,1)S(1)} %get-tuple-element.32), channel_id=1, source_target_pairs={{0,4},{2,6},{4,8},{6,10},{8,12},{10,14},{12,16},{14,18},{16,20},{1... | collective-permute-start | bytes 786440 | tf_op jit(solution)/shard_map/ppermute | solution.py:33
  53.9 1.3 %fusion.67 = (bf16[8,128,128]{2,1,0:T(8,128)(2,1)S(1)}, f32[8,128,128]{2,1,0:T(8,128)S(1)}) fusion(f32[8,128,128]{2,1,0:T(8,128)S(1)} %copy-done.7, f32[8,128,128]{2,1,0:T(8,128)S(1)} %get-tuple-element.31, bf16[8,128,128]{2,1,0:T(8,128)(2,1)} %collective-permute-done.2), kind=kOutput, calls=%fused_computation.159 | convolution fusion | flops 201588736 | bytes 2097152 | tf_op jit(solution)/shard_map/hde,hef->hdf/dot_general | solution.py:147
  55.2 1.4 %collective-permute-start.3 = (bf16[8,128,128]{2,1,0:T(8,128)(2,1)S(1)}, bf16[8,128,128]{2,1,0:T(8,128)(2,1)S(1)}, u32[]{:S(2)}, u32[]{:S(2)}) collective-permute-start(bf16[8,128,128]{2,1,0:T(8,128)(2,1)S(1)} %get-tuple-element.38), channel_id=1, source_target_pairs={{0,4},{2,6},{4,8},{6,10},{8,12},{10,14},{12,16},{14,18},{16,20},{1... | collective-permute-start | bytes 786440 | tf_op jit(solution)/shard_map/ppermute | solution.py:45
  58.0 5.5 %collective-permute-done.4 = bf16[8,128,128]{2,1,0:T(8,128)(2,1)S(1)} collective-permute-done((bf16[8,128,128]{2,1,0:T(8,128)(2,1)S(1)}, bf16[8,128,128]{2,1,0:T(8,128)(2,1)S(1)}, u32[]{:S(2)}, u32[]{:S(2)}) %collective-permute-start.4) | collective-permute-done | bytes 262176 | tf_op jit(solution)/shard_map/ppermute | solution.py:33
  64.1 1.3 %collective-permute-start.6 = (bf16[8,128,128]{2,1,0:T(8,128)(2,1)S(1)}, bf16[8,128,128]{2,1,0:T(8,128)(2,1)S(1)}, u32[]{:S(2)}, u32[]{:S(2)}) collective-permute-start(bf16[8,128,128]{2,1,0:T(8,128)(2,1)S(1)} %get-tuple-element.34), channel_id=1, source_target_pairs={{0,8},{2,10},{4,12},{6,14},{8,16},{10,18},{12,20},{14,22},{16,24},... | collective-permute-start | bytes 786440 | tf_op jit(solution)/shard_map/ppermute | solution.py:33
  65.4 1.5 %collective-permute-done.3 = bf16[8,128,128]{2,1,0:T(8,128)(2,1)S(1)} collective-permute-done((bf16[8,128,128]{2,1,0:T(8,128)(2,1)S(1)}, bf16[8,128,128]{2,1,0:T(8,128)(2,1)S(1)}, u32[]{:S(2)}, u32[]{:S(2)}) %collective-permute-start.3) | collective-permute-done | bytes 262176 | tf_op jit(solution)/shard_map/ppermute | solution.py:45
  67.3 1.5 %collective-permute-start.5 = (bf16[8,128,128]{2,1,0:T(8,128)(2,1)S(1)}, bf16[8,128,128]{2,1,0:T(8,128)(2,1)S(1)}, u32[]{:S(2)}, u32[]{:S(2)}) collective-permute-start(bf16[8,128,128]{2,1,0:T(8,128)(2,1)S(1)} %get-tuple-element.40), channel_id=1, source_target_pairs={{0,8},{2,10},{4,12},{6,14},{8,16},{10,18},{12,20},{14,22},{16,24},... | collective-permute-start | bytes 786440 | tf_op jit(solution)/shard_map/ppermute | solution.py:45
  69.9 9.1 %collective-permute-done.5 = bf16[8,128,128]{2,1,0:T(8,128)(2,1)S(1)} collective-permute-done((bf16[8,128,128]{2,1,0:T(8,128)(2,1)S(1)}, bf16[8,128,128]{2,1,0:T(8,128)(2,1)S(1)}, u32[]{:S(2)}, u32[]{:S(2)}) %collective-permute-start.5) | collective-permute-done | bytes 262176 | tf_op jit(solution)/shard_map/ppermute | solution.py:45
  79.4 1.4 %collective-permute-start.7 = (bf16[8,128,128]{2,1,0:T(8,128)(2,1)S(1)}, bf16[8,128,128]{2,1,0:T(8,128)(2,1)S(1)}, u32[]{:S(2)}, u32[]{:S(2)}) collective-permute-start(bf16[8,128,128]{2,1,0:T(8,128)(2,1)S(1)} %fusion.4), channel_id=1, source_target_pairs={{0,16},{2,18},{4,20},{6,22},{8,24},{10,26},{12,28},{14,30},{1,17},... | collective-permute-start | bytes 786440 | tf_op jit(solution)/shard_map/ppermute | solution.py:45
  81.9 12.4 %collective-permute-done.7 = bf16[8,128,128]{2,1,0:T(8,128)(2,1)S(1)} collective-permute-done((bf16[8,128,128]{2,1,0:T(8,128)(2,1)S(1)}, bf16[8,128,128]{2,1,0:T(8,128)(2,1)S(1)}, u32[]{:S(2)}, u32[]{:S(2)}) %collective-permute-start.7) | collective-permute-done | bytes 262176 | tf_op jit(solution)/shard_map/ppermute | solution.py:45
  94.7 1.8 %multiply_reduce_fusion = (f32[2,64,8]{1,2,0:T(8,128)S(1)}, f32[2,64,8,128]{3,1,2,0:T(8,128)S(1)}) fusion(f32[1,8,64,128]{3,2,1,0:T(8,128)S(1)} %convolution_bitcast_fusion.1, f32[1,8,64,128]{3,2,1,0:T(8,128)S(1)} %slice-done, f32[8,128,128]{2,1,0:T(8,128)S(1)} %fusion.76, f32[8,128,128]{2,1,0:T(8,128)S(1)} %fusion.75, f32[8,128,128]{2,1,0:T(8,128)S(1)} %fusion.27, ...), kind=kOutput, calls=%fused_computation.51 | convolution fusion | flops 202505216 | bytes 3411968 | tf_op jit(solution)/shard_map/bhid,hde->bhie/dot_general | solution.py:243
  97.9 1.0 fusion.30
  (178 shorter events, 36.8 us)
Async XLA Ops:
  0.0 10.9 %copy-start = (f32[128]{0:T(128)S(1)}, f32[128]{0:T(128)}, u32[]{:S(2)}) copy-start(f32[128]{0:T(128)} %param.29) | copy-start | bytes 1540
  0.0 2.4 %copy-start.12 = (bf16[128,512]{1,0:T(8,128)(2,1)S(1)}, bf16[128,512]{1,0:T(8,128)(2,1)}, u32[]{:S(2)}) copy-start(bf16[128,512]{1,0:T(8,128)(2,1)} %param.15) | copy-start | bytes 393220
  4.7 13.1 %collective-permute-start = (f32[3,2048]{1,0:T(4,128)S(1)}, f32[3,2048]{1,0:T(4,128)S(1)}, u32[]{:S(2)}, u32[]{:S(2)}) collective-permute-start(f32[3,2048]{1,0:T(4,128)S(1)} %pad_maximum_fusion.3), channel_id=1, source_target_pairs={{0,2},{2,4},{4,6},{6,8},{8,10},{10,12},{12,14},{14,16},{16,18},{18... | collective-permute-start | bytes 73736 | tf_op jit(solution)/shard_map/ppermute | solution.py:16
  8.1 11.1 %copy-start.17 = (pred[64,64]{1,0:T(8,128)(4,1)}, pred[64,64]{1,0:T(8,128)(4,1)S(1)}, u32[]{:S(2)}) copy-start(pred[64,64]{1,0:T(8,128)(4,1)S(1)} %get-tuple-element.47) | copy-start | bytes 12292
  33.5 10.6 %collective-permute-start.1 = (bf16[8,128,128]{2,1,0:T(8,128)(2,1)S(1)}, bf16[8,128,128]{2,1,0:T(8,128)(2,1)S(1)}, u32[]{:S(2)}, u32[]{:S(2)}) collective-permute-start(bf16[8,128,128]{2,1,0:T(8,128)(2,1)S(1)} %get-tuple-element.30), channel_id=1, source_target_pairs={{0,2},{2,4},{4,6},{6,8},{8,10},{10,12},{12,14},{14,16},{16,18},{18... | collective-permute-start | bytes 786440 | tf_op jit(solution)/shard_map/ppermute | solution.py:33
  37.3 3.5 %copy-start.1 = (f32[2,8,128,128]{3,2,1,0:T(8,128)}, f32[2,8,128,128]{3,2,1,0:T(8,128)S(1)}, u32[]{:S(2)}) copy-start(f32[2,8,128,128]{3,2,1,0:T(8,128)S(1)} %fusion.33) | copy-start | bytes 3145732
  37.3 3.5 %copy-start.9 = (f32[128,512]{1,0:T(8,128)S(1)}, f32[128,512]{1,0:T(8,128)}, u32[]{:S(2)}) copy-start(f32[128,512]{1,0:T(8,128)} %bitcast_multiply_fusion.5) | copy-start | bytes 786436
  37.3 3.5 %copy-start.21 = (f32[3,512]{1,0:T(4,128)S(1)}, f32[3,512]{1,0:T(4,128)}, u32[]{:S(2)}) copy-start(f32[3,512]{1,0:T(4,128)} %get-tuple-element.13) | copy-start | bytes 18436
  38.8 15.0 %collective-permute-start.2 = (bf16[8,128,128]{2,1,0:T(8,128)(2,1)}, bf16[8,128,128]{2,1,0:T(8,128)(2,1)}, u32[]{:S(2)}, u32[]{:S(2)}) collective-permute-start(bf16[8,128,128]{2,1,0:T(8,128)(2,1)} %get-tuple-element.36), channel_id=1, source_target_pairs={{0,2},{2,4},{4,6},{6,8},{8,10},{10,12},{12,14},{14,16},{16,18},{18... | collective-permute-start | bytes 786440 | tf_op jit(solution)/shard_map/ppermute | solution.py:45
  40.8 3.3 %copy-start.31 = (f32[1,512]{1,0:T(1,128)S(1)}, f32[1,512]{1,0:T(1,128)}, u32[]{:S(2)}) copy-start(f32[1,512]{1,0:T(1,128)} %get-tuple-element.24) | copy-start | bytes 6148
  40.8 3.3 %copy-start.32 = (f32[1,512]{1,0:T(1,128)S(1)}, f32[1,512]{1,0:T(1,128)}, u32[]{:S(2)}) copy-start(f32[1,512]{1,0:T(1,128)} %get-tuple-element.25) | copy-start | bytes 6148
  51.1 6.1 %copy-start.3 = (f32[2,8,64,128]{3,2,1,0:T(8,128)}, f32[2,8,64,128]{3,2,1,0:T(8,128)S(1)}, u32[]{:S(2)}) copy-start(f32[2,8,64,128]{3,2,1,0:T(8,128)S(1)} %convolution_subtract_fusion.1) | copy-start | bytes 1572868
  51.8 5.5 %copy-start.5 = (f32[2,8,64,128]{3,2,1,0:T(8,128)}, f32[2,8,64,128]{3,2,1,0:T(8,128)S(1)}, u32[]{:S(2)}) copy-start(f32[2,8,64,128]{3,2,1,0:T(8,128)S(1)} %fusion.74) | copy-start | bytes 1572868
  51.8 2.0 %copy-start.7 = (f32[8,128,128]{2,1,0:T(8,128)S(1)}, f32[8,128,128]{2,1,0:T(8,128)}, u32[]{:S(2)}) copy-start(f32[8,128,128]{2,1,0:T(8,128)} %get-tuple-element.37) | copy-start | bytes 1572868
  52.6 10.9 %collective-permute-start.4 = (bf16[8,128,128]{2,1,0:T(8,128)(2,1)S(1)}, bf16[8,128,128]{2,1,0:T(8,128)(2,1)S(1)}, u32[]{:S(2)}, u32[]{:S(2)}) collective-permute-start(bf16[8,128,128]{2,1,0:T(8,128)(2,1)S(1)} %get-tuple-element.32), channel_id=1, source_target_pairs={{0,4},{2,6},{4,8},{6,10},{8,12},{10,14},{12,16},{14,18},{16,20},{1... | collective-permute-start | bytes 786440 | tf_op jit(solution)/shard_map/ppermute | solution.py:33
  55.2 2.1 %copy-start.2 = (f32[2,8,128,128]{3,2,1,0:T(8,128)S(1)}, f32[2,8,128,128]{3,2,1,0:T(8,128)}, u32[]{:S(2)}) copy-start(f32[2,8,128,128]{3,2,1,0:T(8,128)} %copy-done.1) | copy-start | bytes 3145732
  55.2 11.7 %collective-permute-start.3 = (bf16[8,128,128]{2,1,0:T(8,128)(2,1)S(1)}, bf16[8,128,128]{2,1,0:T(8,128)(2,1)S(1)}, u32[]{:S(2)}, u32[]{:S(2)}) collective-permute-start(bf16[8,128,128]{2,1,0:T(8,128)(2,1)S(1)} %get-tuple-element.38), channel_id=1, source_target_pairs={{0,4},{2,6},{4,8},{6,10},{8,12},{10,14},{12,16},{14,18},{16,20},{1... | collective-permute-start | bytes 786440 | tf_op jit(solution)/shard_map/ppermute | solution.py:45
  57.3 6.1 %copy-start.10 = (f32[128,128]{1,0:T(8,128)S(1)}, f32[128,128]{1,0:T(8,128)}, u32[]{:S(2)}) copy-start(f32[128,128]{1,0:T(8,128)} %fusion.55) | copy-start | bytes 196612
  64.1 17.1 %collective-permute-start.6 = (bf16[8,128,128]{2,1,0:T(8,128)(2,1)S(1)}, bf16[8,128,128]{2,1,0:T(8,128)(2,1)S(1)}, u32[]{:S(2)}, u32[]{:S(2)}) collective-permute-start(bf16[8,128,128]{2,1,0:T(8,128)(2,1)S(1)} %get-tuple-element.34), channel_id=1, source_target_pairs={{0,8},{2,10},{4,12},{6,14},{8,16},{10,18},{12,20},{14,22},{16,24},... | collective-permute-start | bytes 786440 | tf_op jit(solution)/shard_map/ppermute | solution.py:33
  67.3 11.7 %collective-permute-start.5 = (bf16[8,128,128]{2,1,0:T(8,128)(2,1)S(1)}, bf16[8,128,128]{2,1,0:T(8,128)(2,1)S(1)}, u32[]{:S(2)}, u32[]{:S(2)}) collective-permute-start(bf16[8,128,128]{2,1,0:T(8,128)(2,1)S(1)} %get-tuple-element.40), channel_id=1, source_target_pairs={{0,8},{2,10},{4,12},{6,14},{8,16},{10,18},{12,20},{14,22},{16,24},... | collective-permute-start | bytes 786440 | tf_op jit(solution)/shard_map/ppermute | solution.py:45
  79.4 1.8 %copy-start.14 = (f32[128,128]{1,0:T(8,128)S(1)}, f32[128,128]{1,0:T(8,128)}, u32[]{:S(2)}) copy-start(f32[128,128]{1,0:T(8,128)} %fusion.54) | copy-start | bytes 196612
  79.4 14.9 %collective-permute-start.7 = (bf16[8,128,128]{2,1,0:T(8,128)(2,1)S(1)}, bf16[8,128,128]{2,1,0:T(8,128)(2,1)S(1)}, u32[]{:S(2)}, u32[]{:S(2)}) collective-permute-start(bf16[8,128,128]{2,1,0:T(8,128)(2,1)S(1)} %fusion.4), channel_id=1, source_target_pairs={{0,16},{2,18},{4,20},{6,22},{8,24},{10,26},{12,28},{14,30},{1,17},... | collective-permute-start | bytes 786440 | tf_op jit(solution)/shard_map/ppermute | solution.py:45
  81.9 12.8 %slice-start = ((f32[2,8,64,128]{3,2,1,0:T(8,128)}), f32[1,8,64,128]{3,2,1,0:T(8,128)S(1)}, s32[]{:S(2)}) async-start(f32[2,8,64,128]{3,2,1,0:T(8,128)} %copy-done.3), calls=%async_computation | async-start | bytes 524288 | tf_op jit(solution)/shard_map/slice | solution.py:234
  81.9 12.8 %slice-start.1 = ((f32[2,8,64,128]{3,2,1,0:T(8,128)}), f32[1,8,64,128]{3,2,1,0:T(8,128)S(1)}, s32[]{:S(2)}) async-start(f32[2,8,64,128]{3,2,1,0:T(8,128)} %copy-done.5), calls=%async_computation.1 | async-start | bytes 524288 | tf_op jit(solution)/shard_map/slice | solution.py:234
  (24 other events, 20.3 us)

commit v9 on v7

--- a/solution.py
+++ b/solution.py
@@ -33,18 +33,37 @@
         earlier = lax.ppermute((inclusive - eye).astype(jnp.bfloat16), axis, pairs)
         earlier = earlier.astype(jnp.float32) + reached * eye
         last_map = exclusive_maps[-1]
-        exclusive_maps.append(earlier if last_map is None else product(last_map, earlier))
-        if 4 * span < devices:
-            inclusive = jnp.where(mine >= span, product(inclusive, earlier), inclusive)
+        if last_map is None or 4 * span >= devices:
+            exclusive_maps.append(earlier if last_map is None else product(last_map, earlier))
+            if 4 * span < devices:
+                inclusive = jnp.where(mine >= span, product(inclusive, earlier), inclusive)
+        else:
+            both = jnp.einsum(
+                "shde,hef->shdf", jnp.stack([last_map, inclusive]), earlier, precision=HIGHEST
+            )
+            exclusive_maps.append(both[0])
+            inclusive = jnp.where(mine >= span, both[1], inclusive)
     state = jnp.zeros_like(offset)
     carried = offset
     for step, span in enumerate(spans):
         pairs = [(source, source + span) for source in range(devices - span)]
         earlier = lax.ppermute(carried.astype(jnp.bfloat16), axis, pairs).astype(jnp.float32)
         last_map = exclusive_maps[step]
-        state = earlier if last_map is None else state + product(last_map, earlier)
-        if step + 1 < len(spans):
-            carried = product(inclusive_maps[step], earlier) + carried
+        if last_map is None:
+            state = earlier
+            if step + 1 < len(spans):
+                carried = product(inclusive_maps[step], earlier) + carried
+        elif step + 1 < len(spans):
+            both = jnp.einsum(
+                "shde,hef->shdf",
+                jnp.stack([last_map, inclusive_maps[step]]),
+                earlier,
+                precision=HIGHEST,
+            )
+            state = state + both[0]
+            carried = both[1] + carried
+        else:
+            state = state + product(last_map, earlier)
     return state
 
 
@@ -84,13 +103,23 @@
 
 def unit_lower_inverse(strict_part):
     length = strict_part.shape[-1]
-    negated = -strict_part
-    inverse = jnp.eye(length, dtype=jnp.float32) + negated
-    power = negated
+    eye = jnp.eye(length, dtype=jnp.float32)
+    power = -strict_part
+    inverse = eye + power
     span = 2
+    if span < length:
+        power = jnp.einsum("bhij,bhjk->bhik", power, power, precision=HIGHEST)
     while span < length:
-        power = jnp.einsum("bhij,bhjk->bhik", power, power, precision=HIGHEST)
-        inverse = inverse + jnp.einsum("bhij,bhjk->bhik", inverse, power, precision=HIGHEST)
+        if 2 * span < length:
+            both = jnp.einsum(
+                "sbhij,sbhjk->sbhik",
+                jnp.stack([inverse, power]),
+                jnp.stack([eye + power, power]),
+                precision=HIGHEST,
+            )
+            inverse, power = (both[0], both[1])
+        else:
+            inverse = jnp.einsum("bhij,bhjk->bhik", inverse, eye + power, precision=HIGHEST)
         span = span * 2
     return inverse
 

time: 97.3 us -> 96.7 us (level)
  matrix products: 25.2 us -> 24.1 us
    dot_general x5 -> x8, matrix products: 3.29 us -> 7.64 us  [the longest x4 4.74 us: unit_lower_inverse(): jnp.einsum('sbhij,sbhjk->sbhik', jnp.stack([inverse, power]), jnp.stack([...]
    dot_general x12 -> x6, matrix products: 8.15 us -> 5.27 us  [product(): return jnp.einsum('hde,hef->hdf', left, right, precision=HIGHEST)]
    dot_general x5 -> x1, matrix products: 3.22 us -> 0.65 us  [unit_lower_inverse(): power = jnp.einsum('bhij,bhjk->bhik', power, power, precision=HIGHEST)]
  transfers between devices with their start and end apart: 8 -> 8, of which waited for: 7 -> 7; matrix products, arithmetic and copies ran while one was open for 12% -> 13% of each run, Pallas kernels for 0% -> 0%
where the time goes in v9:
time: 96.7 us; the launch traced here: 95.9 us
  waiting for transfers between devices  33.4 us (35%)
  matrix products  24.1 us (25%)
  starting transfers between devices  14.2 us (15%)
  local copies, waits for them, and re-layouts  13.8 us (14%)
  other arithmetic  9.47 us (10%)
    ppermute x4, waiting for transfers between devices, scan_states(): lax.ppermute(carried.astype(jnp.bfloat16), axis, pairs).astype(jnp.float32)  28 us
    unnamed x86, local copies, waits for them, and re-layouts  9.13 us
    ppermute x4, starting transfers between devices, scan_states(): lax.ppermute(carried.astype(jnp.bfloat16), axis, pairs).astype(jnp.float32)  5.92 us
    ppermute x3, waiting for transfers between devices, scan_states(): earlier = lax.ppermute((inclusive - eye).astype(jnp.bfloat16), axis, pairs)  5.48 us
    dot_general x6, matrix products, product(): return jnp.einsum('hde,hef->hdf', left, right, precision=HIGHEST)  5.27 us
    ppermute x3, starting transfers between devices, scan_states(): earlier = lax.ppermute((inclusive - eye).astype(jnp.bfloat16), axis, pairs)  4.86 us
    dot_general x4, matrix products, unit_lower_inverse(): jnp.einsum('sbhij,sbhjk->sbhik', jnp.stack([inverse, power]), jnp.stack([...  4.74 us
    ppermute x1, starting transfers between devices, from_behind(): lax.ppermute(value, axis, [(source, source + steps) for source in range(f...  3.4 us
  transfers between devices with their start and end apart: 8, of which 7 were waited for; matrix products, arithmetic and copies ran while one was open for 13% of the time, Pallas kernels for 0%

profile of v9, /device:TPU:28, one launch (start us, length us, event | category | flops | bytes accessed | tf_op | source)
XLA Modules:
  0.0 95.9 jit_solution(8553672560138188152)
XLA Ops:
  3.2 3.4 %collective-permute-start = (f32[3,2048]{1,0:T(4,128)S(1)}, f32[3,2048]{1,0:T(4,128)S(1)}, u32[]{:S(2)}, u32[]{:S(2)}) collective-permute-start(f32[3,2048]{1,0:T(4,128)S(1)} %pad_maximum_fusion.10), channel_id=1, source_target_pairs={{0,2},{2,4},{4,6},{6,8},{8,10},{10,12},{12,14},{14,16},{16,18},{18... | collective-permute-start | bytes 73736 | tf_op jit(solution)/shard_map/ppermute | solution.py:16
  19.7 1.2 %fusion.5 = f32[2,2,8,64,64]{4,3,2,1,0:T(8,128)S(1)} fusion(f32[1,2,8,64,64]{4,3,2,1,0:T(8,128)S(1)} %bitcast.229, f32[1,2,8,64,64]{4,3,2,1,0:T(8,128)S(1)} %get-tuple-element.22, f32[1,2,8,64,64]{4,3,2,1,0:T(8,128)S(1)} %get-tuple-element.21), kind=kOutput, calls=%fused_computation.20 | convolution fusion | flops 100925440 | bytes 1310720 | tf_op jit(solution)/shard_map/sbhij,sbhjk->sbhik/dot_general | solution.py:114
  21.0 1.2 %fusion.8 = f32[2,2,8,64,64]{4,3,2,1,0:T(8,128)S(1)} fusion(f32[2,2,8,64,64]{4,3,2,1,0:T(8,128)S(1)} %fusion.5, f32[1,2,8,64,64]{4,3,2,1,0:T(8,128)S(1)} %get-tuple-element.16, f32[1,2,8,64,64]{4,3,2,1,0:T(8,128)S(1)} %get-tuple-element.15), kind=kOutput, calls=%fused_computation.23 | convolution fusion | flops 100794368 | bytes 1572864 | tf_op jit(solution)/shard_map/sbhij,sbhjk->sbhik/dot_general | solution.py:114
  22.3 1.2 %fusion.12 = f32[2,2,8,64,64]{4,3,2,1,0:T(8,128)S(1)} fusion(f32[2,2,8,64,64]{4,3,2,1,0:T(8,128)S(1)} %fusion.8, f32[1,2,8,64,64]{4,3,2,1,0:T(8,128)S(1)} %get-tuple-element.14, f32[1,2,8,64,64]{4,3,2,1,0:T(8,128)S(1)} %get-tuple-element.13), kind=kOutput, calls=%fused_computation.27 | convolution fusion | flops 100794368 | bytes 1572864 | tf_op jit(solution)/shard_map/sbhij,sbhjk->sbhik/dot_general | solution.py:114
  23.6 1.2 %fusion.16 = f32[2,2,8,64,64]{4,3,2,1,0:T(8,128)S(1)} fusion(f32[2,2,8,64,64]{4,3,2,1,0:T(8,128)S(1)} %fusion.12, f32[1,2,8,64,64]{4,3,2,1,0:T(8,128)S(1)} %get-tuple-element.12, f32[1,2,8,64,64]{4,3,2,1,0:T(8,128)S(1)} %get-tuple-element.11), kind=kOutput, calls=%fused_computation.31 | convolution fusion | flops 100794368 | bytes 1572864 | tf_op jit(solution)/shard_map/sbhij,sbhjk->sbhik/dot_general | solution.py:114
  26.4 1.9 %convolution_subtract_fusion = f32[2,8,128,128]{3,2,1,0:T(8,128)S(1)} fusion(f32[2,8,64,128]{3,2,1,0:T(8,128)S(1)} %fusion.50, f32[128,128]{1,0:T(8,128)S(1)} %fusion.86, f32[2,8]{1,0:T(2,128)S(1)} %slice_reduce_fusion.1, f32[2,8,64,128]{3,2,0,1:T(8,128)S(1)} %get-tuple-element.17), kind=kOutput, calls=%fused_computation.2 | convolution fusion | flops 201850880 | bytes 2162752 | tf_op jit(solution)/shard_map/bhjd,bhje->bhde/dot_general | solution.py:147
  28.3 1.6 %subtract_convert_fusion.2 = (bf16[8,128,128]{2,1,0:T(8,128)(2,1)}, f32[8,128,128]{2,1,0:T(8,128)S(1)}) fusion(f32[128,128]{1,0:T(8,128)S(1)} %fusion.86, f32[2,8,128,128]{3,2,1,0:T(8,128)S(1)} %convolution_subtract_fusion), kind=kOutput, calls=%fused_computation.94 | convolution fusion | flops 201588736 | bytes 1900544 | tf_op jit(solution)/shard_map/hde,hef->hdf/dot_general | solution.py:171
  32.5 1.8 %fusion.61 = f32[2,8,128,128]{3,2,1,0:T(8,128)S(1)} fusion(f32[2,8,64,128]{3,2,1,0:T(8,128)S(1)} %fusion.48, f32[2,8,64,128]{3,2,0,1:T(8,128)S(1)} %get-tuple-element.17), kind=kOutput, calls=%fused_computation.103 | convolution fusion | flops 201326592 | bytes 2097152 | tf_op jit(solution)/shard_map/bhjd,bhje->bhde/dot_general | solution.py:157
  34.4 1.6 %fusion.103 = (bf16[8,128,128]{2,1,0:T(8,128)(2,1)}, f32[8,128,128]{2,1,0:T(8,128)}) fusion(f32[2,8,128,128]{3,2,1,0:T(8,128)S(1)} %fusion.61, f32[2,8,128,128]{3,2,1,0:T(8,128)S(1)} %convolution_subtract_fusion), kind=kOutput, calls=%fused_computation.201 | convolution fusion | flops 201588736 | bytes 2359296 | tf_op jit(solution)/shard_map/hde,hef->hdf/dot_general | solution.py:171
  41.6 2.0 %collective-permute-start.1 = (bf16[8,128,128]{2,1,0:T(8,128)(2,1)S(1)}, bf16[8,128,128]{2,1,0:T(8,128)(2,1)S(1)}, u32[]{:S(2)}, u32[]{:S(2)}) collective-permute-start(bf16[8,128,128]{2,1,0:T(8,128)(2,1)S(1)} %copy-done.11), channel_id=1, source_target_pairs={{0,2},{2,4},{4,6},{6,8},{8,10},{10,12},{12,14},{14,16},{16,18},{18... | collective-permute-start | bytes 786440 | tf_op jit(solution)/shard_map/ppermute | solution.py:50
  44.3 2.1 %collective-permute-start.3 = (bf16[8,128,128]{2,1,0:T(8,128)(2,1)S(1)}, bf16[8,128,128]{2,1,0:T(8,128)(2,1)S(1)}, u32[]{:S(2)}, u32[]{:S(2)}) collective-permute-start(bf16[8,128,128]{2,1,0:T(8,128)(2,1)S(1)} %copy-done.14), channel_id=1, source_target_pairs={{0,2},{2,4},{4,6},{6,8},{8,10},{10,12},{12,14},{14,16},{16,18},{18... | collective-permute-start | bytes 786440 | tf_op jit(solution)/shard_map/ppermute | solution.py:33
  47.0 6.7 %collective-permute-done.1 = bf16[8,128,128]{2,1,0:T(8,128)(2,1)S(1)} collective-permute-done((bf16[8,128,128]{2,1,0:T(8,128)(2,1)S(1)}, bf16[8,128,128]{2,1,0:T(8,128)(2,1)S(1)}, u32[]{:S(2)}, u32[]{:S(2)}) %collective-permute-start.1) | collective-permute-done | bytes 262176 | tf_op jit(solution)/shard_map/ppermute | solution.py:50
  54.1 1.3 %collective-permute-start.2 = (bf16[8,128,128]{2,1,0:T(8,128)(2,1)S(1)}, bf16[8,128,128]{2,1,0:T(8,128)(2,1)S(1)}, u32[]{:S(2)}, u32[]{:S(2)}) collective-permute-start(bf16[8,128,128]{2,1,0:T(8,128)(2,1)S(1)} %get-tuple-element.44), channel_id=1, source_target_pairs={{0,4},{2,6},{4,8},{6,10},{8,12},{10,14},{12,16},{14,18},{16,20},{1... | collective-permute-start | bytes 786440 | tf_op jit(solution)/shard_map/ppermute | solution.py:50
  55.4 2.6 %collective-permute-done.3 = bf16[8,128,128]{2,1,0:T(8,128)(2,1)S(1)} collective-permute-done((bf16[8,128,128]{2,1,0:T(8,128)(2,1)S(1)}, bf16[8,128,128]{2,1,0:T(8,128)(2,1)S(1)}, u32[]{:S(2)}, u32[]{:S(2)}) %collective-permute-start.3) | collective-permute-done | bytes 262176 | tf_op jit(solution)/shard_map/ppermute | solution.py:33
  58.7 1.3 %collective-permute-start.5 = (bf16[8,128,128]{2,1,0:T(8,128)(2,1)S(1)}, bf16[8,128,128]{2,1,0:T(8,128)(2,1)S(1)}, u32[]{:S(2)}, u32[]{:S(2)}) collective-permute-start(bf16[8,128,128]{2,1,0:T(8,128)(2,1)S(1)} %get-tuple-element.40), channel_id=1, source_target_pairs={{0,4},{2,6},{4,8},{6,10},{8,12},{10,14},{12,16},{14,18},{16,20},{1... | collective-permute-start | bytes 786440 | tf_op jit(solution)/shard_map/ppermute | solution.py:33
  60.0 5.2 %collective-permute-done.2 = bf16[8,128,128]{2,1,0:T(8,128)(2,1)S(1)} collective-permute-done((bf16[8,128,128]{2,1,0:T(8,128)(2,1)S(1)}, bf16[8,128,128]{2,1,0:T(8,128)(2,1)S(1)}, u32[]{:S(2)}, u32[]{:S(2)}) %collective-permute-start.2) | collective-permute-done | bytes 262176 | tf_op jit(solution)/shard_map/ppermute | solution.py:50
  66.0 1.3 %collective-permute-start.4 = (bf16[8,128,128]{2,1,0:T(8,128)(2,1)S(1)}, bf16[8,128,128]{2,1,0:T(8,128)(2,1)S(1)}, u32[]{:S(2)}, u32[]{:S(2)}) collective-permute-start(bf16[8,128,128]{2,1,0:T(8,128)(2,1)S(1)} %fusion.81), channel_id=1, source_target_pairs={{0,8},{2,10},{4,12},{6,14},{8,16},{10,18},{12,20},{14,22},{16,24},... | collective-permute-start | bytes 786440 | tf_op jit(solution)/shard_map/ppermute | solution.py:50
  67.3 1.9 %collective-permute-done.5 = bf16[8,128,128]{2,1,0:T(8,128)(2,1)S(1)} collective-permute-done((bf16[8,128,128]{2,1,0:T(8,128)(2,1)S(1)}, bf16[8,128,128]{2,1,0:T(8,128)(2,1)S(1)}, u32[]{:S(2)}, u32[]{:S(2)}) %collective-permute-start.5) | collective-permute-done | bytes 262176 | tf_op jit(solution)/shard_map/ppermute | solution.py:33
  69.1 1.0 %convolution_bitcast_fusion.2 = f32[2,8,128,128]{3,2,1,0:T(8,128)S(1)} fusion(f32[1,8,128,128]{3,2,1,0:T(8,128)S(1)} %bitcast.231, f32[1,8,128,128]{3,2,1,0:T(8,128)S(1)} %fusion.56, bf16[8,128,128]{2,1,0:T(8,128)(2,1)S(1)} %collective-permute-done.5, f32[128,128]{1,0:T(8,128)S(1)} %copy-done.12), kind=kOutput, calls=%fused_computation.3 | convolution fusion | flops 403177472 | bytes 2424832 | tf_op jit(solution)/shard_map/shde,hef->shdf/dot_general | solution.py:41
  70.3 1.5 %collective-permute-start.6 = (bf16[8,128,128]{2,1,0:T(8,128)(2,1)S(1)}, bf16[8,128,128]{2,1,0:T(8,128)(2,1)S(1)}, u32[]{:S(2)}, u32[]{:S(2)}) collective-permute-start(bf16[8,128,128]{2,1,0:T(8,128)(2,1)S(1)} %get-tuple-element.10), channel_id=1, source_target_pairs={{0,8},{2,10},{4,12},{6,14},{8,16},{10,18},{12,20},{14,22},{16,24},... | collective-permute-start | bytes 786440 | tf_op jit(solution)/shard_map/ppermute | solution.py:33
  71.8 6.4 %collective-permute-done.4 = bf16[8,128,128]{2,1,0:T(8,128)(2,1)S(1)} collective-permute-done((bf16[8,128,128]{2,1,0:T(8,128)(2,1)S(1)}, bf16[8,128,128]{2,1,0:T(8,128)(2,1)S(1)}, u32[]{:S(2)}, u32[]{:S(2)}) %collective-permute-start.4) | collective-permute-done | bytes 262176 | tf_op jit(solution)/shard_map/ppermute | solution.py:50
  78.9 1.3 %collective-permute-start.7 = (bf16[8,128,128]{2,1,0:T(8,128)(2,1)S(1)}, bf16[8,128,128]{2,1,0:T(8,128)(2,1)S(1)}, u32[]{:S(2)}, u32[]{:S(2)}) collective-permute-start(bf16[8,128,128]{2,1,0:T(8,128)(2,1)S(1)} %fusion.29), channel_id=1, source_target_pairs={{0,16},{2,18},{4,20},{6,22},{8,24},{10,26},{12,28},{14,30},{1,17},... | collective-permute-start | bytes 786440 | tf_op jit(solution)/shard_map/ppermute | solution.py:50
  80.9 1.1 %collective-permute-done.6 = bf16[8,128,128]{2,1,0:T(8,128)(2,1)S(1)} collective-permute-done((bf16[8,128,128]{2,1,0:T(8,128)(2,1)S(1)}, bf16[8,128,128]{2,1,0:T(8,128)(2,1)S(1)}, u32[]{:S(2)}, u32[]{:S(2)}) %collective-permute-start.6) | collective-permute-done | bytes 262176 | tf_op jit(solution)/shard_map/ppermute | solution.py:33
  82.6 9.7 %collective-permute-done.7 = bf16[8,128,128]{2,1,0:T(8,128)(2,1)S(1)} collective-permute-done((bf16[8,128,128]{2,1,0:T(8,128)(2,1)S(1)}, bf16[8,128,128]{2,1,0:T(8,128)(2,1)S(1)}, u32[]{:S(2)}, u32[]{:S(2)}) %collective-permute-start.7) | collective-permute-done | bytes 262176 | tf_op jit(solution)/shard_map/ppermute | solution.py:50
  (184 shorter events, 34.8 us)
Async XLA Ops:
  0.0 15.8 %copy-start = (f32[128]{0:T(128)S(1)}, f32[128]{0:T(128)}, u32[]{:S(2)}) copy-start(f32[128]{0:T(128)} %param.29) | copy-start | bytes 1540
  3.2 13.3 %collective-permute-start = (f32[3,2048]{1,0:T(4,128)S(1)}, f32[3,2048]{1,0:T(4,128)S(1)}, u32[]{:S(2)}, u32[]{:S(2)}) collective-permute-start(f32[3,2048]{1,0:T(4,128)S(1)} %pad_maximum_fusion.10), channel_id=1, source_target_pairs={{0,2},{2,4},{4,6},{6,8},{8,10},{10,12},{12,14},{14,16},{16,18},{18... | collective-permute-start | bytes 73736 | tf_op jit(solution)/shard_map/ppermute | solution.py:16
  6.7 11.2 %copy-start.18 = (pred[64,64]{1,0:T(8,128)(4,1)}, pred[64,64]{1,0:T(8,128)(4,1)S(1)}, u32[]{:S(2)}) copy-start(pred[64,64]{1,0:T(8,128)(4,1)S(1)} %get-tuple-element.51) | copy-start | bytes 12292
  8.3 1.4 %copy-start.35 = (f32[128,8]{0,1:T(8,128)S(1)}, f32[128,8]{0,1:T(8,128)}, u32[]{:S(2)}) copy-start(f32[128,8]{0,1:T(8,128)} %param.24) | copy-start | bytes 12292
  16.5 1.4 %copy-start.20 = (f32[2,64,8]{1,2,0:T(8,128)}, f32[2,64,8]{1,2,0:T(8,128)S(1)}, u32[]{:S(2)}) copy-start(f32[2,64,8]{1,2,0:T(8,128)S(1)} %copy.177) | copy-start | bytes 12292
  28.3 1.6 %copy-start.5 = (f32[128,1024]{1,0:T(8,128)S(1)}, f32[128,1024]{1,0:T(8,128)}, u32[]{:S(2)}) copy-start(f32[128,1024]{1,0:T(8,128)} %convert_multiply_fusion.1) | copy-start | bytes 1572868
  34.3 1.7 %copy-start.1 = (f32[2,8,128,128]{3,2,1,0:T(8,128)}, f32[2,8,128,128]{3,2,1,0:T(8,128)S(1)}, u32[]{:S(2)}) copy-start(f32[2,8,128,128]{3,2,1,0:T(8,128)S(1)} %fusion.61) | copy-start | bytes 3145732
  34.3 1.6 %copy-start.8 = (f32[128,512]{1,0:T(8,128)S(1)}, f32[128,512]{1,0:T(8,128)}, u32[]{:S(2)}) copy-start(f32[128,512]{1,0:T(8,128)} %bitcast_multiply_fusion.5) | copy-start | bytes 786436
  34.3 1.6 %copy-start.22 = (f32[3,512]{1,0:T(4,128)S(1)}, f32[3,512]{1,0:T(4,128)}, u32[]{:S(2)}) copy-start(f32[3,512]{1,0:T(4,128)} %get-tuple-element.19) | copy-start | bytes 18436
  41.4 39.5 %copy-start.3 = (f32[2,8,64,128]{3,2,1,0:T(8,128)}, f32[2,8,64,128]{3,2,1,0:T(8,128)S(1)}, u32[]{:S(2)}) copy-start(f32[2,8,64,128]{3,2,1,0:T(8,128)S(1)} %convolution_subtract_fusion.1) | copy-start | bytes 1572868
  41.4 5.0 %copy-start.2 = (f32[2,8,128,128]{3,2,1,0:T(8,128)S(1)}, f32[2,8,128,128]{3,2,1,0:T(8,128)}, u32[]{:S(2)}) copy-start(f32[2,8,128,128]{3,2,1,0:T(8,128)} %copy-done.1) | copy-start | bytes 3145732
  41.6 2.7 %copy-start.14 = (bf16[8,128,128]{2,1,0:T(8,128)(2,1)S(1)}, bf16[8,128,128]{2,1,0:T(8,128)(2,1)}, u32[]{:S(2)}) copy-start(bf16[8,128,128]{2,1,0:T(8,128)(2,1)} %get-tuple-element.38) | copy-start | bytes 786436
  41.6 12.1 %collective-permute-start.1 = (bf16[8,128,128]{2,1,0:T(8,128)(2,1)S(1)}, bf16[8,128,128]{2,1,0:T(8,128)(2,1)S(1)}, u32[]{:S(2)}, u32[]{:S(2)}) collective-permute-start(bf16[8,128,128]{2,1,0:T(8,128)(2,1)S(1)} %copy-done.11), channel_id=1, source_target_pairs={{0,2},{2,4},{4,6},{6,8},{8,10},{10,12},{12,14},{14,16},{16,18},{18... | collective-permute-start | bytes 786440 | tf_op jit(solution)/shard_map/ppermute | solution.py:50
  44.3 36.5 %copy-start.4 = (f32[2,8,64,128]{3,2,1,0:T(8,128)}, f32[2,8,64,128]{3,2,1,0:T(8,128)S(1)}, u32[]{:S(2)}) copy-start(f32[2,8,64,128]{3,2,1,0:T(8,128)S(1)} %fusion.106) | copy-start | bytes 1572868
  44.3 9.4 %copy-start.6 = (f32[8,128,128]{2,1,0:T(8,128)S(1)}, f32[8,128,128]{2,1,0:T(8,128)}, u32[]{:S(2)}) copy-start(f32[8,128,128]{2,1,0:T(8,128)} %get-tuple-element.43) | copy-start | bytes 1572868
  44.3 13.6 %collective-permute-start.3 = (bf16[8,128,128]{2,1,0:T(8,128)(2,1)S(1)}, bf16[8,128,128]{2,1,0:T(8,128)(2,1)S(1)}, u32[]{:S(2)}, u32[]{:S(2)}) collective-permute-start(bf16[8,128,128]{2,1,0:T(8,128)(2,1)S(1)} %copy-done.14), channel_id=1, source_target_pairs={{0,2},{2,4},{4,6},{6,8},{8,10},{10,12},{12,14},{14,16},{16,18},{18... | collective-permute-start | bytes 786440 | tf_op jit(solution)/shard_map/ppermute | solution.py:33
  54.1 11.1 %collective-permute-start.2 = (bf16[8,128,128]{2,1,0:T(8,128)(2,1)S(1)}, bf16[8,128,128]{2,1,0:T(8,128)(2,1)S(1)}, u32[]{:S(2)}, u32[]{:S(2)}) collective-permute-start(bf16[8,128,128]{2,1,0:T(8,128)(2,1)S(1)} %get-tuple-element.44), channel_id=1, source_target_pairs={{0,4},{2,6},{4,8},{6,10},{8,12},{10,14},{12,16},{14,18},{16,20},{1... | collective-permute-start | bytes 786440 | tf_op jit(solution)/shard_map/ppermute | solution.py:50
  58.7 10.4 %collective-permute-start.5 = (bf16[8,128,128]{2,1,0:T(8,128)(2,1)S(1)}, bf16[8,128,128]{2,1,0:T(8,128)(2,1)S(1)}, u32[]{:S(2)}, u32[]{:S(2)}) collective-permute-start(bf16[8,128,128]{2,1,0:T(8,128)(2,1)S(1)} %get-tuple-element.40), channel_id=1, source_target_pairs={{0,4},{2,6},{4,8},{6,10},{8,12},{10,14},{12,16},{14,18},{16,20},{1... | collective-permute-start | bytes 786440 | tf_op jit(solution)/shard_map/ppermute | solution.py:33
  65.9 3.2 %copy-start.12 = (f32[128,128]{1,0:T(8,128)S(1)}, f32[128,128]{1,0:T(8,128)}, u32[]{:S(2)}) copy-start(f32[128,128]{1,0:T(8,128)} %fusion.84) | copy-start | bytes 196612
  66.0 12.2 %collective-permute-start.4 = (bf16[8,128,128]{2,1,0:T(8,128)(2,1)S(1)}, bf16[8,128,128]{2,1,0:T(8,128)(2,1)S(1)}, u32[]{:S(2)}, u32[]{:S(2)}) collective-permute-start(bf16[8,128,128]{2,1,0:T(8,128)(2,1)S(1)} %fusion.81), channel_id=1, source_target_pairs={{0,8},{2,10},{4,12},{6,14},{8,16},{10,18},{12,20},{14,22},{16,24},... | collective-permute-start | bytes 786440 | tf_op jit(solution)/shard_map/ppermute | solution.py:50
  70.3 11.6 %collective-permute-start.6 = (bf16[8,128,128]{2,1,0:T(8,128)(2,1)S(1)}, bf16[8,128,128]{2,1,0:T(8,128)(2,1)S(1)}, u32[]{:S(2)}, u32[]{:S(2)}) collective-permute-start(bf16[8,128,128]{2,1,0:T(8,128)(2,1)S(1)} %get-tuple-element.10), channel_id=1, source_target_pairs={{0,8},{2,10},{4,12},{6,14},{8,16},{10,18},{12,20},{14,22},{16,24},... | collective-permute-start | bytes 786440 | tf_op jit(solution)/shard_map/ppermute | solution.py:33
  78.9 13.4 %collective-permute-start.7 = (bf16[8,128,128]{2,1,0:T(8,128)(2,1)S(1)}, bf16[8,128,128]{2,1,0:T(8,128)(2,1)S(1)}, u32[]{:S(2)}, u32[]{:S(2)}) collective-permute-start(bf16[8,128,128]{2,1,0:T(8,128)(2,1)S(1)} %fusion.29), channel_id=1, source_target_pairs={{0,16},{2,18},{4,20},{6,22},{8,24},{10,26},{12,28},{14,30},{1,17},... | collective-permute-start | bytes 786440 | tf_op jit(solution)/shard_map/ppermute | solution.py:50
  82.6 10.1 %slice-start = ((f32[2,8,64,128]{3,2,1,0:T(8,128)}), f32[1,8,64,128]{3,2,1,0:T(8,128)S(1)}, s32[]{:S(2)}) async-start(f32[2,8,64,128]{3,2,1,0:T(8,128)} %copy-done.3), calls=%async_computation | async-start | bytes 524288 | tf_op jit(solution)/shard_map/slice | solution.py:258
  82.6 10.1 %slice-start.1 = ((f32[2,8,64,128]{3,2,1,0:T(8,128)}), f32[1,8,64,128]{3,2,1,0:T(8,128)S(1)}, s32[]{:S(2)}) async-start(f32[2,8,64,128]{3,2,1,0:T(8,128)} %copy-done.4), calls=%async_computation.1 | async-start | bytes 524288 | tf_op jit(solution)/shard_map/slice | solution.py:258
  (26 other events, 20.5 us)

commit v10 on v9

--- a/solution.py
+++ b/solution.py
@@ -124,7 +124,7 @@
     return inverse
 
 
-def key_terms(key_units, logdec, beta_units):
+def block_maps(key_units, value_units, logdec, beta_units):
     length = logdec.shape[-1]
     positions = jnp.arange(length)
     lower_incl = positions[:, None] >= positions[None, :]
@@ -136,26 +136,18 @@
     key_gram = jnp.einsum("bhid,bhjd->bhij", key_units, key_units, precision=HIGHEST)
     inverse = unit_lower_inverse(beta_units[..., :, None] * key_gram * decay_strict)
     growth = jnp.exp(cumulative)
-    weight_keys = jnp.einsum(
-        "bhij,bhjd->bhid",
-        inverse,
-        (beta_units * growth)[..., None] * key_units,
-        precision=HIGHEST,
-    )
+    stacked = jnp.concatenate(
+        [(beta_units * growth)[..., None] * key_units, beta_units[..., None] * value_units],
+        axis=-1,
+    )
+    solved = jnp.einsum("bhij,bhjd->bhid", inverse, stacked, precision=HIGHEST)
+    key_width = key_units.shape[-1]
     fading = jnp.exp(cumulative[..., -1:] - cumulative)[..., None] * key_units
-    eye_key = jnp.eye(key_units.shape[-1], dtype=jnp.float32)
-    transition = growth[..., -1][..., None, None] * eye_key - jnp.einsum(
-        "bhjd,bhje->bhde", fading, weight_keys, precision=HIGHEST
-    )
-    return (inverse, weight_keys, fading, transition, decay_incl, growth)
-
-
-def value_terms(inverse, fading, value_units, beta_units):
-    weight_values = jnp.einsum(
-        "bhij,bhjd->bhid", inverse, beta_units[..., None] * value_units, precision=HIGHEST
-    )
-    offset = jnp.einsum("bhjd,bhje->bhde", fading, weight_values, precision=HIGHEST)
-    return (weight_values, offset)
+    faded = jnp.einsum("bhjd,bhje->bhde", fading, solved, precision=HIGHEST)
+    eye_key = jnp.eye(key_width, dtype=jnp.float32)
+    transition = growth[..., -1][..., None, None] * eye_key - faded[..., :key_width]
+    maps = jnp.concatenate([transition, faded[..., key_width:]], axis=-1)
+    return (solved[..., key_width:], solved[..., :key_width], maps, decay_incl, growth)
 
 
 def query_terms(queries, key_units, decay_incl, growth, weight_values, weight_keys):
@@ -227,25 +219,20 @@
     logdec = -jnp.exp(base_part)[None, :] * jax.nn.softplus(gate_input + bias_part[None, :])
     logdec = to_block_rows(logdec, CH)
     beta_units = to_block_rows(jax.nn.sigmoid(beta_logit), CH)
-    inverse, weight_keys, fading, transition, decay_incl, growth = key_terms(
-        key_units, logdec, beta_units
-    )
-    dev_trans = transition[0]
-    trans_before = [None]
-    for block in range(1, transition.shape[0]):
-        trans_before.append(dev_trans)
-        dev_trans = product(transition[block], dev_trans)
-    value_window, _ = lax.optimization_barrier(
-        (jnp.concatenate([tail_rows[2], value_deq], axis=0), dev_trans)
-    )
-    value_conv = causal_filter(value_window, conv_value)
+    value_conv = causal_filter(jnp.concatenate([tail_rows[2], value_deq], axis=0), conv_value)
     value_units = to_blocks(value_conv.astype(jnp.float32).reshape(row_count, -1, head_width), CH)
-    weight_values, offset = value_terms(inverse, fading, value_units, beta_units)
-    dev_offset = offset[0]
-    offset_before = [None]
-    for block in range(1, transition.shape[0]):
-        offset_before.append(dev_offset)
-        dev_offset = product(transition[block], dev_offset) + offset[block]
+    weight_values, weight_keys, maps, decay_incl, growth = block_maps(
+        key_units, value_units, logdec, beta_units
+    )
+    key_width = key_units.shape[-1]
+    device_map = maps[0]
+    maps_before = [None]
+    for block in range(1, maps.shape[0]):
+        maps_before.append(device_map)
+        device_map = jnp.einsum(
+            "hde,hef->hdf", maps[block][..., :key_width], device_map, precision=HIGHEST
+        ).at[..., key_width:].add(maps[block][..., key_width:])
+    dev_trans, dev_offset = (device_map[..., :key_width], device_map[..., key_width:])
     query_window, _ = lax.optimization_barrier(
         (jnp.concatenate([tail_rows[0], query_deq], axis=0), dev_offset)
     )
@@ -256,14 +243,10 @@
         queries, key_units, decay_incl, growth, weight_values, weight_keys
     )
     local_outs, read_maps = ([zero_out[0]], [readout[0]])
-    for block in range(1, transition.shape[0]):
-        read_maps.append(
-            jnp.einsum("hid,hde->hie", readout[block], trans_before[block], precision=HIGHEST)
-        )
-        local_outs.append(
-            zero_out[block]
-            + jnp.einsum("hid,hde->hie", readout[block], offset_before[block], precision=HIGHEST)
-        )
+    for block in range(1, maps.shape[0]):
+        read = jnp.einsum("hid,hde->hie", readout[block], maps_before[block], precision=HIGHEST)
+        read_maps.append(read[..., :key_width])
+        local_outs.append(zero_out[block] + read[..., key_width:])
     incoming = scan_states(dev_trans, dev_offset, "seq")
     outputs = jnp.stack(local_outs) + jnp.einsum(
         "bhid,hde->bhie", jnp.stack(read_maps), incoming, precision=HIGHEST

time: 96.7 us -> 90.8 us (0.939)
  local copies, waits for them, and re-layouts: 13.8 us -> 8.05 us
  matrix products: 24.1 us -> 19.6 us
  waiting for transfers between devices: 33.4 us -> 37.3 us
    ppermute x3, waiting for transfers between devices: 5.48 us -> 14.5 us  [scan_states(): earlier = lax.ppermute((inclusive - eye).astype(jnp.bfloat16), axis, pairs)]
    unnamed x86 -> x74, local copies, waits for them, and re-layouts: 9.13 us -> 3.71 us
    ppermute x4, waiting for transfers between devices: 28 us -> 22.8 us  [scan_states(): lax.ppermute(carried.astype(jnp.bfloat16), axis, pairs).astype(jnp.float32)]
    dot_general x6 -> x4, matrix products: 5.27 us -> 2.11 us  [product(): return jnp.einsum('hde,hef->hdf', left, right, precision=HIGHEST)]
    mul x3, other arithmetic: 1.69 us -> 0.19 us  [expand_quantized(): raw_rows.astype(jnp.float32).reshape(row_count, head_count, -1)]
    dot_general x7 -> x5, matrix products: 7.34 us -> 6.03 us  [the longest x1 2.29 us: block_maps(): faded = jnp.einsum('bhjd,bhje->bhde', fading, solved, precision=HIGHEST)]
    convert_element_type x2 -> x3, other arithmetic: 0.18 us -> 1.22 us  [scan_states(): carried.astype(jnp.bfloat16)]
  transfers between devices with their start and end apart: 8 -> 8, of which waited for: 7 -> 7; matrix products, arithmetic and copies ran while one was open for 13% -> 10% of each run, Pallas kernels for 0% -> 0%
where the time goes in v10:
time: 90.8 us; the launch traced here: 89.9 us
  waiting for transfers between devices  37.3 us (41%)
  matrix products  19.6 us (22%)
  starting transfers between devices  14.1 us (16%)
  other arithmetic  9.86 us (11%)
  local copies, waits for them, and re-layouts  8.05 us (9%)
  between operations  1.02 us (1%)
    ppermute x4, waiting for transfers between devices, scan_states(): lax.ppermute(carried.astype(jnp.bfloat16), axis, pairs).astype(jnp.float32)  22.8 us
    ppermute x3, waiting for transfers between devices, scan_states(): earlier = lax.ppermute((inclusive - eye).astype(jnp.bfloat16), axis, pairs)  14.5 us
    ppermute x4, starting transfers between devices, scan_states(): lax.ppermute(carried.astype(jnp.bfloat16), axis, pairs).astype(jnp.float32)  6.02 us
    dot_general x4, matrix products, unit_lower_inverse(): jnp.einsum('sbhij,sbhjk->sbhik', jnp.stack([inverse, power]), jnp.stack([...  4.72 us
    ppermute x3, starting transfers between devices, scan_states(): earlier = lax.ppermute((inclusive - eye).astype(jnp.bfloat16), axis, pairs)  4.64 us
    unnamed x74, local copies, waits for them, and re-layouts  3.71 us
    ppermute x1, starting transfers between devices, from_behind(): lax.ppermute(value, axis, [(source, source + steps) for source in range(f...  3.4 us
    dot_general x1, matrix products, block_maps(): faded = jnp.einsum('bhjd,bhje->bhde', fading, solved, precision=HIGHEST)  2.29 us
  transfers between devices with their start and end apart: 8, of which 7 were waited for; matrix products, arithmetic and copies ran while one was open for 10% of the time, Pallas kernels for 0%

profile of v10, /device:TPU:28, one launch (start us, length us, event | category | flops | bytes accessed | tf_op | source)
XLA Modules:
  0.0 89.9 jit_solution(8398341236935129563)
XLA Ops:
  3.5 3.4 %collective-permute-start = (f32[3,2048]{1,0:T(4,128)S(1)}, f32[3,2048]{1,0:T(4,128)S(1)}, u32[]{:S(2)}, u32[]{:S(2)}) collective-permute-start(f32[3,2048]{1,0:T(4,128)S(1)} %pad_maximum_fusion.11), channel_id=1, source_target_pairs={{0,2},{2,4},{4,6},{6,8},{8,10},{10,12},{12,14},{14,16},{16,18},{18... | collective-permute-start | bytes 73736 | tf_op jit(solution)/shard_map/ppermute | solution.py:16
  14.8 1.2 %fusion.4 = f32[2,2,8,64,64]{4,3,2,1,0:T(8,128)S(1)} fusion(f32[1,2,8,64,64]{4,3,2,1,0:T(8,128)S(1)} %bitcast.213, f32[1,2,8,64,64]{4,3,2,1,0:T(8,128)S(1)} %get-tuple-element.37, f32[1,2,8,64,64]{4,3,2,1,0:T(8,128)S(1)} %get-tuple-element.36), kind=kOutput, calls=%fused_computation.17 | convolution fusion | flops 100925440 | bytes 1310720 | tf_op jit(solution)/shard_map/sbhij,sbhjk->sbhik/dot_general | solution.py:114
  16.1 1.2 %fusion.10 = f32[2,2,8,64,64]{4,3,2,1,0:T(8,128)S(1)} fusion(f32[2,2,8,64,64]{4,3,2,1,0:T(8,128)S(1)} %fusion.4, f32[1,2,8,64,64]{4,3,2,1,0:T(8,128)S(1)} %get-tuple-element.31, f32[1,2,8,64,64]{4,3,2,1,0:T(8,128)S(1)} %get-tuple-element.30), kind=kOutput, calls=%fused_computation.25 | convolution fusion | flops 100794368 | bytes 1572864 | tf_op jit(solution)/shard_map/sbhij,sbhjk->sbhik/dot_general | solution.py:114
  17.4 1.2 %fusion.14 = f32[2,2,8,64,64]{4,3,2,1,0:T(8,128)S(1)} fusion(f32[2,2,8,64,64]{4,3,2,1,0:T(8,128)S(1)} %fusion.10, f32[1,2,8,64,64]{4,3,2,1,0:T(8,128)S(1)} %get-tuple-element.29, f32[1,2,8,64,64]{4,3,2,1,0:T(8,128)S(1)} %get-tuple-element.28), kind=kOutput, calls=%fused_computation.29 | convolution fusion | flops 100794368 | bytes 1572864 | tf_op jit(solution)/shard_map/sbhij,sbhjk->sbhik/dot_general | solution.py:114
  18.7 1.2 %fusion.18 = f32[2,2,8,64,64]{4,3,2,1,0:T(8,128)S(1)} fusion(f32[2,2,8,64,64]{4,3,2,1,0:T(8,128)S(1)} %fusion.14, f32[1,2,8,64,64]{4,3,2,1,0:T(8,128)S(1)} %get-tuple-element.27, f32[1,2,8,64,64]{4,3,2,1,0:T(8,128)S(1)} %get-tuple-element.26), kind=kOutput, calls=%fused_computation.33 | convolution fusion | flops 100794368 | bytes 1572864 | tf_op jit(solution)/shard_map/sbhij,sbhjk->sbhik/dot_general | solution.py:114
  21.5 1.0 %fusion.22 = f32[2,8,64,256]{3,2,1,0:T(8,128)S(1)} fusion(f32[2,8,64,64]{3,2,1,0:T(8,128)S(1)} %fusion.58, f32[2,8,64,128]{3,2,1,0:T(8,128)S(1)} %bitcast_multiply_fusion.2, f32[2,8,64,128]{3,2,1,0:T(8,128)S(1)} %bitcast_multiply_fusion.3), kind=kOutput, calls=%fused_computation.37 | convolution fusion | flops 201588736 | bytes 2359296 | tf_op jit(solution)/shard_map/bhij,bhjd->bhid/dot_general | solution.py:143
  22.6 2.3 %fusion.69 = f32[2,8,128,256]{3,2,1,0:T(8,128)S(1)} fusion(f32[2,8,64,256]{3,2,1,0:T(8,128)S(1)} %fusion.22, f32[2,64,8,128]{3,1,0,2:T(8,128)S(1)} %bitcast.211, f32[2,8,64]{2,1,0:T(8,128)S(1)} %get-tuple-element.40), kind=kOutput, calls=%fused_computation.104 | convolution fusion | flops 402784256 | bytes 3674112 | tf_op jit(solution)/shard_map/bhjd,bhje->bhde/dot_general | solution.py:146
  25.2 1.0 %fusion.54 = f32[8,128,256]{2,1,0:T(8,128)S(1)} fusion(f32[8,128,256]{2,1,0:T(8,128)S(1)} %fusion.6, f32[2,8,128,128]{3,2,1,0:T(8,128)S(1)} %get-tuple-element.21, f32[2,8,128,128]{3,2,1,0:T(8,128)S(1)} %get-tuple-element.22), kind=kOutput, calls=%fused_computation.83 | convolution fusion | flops 402915328 | bytes 3670016 | tf_op jit(solution)/shard_map/hde,hef->hdf/dot_general | solution.py:232
  27.3 1.0 %fusion.126 = (bf16[8,128,128]{2,1,0:T(8,128)(2,1)}, f32[8,128,128]{2,1,0:T(8,128)}, bf16[8,128,128]{2,1,0:T(8,128)(2,1)}) fusion(f32[8,128,256]{2,1,0:T(8,128)S(1)} %fusion.6, f32[8,128,256]{2,1,0:T(8,128)S(1)} %fusion.54, f32[128,128]{1,0:T(8,128)S(1)} %fusion.107), kind=kLoop, calls=%fused_computation.225 | loop fusion | flops 524288 | bytes 2686976 | tf_op jit(solution)/shard_map/convert_element_type | solution.py:50
  33.7 2.1 %collective-permute-start.3 = (bf16[8,128,128]{2,1,0:T(8,128)(2,1)S(1)}, bf16[8,128,128]{2,1,0:T(8,128)(2,1)S(1)}, u32[]{:S(2)}, u32[]{:S(2)}) collective-permute-start(bf16[8,128,128]{2,1,0:T(8,128)(2,1)S(1)} %copy-done.14), channel_id=1, source_target_pairs={{0,2},{2,4},{4,6},{6,8},{8,10},{10,12},{12,14},{14,16},{16,18},{18... | collective-permute-start | bytes 786440 | tf_op jit(solution)/shard_map/ppermute | solution.py:33
  35.8 1.9 %collective-permute-start.1 = (bf16[8,128,128]{2,1,0:T(8,128)(2,1)S(1)}, bf16[8,128,128]{2,1,0:T(8,128)(2,1)S(1)}, u32[]{:S(2)}, u32[]{:S(2)}) collective-permute-start(bf16[8,128,128]{2,1,0:T(8,128)(2,1)S(1)} %copy-done.13), channel_id=1, source_target_pairs={{0,2},{2,4},{4,6},{6,8},{8,10},{10,12},{12,14},{14,16},{16,18},{18... | collective-permute-start | bytes 786440 | tf_op jit(solution)/shard_map/ppermute | solution.py:50
  38.4 7.5 %collective-permute-done.3 = bf16[8,128,128]{2,1,0:T(8,128)(2,1)S(1)} collective-permute-done((bf16[8,128,128]{2,1,0:T(8,128)(2,1)S(1)}, bf16[8,128,128]{2,1,0:T(8,128)(2,1)S(1)}, u32[]{:S(2)}, u32[]{:S(2)}) %collective-permute-start.3) | collective-permute-done | bytes 262176 | tf_op jit(solution)/shard_map/ppermute | solution.py:33
  46.6 1.3 %collective-permute-start.5 = (bf16[8,128,128]{2,1,0:T(8,128)(2,1)S(1)}, bf16[8,128,128]{2,1,0:T(8,128)(2,1)S(1)}, u32[]{:S(2)}, u32[]{:S(2)}) collective-permute-start(bf16[8,128,128]{2,1,0:T(8,128)(2,1)S(1)} %get-tuple-element.53), channel_id=1, source_target_pairs={{0,4},{2,6},{4,8},{6,10},{8,12},{10,14},{12,16},{14,18},{16,20},{1... | collective-permute-start | bytes 786440 | tf_op jit(solution)/shard_map/ppermute | solution.py:33
  47.9 2.2 %collective-permute-done.1 = bf16[8,128,128]{2,1,0:T(8,128)(2,1)S(1)} collective-permute-done((bf16[8,128,128]{2,1,0:T(8,128)(2,1)S(1)}, bf16[8,128,128]{2,1,0:T(8,128)(2,1)S(1)}, u32[]{:S(2)}, u32[]{:S(2)}) %collective-permute-start.1) | collective-permute-done | bytes 262176 | tf_op jit(solution)/shard_map/ppermute | solution.py:50
  50.5 1.3 %collective-permute-start.2 = (bf16[8,128,128]{2,1,0:T(8,128)(2,1)S(1)}, bf16[8,128,128]{2,1,0:T(8,128)(2,1)S(1)}, u32[]{:S(2)}, u32[]{:S(2)}) collective-permute-start(bf16[8,128,128]{2,1,0:T(8,128)(2,1)S(1)} %get-tuple-element.55), channel_id=1, source_target_pairs={{0,4},{2,6},{4,8},{6,10},{8,12},{10,14},{12,16},{14,18},{16,20},{1... | collective-permute-start | bytes 786440 | tf_op jit(solution)/shard_map/ppermute | solution.py:50
  51.9 5.8 %collective-permute-done.5 = bf16[8,128,128]{2,1,0:T(8,128)(2,1)S(1)} collective-permute-done((bf16[8,128,128]{2,1,0:T(8,128)(2,1)S(1)}, bf16[8,128,128]{2,1,0:T(8,128)(2,1)S(1)}, u32[]{:S(2)}, u32[]{:S(2)}) %collective-permute-start.5) | collective-permute-done | bytes 262176 | tf_op jit(solution)/shard_map/ppermute | solution.py:33
  57.7 1.0 %convolution_bitcast_fusion.2 = f32[2,8,128,128]{3,2,1,0:T(8,128)S(1)} fusion(f32[1,8,128,128]{3,2,1,0:T(8,128)S(1)} %bitcast.214, f32[1,8,128,128]{3,2,1,0:T(8,128)S(1)} %fusion.74, bf16[8,128,128]{2,1,0:T(8,128)(2,1)S(1)} %collective-permute-done.5, f32[128,128]{1,0:T(8,128)S(1)} %copy-done.11), kind=kOutput, calls=%fused_computation.4 | convolution fusion | flops 403177472 | bytes 2424832 | tf_op jit(solution)/shard_map/shde,hef->shdf/dot_general | solution.py:41
  58.8 2.5 %collective-permute-done.2 = bf16[8,128,128]{2,1,0:T(8,128)(2,1)S(1)} collective-permute-done((bf16[8,128,128]{2,1,0:T(8,128)(2,1)S(1)}, bf16[8,128,128]{2,1,0:T(8,128)(2,1)S(1)}, u32[]{:S(2)}, u32[]{:S(2)}) %collective-permute-start.2) | collective-permute-done | bytes 262176 | tf_op jit(solution)/shard_map/ppermute | solution.py:50
  61.9 1.3 %collective-permute-start.4 = (bf16[8,128,128]{2,1,0:T(8,128)(2,1)S(1)}, bf16[8,128,128]{2,1,0:T(8,128)(2,1)S(1)}, u32[]{:S(2)}, u32[]{:S(2)}) collective-permute-start(bf16[8,128,128]{2,1,0:T(8,128)(2,1)S(1)} %fusion.102), channel_id=1, source_target_pairs={{0,8},{2,10},{4,12},{6,14},{8,16},{10,18},{12,20},{14,22},{16,24},... | collective-permute-start | bytes 786440 | tf_op jit(solution)/shard_map/ppermute | solution.py:50
  63.3 1.3 %collective-permute-start.6 = (bf16[8,128,128]{2,1,0:T(8,128)(2,1)S(1)}, bf16[8,128,128]{2,1,0:T(8,128)(2,1)S(1)}, u32[]{:S(2)}, u32[]{:S(2)}) collective-permute-start(bf16[8,128,128]{2,1,0:T(8,128)(2,1)S(1)} %get-tuple-element.24), channel_id=1, source_target_pairs={{0,8},{2,10},{4,12},{6,14},{8,16},{10,18},{12,20},{14,22},{16,24},... | collective-permute-start | bytes 786440 | tf_op jit(solution)/shard_map/ppermute | solution.py:33
  64.6 8.3 %collective-permute-done.4 = bf16[8,128,128]{2,1,0:T(8,128)(2,1)S(1)} collective-permute-done((bf16[8,128,128]{2,1,0:T(8,128)(2,1)S(1)}, bf16[8,128,128]{2,1,0:T(8,128)(2,1)S(1)}, u32[]{:S(2)}, u32[]{:S(2)}) %collective-permute-start.4) | collective-permute-done | bytes 262176 | tf_op jit(solution)/shard_map/ppermute | solution.py:50
  73.6 1.5 %collective-permute-start.7 = (bf16[8,128,128]{2,1,0:T(8,128)(2,1)S(1)}, bf16[8,128,128]{2,1,0:T(8,128)(2,1)S(1)}, u32[]{:S(2)}, u32[]{:S(2)}) collective-permute-start(bf16[8,128,128]{2,1,0:T(8,128)(2,1)S(1)} %fusion.42), channel_id=1, source_target_pairs={{0,16},{2,18},{4,20},{6,22},{8,24},{10,26},{12,28},{14,30},{1,17},... | collective-permute-start | bytes 786440 | tf_op jit(solution)/shard_map/ppermute | solution.py:50
  75.3 1.2 %collective-permute-done.6 = bf16[8,128,128]{2,1,0:T(8,128)(2,1)S(1)} collective-permute-done((bf16[8,128,128]{2,1,0:T(8,128)(2,1)S(1)}, bf16[8,128,128]{2,1,0:T(8,128)(2,1)S(1)}, u32[]{:S(2)}, u32[]{:S(2)}) %collective-permute-start.6) | collective-permute-done | bytes 262176 | tf_op jit(solution)/shard_map/ppermute | solution.py:33
  77.1 9.8 %collective-permute-done.7 = bf16[8,128,128]{2,1,0:T(8,128)(2,1)S(1)} collective-permute-done((bf16[8,128,128]{2,1,0:T(8,128)(2,1)S(1)}, bf16[8,128,128]{2,1,0:T(8,128)(2,1)S(1)}, u32[]{:S(2)}, u32[]{:S(2)}) %collective-permute-start.7) | collective-permute-done | bytes 262176 | tf_op jit(solution)/shard_map/ppermute | solution.py:50
  (170 shorter events, 26.4 us)
Async XLA Ops:
  0.0 10.9 %copy-start = (f32[128]{0:T(128)S(1)}, f32[128]{0:T(128)}, u32[]{:S(2)}) copy-start(f32[128]{0:T(128)} %param.31) | copy-start | bytes 1540
  0.0 7.2 %copy-start.22 = (bf16[4,512]{1,0:T(4,128)(2,1)S(1)}, bf16[4,512]{1,0:T(4,128)(2,1)}, u32[]{:S(2)}) copy-start(bf16[4,512]{1,0:T(4,128)(2,1)} %param.24) | copy-start | bytes 12292
  0.0 7.3 %copy-start.29 = (f32[128,8]{0,1:T(8,128)S(1)}, f32[128,8]{0,1:T(8,128)}, u32[]{:S(2)}) copy-start(f32[128,8]{0,1:T(8,128)} %param.27) | copy-start | bytes 12292
  0.0 7.3 %copy-start.32 = (f32[16]{0:T(128)S(1)}, f32[16]{0:T(128)}, u32[]{:S(2)}) copy-start(f32[16]{0:T(128)} %param.29) | copy-start | bytes 196
  0.1 7.4 %copy-start.33 = (f32[16]{0:T(128)S(1)}, f32[16]{0:T(128)}, u32[]{:S(2)}) copy-start(f32[16]{0:T(128)} %param.28) | copy-start | bytes 196
  0.1 7.5 %copy-start.30 = (f32[128,8]{0,1:T(8,128)S(1)}, f32[128,8]{0,1:T(8,128)}, u32[]{:S(2)}) copy-start(f32[128,8]{0,1:T(8,128)} %param.26) | copy-start | bytes 12292
  2.1 5.9 %copy-start.21 = (bf16[4,1024]{1,0:T(4,128)(2,1)S(1)}, bf16[4,1024]{1,0:T(4,128)(2,1)}, u32[]{:S(2)}) copy-start(bf16[4,1024]{1,0:T(4,128)(2,1)} %param.25) | copy-start | bytes 24580
  3.5 8.1 %collective-permute-start = (f32[3,2048]{1,0:T(4,128)S(1)}, f32[3,2048]{1,0:T(4,128)S(1)}, u32[]{:S(2)}, u32[]{:S(2)}) collective-permute-start(f32[3,2048]{1,0:T(4,128)S(1)} %pad_maximum_fusion.11), channel_id=1, source_target_pairs={{0,2},{2,4},{4,6},{6,8},{8,10},{10,12},{12,14},{14,16},{16,18},{18... | collective-permute-start | bytes 73736 | tf_op jit(solution)/shard_map/ppermute | solution.py:16
  7.0 6.1 %copy-start.18 = (pred[64,64]{1,0:T(8,128)(4,1)}, pred[64,64]{1,0:T(8,128)(4,1)S(1)}, u32[]{:S(2)}) copy-start(pred[64,64]{1,0:T(8,128)(4,1)S(1)} %get-tuple-element.62) | copy-start | bytes 12292
  13.1 9.5 %copy-start.3 = (f32[128,4,2,128]{3,0,2,1:T(8,128)}, f32[128,4,2,128]{3,0,2,1:T(8,128)S(1)}, u32[]{:S(2)}) copy-start(f32[128,4,2,128]{3,0,2,1:T(8,128)S(1)} %broadcast_in_dim.20) | copy-start | bytes 1572868
  32.9 42.3 %copy-start.7 = (f32[2,8,64,128]{3,2,1,0:T(8,128)}, f32[2,8,64,128]{3,2,1,0:T(8,128)S(1)}, u32[]{:S(2)}) copy-start(f32[2,8,64,128]{3,2,1,0:T(8,128)S(1)} %convolution_subtract_fusion) | copy-start | bytes 1572868
  32.9 12.9 %copy-start.2 = (f32[8,128,256]{2,1,0:T(8,128)S(1)}, f32[8,128,256]{2,1,0:T(8,128)}, u32[]{:S(2)}) copy-start(f32[8,128,256]{2,1,0:T(8,128)} %copy-done.1) | copy-start | bytes 3145732
  33.7 16.4 %copy-start.6 = (f32[8,128,128]{2,1,0:T(8,128)S(1)}, f32[8,128,128]{2,1,0:T(8,128)}, u32[]{:S(2)}) copy-start(f32[8,128,128]{2,1,0:T(8,128)} %get-tuple-element.20) | copy-start | bytes 1572868
  33.7 12.2 %collective-permute-start.3 = (bf16[8,128,128]{2,1,0:T(8,128)(2,1)S(1)}, bf16[8,128,128]{2,1,0:T(8,128)(2,1)S(1)}, u32[]{:S(2)}, u32[]{:S(2)}) collective-permute-start(bf16[8,128,128]{2,1,0:T(8,128)(2,1)S(1)} %copy-done.14), channel_id=1, source_target_pairs={{0,2},{2,4},{4,6},{6,8},{8,10},{10,12},{12,14},{14,16},{16,18},{18... | collective-permute-start | bytes 786440 | tf_op jit(solution)/shard_map/ppermute | solution.py:33
  35.8 14.3 %collective-permute-start.1 = (bf16[8,128,128]{2,1,0:T(8,128)(2,1)S(1)}, bf16[8,128,128]{2,1,0:T(8,128)(2,1)S(1)}, u32[]{:S(2)}, u32[]{:S(2)}) collective-permute-start(bf16[8,128,128]{2,1,0:T(8,128)(2,1)S(1)} %copy-done.13), channel_id=1, source_target_pairs={{0,2},{2,4},{4,6},{6,8},{8,10},{10,12},{12,14},{14,16},{16,18},{18... | collective-permute-start | bytes 786440 | tf_op jit(solution)/shard_map/ppermute | solution.py:50
  38.4 36.9 %copy-start.5 = (f32[2,8,64,128]{3,2,1,0:T(8,128)}, f32[2,8,64,128]{3,2,1,0:T(8,128)S(1)}, u32[]{:S(2)}) copy-start(f32[2,8,64,128]{3,2,1,0:T(8,128)S(1)} %fusion.52) | copy-start | bytes 1572868
  38.4 19.3 %copy-start.11 = (f32[128,128]{1,0:T(8,128)S(1)}, f32[128,128]{1,0:T(8,128)}, u32[]{:S(2)}) copy-start(f32[128,128]{1,0:T(8,128)} %fusion.105) | copy-start | bytes 196612
  46.6 11.1 %collective-permute-start.5 = (bf16[8,128,128]{2,1,0:T(8,128)(2,1)S(1)}, bf16[8,128,128]{2,1,0:T(8,128)(2,1)S(1)}, u32[]{:S(2)}, u32[]{:S(2)}) collective-permute-start(bf16[8,128,128]{2,1,0:T(8,128)(2,1)S(1)} %get-tuple-element.53), channel_id=1, source_target_pairs={{0,4},{2,6},{4,8},{6,10},{8,12},{10,14},{12,16},{14,18},{16,20},{1... | collective-permute-start | bytes 786440 | tf_op jit(solution)/shard_map/ppermute | solution.py:33
  50.5 10.7 %collective-permute-start.2 = (bf16[8,128,128]{2,1,0:T(8,128)(2,1)S(1)}, bf16[8,128,128]{2,1,0:T(8,128)(2,1)S(1)}, u32[]{:S(2)}, u32[]{:S(2)}) collective-permute-start(bf16[8,128,128]{2,1,0:T(8,128)(2,1)S(1)} %get-tuple-element.55), channel_id=1, source_target_pairs={{0,4},{2,6},{4,8},{6,10},{8,12},{10,14},{12,16},{14,18},{16,20},{1... | collective-permute-start | bytes 786440 | tf_op jit(solution)/shard_map/ppermute | solution.py:50
  61.9 10.9 %collective-permute-start.4 = (bf16[8,128,128]{2,1,0:T(8,128)(2,1)S(1)}, bf16[8,128,128]{2,1,0:T(8,128)(2,1)S(1)}, u32[]{:S(2)}, u32[]{:S(2)}) collective-permute-start(bf16[8,128,128]{2,1,0:T(8,128)(2,1)S(1)} %fusion.102), channel_id=1, source_target_pairs={{0,8},{2,10},{4,12},{6,14},{8,16},{10,18},{12,20},{14,22},{16,24},... | collective-permute-start | bytes 786440 | tf_op jit(solution)/shard_map/ppermute | solution.py:50
  63.3 13.1 %collective-permute-start.6 = (bf16[8,128,128]{2,1,0:T(8,128)(2,1)S(1)}, bf16[8,128,128]{2,1,0:T(8,128)(2,1)S(1)}, u32[]{:S(2)}, u32[]{:S(2)}) collective-permute-start(bf16[8,128,128]{2,1,0:T(8,128)(2,1)S(1)} %get-tuple-element.24), channel_id=1, source_target_pairs={{0,8},{2,10},{4,12},{6,14},{8,16},{10,18},{12,20},{14,22},{16,24},... | collective-permute-start | bytes 786440 | tf_op jit(solution)/shard_map/ppermute | solution.py:33
  73.6 13.3 %collective-permute-start.7 = (bf16[8,128,128]{2,1,0:T(8,128)(2,1)S(1)}, bf16[8,128,128]{2,1,0:T(8,128)(2,1)S(1)}, u32[]{:S(2)}, u32[]{:S(2)}) collective-permute-start(bf16[8,128,128]{2,1,0:T(8,128)(2,1)S(1)} %fusion.42), channel_id=1, source_target_pairs={{0,16},{2,18},{4,20},{6,22},{8,24},{10,26},{12,28},{14,30},{1,17},... | collective-permute-start | bytes 786440 | tf_op jit(solution)/shard_map/ppermute | solution.py:50
  75.2 12.1 %slice-start.1 = ((f32[2,8,64,128]{3,2,1,0:T(8,128)}), f32[1,8,64,128]{3,2,1,0:T(8,128)S(1)}, s32[]{:S(2)}) async-start(f32[2,8,64,128]{3,2,1,0:T(8,128)} %copy-done.7), calls=%async_computation.1 | async-start | bytes 524288 | tf_op jit(solution)/shard_map/slice | solution.py:245
  75.2 12.1 %slice-start = ((f32[2,8,64,128]{3,2,1,0:T(8,128)}), f32[1,8,64,128]{3,2,1,0:T(8,128)S(1)}, s32[]{:S(2)}) async-start(f32[2,8,64,128]{3,2,1,0:T(8,128)} %copy-done.5), calls=%async_computation | async-start | bytes 524288 | tf_op jit(solution)/shard_map/slice | solution.py:245
  (20 other events, 44.8 us)

commit v11 on v10

--- a/solution.py
+++ b/solution.py
@@ -16,7 +16,7 @@
     return lax.ppermute(value, axis, [(source, source + steps) for source in range(first, last)])
 
 
-def scan_states(trans, offset, axis):
+def scan_states(trans, offset, axis, rider):
     devices, mine = (lax.axis_size(axis), lax.axis_index(axis))
     spans = []
     span = 1
@@ -47,7 +47,10 @@
     carried = offset
     for step, span in enumerate(spans):
         pairs = [(source, source + span) for source in range(devices - span)]
-        earlier = lax.ppermute(carried.astype(jnp.bfloat16), axis, pairs).astype(jnp.float32)
+        earlier = lax.ppermute(carried.astype(jnp.bfloat16), axis, pairs)
+        if step == 0:
+            rider, earlier = lax.optimization_barrier((rider, earlier))
+        earlier = earlier.astype(jnp.float32)
         last_map = exclusive_maps[step]
         if last_map is None:
             state = earlier
@@ -64,7 +67,7 @@
             carried = both[1] + carried
         else:
             state = state + product(last_map, earlier)
-    return state
+    return (state, rider)
 
 
 def expand_quantized(raw_rows, scales):
@@ -233,8 +236,8 @@
             "hde,hef->hdf", maps[block][..., :key_width], device_map, precision=HIGHEST
         ).at[..., key_width:].add(maps[block][..., key_width:])
     dev_trans, dev_offset = (device_map[..., :key_width], device_map[..., key_width:])
-    query_window, _ = lax.optimization_barrier(
-        (jnp.concatenate([tail_rows[0], query_deq], axis=0), dev_offset)
+    incoming, query_window = scan_states(
+        dev_trans, dev_offset, "seq", jnp.concatenate([tail_rows[0], query_deq], axis=0)
     )
     query_conv = causal_filter(query_window, conv_query)
     query_rows = unit_heads(query_conv, head_width) * head_width ** (-0.5)
@@ -247,7 +250,6 @@
         read = jnp.einsum("hid,hde->hie", readout[block], maps_before[block], precision=HIGHEST)
         read_maps.append(read[..., :key_width])
         local_outs.append(zero_out[block] + read[..., key_width:])
-    incoming = scan_states(dev_trans, dev_offset, "seq")
     outputs = jnp.stack(local_outs) + jnp.einsum(
         "bhid,hde->bhie", jnp.stack(read_maps), incoming, precision=HIGHEST
     )

time: 90.8 us -> 90.7 us (level)
  the two profiles are of different devices: /device:TPU:28 before, /device:TPU:24 now
where the time goes in v11:
time: 90.7 us; the launch traced here: 90 us
  waiting for transfers between devices  29.1 us (32%)
  matrix products  22.7 us (25%)
  starting transfers between devices  17.8 us (20%)
  other arithmetic  12.1 us (13%)
  local copies, waits for them, and re-layouts  7.4 us (8%)
  between operations  0.96 us (1%)
    ppermute x4, waiting for transfers between devices, scan_states(): earlier = lax.ppermute(carried.astype(jnp.bfloat16), axis, pairs)  23 us
    ppermute x3, starting transfers between devices, scan_states(): earlier = lax.ppermute((inclusive - eye).astype(jnp.bfloat16), axis, pairs)  7.45 us
    ppermute x4, starting transfers between devices, scan_states(): earlier = lax.ppermute(carried.astype(jnp.bfloat16), axis, pairs)  6.97 us
    ppermute x3, waiting for transfers between devices, scan_states(): earlier = lax.ppermute((inclusive - eye).astype(jnp.bfloat16), axis, pairs)  4.79 us
    dot_general x4, matrix products, unit_lower_inverse(): jnp.einsum('sbhij,sbhjk->sbhik', jnp.stack([inverse, power]), jnp.stack([...  4.72 us
    dot_general x4, matrix products, product(): return jnp.einsum('hde,hef->hdf', left, right, precision=HIGHEST)  4.25 us
    unnamed x60, local copies, waits for them, and re-layouts  3.62 us
    ppermute x1, starting transfers between devices, from_behind(): lax.ppermute(value, axis, [(source, source + steps) for source in range(f...  3.4 us
  transfers between devices with their start and end apart: 8, of which 7 were waited for; matrix products, arithmetic and copies ran while one was open for 17% of the time, Pallas kernels for 0%

profile of v11, /device:TPU:24, one launch (start us, length us, event | category | flops | bytes accessed | tf_op | source)
XLA Modules:
  0.0 90.0 jit_solution(13155904108340919512)
XLA Ops:
  3.5 3.4 %collective-permute-start = (f32[3,2048]{1,0:T(4,128)S(1)}, f32[3,2048]{1,0:T(4,128)S(1)}, u32[]{:S(2)}, u32[]{:S(2)}) collective-permute-start(f32[3,2048]{1,0:T(4,128)S(1)} %pad_maximum_fusion.11), channel_id=1, source_target_pairs={{0,2},{2,4},{4,6},{6,8},{8,10},{10,12},{12,14},{14,16},{16,18},{18... | collective-permute-start | bytes 73736 | tf_op jit(solution)/shard_map/ppermute | solution.py:16
  9.8 1.3 %collective-permute-done = f32[3,2048]{1,0:T(4,128)S(1)} collective-permute-done((f32[3,2048]{1,0:T(4,128)S(1)}, f32[3,2048]{1,0:T(4,128)S(1)}, u32[]{:S(2)}, u32[]{:S(2)}) %collective-permute-start) | collective-permute-done | bytes 24608 | tf_op jit(solution)/shard_map/ppermute | solution.py:16
  14.3 1.2 %fusion.4 = f32[2,2,8,64,64]{4,3,2,1,0:T(8,128)S(1)} fusion(f32[1,2,8,64,64]{4,3,2,1,0:T(8,128)S(1)} %bitcast.213, f32[1,2,8,64,64]{4,3,2,1,0:T(8,128)S(1)} %get-tuple-element.38, f32[1,2,8,64,64]{4,3,2,1,0:T(8,128)S(1)} %get-tuple-element.37), kind=kOutput, calls=%fused_computation.17 | convolution fusion | flops 100925440 | bytes 1310720 | tf_op jit(solution)/shard_map/sbhij,sbhjk->sbhik/dot_general | solution.py:117
  15.6 1.2 %fusion.10 = f32[2,2,8,64,64]{4,3,2,1,0:T(8,128)S(1)} fusion(f32[2,2,8,64,64]{4,3,2,1,0:T(8,128)S(1)} %fusion.4, f32[1,2,8,64,64]{4,3,2,1,0:T(8,128)S(1)} %get-tuple-element.32, f32[1,2,8,64,64]{4,3,2,1,0:T(8,128)S(1)} %get-tuple-element.31), kind=kOutput, calls=%fused_computation.25 | convolution fusion | flops 100794368 | bytes 1572864 | tf_op jit(solution)/shard_map/sbhij,sbhjk->sbhik/dot_general | solution.py:117
  16.9 1.2 %fusion.14 = f32[2,2,8,64,64]{4,3,2,1,0:T(8,128)S(1)} fusion(f32[2,2,8,64,64]{4,3,2,1,0:T(8,128)S(1)} %fusion.10, f32[1,2,8,64,64]{4,3,2,1,0:T(8,128)S(1)} %get-tuple-element.30, f32[1,2,8,64,64]{4,3,2,1,0:T(8,128)S(1)} %get-tuple-element.29), kind=kOutput, calls=%fused_computation.29 | convolution fusion | flops 100794368 | bytes 1572864 | tf_op jit(solution)/shard_map/sbhij,sbhjk->sbhik/dot_general | solution.py:117
  18.2 1.2 %fusion.18 = f32[2,2,8,64,64]{4,3,2,1,0:T(8,128)S(1)} fusion(f32[2,2,8,64,64]{4,3,2,1,0:T(8,128)S(1)} %fusion.14, f32[1,2,8,64,64]{4,3,2,1,0:T(8,128)S(1)} %get-tuple-element.28, f32[1,2,8,64,64]{4,3,2,1,0:T(8,128)S(1)} %get-tuple-element.27), kind=kOutput, calls=%fused_computation.33 | convolution fusion | flops 100794368 | bytes 1572864 | tf_op jit(solution)/shard_map/sbhij,sbhjk->sbhik/dot_general | solution.py:117
  23.0 2.3 %fusion.69 = f32[2,8,128,256]{3,2,1,0:T(8,128)S(1)} fusion(f32[2,8,64,256]{3,2,1,0:T(8,128)S(1)} %fusion.22, f32[2,64,8,128]{3,1,0,2:T(8,128)S(1)} %bitcast.211, f32[2,8,64]{2,1,0:T(8,128)S(1)} %get-tuple-element.41), kind=kOutput, calls=%fused_computation.104 | convolution fusion | flops 402784256 | bytes 3674112 | tf_op jit(solution)/shard_map/bhjd,bhje->bhde/dot_general | solution.py:149
  27.6 2.1 %collective-permute-start.1 = (bf16[8,128,128]{2,1,0:T(8,128)(2,1)}, bf16[8,128,128]{2,1,0:T(8,128)(2,1)}, u32[]{:S(2)}, u32[]{:S(2)}) collective-permute-start(bf16[8,128,128]{2,1,0:T(8,128)(2,1)} %get-tuple-element.25), channel_id=1, source_target_pairs={{0,2},{2,4},{4,6},{6,8},{8,10},{10,12},{12,14},{14,16},{16,18},{18... | collective-permute-start | bytes 786440 | tf_op jit(solution)/shard_map/ppermute | solution.py:50
  31.0 3.8 %collective-permute-start.3 = (bf16[8,128,128]{2,1,0:T(8,128)(2,1)}, bf16[8,128,128]{2,1,0:T(8,128)(2,1)}, u32[]{:S(2)}, u32[]{:S(2)}) collective-permute-start(bf16[8,128,128]{2,1,0:T(8,128)(2,1)} %get-tuple-element.26), channel_id=1, source_target_pairs={{0,2},{2,4},{4,6},{6,8},{8,10},{10,12},{12,14},{14,16},{16,18},{18... | collective-permute-start | bytes 786440 | tf_op jit(solution)/shard_map/ppermute | solution.py:33
  35.5 4.6 %collective-permute-done.1 = bf16[8,128,128]{2,1,0:T(8,128)(2,1)} collective-permute-done((bf16[8,128,128]{2,1,0:T(8,128)(2,1)}, bf16[8,128,128]{2,1,0:T(8,128)(2,1)}, u32[]{:S(2)}, u32[]{:S(2)}) %collective-permute-start.1) | collective-permute-done | bytes 262176 | tf_op jit(solution)/shard_map/ppermute | solution.py:50
  40.1 1.5 %multiply_convert_fusion.1 = bf16[128,512]{1,0:T(8,128)(2,1)} fusion(f32[131,512]{1,0:T(8,128)S(1)} %pad_maximum_fusion.9, f32[512]{0:T(512)} %bitcast.236, f32[512]{0:T(512)} %bitcast.237, f32[512]{0:T(512)} %bitcast.235, f32[512]{0:T(512)} %bitcast.234), kind=kLoop, calls=%fused_computation.157 | loop fusion | flops 786432 | bytes 1187840 | tf_op jit(solution)/shard_map/convert_element_type | solution.py:88
  46.0 1.8 %subtract_convert_fusion.1 = (bf16[8,128,128]{2,1,0:T(8,128)(2,1)S(1)}, f32[8,128,128]{2,1,0:T(8,128)S(1)}) fusion(f32[128,128]{1,0:T(8,128)S(1)} %fusion.108, f32[8,128,256]{2,1,0:T(8,128)S(1)} %fusion.54, bf16[8,128,128]{2,1,0:T(8,128)(2,1)} %collective-permute-done.3, f32[128,128]{1,0:T(8,128)S(1)} %fusion.107, pred[]{:T(512)S(6)} %ge.39), kind=kOutput, calls=%fused_computation.112 | convolution fusion | flops 201981952 | bytes 2228225 | tf_op jit(solution)/shard_map/hde,hef->hdf/dot_general | solution.py:166
  47.8 2.4 %collective-permute-start.5 = (bf16[8,128,128]{2,1,0:T(8,128)(2,1)S(1)}, bf16[8,128,128]{2,1,0:T(8,128)(2,1)S(1)}, u32[]{:S(2)}, u32[]{:S(2)}) collective-permute-start(bf16[8,128,128]{2,1,0:T(8,128)(2,1)S(1)} %get-tuple-element.54), channel_id=1, source_target_pairs={{0,4},{2,6},{4,8},{6,10},{8,12},{10,14},{12,16},{14,18},{16,20},{1... | collective-permute-start | bytes 786440 | tf_op jit(solution)/shard_map/ppermute | solution.py:33
  50.2 1.4 %fusion.130 = (bf16[8,128,128]{2,1,0:T(8,128)(2,1)S(1)}, f32[8,128,128]{2,1,0:T(8,128)S(1)}) fusion(f32[8,128,256]{2,1,0:T(8,128)S(1)} %copy-done.6, f32[8,128,256]{2,1,0:T(8,128)S(1)} %fusion.54, bf16[8,128,128]{2,1,0:T(8,128)(2,1)} %collective-permute-done.1), kind=kOutput, calls=%fused_computation.229 | convolution fusion | flops 201719808 | bytes 2621440 | tf_op jit(solution)/shard_map/hde,hef->hdf/dot_general | solution.py:166
  51.6 2.1 %collective-permute-start.2 = (bf16[8,128,128]{2,1,0:T(8,128)(2,1)S(1)}, bf16[8,128,128]{2,1,0:T(8,128)(2,1)S(1)}, u32[]{:S(2)}, u32[]{:S(2)}) collective-permute-start(bf16[8,128,128]{2,1,0:T(8,128)(2,1)S(1)} %get-tuple-element.56), channel_id=1, source_target_pairs={{0,4},{2,6},{4,8},{6,10},{8,12},{10,14},{12,16},{14,18},{16,20},{1... | collective-permute-start | bytes 786440 | tf_op jit(solution)/shard_map/ppermute | solution.py:50
  55.4 3.5 %collective-permute-done.5 = bf16[8,128,128]{2,1,0:T(8,128)(2,1)S(1)} collective-permute-done((bf16[8,128,128]{2,1,0:T(8,128)(2,1)S(1)}, bf16[8,128,128]{2,1,0:T(8,128)(2,1)S(1)}, u32[]{:S(2)}, u32[]{:S(2)}) %collective-permute-start.5) | collective-permute-done | bytes 262176 | tf_op jit(solution)/shard_map/ppermute | solution.py:33
  60.0 1.7 %collective-permute-done.2 = bf16[8,128,128]{2,1,0:T(8,128)(2,1)S(1)} collective-permute-done((bf16[8,128,128]{2,1,0:T(8,128)(2,1)S(1)}, bf16[8,128,128]{2,1,0:T(8,128)(2,1)S(1)}, u32[]{:S(2)}, u32[]{:S(2)}) %collective-permute-start.2) | collective-permute-done | bytes 262176 | tf_op jit(solution)/shard_map/ppermute | solution.py:50
  62.4 1.3 %collective-permute-start.4 = (bf16[8,128,128]{2,1,0:T(8,128)(2,1)S(1)}, bf16[8,128,128]{2,1,0:T(8,128)(2,1)S(1)}, u32[]{:S(2)}, u32[]{:S(2)}) collective-permute-start(bf16[8,128,128]{2,1,0:T(8,128)(2,1)S(1)} %fusion.102), channel_id=1, source_target_pairs={{0,8},{2,10},{4,12},{6,14},{8,16},{10,18},{12,20},{14,22},{16,24},... | collective-permute-start | bytes 786440 | tf_op jit(solution)/shard_map/ppermute | solution.py:50
  63.8 1.3 %collective-permute-start.6 = (bf16[8,128,128]{2,1,0:T(8,128)(2,1)S(1)}, bf16[8,128,128]{2,1,0:T(8,128)(2,1)S(1)}, u32[]{:S(2)}, u32[]{:S(2)}) collective-permute-start(bf16[8,128,128]{2,1,0:T(8,128)(2,1)S(1)} %get-tuple-element.24), channel_id=1, source_target_pairs={{0,8},{2,10},{4,12},{6,14},{8,16},{10,18},{12,20},{14,22},{16,24},... | collective-permute-start | bytes 786440 | tf_op jit(solution)/shard_map/ppermute | solution.py:33
  65.1 6.6 %collective-permute-done.4 = bf16[8,128,128]{2,1,0:T(8,128)(2,1)S(1)} collective-permute-done((bf16[8,128,128]{2,1,0:T(8,128)(2,1)S(1)}, bf16[8,128,128]{2,1,0:T(8,128)(2,1)S(1)}, u32[]{:S(2)}, u32[]{:S(2)}) %collective-permute-start.4) | collective-permute-done | bytes 262176 | tf_op jit(solution)/shard_map/ppermute | solution.py:50
  72.4 1.5 %collective-permute-start.7 = (bf16[8,128,128]{2,1,0:T(8,128)(2,1)S(1)}, bf16[8,128,128]{2,1,0:T(8,128)(2,1)S(1)}, u32[]{:S(2)}, u32[]{:S(2)}) collective-permute-start(bf16[8,128,128]{2,1,0:T(8,128)(2,1)S(1)} %fusion.42), channel_id=1, source_target_pairs={{0,16},{2,18},{4,20},{6,22},{8,24},{10,26},{12,28},{14,30},{1,17},... | collective-permute-start | bytes 786440 | tf_op jit(solution)/shard_map/ppermute | solution.py:50
  74.1 1.3 %collective-permute-done.6 = bf16[8,128,128]{2,1,0:T(8,128)(2,1)S(1)} collective-permute-done((bf16[8,128,128]{2,1,0:T(8,128)(2,1)S(1)}, bf16[8,128,128]{2,1,0:T(8,128)(2,1)S(1)}, u32[]{:S(2)}, u32[]{:S(2)}) %collective-permute-start.6) | collective-permute-done | bytes 262176 | tf_op jit(solution)/shard_map/ppermute | solution.py:33
  76.1 10.1 %collective-permute-done.7 = bf16[8,128,128]{2,1,0:T(8,128)(2,1)S(1)} collective-permute-done((bf16[8,128,128]{2,1,0:T(8,128)(2,1)S(1)}, bf16[8,128,128]{2,1,0:T(8,128)(2,1)S(1)}, u32[]{:S(2)}, u32[]{:S(2)}) %collective-permute-start.7) | collective-permute-done | bytes 262176 | tf_op jit(solution)/shard_map/ppermute | solution.py:50
  86.5 1.9 %multiply_reduce_fusion = (f32[2,64,8]{1,2,0:T(8,128)S(1)}, f32[2,64,8,128]{3,1,2,0:T(8,128)S(1)}) fusion(f32[1,8,64,128]{3,2,1,0:T(8,128)S(1)} %get-tuple-element.33, f32[1,8,64,128]{3,2,1,0:T(8,128)S(1)} %slice-done.1, f32[8,128,128]{2,1,0:T(8,128)S(1)} %fusion.132, f32[2,8,128,128]{3,2,1,0:T(8,128)S(1)} %convolution_bitcast_fusion, ...), kind=kOutput, calls=%fused_computation.106 | convolution fusion | flops 202505216 | bytes 3411968 | tf_op jit(solution)/shard_map/bhid,hde->bhie/dot_general | solution.py:253
  (156 shorter events, 28.6 us)
Async XLA Ops:
  0.0 9.6 %copy-start = (f32[128]{0:T(128)S(1)}, f32[128]{0:T(128)}, u32[]{:S(2)}) copy-start(f32[128]{0:T(128)} %param.31) | copy-start | bytes 1540
  0.0 7.2 %copy-start.20 = (bf16[4,512]{1,0:T(4,128)(2,1)S(1)}, bf16[4,512]{1,0:T(4,128)(2,1)}, u32[]{:S(2)}) copy-start(bf16[4,512]{1,0:T(4,128)(2,1)} %param.24) | copy-start | bytes 12292
  0.0 7.3 %copy-start.22 = (f32[128,8]{0,1:T(8,128)S(1)}, f32[128,8]{0,1:T(8,128)}, u32[]{:S(2)}) copy-start(f32[128,8]{0,1:T(8,128)} %param.27) | copy-start | bytes 12292
  0.0 7.3 %copy-start.25 = (f32[16]{0:T(128)S(1)}, f32[16]{0:T(128)}, u32[]{:S(2)}) copy-start(f32[16]{0:T(128)} %param.29) | copy-start | bytes 196
  0.1 7.4 %copy-start.26 = (f32[16]{0:T(128)S(1)}, f32[16]{0:T(128)}, u32[]{:S(2)}) copy-start(f32[16]{0:T(128)} %param.28) | copy-start | bytes 196
  0.1 7.5 %copy-start.23 = (f32[128,8]{0,1:T(8,128)S(1)}, f32[128,8]{0,1:T(8,128)}, u32[]{:S(2)}) copy-start(f32[128,8]{0,1:T(8,128)} %param.26) | copy-start | bytes 12292
  2.0 5.9 %copy-start.9 = (bf16[128,1024]{1,0:T(8,128)(2,1)S(1)}, bf16[128,1024]{1,0:T(8,128)(2,1)}, u32[]{:S(2)}) copy-start(bf16[128,1024]{1,0:T(8,128)(2,1)} %param.19) | copy-start | bytes 786436
  2.1 5.9 %copy-start.19 = (bf16[4,1024]{1,0:T(4,128)(2,1)S(1)}, bf16[4,1024]{1,0:T(4,128)(2,1)}, u32[]{:S(2)}) copy-start(bf16[4,1024]{1,0:T(4,128)(2,1)} %param.25) | copy-start | bytes 24580
  3.5 5.4 %copy-start.21 = (bf16[4,512]{1,0:T(4,128)(2,1)S(1)}, bf16[4,512]{1,0:T(4,128)(2,1)}, u32[]{:S(2)}) copy-start(bf16[4,512]{1,0:T(4,128)(2,1)} %param.23) | copy-start | bytes 12292
  3.5 7.6 %collective-permute-start = (f32[3,2048]{1,0:T(4,128)S(1)}, f32[3,2048]{1,0:T(4,128)S(1)}, u32[]{:S(2)}, u32[]{:S(2)}) collective-permute-start(f32[3,2048]{1,0:T(4,128)S(1)} %pad_maximum_fusion.11), channel_id=1, source_target_pairs={{0,2},{2,4},{4,6},{6,8},{8,10},{10,12},{12,14},{14,16},{16,18},{18... | collective-permute-start | bytes 73736 | tf_op jit(solution)/shard_map/ppermute | solution.py:16
  7.0 5.6 %copy-start.17 = (pred[64,64]{1,0:T(8,128)(4,1)}, pred[64,64]{1,0:T(8,128)(4,1)S(1)}, u32[]{:S(2)}) copy-start(pred[64,64]{1,0:T(8,128)(4,1)S(1)} %get-tuple-element.63) | copy-start | bytes 12292
  12.5 9.5 %copy-start.3 = (f32[128,4,2,128]{3,0,2,1:T(8,128)}, f32[128,4,2,128]{3,0,2,1:T(8,128)S(1)}, u32[]{:S(2)}) copy-start(f32[128,4,2,128]{3,0,2,1:T(8,128)S(1)} %broadcast_in_dim.20) | copy-start | bytes 1572868
  27.6 12.5 %collective-permute-start.1 = (bf16[8,128,128]{2,1,0:T(8,128)(2,1)}, bf16[8,128,128]{2,1,0:T(8,128)(2,1)}, u32[]{:S(2)}, u32[]{:S(2)}) collective-permute-start(bf16[8,128,128]{2,1,0:T(8,128)(2,1)} %get-tuple-element.25), channel_id=1, source_target_pairs={{0,2},{2,4},{4,6},{6,8},{8,10},{10,12},{12,14},{14,16},{16,18},{18... | collective-permute-start | bytes 786440 | tf_op jit(solution)/shard_map/ppermute | solution.py:50
  31.0 15.0 %collective-permute-start.3 = (bf16[8,128,128]{2,1,0:T(8,128)(2,1)}, bf16[8,128,128]{2,1,0:T(8,128)(2,1)}, u32[]{:S(2)}, u32[]{:S(2)}) collective-permute-start(bf16[8,128,128]{2,1,0:T(8,128)(2,1)} %get-tuple-element.26), channel_id=1, source_target_pairs={{0,2},{2,4},{4,6},{6,8},{8,10},{10,12},{12,14},{14,16},{16,18},{18... | collective-permute-start | bytes 786440 | tf_op jit(solution)/shard_map/ppermute | solution.py:33
  45.3 28.8 %copy-start.8 = (f32[2,8,64,128]{3,2,1,0:T(8,128)}, f32[2,8,64,128]{3,2,1,0:T(8,128)S(1)}, u32[]{:S(2)}) copy-start(f32[2,8,64,128]{3,2,1,0:T(8,128)S(1)} %convolution_subtract_fusion) | copy-start | bytes 1572868
  46.0 28.1 %copy-start.7 = (f32[2,8,64,128]{3,2,1,0:T(8,128)}, f32[2,8,64,128]{3,2,1,0:T(8,128)S(1)}, u32[]{:S(2)}) copy-start(f32[2,8,64,128]{3,2,1,0:T(8,128)S(1)} %fusion.52) | copy-start | bytes 1572868
  47.8 11.1 %collective-permute-start.5 = (bf16[8,128,128]{2,1,0:T(8,128)(2,1)S(1)}, bf16[8,128,128]{2,1,0:T(8,128)(2,1)S(1)}, u32[]{:S(2)}, u32[]{:S(2)}) collective-permute-start(bf16[8,128,128]{2,1,0:T(8,128)(2,1)S(1)} %get-tuple-element.54), channel_id=1, source_target_pairs={{0,4},{2,6},{4,8},{6,10},{8,12},{10,14},{12,16},{14,18},{16,20},{1... | collective-permute-start | bytes 786440 | tf_op jit(solution)/shard_map/ppermute | solution.py:33
  51.6 7.3 %copy-start.12 = (f32[128,128]{1,0:T(8,128)S(1)}, f32[128,128]{1,0:T(8,128)}, u32[]{:S(2)}) copy-start(f32[128,128]{1,0:T(8,128)} %fusion.106) | copy-start | bytes 196612
  51.6 10.1 %collective-permute-start.2 = (bf16[8,128,128]{2,1,0:T(8,128)(2,1)S(1)}, bf16[8,128,128]{2,1,0:T(8,128)(2,1)S(1)}, u32[]{:S(2)}, u32[]{:S(2)}) collective-permute-start(bf16[8,128,128]{2,1,0:T(8,128)(2,1)S(1)} %get-tuple-element.56), channel_id=1, source_target_pairs={{0,4},{2,6},{4,8},{6,10},{8,12},{10,14},{12,16},{14,18},{16,20},{1... | collective-permute-start | bytes 786440 | tf_op jit(solution)/shard_map/ppermute | solution.py:50
  62.4 9.3 %collective-permute-start.4 = (bf16[8,128,128]{2,1,0:T(8,128)(2,1)S(1)}, bf16[8,128,128]{2,1,0:T(8,128)(2,1)S(1)}, u32[]{:S(2)}, u32[]{:S(2)}) collective-permute-start(bf16[8,128,128]{2,1,0:T(8,128)(2,1)S(1)} %fusion.102), channel_id=1, source_target_pairs={{0,8},{2,10},{4,12},{6,14},{8,16},{10,18},{12,20},{14,22},{16,24},... | collective-permute-start | bytes 786440 | tf_op jit(solution)/shard_map/ppermute | solution.py:50
  63.8 11.6 %collective-permute-start.6 = (bf16[8,128,128]{2,1,0:T(8,128)(2,1)S(1)}, bf16[8,128,128]{2,1,0:T(8,128)(2,1)S(1)}, u32[]{:S(2)}, u32[]{:S(2)}) collective-permute-start(bf16[8,128,128]{2,1,0:T(8,128)(2,1)S(1)} %get-tuple-element.24), channel_id=1, source_target_pairs={{0,8},{2,10},{4,12},{6,14},{8,16},{10,18},{12,20},{14,22},{16,24},... | collective-permute-start | bytes 786440 | tf_op jit(solution)/shard_map/ppermute | solution.py:33
  72.4 13.7 %collective-permute-start.7 = (bf16[8,128,128]{2,1,0:T(8,128)(2,1)S(1)}, bf16[8,128,128]{2,1,0:T(8,128)(2,1)S(1)}, u32[]{:S(2)}, u32[]{:S(2)}) collective-permute-start(bf16[8,128,128]{2,1,0:T(8,128)(2,1)S(1)} %fusion.42), channel_id=1, source_target_pairs={{0,16},{2,18},{4,20},{6,22},{8,24},{10,26},{12,28},{14,30},{1,17},... | collective-permute-start | bytes 786440 | tf_op jit(solution)/shard_map/ppermute | solution.py:50
  74.1 12.4 %slice-start.1 = ((f32[2,8,64,128]{3,2,1,0:T(8,128)}), f32[1,8,64,128]{3,2,1,0:T(8,128)S(1)}, s32[]{:S(2)}) async-start(f32[2,8,64,128]{3,2,1,0:T(8,128)} %copy-done.8), calls=%async_computation.1 | async-start | bytes 524288 | tf_op jit(solution)/shard_map/slice | solution.py:248
  74.1 12.4 %slice-start = ((f32[2,8,64,128]{3,2,1,0:T(8,128)}), f32[1,8,64,128]{3,2,1,0:T(8,128)S(1)}, s32[]{:S(2)}) async-start(f32[2,8,64,128]{3,2,1,0:T(8,128)} %copy-done.7), calls=%async_computation | async-start | bytes 524288 | tf_op jit(solution)/shard_map/slice | solution.py:248
  (13 other events, 31.0 us)

commit v12 on v11

--- a/solution.py
+++ b/solution.py
@@ -71,10 +71,9 @@
 
 
 def expand_quantized(raw_rows, scales):
-    row_count = raw_rows.shape[0]
     head_count = scales.shape[1]
-    shaped = raw_rows.astype(jnp.float32).reshape(row_count, head_count, -1) * scales[:, :, None]
-    return shaped.reshape(row_count, -1)
+    width = raw_rows.shape[1] // head_count
+    return raw_rows.astype(jnp.float32) * jnp.repeat(scales, width, axis=1)
 
 
 def causal_filter(window, weights):

time: 90.7 us -> 90.1 us (level)
  the two profiles are of different devices: /device:TPU:24 before, /device:TPU:28 now
where the time goes in v12:
time: 90.1 us; the launch traced here: 89.5 us
  waiting for transfers between devices  32.5 us (36%)
  matrix products  22.7 us (25%)
  starting transfers between devices  14.6 us (16%)
  other arithmetic  11.8 us (13%)
  local copies, waits for them, and re-layouts  6.97 us (8%)
  between operations  0.91 us (1%)
    ppermute x4, waiting for transfers between devices, scan_states(): earlier = lax.ppermute(carried.astype(jnp.bfloat16), axis, pairs)  25.7 us
    ppermute x4, starting transfers between devices, scan_states(): earlier = lax.ppermute(carried.astype(jnp.bfloat16), axis, pairs)  6.74 us
    ppermute x3, waiting for transfers between devices, scan_states(): earlier = lax.ppermute((inclusive - eye).astype(jnp.bfloat16), axis, pairs)  5.56 us
    dot_general x4, matrix products, unit_lower_inverse(): jnp.einsum('sbhij,sbhjk->sbhik', jnp.stack([inverse, power]), jnp.stack([...  4.71 us
    ppermute x3, starting transfers between devices, scan_states(): earlier = lax.ppermute((inclusive - eye).astype(jnp.bfloat16), axis, pairs)  4.49 us
    dot_general x4, matrix products, product(): return jnp.einsum('hde,hef->hdf', left, right, precision=HIGHEST)  4.25 us
    ppermute x1, starting transfers between devices, from_behind(): lax.ppermute(value, axis, [(source, source + steps) for source in range(f...  3.4 us
    unnamed x56, local copies, waits for them, and re-layouts  3.4 us
  transfers between devices with their start and end apart: 8, of which 7 were waited for; matrix products, arithmetic and copies ran while one was open for 17% of the time, Pallas kernels for 0%

profile of v12, /device:TPU:28, one launch (start us, length us, event | category | flops | bytes accessed | tf_op | source)
XLA Modules:
  0.0 89.5 jit_solution(10767793457375423588)
XLA Ops:
  3.7 3.4 %collective-permute-start = (f32[3,2048]{1,0:T(4,128)S(1)}, f32[3,2048]{1,0:T(4,128)S(1)}, u32[]{:S(2)}, u32[]{:S(2)}) collective-permute-start(f32[3,2048]{1,0:T(4,128)S(1)} %pad_maximum_fusion.11), channel_id=1, source_target_pairs={{0,2},{2,4},{4,6},{6,8},{8,10},{10,12},{12,14},{14,16},{16,18},{18... | collective-permute-start | bytes 73736 | tf_op jit(solution)/shard_map/ppermute | solution.py:16
  9.1 1.2 %collective-permute-done = f32[3,2048]{1,0:T(4,128)S(1)} collective-permute-done((f32[3,2048]{1,0:T(4,128)S(1)}, f32[3,2048]{1,0:T(4,128)S(1)}, u32[]{:S(2)}, u32[]{:S(2)}) %collective-permute-start) | collective-permute-done | bytes 24608 | tf_op jit(solution)/shard_map/ppermute | solution.py:16
  13.5 1.2 %fusion.4 = f32[2,2,8,64,64]{4,3,2,1,0:T(8,128)S(1)} fusion(f32[1,2,8,64,64]{4,3,2,1,0:T(8,128)S(1)} %bitcast.193, f32[1,2,8,64,64]{4,3,2,1,0:T(8,128)S(1)} %get-tuple-element.38, f32[1,2,8,64,64]{4,3,2,1,0:T(8,128)S(1)} %get-tuple-element.37), kind=kOutput, calls=%fused_computation.17 | convolution fusion | flops 100925440 | bytes 1310720 | tf_op jit(solution)/shard_map/sbhij,sbhjk->sbhik/dot_general | solution.py:116
  14.8 1.2 %fusion.10 = f32[2,2,8,64,64]{4,3,2,1,0:T(8,128)S(1)} fusion(f32[2,2,8,64,64]{4,3,2,1,0:T(8,128)S(1)} %fusion.4, f32[1,2,8,64,64]{4,3,2,1,0:T(8,128)S(1)} %get-tuple-element.32, f32[1,2,8,64,64]{4,3,2,1,0:T(8,128)S(1)} %get-tuple-element.31), kind=kOutput, calls=%fused_computation.25 | convolution fusion | flops 100794368 | bytes 1572864 | tf_op jit(solution)/shard_map/sbhij,sbhjk->sbhik/dot_general | solution.py:116
  16.1 1.2 %fusion.14 = f32[2,2,8,64,64]{4,3,2,1,0:T(8,128)S(1)} fusion(f32[2,2,8,64,64]{4,3,2,1,0:T(8,128)S(1)} %fusion.10, f32[1,2,8,64,64]{4,3,2,1,0:T(8,128)S(1)} %get-tuple-element.30, f32[1,2,8,64,64]{4,3,2,1,0:T(8,128)S(1)} %get-tuple-element.29), kind=kOutput, calls=%fused_computation.29 | convolution fusion | flops 100794368 | bytes 1572864 | tf_op jit(solution)/shard_map/sbhij,sbhjk->sbhik/dot_general | solution.py:116
  17.4 1.2 %fusion.18 = f32[2,2,8,64,64]{4,3,2,1,0:T(8,128)S(1)} fusion(f32[2,2,8,64,64]{4,3,2,1,0:T(8,128)S(1)} %fusion.14, f32[1,2,8,64,64]{4,3,2,1,0:T(8,128)S(1)} %get-tuple-element.28, f32[1,2,8,64,64]{4,3,2,1,0:T(8,128)S(1)} %get-tuple-element.27), kind=kOutput, calls=%fused_computation.33 | convolution fusion | flops 100794368 | bytes 1572864 | tf_op jit(solution)/shard_map/sbhij,sbhjk->sbhik/dot_general | solution.py:116
  22.2 2.3 %fusion.69 = f32[2,8,128,256]{3,2,1,0:T(8,128)S(1)} fusion(f32[2,8,64,256]{3,2,1,0:T(8,128)S(1)} %fusion.22, f32[2,64,8,128]{3,1,0,2:T(8,128)S(1)} %bitcast.196, f32[2,8,64]{2,1,0:T(8,128)S(1)} %get-tuple-element.41), kind=kOutput, calls=%fused_computation.103 | convolution fusion | flops 402784256 | bytes 3674112 | tf_op jit(solution)/shard_map/bhjd,bhje->bhde/dot_general | solution.py:148
  26.7 2.5 %collective-permute-start.1 = (bf16[8,128,128]{2,1,0:T(8,128)(2,1)}, bf16[8,128,128]{2,1,0:T(8,128)(2,1)}, u32[]{:S(2)}, u32[]{:S(2)}) collective-permute-start(bf16[8,128,128]{2,1,0:T(8,128)(2,1)} %get-tuple-element.25), channel_id=1, source_target_pairs={{0,2},{2,4},{4,6},{6,8},{8,10},{10,12},{12,14},{14,16},{16,18},{18... | collective-permute-start | bytes 786440 | tf_op jit(solution)/shard_map/ppermute | solution.py:50
  30.5 1.9 %collective-permute-start.3 = (bf16[8,128,128]{2,1,0:T(8,128)(2,1)}, bf16[8,128,128]{2,1,0:T(8,128)(2,1)}, u32[]{:S(2)}, u32[]{:S(2)}) collective-permute-start(bf16[8,128,128]{2,1,0:T(8,128)(2,1)} %get-tuple-element.26), channel_id=1, source_target_pairs={{0,2},{2,4},{4,6},{6,8},{8,10},{10,12},{12,14},{14,16},{16,18},{18... | collective-permute-start | bytes 786440 | tf_op jit(solution)/shard_map/ppermute | solution.py:33
  33.2 5.7 %collective-permute-done.1 = bf16[8,128,128]{2,1,0:T(8,128)(2,1)} collective-permute-done((bf16[8,128,128]{2,1,0:T(8,128)(2,1)}, bf16[8,128,128]{2,1,0:T(8,128)(2,1)}, u32[]{:S(2)}, u32[]{:S(2)}) %collective-permute-start.1) | collective-permute-done | bytes 262176 | tf_op jit(solution)/shard_map/ppermute | solution.py:50
  38.9 1.5 %multiply_convert_fusion.1 = bf16[128,512]{1,0:T(8,128)(2,1)} fusion(f32[131,512]{1,0:T(8,128)S(1)} %pad_maximum_fusion.9, f32[512]{0:T(512)} %bitcast.218, f32[512]{0:T(512)} %bitcast.219, f32[512]{0:T(512)} %bitcast.217, f32[512]{0:T(512)} %bitcast.216), kind=kLoop, calls=%fused_computation.156 | loop fusion | flops 786432 | bytes 1187840 | tf_op jit(solution)/shard_map/convert_element_type | solution.py:87
  44.8 1.8 %subtract_convert_fusion.1 = (bf16[8,128,128]{2,1,0:T(8,128)(2,1)S(1)}, f32[8,128,128]{2,1,0:T(8,128)S(1)}) fusion(f32[128,128]{1,0:T(8,128)S(1)} %fusion.108, f32[8,128,256]{2,1,0:T(8,128)S(1)} %fusion.54, bf16[8,128,128]{2,1,0:T(8,128)(2,1)} %collective-permute-done.3, f32[128,128]{1,0:T(8,128)S(1)} %fusion.107, pred[]{:T(512)S(6)} %ge.39), kind=kOutput, calls=%fused_computation.111 | convolution fusion | flops 201981952 | bytes 2228225 | tf_op jit(solution)/shard_map/hde,hef->hdf/dot_general | solution.py:165
  46.6 1.3 %collective-permute-start.5 = (bf16[8,128,128]{2,1,0:T(8,128)(2,1)S(1)}, bf16[8,128,128]{2,1,0:T(8,128)(2,1)S(1)}, u32[]{:S(2)}, u32[]{:S(2)}) collective-permute-start(bf16[8,128,128]{2,1,0:T(8,128)(2,1)S(1)} %get-tuple-element.54), channel_id=1, source_target_pairs={{0,4},{2,6},{4,8},{6,10},{8,12},{10,14},{12,16},{14,18},{16,20},{1... | collective-permute-start | bytes 786440 | tf_op jit(solution)/shard_map/ppermute | solution.py:33
  47.9 1.4 %fusion.127 = (bf16[8,128,128]{2,1,0:T(8,128)(2,1)S(1)}, f32[8,128,128]{2,1,0:T(8,128)S(1)}) fusion(f32[8,128,256]{2,1,0:T(8,128)S(1)} %copy-done.6, f32[8,128,256]{2,1,0:T(8,128)S(1)} %fusion.54, bf16[8,128,128]{2,1,0:T(8,128)(2,1)} %collective-permute-done.1), kind=kOutput, calls=%fused_computation.219 | convolution fusion | flops 201719808 | bytes 2621440 | tf_op jit(solution)/shard_map/hde,hef->hdf/dot_general | solution.py:165
  49.3 1.4 %collective-permute-start.2 = (bf16[8,128,128]{2,1,0:T(8,128)(2,1)S(1)}, bf16[8,128,128]{2,1,0:T(8,128)(2,1)S(1)}, u32[]{:S(2)}, u32[]{:S(2)}) collective-permute-start(bf16[8,128,128]{2,1,0:T(8,128)(2,1)S(1)} %get-tuple-element.56), channel_id=1, source_target_pairs={{0,4},{2,6},{4,8},{6,10},{8,12},{10,14},{12,16},{14,18},{16,20},{1... | collective-permute-start | bytes 786440 | tf_op jit(solution)/shard_map/ppermute | solution.py:50
  52.5 3.9 %collective-permute-done.5 = bf16[8,128,128]{2,1,0:T(8,128)(2,1)S(1)} collective-permute-done((bf16[8,128,128]{2,1,0:T(8,128)(2,1)S(1)}, bf16[8,128,128]{2,1,0:T(8,128)(2,1)S(1)}, u32[]{:S(2)}, u32[]{:S(2)}) %collective-permute-start.5) | collective-permute-done | bytes 262176 | tf_op jit(solution)/shard_map/ppermute | solution.py:33
  57.5 1.7 %collective-permute-done.2 = bf16[8,128,128]{2,1,0:T(8,128)(2,1)S(1)} collective-permute-done((bf16[8,128,128]{2,1,0:T(8,128)(2,1)S(1)}, bf16[8,128,128]{2,1,0:T(8,128)(2,1)S(1)}, u32[]{:S(2)}, u32[]{:S(2)}) %collective-permute-start.2) | collective-permute-done | bytes 262176 | tf_op jit(solution)/shard_map/ppermute | solution.py:50
  59.9 1.3 %collective-permute-start.4 = (bf16[8,128,128]{2,1,0:T(8,128)(2,1)S(1)}, bf16[8,128,128]{2,1,0:T(8,128)(2,1)S(1)}, u32[]{:S(2)}, u32[]{:S(2)}) collective-permute-start(bf16[8,128,128]{2,1,0:T(8,128)(2,1)S(1)} %fusion.102), channel_id=1, source_target_pairs={{0,8},{2,10},{4,12},{6,14},{8,16},{10,18},{12,20},{14,22},{16,24},... | collective-permute-start | bytes 786440 | tf_op jit(solution)/shard_map/ppermute | solution.py:50
  61.3 1.3 %collective-permute-start.6 = (bf16[8,128,128]{2,1,0:T(8,128)(2,1)S(1)}, bf16[8,128,128]{2,1,0:T(8,128)(2,1)S(1)}, u32[]{:S(2)}, u32[]{:S(2)}) collective-permute-start(bf16[8,128,128]{2,1,0:T(8,128)(2,1)S(1)} %get-tuple-element.24), channel_id=1, source_target_pairs={{0,8},{2,10},{4,12},{6,14},{8,16},{10,18},{12,20},{14,22},{16,24},... | collective-permute-start | bytes 786440 | tf_op jit(solution)/shard_map/ppermute | solution.py:33
  62.6 7.8 %collective-permute-done.4 = bf16[8,128,128]{2,1,0:T(8,128)(2,1)S(1)} collective-permute-done((bf16[8,128,128]{2,1,0:T(8,128)(2,1)S(1)}, bf16[8,128,128]{2,1,0:T(8,128)(2,1)S(1)}, u32[]{:S(2)}, u32[]{:S(2)}) %collective-permute-start.4) | collective-permute-done | bytes 262176 | tf_op jit(solution)/shard_map/ppermute | solution.py:50
  71.1 1.5 %collective-permute-start.7 = (bf16[8,128,128]{2,1,0:T(8,128)(2,1)S(1)}, bf16[8,128,128]{2,1,0:T(8,128)(2,1)S(1)}, u32[]{:S(2)}, u32[]{:S(2)}) collective-permute-start(bf16[8,128,128]{2,1,0:T(8,128)(2,1)S(1)} %fusion.42), channel_id=1, source_target_pairs={{0,16},{2,18},{4,20},{6,22},{8,24},{10,26},{12,28},{14,30},{1,17},... | collective-permute-start | bytes 786440 | tf_op jit(solution)/shard_map/ppermute | solution.py:50
  72.7 1.6 %collective-permute-done.6 = bf16[8,128,128]{2,1,0:T(8,128)(2,1)S(1)} collective-permute-done((bf16[8,128,128]{2,1,0:T(8,128)(2,1)S(1)}, bf16[8,128,128]{2,1,0:T(8,128)(2,1)S(1)}, u32[]{:S(2)}, u32[]{:S(2)}) %collective-permute-start.6) | collective-permute-done | bytes 262176 | tf_op jit(solution)/shard_map/ppermute | solution.py:33
  75.0 10.5 %collective-permute-done.7 = bf16[8,128,128]{2,1,0:T(8,128)(2,1)S(1)} collective-permute-done((bf16[8,128,128]{2,1,0:T(8,128)(2,1)S(1)}, bf16[8,128,128]{2,1,0:T(8,128)(2,1)S(1)}, u32[]{:S(2)}, u32[]{:S(2)}) %collective-permute-start.7) | collective-permute-done | bytes 262176 | tf_op jit(solution)/shard_map/ppermute | solution.py:50
  86.0 1.9 %multiply_reduce_fusion = (f32[2,64,8]{1,2,0:T(8,128)S(1)}, f32[2,64,8,128]{3,1,2,0:T(8,128)S(1)}) fusion(f32[1,8,64,128]{3,2,1,0:T(8,128)S(1)} %get-tuple-element.33, f32[1,8,64,128]{3,2,1,0:T(8,128)S(1)} %slice-done.1, f32[8,128,128]{2,1,0:T(8,128)S(1)} %fusion.129, f32[2,8,128,128]{3,2,1,0:T(8,128)S(1)} %convolution_bitcast_fusion, ...), kind=kOutput, calls=%fused_computation.105 | convolution fusion | flops 202505216 | bytes 3411968 | tf_op jit(solution)/shard_map/bhid,hde->bhie/dot_general | solution.py:252
  (144 shorter events, 27.9 us)
Async XLA Ops:
  0.0 8.9 %copy-start = (f32[128]{0:T(128)S(1)}, f32[128]{0:T(128)}, u32[]{:S(2)}) copy-start(f32[128]{0:T(128)} %param.31) | copy-start | bytes 1540
  1.6 5.5 %copy-start.19 = (bf16[4,512]{1,0:T(4,128)(2,1)S(1)}, bf16[4,512]{1,0:T(4,128)(2,1)}, u32[]{:S(2)}) copy-start(bf16[4,512]{1,0:T(4,128)(2,1)} %param.24) | copy-start | bytes 12292
  1.6 5.5 %copy-start.21 = (f32[128,8]{0,1:T(8,128)S(1)}, f32[128,8]{0,1:T(8,128)}, u32[]{:S(2)}) copy-start(f32[128,8]{0,1:T(8,128)} %param.27) | copy-start | bytes 12292
  1.7 5.6 %copy-start.24 = (f32[16]{0:T(128)S(1)}, f32[16]{0:T(128)}, u32[]{:S(2)}) copy-start(f32[16]{0:T(128)} %param.29) | copy-start | bytes 196
  1.7 5.7 %copy-start.25 = (f32[16]{0:T(128)S(1)}, f32[16]{0:T(128)}, u32[]{:S(2)}) copy-start(f32[16]{0:T(128)} %param.28) | copy-start | bytes 196
  1.7 5.8 %copy-start.22 = (f32[128,8]{0,1:T(8,128)S(1)}, f32[128,8]{0,1:T(8,128)}, u32[]{:S(2)}) copy-start(f32[128,8]{0,1:T(8,128)} %param.26) | copy-start | bytes 12292
  1.7 5.9 %copy-start.18 = (bf16[4,1024]{1,0:T(4,128)(2,1)S(1)}, bf16[4,1024]{1,0:T(4,128)(2,1)}, u32[]{:S(2)}) copy-start(bf16[4,1024]{1,0:T(4,128)(2,1)} %param.25) | copy-start | bytes 24580
  1.7 6.6 %copy-start.20 = (bf16[4,512]{1,0:T(4,128)(2,1)S(1)}, bf16[4,512]{1,0:T(4,128)(2,1)}, u32[]{:S(2)}) copy-start(bf16[4,512]{1,0:T(4,128)(2,1)} %param.23) | copy-start | bytes 12292
  3.7 6.7 %collective-permute-start = (f32[3,2048]{1,0:T(4,128)S(1)}, f32[3,2048]{1,0:T(4,128)S(1)}, u32[]{:S(2)}, u32[]{:S(2)}) collective-permute-start(f32[3,2048]{1,0:T(4,128)S(1)} %pad_maximum_fusion.11), channel_id=1, source_target_pairs={{0,2},{2,4},{4,6},{6,8},{8,10},{10,12},{12,14},{14,16},{16,18},{18... | collective-permute-start | bytes 73736 | tf_op jit(solution)/shard_map/ppermute | solution.py:16
  7.1 5.6 %copy-start.16 = (pred[64,64]{1,0:T(8,128)(4,1)}, pred[64,64]{1,0:T(8,128)(4,1)S(1)}, u32[]{:S(2)}) copy-start(pred[64,64]{1,0:T(8,128)(4,1)S(1)} %get-tuple-element.61) | copy-start | bytes 12292
  11.8 9.4 %copy-start.3 = (f32[128,4,2,128]{3,0,2,1:T(8,128)}, f32[128,4,2,128]{3,0,2,1:T(8,128)S(1)}, u32[]{:S(2)}) copy-start(f32[128,4,2,128]{3,0,2,1:T(8,128)S(1)} %broadcast_in_dim.31) | copy-start | bytes 1572868
  26.7 12.1 %collective-permute-start.1 = (bf16[8,128,128]{2,1,0:T(8,128)(2,1)}, bf16[8,128,128]{2,1,0:T(8,128)(2,1)}, u32[]{:S(2)}, u32[]{:S(2)}) collective-permute-start(bf16[8,128,128]{2,1,0:T(8,128)(2,1)} %get-tuple-element.25), channel_id=1, source_target_pairs={{0,2},{2,4},{4,6},{6,8},{8,10},{10,12},{12,14},{14,16},{16,18},{18... | collective-permute-start | bytes 786440 | tf_op jit(solution)/shard_map/ppermute | solution.py:50
  30.5 14.2 %collective-permute-start.3 = (bf16[8,128,128]{2,1,0:T(8,128)(2,1)}, bf16[8,128,128]{2,1,0:T(8,128)(2,1)}, u32[]{:S(2)}, u32[]{:S(2)}) collective-permute-start(bf16[8,128,128]{2,1,0:T(8,128)(2,1)} %get-tuple-element.26), channel_id=1, source_target_pairs={{0,2},{2,4},{4,6},{6,8},{8,10},{10,12},{12,14},{14,16},{16,18},{18... | collective-permute-start | bytes 786440 | tf_op jit(solution)/shard_map/ppermute | solution.py:33
  44.1 28.6 %copy-start.8 = (f32[2,8,64,128]{3,2,1,0:T(8,128)}, f32[2,8,64,128]{3,2,1,0:T(8,128)S(1)}, u32[]{:S(2)}) copy-start(f32[2,8,64,128]{3,2,1,0:T(8,128)S(1)} %convolution_subtract_fusion) | copy-start | bytes 1572868
  44.1 3.8 %copy-start.6 = (f32[8,128,256]{2,1,0:T(8,128)S(1)}, f32[8,128,256]{2,1,0:T(8,128)}, u32[]{:S(2)}) copy-start(f32[8,128,256]{2,1,0:T(8,128)} %copy-done.5) | copy-start | bytes 3145732
  44.7 28.0 %copy-start.7 = (f32[2,8,64,128]{3,2,1,0:T(8,128)}, f32[2,8,64,128]{3,2,1,0:T(8,128)S(1)}, u32[]{:S(2)}) copy-start(f32[2,8,64,128]{3,2,1,0:T(8,128)S(1)} %fusion.52) | copy-start | bytes 1572868
  46.6 9.8 %collective-permute-start.5 = (bf16[8,128,128]{2,1,0:T(8,128)(2,1)S(1)}, bf16[8,128,128]{2,1,0:T(8,128)(2,1)S(1)}, u32[]{:S(2)}, u32[]{:S(2)}) collective-permute-start(bf16[8,128,128]{2,1,0:T(8,128)(2,1)S(1)} %get-tuple-element.54), channel_id=1, source_target_pairs={{0,4},{2,6},{4,8},{6,10},{8,12},{10,14},{12,16},{14,18},{16,20},{1... | collective-permute-start | bytes 786440 | tf_op jit(solution)/shard_map/ppermute | solution.py:33
  49.3 7.1 %copy-start.9 = (f32[128,128]{1,0:T(8,128)S(1)}, f32[128,128]{1,0:T(8,128)}, u32[]{:S(2)}) copy-start(f32[128,128]{1,0:T(8,128)} %fusion.106) | copy-start | bytes 196612
  49.3 9.9 %collective-permute-start.2 = (bf16[8,128,128]{2,1,0:T(8,128)(2,1)S(1)}, bf16[8,128,128]{2,1,0:T(8,128)(2,1)S(1)}, u32[]{:S(2)}, u32[]{:S(2)}) collective-permute-start(bf16[8,128,128]{2,1,0:T(8,128)(2,1)S(1)} %get-tuple-element.56), channel_id=1, source_target_pairs={{0,4},{2,6},{4,8},{6,10},{8,12},{10,14},{12,16},{14,18},{16,20},{1... | collective-permute-start | bytes 786440 | tf_op jit(solution)/shard_map/ppermute | solution.py:50
  59.9 10.5 %collective-permute-start.4 = (bf16[8,128,128]{2,1,0:T(8,128)(2,1)S(1)}, bf16[8,128,128]{2,1,0:T(8,128)(2,1)S(1)}, u32[]{:S(2)}, u32[]{:S(2)}) collective-permute-start(bf16[8,128,128]{2,1,0:T(8,128)(2,1)S(1)} %fusion.102), channel_id=1, source_target_pairs={{0,8},{2,10},{4,12},{6,14},{8,16},{10,18},{12,20},{14,22},{16,24},... | collective-permute-start | bytes 786440 | tf_op jit(solution)/shard_map/ppermute | solution.py:50
  61.3 13.1 %collective-permute-start.6 = (bf16[8,128,128]{2,1,0:T(8,128)(2,1)S(1)}, bf16[8,128,128]{2,1,0:T(8,128)(2,1)S(1)}, u32[]{:S(2)}, u32[]{:S(2)}) collective-permute-start(bf16[8,128,128]{2,1,0:T(8,128)(2,1)S(1)} %get-tuple-element.24), channel_id=1, source_target_pairs={{0,8},{2,10},{4,12},{6,14},{8,16},{10,18},{12,20},{14,22},{16,24},... | collective-permute-start | bytes 786440 | tf_op jit(solution)/shard_map/ppermute | solution.py:33
  71.1 14.5 %collective-permute-start.7 = (bf16[8,128,128]{2,1,0:T(8,128)(2,1)S(1)}, bf16[8,128,128]{2,1,0:T(8,128)(2,1)S(1)}, u32[]{:S(2)}, u32[]{:S(2)}) collective-permute-start(bf16[8,128,128]{2,1,0:T(8,128)(2,1)S(1)} %fusion.42), channel_id=1, source_target_pairs={{0,16},{2,18},{4,20},{6,22},{8,24},{10,26},{12,28},{14,30},{1,17},... | collective-permute-start | bytes 786440 | tf_op jit(solution)/shard_map/ppermute | solution.py:50
  72.7 13.2 %slice-start.1 = ((f32[2,8,64,128]{3,2,1,0:T(8,128)}), f32[1,8,64,128]{3,2,1,0:T(8,128)S(1)}, s32[]{:S(2)}) async-start(f32[2,8,64,128]{3,2,1,0:T(8,128)} %copy-done.8), calls=%async_computation.1 | async-start | bytes 524288 | tf_op jit(solution)/shard_map/slice | solution.py:247
  72.7 13.2 %slice-start = ((f32[2,8,64,128]{3,2,1,0:T(8,128)}), f32[1,8,64,128]{3,2,1,0:T(8,128)S(1)}, s32[]{:S(2)}) async-start(f32[2,8,64,128]{3,2,1,0:T(8,128)} %copy-done.7), calls=%async_computation | async-start | bytes 524288 | tf_op jit(solution)/shard_map/slice | solution.py:247
  (12 other events, 26.9 us)

commit v13 on v12

--- a/solution.py
+++ b/solution.py
@@ -88,9 +88,12 @@
 
 
 def unit_heads(conv_rows, head_width):
-    row_count = conv_rows.shape[0]
-    shaped = conv_rows.astype(jnp.float32).reshape(row_count, -1, head_width)
-    return shaped * lax.rsqrt(jnp.sum(shaped * shaped, axis=-1, keepdims=True) + EPSILON)
+    rows = conv_rows.astype(jnp.float32)
+    head_count = rows.shape[1] // head_width
+    member = jnp.arange(rows.shape[1])[:, None] // head_width == jnp.arange(head_count)[None, :]
+    sums = jnp.dot(rows * rows, member.astype(jnp.float32), precision=HIGHEST)
+    scale = jnp.repeat(lax.rsqrt(sums + EPSILON), head_width, axis=1)
+    return (rows * scale).reshape(rows.shape[0], head_count, head_width)
 
 
 def to_blocks(array, block):

time: 90.1 us -> 90.4 us (level)
  matrix products: 22.7 us -> 25.4 us
  other arithmetic: 11.8 us -> 10.4 us
    dot_general x0 -> x2, matrix products: none -> 1.55 us  [unit_heads(): sums = jnp.dot(rows * rows, member.astype(jnp.float32), precision=HIGHEST)]
    dot_general x1, matrix products: 0.95 us -> 2.04 us  [query_terms(): jnp.einsum('bhid,bhjd->bhij', queries, key_units, precision=HIGHEST)]
    reshape x2 -> x0, local copies, waits for them, and re-layouts: 1.07 us -> none  [unit_heads(): shaped = conv_rows.astype(jnp.float32).reshape(row_count, -1, head_width)]
where the time goes in v13:
time: 90.4 us; the launch traced here: 89.8 us
  waiting for transfers between devices  32.4 us (36%)
  matrix products  25.4 us (28%)
  starting transfers between devices  14.6 us (16%)
  other arithmetic  10.4 us (12%)
  local copies, waits for them, and re-layouts  6.11 us (7%)
  between operations  0.91 us (1%)
    ppermute x4, waiting for transfers between devices, scan_states(): earlier = lax.ppermute(carried.astype(jnp.bfloat16), axis, pairs)  25.6 us
    ppermute x4, starting transfers between devices, scan_states(): earlier = lax.ppermute(carried.astype(jnp.bfloat16), axis, pairs)  6.72 us
    ppermute x3, waiting for transfers between devices, scan_states(): earlier = lax.ppermute((inclusive - eye).astype(jnp.bfloat16), axis, pairs)  5.58 us
    dot_general x4, matrix products, unit_lower_inverse(): jnp.einsum('sbhij,sbhjk->sbhik', jnp.stack([inverse, power]), jnp.stack([...  4.73 us
    ppermute x3, starting transfers between devices, scan_states(): earlier = lax.ppermute((inclusive - eye).astype(jnp.bfloat16), axis, pairs)  4.49 us
    dot_general x4, matrix products, product(): return jnp.einsum('hde,hef->hdf', left, right, precision=HIGHEST)  4.25 us
    ppermute x1, starting transfers between devices, from_behind(): lax.ppermute(value, axis, [(source, source + steps) for source in range(f...  3.4 us
    unnamed x56, local copies, waits for them, and re-layouts  2.91 us
  transfers between devices with their start and end apart: 8, of which 7 were waited for; matrix products, arithmetic and copies ran while one was open for 17% of the time, Pallas kernels for 0%

profile of v13, /device:TPU:28, one launch (start us, length us, event | category | flops | bytes accessed | tf_op | source)
XLA Modules:
  0.0 89.8 jit_solution(8753889334464627540)
XLA Ops:
  3.7 3.4 %collective-permute-start = (f32[3,2048]{1,0:T(4,128)S(1)}, f32[3,2048]{1,0:T(4,128)S(1)}, u32[]{:S(2)}, u32[]{:S(2)}) collective-permute-start(f32[3,2048]{1,0:T(4,128)S(1)} %pad_maximum_fusion.11), channel_id=1, source_target_pairs={{0,2},{2,4},{4,6},{6,8},{8,10},{10,12},{12,14},{14,16},{16,18},{18... | collective-permute-start | bytes 73736 | tf_op jit(solution)/shard_map/ppermute | solution.py:16
  9.2 1.2 %collective-permute-done = f32[3,2048]{1,0:T(4,128)S(1)} collective-permute-done((f32[3,2048]{1,0:T(4,128)S(1)}, f32[3,2048]{1,0:T(4,128)S(1)}, u32[]{:S(2)}, u32[]{:S(2)}) %collective-permute-start) | collective-permute-done | bytes 24608 | tf_op jit(solution)/shard_map/ppermute | solution.py:16
  13.8 1.2 %fusion.6 = f32[2,2,8,64,64]{4,3,2,1,0:T(8,128)S(1)} fusion(f32[1,2,8,64,64]{4,3,2,1,0:T(8,128)S(1)} %bitcast.211, f32[1,2,8,64,64]{4,3,2,1,0:T(8,128)S(1)} %get-tuple-element.38, f32[1,2,8,64,64]{4,3,2,1,0:T(8,128)S(1)} %get-tuple-element.37), kind=kOutput, calls=%fused_computation.21 | convolution fusion | flops 100925440 | bytes 1310720 | tf_op jit(solution)/shard_map/sbhij,sbhjk->sbhik/dot_general | solution.py:119
  15.2 1.2 %fusion.12 = f32[2,2,8,64,64]{4,3,2,1,0:T(8,128)S(1)} fusion(f32[2,2,8,64,64]{4,3,2,1,0:T(8,128)S(1)} %fusion.6, f32[1,2,8,64,64]{4,3,2,1,0:T(8,128)S(1)} %get-tuple-element.32, f32[1,2,8,64,64]{4,3,2,1,0:T(8,128)S(1)} %get-tuple-element.31), kind=kOutput, calls=%fused_computation.29 | convolution fusion | flops 100794368 | bytes 1572864 | tf_op jit(solution)/shard_map/sbhij,sbhjk->sbhik/dot_general | solution.py:119
  16.5 1.2 %fusion.16 = f32[2,2,8,64,64]{4,3,2,1,0:T(8,128)S(1)} fusion(f32[2,2,8,64,64]{4,3,2,1,0:T(8,128)S(1)} %fusion.12, f32[1,2,8,64,64]{4,3,2,1,0:T(8,128)S(1)} %get-tuple-element.30, f32[1,2,8,64,64]{4,3,2,1,0:T(8,128)S(1)} %get-tuple-element.29), kind=kOutput, calls=%fused_computation.33 | convolution fusion | flops 100794368 | bytes 1572864 | tf_op jit(solution)/shard_map/sbhij,sbhjk->sbhik/dot_general | solution.py:119
  17.8 1.2 %fusion.20 = f32[2,2,8,64,64]{4,3,2,1,0:T(8,128)S(1)} fusion(f32[2,2,8,64,64]{4,3,2,1,0:T(8,128)S(1)} %fusion.16, f32[1,2,8,64,64]{4,3,2,1,0:T(8,128)S(1)} %get-tuple-element.28, f32[1,2,8,64,64]{4,3,2,1,0:T(8,128)S(1)} %get-tuple-element.27), kind=kOutput, calls=%fused_computation.37 | convolution fusion | flops 100794368 | bytes 1572864 | tf_op jit(solution)/shard_map/sbhij,sbhjk->sbhik/dot_general | solution.py:119
  22.5 2.3 %fusion.71 = f32[2,8,128,256]{3,2,1,0:T(8,128)S(1)} fusion(f32[2,8,64,256]{3,2,1,0:T(8,128)S(1)} %fusion.24, f32[2,64,8,128]{3,1,0,2:T(8,128)S(1)} %bitcast.214, f32[2,8,64]{2,1,0:T(8,128)S(1)} %get-tuple-element.41), kind=kOutput, calls=%fused_computation.107 | convolution fusion | flops 402784256 | bytes 3674112 | tf_op jit(solution)/shard_map/bhjd,bhje->bhde/dot_general | solution.py:151
  27.1 2.5 %collective-permute-start.1 = (bf16[8,128,128]{2,1,0:T(8,128)(2,1)}, bf16[8,128,128]{2,1,0:T(8,128)(2,1)}, u32[]{:S(2)}, u32[]{:S(2)}) collective-permute-start(bf16[8,128,128]{2,1,0:T(8,128)(2,1)} %get-tuple-element.25), channel_id=1, source_target_pairs={{0,2},{2,4},{4,6},{6,8},{8,10},{10,12},{12,14},{14,16},{16,18},{18... | collective-permute-start | bytes 786440 | tf_op jit(solution)/shard_map/ppermute | solution.py:50
  30.9 1.9 %collective-permute-start.3 = (bf16[8,128,128]{2,1,0:T(8,128)(2,1)}, bf16[8,128,128]{2,1,0:T(8,128)(2,1)}, u32[]{:S(2)}, u32[]{:S(2)}) collective-permute-start(bf16[8,128,128]{2,1,0:T(8,128)(2,1)} %get-tuple-element.26), channel_id=1, source_target_pairs={{0,2},{2,4},{4,6},{6,8},{8,10},{10,12},{12,14},{14,16},{16,18},{18... | collective-permute-start | bytes 786440 | tf_op jit(solution)/shard_map/ppermute | solution.py:33
  33.5 5.7 %collective-permute-done.1 = bf16[8,128,128]{2,1,0:T(8,128)(2,1)} collective-permute-done((bf16[8,128,128]{2,1,0:T(8,128)(2,1)}, bf16[8,128,128]{2,1,0:T(8,128)(2,1)}, u32[]{:S(2)}, u32[]{:S(2)}) %collective-permute-start.1) | collective-permute-done | bytes 262176 | tf_op jit(solution)/shard_map/ppermute | solution.py:50
  41.6 2.0 %convolution_multiply_fusion = f32[2,8,64,64]{3,2,1,0:T(8,128)S(1)} fusion(f32[2,64,8,128]{3,1,0,2:T(8,128)S(1)} %bitcast.218, f32[2,64,8,128]{3,1,0,2:T(8,128)} %bitcast.215, f32[2,8,64]{2,1,0:T(8,128)S(1)} %reduce_window_sum.11, pred[64,64]{1,0:T(8,128)(4,1)S(1)} %copy-done.16), kind=kOutput, calls=%fused_computation.9 | convolution fusion | flops 100925440 | bytes 1318912 | tf_op jit(solution)/shard_map/bhid,bhjd->bhij/dot_general | solution.py:159
  45.1 1.8 %subtract_convert_fusion.1 = (bf16[8,128,128]{2,1,0:T(8,128)(2,1)S(1)}, f32[8,128,128]{2,1,0:T(8,128)S(1)}) fusion(f32[128,128]{1,0:T(8,128)S(1)} %fusion.115, f32[8,128,256]{2,1,0:T(8,128)S(1)} %fusion.56, bf16[8,128,128]{2,1,0:T(8,128)(2,1)} %collective-permute-done.3, f32[128,128]{1,0:T(8,128)S(1)} %fusion.114, pred[]{:T(512)S(6)} %ge.39), kind=kOutput, calls=%fused_computation.115 | convolution fusion | flops 201981952 | bytes 2228225 | tf_op jit(solution)/shard_map/hde,hef->hdf/dot_general | solution.py:168
  47.0 1.3 %collective-permute-start.5 = (bf16[8,128,128]{2,1,0:T(8,128)(2,1)S(1)}, bf16[8,128,128]{2,1,0:T(8,128)(2,1)S(1)}, u32[]{:S(2)}, u32[]{:S(2)}) collective-permute-start(bf16[8,128,128]{2,1,0:T(8,128)(2,1)S(1)} %get-tuple-element.54), channel_id=1, source_target_pairs={{0,4},{2,6},{4,8},{6,10},{8,12},{10,14},{12,16},{14,18},{16,20},{1... | collective-permute-start | bytes 786440 | tf_op jit(solution)/shard_map/ppermute | solution.py:33
  48.3 1.4 %fusion.137 = (bf16[8,128,128]{2,1,0:T(8,128)(2,1)S(1)}, f32[8,128,128]{2,1,0:T(8,128)S(1)}) fusion(f32[8,128,256]{2,1,0:T(8,128)S(1)} %copy-done.5, f32[8,128,256]{2,1,0:T(8,128)S(1)} %fusion.56, bf16[8,128,128]{2,1,0:T(8,128)(2,1)} %collective-permute-done.1), kind=kOutput, calls=%fused_computation.236 | convolution fusion | flops 201719808 | bytes 2621440 | tf_op jit(solution)/shard_map/hde,hef->hdf/dot_general | solution.py:168
  49.7 1.4 %collective-permute-start.2 = (bf16[8,128,128]{2,1,0:T(8,128)(2,1)S(1)}, bf16[8,128,128]{2,1,0:T(8,128)(2,1)S(1)}, u32[]{:S(2)}, u32[]{:S(2)}) collective-permute-start(bf16[8,128,128]{2,1,0:T(8,128)(2,1)S(1)} %get-tuple-element.56), channel_id=1, source_target_pairs={{0,4},{2,6},{4,8},{6,10},{8,12},{10,14},{12,16},{14,18},{16,20},{1... | collective-permute-start | bytes 786440 | tf_op jit(solution)/shard_map/ppermute | solution.py:50
  52.8 3.9 %collective-permute-done.5 = bf16[8,128,128]{2,1,0:T(8,128)(2,1)S(1)} collective-permute-done((bf16[8,128,128]{2,1,0:T(8,128)(2,1)S(1)}, bf16[8,128,128]{2,1,0:T(8,128)(2,1)S(1)}, u32[]{:S(2)}, u32[]{:S(2)}) %collective-permute-start.5) | collective-permute-done | bytes 262176 | tf_op jit(solution)/shard_map/ppermute | solution.py:33
  57.9 1.7 %collective-permute-done.2 = bf16[8,128,128]{2,1,0:T(8,128)(2,1)S(1)} collective-permute-done((bf16[8,128,128]{2,1,0:T(8,128)(2,1)S(1)}, bf16[8,128,128]{2,1,0:T(8,128)(2,1)S(1)}, u32[]{:S(2)}, u32[]{:S(2)}) %collective-permute-start.2) | collective-permute-done | bytes 262176 | tf_op jit(solution)/shard_map/ppermute | solution.py:50
  60.3 1.3 %collective-permute-start.4 = (bf16[8,128,128]{2,1,0:T(8,128)(2,1)S(1)}, bf16[8,128,128]{2,1,0:T(8,128)(2,1)S(1)}, u32[]{:S(2)}, u32[]{:S(2)}) collective-permute-start(bf16[8,128,128]{2,1,0:T(8,128)(2,1)S(1)} %fusion.107), channel_id=1, source_target_pairs={{0,8},{2,10},{4,12},{6,14},{8,16},{10,18},{12,20},{14,22},{16,24},... | collective-permute-start | bytes 786440 | tf_op jit(solution)/shard_map/ppermute | solution.py:50
  61.6 1.3 %collective-permute-start.6 = (bf16[8,128,128]{2,1,0:T(8,128)(2,1)S(1)}, bf16[8,128,128]{2,1,0:T(8,128)(2,1)S(1)}, u32[]{:S(2)}, u32[]{:S(2)}) collective-permute-start(bf16[8,128,128]{2,1,0:T(8,128)(2,1)S(1)} %get-tuple-element.24), channel_id=1, source_target_pairs={{0,8},{2,10},{4,12},{6,14},{8,16},{10,18},{12,20},{14,22},{16,24},... | collective-permute-start | bytes 786440 | tf_op jit(solution)/shard_map/ppermute | solution.py:33
  62.9 7.8 %collective-permute-done.4 = bf16[8,128,128]{2,1,0:T(8,128)(2,1)S(1)} collective-permute-done((bf16[8,128,128]{2,1,0:T(8,128)(2,1)S(1)}, bf16[8,128,128]{2,1,0:T(8,128)(2,1)S(1)}, u32[]{:S(2)}, u32[]{:S(2)}) %collective-permute-start.4) | collective-permute-done | bytes 262176 | tf_op jit(solution)/shard_map/ppermute | solution.py:50
  71.4 1.5 %collective-permute-start.7 = (bf16[8,128,128]{2,1,0:T(8,128)(2,1)S(1)}, bf16[8,128,128]{2,1,0:T(8,128)(2,1)S(1)}, u32[]{:S(2)}, u32[]{:S(2)}) collective-permute-start(bf16[8,128,128]{2,1,0:T(8,128)(2,1)S(1)} %fusion.44), channel_id=1, source_target_pairs={{0,16},{2,18},{4,20},{6,22},{8,24},{10,26},{12,28},{14,30},{1,17},... | collective-permute-start | bytes 786440 | tf_op jit(solution)/shard_map/ppermute | solution.py:50
  73.1 1.6 %collective-permute-done.6 = bf16[8,128,128]{2,1,0:T(8,128)(2,1)S(1)} collective-permute-done((bf16[8,128,128]{2,1,0:T(8,128)(2,1)S(1)}, bf16[8,128,128]{2,1,0:T(8,128)(2,1)S(1)}, u32[]{:S(2)}, u32[]{:S(2)}) %collective-permute-start.6) | collective-permute-done | bytes 262176 | tf_op jit(solution)/shard_map/ppermute | solution.py:33
  75.4 10.5 %collective-permute-done.7 = bf16[8,128,128]{2,1,0:T(8,128)(2,1)S(1)} collective-permute-done((bf16[8,128,128]{2,1,0:T(8,128)(2,1)S(1)}, bf16[8,128,128]{2,1,0:T(8,128)(2,1)S(1)}, u32[]{:S(2)}, u32[]{:S(2)}) %collective-permute-start.7) | collective-permute-done | bytes 262176 | tf_op jit(solution)/shard_map/ppermute | solution.py:50
  86.3 1.8 %multiply_reduce_fusion = (f32[2,64,8]{1,2,0:T(8,128)S(1)}, f32[2,64,8,128]{3,1,2,0:T(8,128)S(1)}) fusion(f32[1,8,64,128]{3,2,1,0:T(8,128)S(1)} %get-tuple-element.33, f32[1,8,64,128]{3,2,1,0:T(8,128)S(1)} %slice-done.1, f32[8,128,128]{2,1,0:T(8,128)S(1)} %fusion.139, f32[2,8,128,128]{3,2,1,0:T(8,128)S(1)} %convolution_bitcast_fusion, ...), kind=kOutput, calls=%fused_computation.109 | convolution fusion | flops 202505216 | bytes 3411968 | tf_op jit(solution)/shard_map/bhid,hde->bhie/dot_general | solution.py:255
  (143 shorter events, 27.7 us)
Async XLA Ops:
  0.0 9.1 %copy-start = (f32[128]{0:T(128)S(1)}, f32[128]{0:T(128)}, u32[]{:S(2)}) copy-start(f32[128]{0:T(128)} %param.31) | copy-start | bytes 1540
  1.6 5.5 %copy-start.18 = (bf16[4,512]{1,0:T(4,128)(2,1)S(1)}, bf16[4,512]{1,0:T(4,128)(2,1)}, u32[]{:S(2)}) copy-start(bf16[4,512]{1,0:T(4,128)(2,1)} %param.24) | copy-start | bytes 12292
  1.6 5.5 %copy-start.20 = (f32[128,8]{0,1:T(8,128)S(1)}, f32[128,8]{0,1:T(8,128)}, u32[]{:S(2)}) copy-start(f32[128,8]{0,1:T(8,128)} %param.27) | copy-start | bytes 12292
  1.7 5.6 %copy-start.24 = (f32[16]{0:T(128)S(1)}, f32[16]{0:T(128)}, u32[]{:S(2)}) copy-start(f32[16]{0:T(128)} %param.29) | copy-start | bytes 196
  1.7 5.7 %copy-start.25 = (f32[16]{0:T(128)S(1)}, f32[16]{0:T(128)}, u32[]{:S(2)}) copy-start(f32[16]{0:T(128)} %param.28) | copy-start | bytes 196
  1.7 5.8 %copy-start.21 = (f32[128,8]{0,1:T(8,128)S(1)}, f32[128,8]{0,1:T(8,128)}, u32[]{:S(2)}) copy-start(f32[128,8]{0,1:T(8,128)} %param.26) | copy-start | bytes 12292
  1.7 5.9 %copy-start.17 = (bf16[4,1024]{1,0:T(4,128)(2,1)S(1)}, bf16[4,1024]{1,0:T(4,128)(2,1)}, u32[]{:S(2)}) copy-start(bf16[4,1024]{1,0:T(4,128)(2,1)} %param.25) | copy-start | bytes 24580
  1.7 6.8 %copy-start.19 = (bf16[4,512]{1,0:T(4,128)(2,1)S(1)}, bf16[4,512]{1,0:T(4,128)(2,1)}, u32[]{:S(2)}) copy-start(bf16[4,512]{1,0:T(4,128)(2,1)} %param.23) | copy-start | bytes 12292
  3.7 6.7 %collective-permute-start = (f32[3,2048]{1,0:T(4,128)S(1)}, f32[3,2048]{1,0:T(4,128)S(1)}, u32[]{:S(2)}, u32[]{:S(2)}) collective-permute-start(f32[3,2048]{1,0:T(4,128)S(1)} %pad_maximum_fusion.11), channel_id=1, source_target_pairs={{0,2},{2,4},{4,6},{6,8},{8,10},{10,12},{12,14},{14,16},{16,18},{18... | collective-permute-start | bytes 73736 | tf_op jit(solution)/shard_map/ppermute | solution.py:16
  7.1 5.9 %copy-start.15 = (pred[64,64]{1,0:T(8,128)(4,1)}, pred[64,64]{1,0:T(8,128)(4,1)S(1)}, u32[]{:S(2)}) copy-start(pred[64,64]{1,0:T(8,128)(4,1)S(1)} %get-tuple-element.61) | copy-start | bytes 12292
  12.0 9.5 %copy-start.3 = (f32[128,4,2,128]{3,0,2,1:T(8,128)}, f32[128,4,2,128]{3,0,2,1:T(8,128)S(1)}, u32[]{:S(2)}) copy-start(f32[128,4,2,128]{3,0,2,1:T(8,128)S(1)} %broadcast_in_dim.36) | copy-start | bytes 1572868
  27.1 12.1 %collective-permute-start.1 = (bf16[8,128,128]{2,1,0:T(8,128)(2,1)}, bf16[8,128,128]{2,1,0:T(8,128)(2,1)}, u32[]{:S(2)}, u32[]{:S(2)}) collective-permute-start(bf16[8,128,128]{2,1,0:T(8,128)(2,1)} %get-tuple-element.25), channel_id=1, source_target_pairs={{0,2},{2,4},{4,6},{6,8},{8,10},{10,12},{12,14},{14,16},{16,18},{18... | collective-permute-start | bytes 786440 | tf_op jit(solution)/shard_map/ppermute | solution.py:50
  30.9 14.2 %collective-permute-start.3 = (bf16[8,128,128]{2,1,0:T(8,128)(2,1)}, bf16[8,128,128]{2,1,0:T(8,128)(2,1)}, u32[]{:S(2)}, u32[]{:S(2)}) collective-permute-start(bf16[8,128,128]{2,1,0:T(8,128)(2,1)} %get-tuple-element.26), channel_id=1, source_target_pairs={{0,2},{2,4},{4,6},{6,8},{8,10},{10,12},{12,14},{14,16},{16,18},{18... | collective-permute-start | bytes 786440 | tf_op jit(solution)/shard_map/ppermute | solution.py:33
  33.5 8.1 %copy-start.16 = (pred[64,64]{1,0:T(8,128)(4,1)S(1)}, pred[64,64]{1,0:T(8,128)(4,1)}, u32[]{:S(2)}) copy-start(pred[64,64]{1,0:T(8,128)(4,1)} %copy-done.15) | copy-start | bytes 12292
  44.4 28.6 %copy-start.7 = (f32[2,8,64,128]{3,2,1,0:T(8,128)}, f32[2,8,64,128]{3,2,1,0:T(8,128)S(1)}, u32[]{:S(2)}) copy-start(f32[2,8,64,128]{3,2,1,0:T(8,128)S(1)} %convolution_subtract_fusion) | copy-start | bytes 1572868
  45.1 28.0 %copy-start.6 = (f32[2,8,64,128]{3,2,1,0:T(8,128)}, f32[2,8,64,128]{3,2,1,0:T(8,128)S(1)}, u32[]{:S(2)}) copy-start(f32[2,8,64,128]{3,2,1,0:T(8,128)S(1)} %fusion.54) | copy-start | bytes 1572868
  47.0 9.8 %collective-permute-start.5 = (bf16[8,128,128]{2,1,0:T(8,128)(2,1)S(1)}, bf16[8,128,128]{2,1,0:T(8,128)(2,1)S(1)}, u32[]{:S(2)}, u32[]{:S(2)}) collective-permute-start(bf16[8,128,128]{2,1,0:T(8,128)(2,1)S(1)} %get-tuple-element.54), channel_id=1, source_target_pairs={{0,4},{2,6},{4,8},{6,10},{8,12},{10,14},{12,16},{14,18},{16,20},{1... | collective-permute-start | bytes 786440 | tf_op jit(solution)/shard_map/ppermute | solution.py:33
  49.7 7.1 %copy-start.8 = (f32[128,128]{1,0:T(8,128)S(1)}, f32[128,128]{1,0:T(8,128)}, u32[]{:S(2)}) copy-start(f32[128,128]{1,0:T(8,128)} %fusion.113) | copy-start | bytes 196612
  49.7 9.9 %collective-permute-start.2 = (bf16[8,128,128]{2,1,0:T(8,128)(2,1)S(1)}, bf16[8,128,128]{2,1,0:T(8,128)(2,1)S(1)}, u32[]{:S(2)}, u32[]{:S(2)}) collective-permute-start(bf16[8,128,128]{2,1,0:T(8,128)(2,1)S(1)} %get-tuple-element.56), channel_id=1, source_target_pairs={{0,4},{2,6},{4,8},{6,10},{8,12},{10,14},{12,16},{14,18},{16,20},{1... | collective-permute-start | bytes 786440 | tf_op jit(solution)/shard_map/ppermute | solution.py:50
  60.3 10.5 %collective-permute-start.4 = (bf16[8,128,128]{2,1,0:T(8,128)(2,1)S(1)}, bf16[8,128,128]{2,1,0:T(8,128)(2,1)S(1)}, u32[]{:S(2)}, u32[]{:S(2)}) collective-permute-start(bf16[8,128,128]{2,1,0:T(8,128)(2,1)S(1)} %fusion.107), channel_id=1, source_target_pairs={{0,8},{2,10},{4,12},{6,14},{8,16},{10,18},{12,20},{14,22},{16,24},... | collective-permute-start | bytes 786440 | tf_op jit(solution)/shard_map/ppermute | solution.py:50
  61.6 13.1 %collective-permute-start.6 = (bf16[8,128,128]{2,1,0:T(8,128)(2,1)S(1)}, bf16[8,128,128]{2,1,0:T(8,128)(2,1)S(1)}, u32[]{:S(2)}, u32[]{:S(2)}) collective-permute-start(bf16[8,128,128]{2,1,0:T(8,128)(2,1)S(1)} %get-tuple-element.24), channel_id=1, source_target_pairs={{0,8},{2,10},{4,12},{6,14},{8,16},{10,18},{12,20},{14,22},{16,24},... | collective-permute-start | bytes 786440 | tf_op jit(solution)/shard_map/ppermute | solution.py:33
  71.4 14.5 %collective-permute-start.7 = (bf16[8,128,128]{2,1,0:T(8,128)(2,1)S(1)}, bf16[8,128,128]{2,1,0:T(8,128)(2,1)S(1)}, u32[]{:S(2)}, u32[]{:S(2)}) collective-permute-start(bf16[8,128,128]{2,1,0:T(8,128)(2,1)S(1)} %fusion.44), channel_id=1, source_target_pairs={{0,16},{2,18},{4,20},{6,22},{8,24},{10,26},{12,28},{14,30},{1,17},... | collective-permute-start | bytes 786440 | tf_op jit(solution)/shard_map/ppermute | solution.py:50
  73.1 13.3 %slice-start.1 = ((f32[2,8,64,128]{3,2,1,0:T(8,128)}), f32[1,8,64,128]{3,2,1,0:T(8,128)S(1)}, s32[]{:S(2)}) async-start(f32[2,8,64,128]{3,2,1,0:T(8,128)} %copy-done.7), calls=%async_computation.1 | async-start | bytes 524288 | tf_op jit(solution)/shard_map/slice | solution.py:250
  73.1 13.2 %slice-start = ((f32[2,8,64,128]{3,2,1,0:T(8,128)}), f32[1,8,64,128]{3,2,1,0:T(8,128)S(1)}, s32[]{:S(2)}) async-start(f32[2,8,64,128]{3,2,1,0:T(8,128)} %copy-done.6), calls=%async_computation | async-start | bytes 524288 | tf_op jit(solution)/shard_map/slice | solution.py:250
  (12 other events, 33.4 us)

commit v14 on v12

--- a/solution.py
+++ b/solution.py
@@ -34,12 +34,12 @@
         earlier = earlier.astype(jnp.float32) + reached * eye
         last_map = exclusive_maps[-1]
         if last_map is None or 4 * span >= devices:
-            exclusive_maps.append(earlier if last_map is None else product(last_map, earlier))
+            exclusive_maps.append(earlier if last_map is None else product_high(last_map, earlier))
             if 4 * span < devices:
-                inclusive = jnp.where(mine >= span, product(inclusive, earlier), inclusive)
+                inclusive = jnp.where(mine >= span, product_high(inclusive, earlier), inclusive)
         else:
             both = jnp.einsum(
-                "shde,hef->shdf", jnp.stack([last_map, inclusive]), earlier, precision=HIGHEST
+                "shde,hef->shdf", jnp.stack([last_map, inclusive]), earlier, precision=lax.Precision.HIGH
             )
             exclusive_maps.append(both[0])
             inclusive = jnp.where(mine >= span, both[1], inclusive)
@@ -55,18 +55,18 @@
         if last_map is None:
             state = earlier
             if step + 1 < len(spans):
-                carried = product(inclusive_maps[step], earlier) + carried
+                carried = product_high(inclusive_maps[step], earlier) + carried
         elif step + 1 < len(spans):
             both = jnp.einsum(
                 "shde,hef->shdf",
                 jnp.stack([last_map, inclusive_maps[step]]),
                 earlier,
-                precision=HIGHEST,
+                precision=lax.Precision.HIGH,
             )
             state = state + both[0]
             carried = both[1] + carried
         else:
-            state = state + product(last_map, earlier)
+            state = state + product_high(last_map, earlier)
     return (state, rider)
 
 
@@ -159,6 +159,10 @@
         "bhij,bhjd->bhid", mixing, weight_keys, precision=HIGHEST
     )
     return (zero_out, readout)
+
+
+def product_high(left, right):
+    return jnp.einsum("hde,hef->hdf", left, right, precision=lax.Precision.HIGH)
 
 
 def product(left, right):

time: 90.1 us -> 89.6 us (level)
  matrix products: 22.7 us -> 21.1 us
  waiting for transfers between devices: 32.5 us -> 33.7 us
  transfers between devices with their start and end apart: 8 -> 8, of which waited for: 7 -> 7; matrix products, arithmetic and copies ran while one was open for 17% -> 16% of each run, Pallas kernels for 0% -> 0%
where the time goes in v14:
time: 89.6 us; the launch traced here: 88.9 us
  waiting for transfers between devices  33.7 us (38%)
  matrix products  21.1 us (24%)
  starting transfers between devices  14.4 us (16%)
  other arithmetic  11.8 us (13%)
  local copies, waits for them, and re-layouts  6.97 us (8%)
  between operations  0.92 us (1%)
    ppermute x4, waiting for transfers between devices, scan_states(): earlier = lax.ppermute(carried.astype(jnp.bfloat16), axis, pairs)  26.5 us
    ppermute x4, starting transfers between devices, scan_states(): earlier = lax.ppermute(carried.astype(jnp.bfloat16), axis, pairs)  6.52 us
    ppermute x3, waiting for transfers between devices, scan_states(): earlier = lax.ppermute((inclusive - eye).astype(jnp.bfloat16), axis, pairs)  6.02 us
    dot_general x4, matrix products, unit_lower_inverse(): jnp.einsum('sbhij,sbhjk->sbhik', jnp.stack([inverse, power]), jnp.stack([...  4.71 us
    ppermute x3, starting transfers between devices, scan_states(): earlier = lax.ppermute((inclusive - eye).astype(jnp.bfloat16), axis, pairs)  4.49 us
    dot_general x4, matrix products, product_high(): return jnp.einsum('hde,hef->hdf', left, right, precision=lax.Precision.HIGH)  3.5 us
    ppermute x1, starting transfers between devices, from_behind(): lax.ppermute(value, axis, [(source, source + steps) for source in range(f...  3.4 us
    unnamed x56, local copies, waits for them, and re-layouts  3.4 us
  transfers between devices with their start and end apart: 8, of which 7 were waited for; matrix products, arithmetic and copies ran while one was open for 16% of the time, Pallas kernels for 0%

profile of v14, /device:TPU:28, one launch (start us, length us, event | category | flops | bytes accessed | tf_op | source)
XLA Modules:
  0.0 88.9 jit_solution(11341948317791953458)
XLA Ops:
  3.7 3.4 %collective-permute-start = (f32[3,2048]{1,0:T(4,128)S(1)}, f32[3,2048]{1,0:T(4,128)S(1)}, u32[]{:S(2)}, u32[]{:S(2)}) collective-permute-start(f32[3,2048]{1,0:T(4,128)S(1)} %pad_maximum_fusion.11), channel_id=1, source_target_pairs={{0,2},{2,4},{4,6},{6,8},{8,10},{10,12},{12,14},{14,16},{16,18},{18... | collective-permute-start | bytes 73736 | tf_op jit(solution)/shard_map/ppermute | solution.py:16
  9.1 1.2 %collective-permute-done = f32[3,2048]{1,0:T(4,128)S(1)} collective-permute-done((f32[3,2048]{1,0:T(4,128)S(1)}, f32[3,2048]{1,0:T(4,128)S(1)}, u32[]{:S(2)}, u32[]{:S(2)}) %collective-permute-start) | collective-permute-done | bytes 24608 | tf_op jit(solution)/shard_map/ppermute | solution.py:16
  13.5 1.2 %fusion.4 = f32[2,2,8,64,64]{4,3,2,1,0:T(8,128)S(1)} fusion(f32[1,2,8,64,64]{4,3,2,1,0:T(8,128)S(1)} %bitcast.193, f32[1,2,8,64,64]{4,3,2,1,0:T(8,128)S(1)} %get-tuple-element.38, f32[1,2,8,64,64]{4,3,2,1,0:T(8,128)S(1)} %get-tuple-element.37), kind=kOutput, calls=%fused_computation.17 | convolution fusion | flops 100925440 | bytes 1310720 | tf_op jit(solution)/shard_map/sbhij,sbhjk->sbhik/dot_general | solution.py:116
  14.8 1.2 %fusion.10 = f32[2,2,8,64,64]{4,3,2,1,0:T(8,128)S(1)} fusion(f32[2,2,8,64,64]{4,3,2,1,0:T(8,128)S(1)} %fusion.4, f32[1,2,8,64,64]{4,3,2,1,0:T(8,128)S(1)} %get-tuple-element.32, f32[1,2,8,64,64]{4,3,2,1,0:T(8,128)S(1)} %get-tuple-element.31), kind=kOutput, calls=%fused_computation.25 | convolution fusion | flops 100794368 | bytes 1572864 | tf_op jit(solution)/shard_map/sbhij,sbhjk->sbhik/dot_general | solution.py:116
  16.1 1.2 %fusion.14 = f32[2,2,8,64,64]{4,3,2,1,0:T(8,128)S(1)} fusion(f32[2,2,8,64,64]{4,3,2,1,0:T(8,128)S(1)} %fusion.10, f32[1,2,8,64,64]{4,3,2,1,0:T(8,128)S(1)} %get-tuple-element.30, f32[1,2,8,64,64]{4,3,2,1,0:T(8,128)S(1)} %get-tuple-element.29), kind=kOutput, calls=%fused_computation.29 | convolution fusion | flops 100794368 | bytes 1572864 | tf_op jit(solution)/shard_map/sbhij,sbhjk->sbhik/dot_general | solution.py:116
  17.4 1.2 %fusion.18 = f32[2,2,8,64,64]{4,3,2,1,0:T(8,128)S(1)} fusion(f32[2,2,8,64,64]{4,3,2,1,0:T(8,128)S(1)} %fusion.14, f32[1,2,8,64,64]{4,3,2,1,0:T(8,128)S(1)} %get-tuple-element.28, f32[1,2,8,64,64]{4,3,2,1,0:T(8,128)S(1)} %get-tuple-element.27), kind=kOutput, calls=%fused_computation.33 | convolution fusion | flops 100794368 | bytes 1572864 | tf_op jit(solution)/shard_map/sbhij,sbhjk->sbhik/dot_general | solution.py:116
  22.2 2.3 %fusion.69 = f32[2,8,128,256]{3,2,1,0:T(8,128)S(1)} fusion(f32[2,8,64,256]{3,2,1,0:T(8,128)S(1)} %fusion.22, f32[2,64,8,128]{3,1,0,2:T(8,128)S(1)} %bitcast.196, f32[2,8,64]{2,1,0:T(8,128)S(1)} %get-tuple-element.41), kind=kOutput, calls=%fused_computation.103 | convolution fusion | flops 402784256 | bytes 3674112 | tf_op jit(solution)/shard_map/bhjd,bhje->bhde/dot_general | solution.py:148
  26.7 2.5 %collective-permute-start.1 = (bf16[8,128,128]{2,1,0:T(8,128)(2,1)}, bf16[8,128,128]{2,1,0:T(8,128)(2,1)}, u32[]{:S(2)}, u32[]{:S(2)}) collective-permute-start(bf16[8,128,128]{2,1,0:T(8,128)(2,1)} %get-tuple-element.25), channel_id=1, source_target_pairs={{0,2},{2,4},{4,6},{6,8},{8,10},{10,12},{12,14},{14,16},{16,18},{18... | collective-permute-start | bytes 786440 | tf_op jit(solution)/shard_map/ppermute | solution.py:50
  30.5 1.9 %collective-permute-start.3 = (bf16[8,128,128]{2,1,0:T(8,128)(2,1)}, bf16[8,128,128]{2,1,0:T(8,128)(2,1)}, u32[]{:S(2)}, u32[]{:S(2)}) collective-permute-start(bf16[8,128,128]{2,1,0:T(8,128)(2,1)} %get-tuple-element.26), channel_id=1, source_target_pairs={{0,2},{2,4},{4,6},{6,8},{8,10},{10,12},{12,14},{14,16},{16,18},{18... | collective-permute-start | bytes 786440 | tf_op jit(solution)/shard_map/ppermute | solution.py:33
  33.2 5.7 %collective-permute-done.1 = bf16[8,128,128]{2,1,0:T(8,128)(2,1)} collective-permute-done((bf16[8,128,128]{2,1,0:T(8,128)(2,1)}, bf16[8,128,128]{2,1,0:T(8,128)(2,1)}, u32[]{:S(2)}, u32[]{:S(2)}) %collective-permute-start.1) | collective-permute-done | bytes 262176 | tf_op jit(solution)/shard_map/ppermute | solution.py:50
  38.9 1.5 %multiply_convert_fusion.1 = bf16[128,512]{1,0:T(8,128)(2,1)} fusion(f32[131,512]{1,0:T(8,128)S(1)} %pad_maximum_fusion.9, f32[512]{0:T(512)} %bitcast.218, f32[512]{0:T(512)} %bitcast.219, f32[512]{0:T(512)} %bitcast.217, f32[512]{0:T(512)} %bitcast.216), kind=kLoop, calls=%fused_computation.156 | loop fusion | flops 786432 | bytes 1187840 | tf_op jit(solution)/shard_map/convert_element_type | solution.py:87
  44.8 1.6 %subtract_convert_fusion.1 = (bf16[8,128,128]{2,1,0:T(8,128)(2,1)S(1)}, f32[8,128,128]{2,1,0:T(8,128)S(1)}) fusion(f32[128,128]{1,0:T(8,128)S(1)} %fusion.108, f32[8,128,256]{2,1,0:T(8,128)S(1)} %fusion.54, bf16[8,128,128]{2,1,0:T(8,128)(2,1)} %collective-permute-done.3, f32[128,128]{1,0:T(8,128)S(1)} %fusion.107, pred[]{:T(512)S(6)} %ge.39), kind=kOutput, calls=%fused_computation.111 | convolution fusion | flops 101318656 | bytes 2228225 | tf_op jit(solution)/shard_map/hde,hef->hdf/dot_general | solution.py:165
  46.3 1.3 %collective-permute-start.5 = (bf16[8,128,128]{2,1,0:T(8,128)(2,1)S(1)}, bf16[8,128,128]{2,1,0:T(8,128)(2,1)S(1)}, u32[]{:S(2)}, u32[]{:S(2)}) collective-permute-start(bf16[8,128,128]{2,1,0:T(8,128)(2,1)S(1)} %get-tuple-element.54), channel_id=1, source_target_pairs={{0,4},{2,6},{4,8},{6,10},{8,12},{10,14},{12,16},{14,18},{16,20},{1... | collective-permute-start | bytes 786440 | tf_op jit(solution)/shard_map/ppermute | solution.py:33
  47.6 1.3 %fusion.127 = (bf16[8,128,128]{2,1,0:T(8,128)(2,1)S(1)}, f32[8,128,128]{2,1,0:T(8,128)S(1)}) fusion(f32[8,128,256]{2,1,0:T(8,128)S(1)} %copy-done.6, f32[8,128,256]{2,1,0:T(8,128)S(1)} %fusion.54, bf16[8,128,128]{2,1,0:T(8,128)(2,1)} %collective-permute-done.1), kind=kOutput, calls=%fused_computation.219 | convolution fusion | flops 101056512 | bytes 2621440 | tf_op jit(solution)/shard_map/hde,hef->hdf/dot_general | solution.py:165
  48.9 1.4 %collective-permute-start.2 = (bf16[8,128,128]{2,1,0:T(8,128)(2,1)S(1)}, bf16[8,128,128]{2,1,0:T(8,128)(2,1)S(1)}, u32[]{:S(2)}, u32[]{:S(2)}) collective-permute-start(bf16[8,128,128]{2,1,0:T(8,128)(2,1)S(1)} %get-tuple-element.56), channel_id=1, source_target_pairs={{0,4},{2,6},{4,8},{6,10},{8,12},{10,14},{12,16},{14,18},{16,20},{1... | collective-permute-start | bytes 786440 | tf_op jit(solution)/shard_map/ppermute | solution.py:50
  52.1 3.9 %collective-permute-done.5 = bf16[8,128,128]{2,1,0:T(8,128)(2,1)S(1)} collective-permute-done((bf16[8,128,128]{2,1,0:T(8,128)(2,1)S(1)}, bf16[8,128,128]{2,1,0:T(8,128)(2,1)S(1)}, u32[]{:S(2)}, u32[]{:S(2)}) %collective-permute-start.5) | collective-permute-done | bytes 262176 | tf_op jit(solution)/shard_map/ppermute | solution.py:33
  56.6 2.2 %collective-permute-done.2 = bf16[8,128,128]{2,1,0:T(8,128)(2,1)S(1)} collective-permute-done((bf16[8,128,128]{2,1,0:T(8,128)(2,1)S(1)}, bf16[8,128,128]{2,1,0:T(8,128)(2,1)S(1)}, u32[]{:S(2)}, u32[]{:S(2)}) %collective-permute-start.2) | collective-permute-done | bytes 262176 | tf_op jit(solution)/shard_map/ppermute | solution.py:50
  59.3 1.3 %collective-permute-start.4 = (bf16[8,128,128]{2,1,0:T(8,128)(2,1)S(1)}, bf16[8,128,128]{2,1,0:T(8,128)(2,1)S(1)}, u32[]{:S(2)}, u32[]{:S(2)}) collective-permute-start(bf16[8,128,128]{2,1,0:T(8,128)(2,1)S(1)} %fusion.102), channel_id=1, source_target_pairs={{0,8},{2,10},{4,12},{6,14},{8,16},{10,18},{12,20},{14,22},{16,24},... | collective-permute-start | bytes 786440 | tf_op jit(solution)/shard_map/ppermute | solution.py:50
  60.7 1.3 %collective-permute-start.6 = (bf16[8,128,128]{2,1,0:T(8,128)(2,1)S(1)}, bf16[8,128,128]{2,1,0:T(8,128)(2,1)S(1)}, u32[]{:S(2)}, u32[]{:S(2)}) collective-permute-start(bf16[8,128,128]{2,1,0:T(8,128)(2,1)S(1)} %get-tuple-element.24), channel_id=1, source_target_pairs={{0,8},{2,10},{4,12},{6,14},{8,16},{10,18},{12,20},{14,22},{16,24},... | collective-permute-start | bytes 786440 | tf_op jit(solution)/shard_map/ppermute | solution.py:33
  62.0 7.9 %collective-permute-done.4 = bf16[8,128,128]{2,1,0:T(8,128)(2,1)S(1)} collective-permute-done((bf16[8,128,128]{2,1,0:T(8,128)(2,1)S(1)}, bf16[8,128,128]{2,1,0:T(8,128)(2,1)S(1)}, u32[]{:S(2)}, u32[]{:S(2)}) %collective-permute-start.4) | collective-permute-done | bytes 262176 | tf_op jit(solution)/shard_map/ppermute | solution.py:50
  70.5 1.3 %collective-permute-start.7 = (bf16[8,128,128]{2,1,0:T(8,128)(2,1)S(1)}, bf16[8,128,128]{2,1,0:T(8,128)(2,1)S(1)}, u32[]{:S(2)}, u32[]{:S(2)}) collective-permute-start(bf16[8,128,128]{2,1,0:T(8,128)(2,1)S(1)} %fusion.42), channel_id=1, source_target_pairs={{0,16},{2,18},{4,20},{6,22},{8,24},{10,26},{12,28},{14,30},{1,17},... | collective-permute-start | bytes 786440 | tf_op jit(solution)/shard_map/ppermute | solution.py:50
  71.9 2.1 %collective-permute-done.6 = bf16[8,128,128]{2,1,0:T(8,128)(2,1)S(1)} collective-permute-done((bf16[8,128,128]{2,1,0:T(8,128)(2,1)S(1)}, bf16[8,128,128]{2,1,0:T(8,128)(2,1)S(1)}, u32[]{:S(2)}, u32[]{:S(2)}) %collective-permute-start.6) | collective-permute-done | bytes 262176 | tf_op jit(solution)/shard_map/ppermute | solution.py:33
  74.3 10.8 %collective-permute-done.7 = bf16[8,128,128]{2,1,0:T(8,128)(2,1)S(1)} collective-permute-done((bf16[8,128,128]{2,1,0:T(8,128)(2,1)S(1)}, bf16[8,128,128]{2,1,0:T(8,128)(2,1)S(1)}, u32[]{:S(2)}, u32[]{:S(2)}) %collective-permute-start.7) | collective-permute-done | bytes 262176 | tf_op jit(solution)/shard_map/ppermute | solution.py:50
  85.4 1.9 %multiply_reduce_fusion = (f32[2,64,8]{1,2,0:T(8,128)S(1)}, f32[2,64,8,128]{3,1,2,0:T(8,128)S(1)}) fusion(f32[1,8,64,128]{3,2,1,0:T(8,128)S(1)} %get-tuple-element.33, f32[1,8,64,128]{3,2,1,0:T(8,128)S(1)} %slice-done.1, f32[8,128,128]{2,1,0:T(8,128)S(1)} %fusion.129, f32[2,8,128,128]{3,2,1,0:T(8,128)S(1)} %convolution_bitcast_fusion, ...), kind=kOutput, calls=%fused_computation.105 | convolution fusion | flops 202505216 | bytes 3411968 | tf_op jit(solution)/shard_map/bhid,hde->bhie/dot_general | solution.py:256
  (144 shorter events, 26.7 us)
Async XLA Ops:
  0.0 8.9 %copy-start = (f32[128]{0:T(128)S(1)}, f32[128]{0:T(128)}, u32[]{:S(2)}) copy-start(f32[128]{0:T(128)} %param.31) | copy-start | bytes 1540
  1.6 5.5 %copy-start.19 = (bf16[4,512]{1,0:T(4,128)(2,1)S(1)}, bf16[4,512]{1,0:T(4,128)(2,1)}, u32[]{:S(2)}) copy-start(bf16[4,512]{1,0:T(4,128)(2,1)} %param.24) | copy-start | bytes 12292
  1.6 5.5 %copy-start.21 = (f32[128,8]{0,1:T(8,128)S(1)}, f32[128,8]{0,1:T(8,128)}, u32[]{:S(2)}) copy-start(f32[128,8]{0,1:T(8,128)} %param.27) | copy-start | bytes 12292
  1.7 5.6 %copy-start.24 = (f32[16]{0:T(128)S(1)}, f32[16]{0:T(128)}, u32[]{:S(2)}) copy-start(f32[16]{0:T(128)} %param.29) | copy-start | bytes 196
  1.7 5.7 %copy-start.25 = (f32[16]{0:T(128)S(1)}, f32[16]{0:T(128)}, u32[]{:S(2)}) copy-start(f32[16]{0:T(128)} %param.28) | copy-start | bytes 196
  1.7 5.8 %copy-start.22 = (f32[128,8]{0,1:T(8,128)S(1)}, f32[128,8]{0,1:T(8,128)}, u32[]{:S(2)}) copy-start(f32[128,8]{0,1:T(8,128)} %param.26) | copy-start | bytes 12292
  1.7 5.9 %copy-start.18 = (bf16[4,1024]{1,0:T(4,128)(2,1)S(1)}, bf16[4,1024]{1,0:T(4,128)(2,1)}, u32[]{:S(2)}) copy-start(bf16[4,1024]{1,0:T(4,128)(2,1)} %param.25) | copy-start | bytes 24580
  1.7 6.6 %copy-start.20 = (bf16[4,512]{1,0:T(4,128)(2,1)S(1)}, bf16[4,512]{1,0:T(4,128)(2,1)}, u32[]{:S(2)}) copy-start(bf16[4,512]{1,0:T(4,128)(2,1)} %param.23) | copy-start | bytes 12292
  3.7 6.7 %collective-permute-start = (f32[3,2048]{1,0:T(4,128)S(1)}, f32[3,2048]{1,0:T(4,128)S(1)}, u32[]{:S(2)}, u32[]{:S(2)}) collective-permute-start(f32[3,2048]{1,0:T(4,128)S(1)} %pad_maximum_fusion.11), channel_id=1, source_target_pairs={{0,2},{2,4},{4,6},{6,8},{8,10},{10,12},{12,14},{14,16},{16,18},{18... | collective-permute-start | bytes 73736 | tf_op jit(solution)/shard_map/ppermute | solution.py:16
  7.1 5.6 %copy-start.16 = (pred[64,64]{1,0:T(8,128)(4,1)}, pred[64,64]{1,0:T(8,128)(4,1)S(1)}, u32[]{:S(2)}) copy-start(pred[64,64]{1,0:T(8,128)(4,1)S(1)} %get-tuple-element.61) | copy-start | bytes 12292
  11.8 9.4 %copy-start.3 = (f32[128,4,2,128]{3,0,2,1:T(8,128)}, f32[128,4,2,128]{3,0,2,1:T(8,128)S(1)}, u32[]{:S(2)}) copy-start(f32[128,4,2,128]{3,0,2,1:T(8,128)S(1)} %broadcast_in_dim.31) | copy-start | bytes 1572868
  26.7 12.1 %collective-permute-start.1 = (bf16[8,128,128]{2,1,0:T(8,128)(2,1)}, bf16[8,128,128]{2,1,0:T(8,128)(2,1)}, u32[]{:S(2)}, u32[]{:S(2)}) collective-permute-start(bf16[8,128,128]{2,1,0:T(8,128)(2,1)} %get-tuple-element.25), channel_id=1, source_target_pairs={{0,2},{2,4},{4,6},{6,8},{8,10},{10,12},{12,14},{14,16},{16,18},{18... | collective-permute-start | bytes 786440 | tf_op jit(solution)/shard_map/ppermute | solution.py:50
  30.5 14.2 %collective-permute-start.3 = (bf16[8,128,128]{2,1,0:T(8,128)(2,1)}, bf16[8,128,128]{2,1,0:T(8,128)(2,1)}, u32[]{:S(2)}, u32[]{:S(2)}) collective-permute-start(bf16[8,128,128]{2,1,0:T(8,128)(2,1)} %get-tuple-element.26), channel_id=1, source_target_pairs={{0,2},{2,4},{4,6},{6,8},{8,10},{10,12},{12,14},{14,16},{16,18},{18... | collective-permute-start | bytes 786440 | tf_op jit(solution)/shard_map/ppermute | solution.py:33
  44.1 27.8 %copy-start.8 = (f32[2,8,64,128]{3,2,1,0:T(8,128)}, f32[2,8,64,128]{3,2,1,0:T(8,128)S(1)}, u32[]{:S(2)}) copy-start(f32[2,8,64,128]{3,2,1,0:T(8,128)S(1)} %convolution_subtract_fusion) | copy-start | bytes 1572868
  44.7 27.1 %copy-start.7 = (f32[2,8,64,128]{3,2,1,0:T(8,128)}, f32[2,8,64,128]{3,2,1,0:T(8,128)S(1)}, u32[]{:S(2)}) copy-start(f32[2,8,64,128]{3,2,1,0:T(8,128)S(1)} %fusion.52) | copy-start | bytes 1572868
  46.3 9.7 %collective-permute-start.5 = (bf16[8,128,128]{2,1,0:T(8,128)(2,1)S(1)}, bf16[8,128,128]{2,1,0:T(8,128)(2,1)S(1)}, u32[]{:S(2)}, u32[]{:S(2)}) collective-permute-start(bf16[8,128,128]{2,1,0:T(8,128)(2,1)S(1)} %get-tuple-element.54), channel_id=1, source_target_pairs={{0,4},{2,6},{4,8},{6,10},{8,12},{10,14},{12,16},{14,18},{16,20},{1... | collective-permute-start | bytes 786440 | tf_op jit(solution)/shard_map/ppermute | solution.py:33
  48.9 7.1 %copy-start.9 = (f32[128,128]{1,0:T(8,128)S(1)}, f32[128,128]{1,0:T(8,128)}, u32[]{:S(2)}) copy-start(f32[128,128]{1,0:T(8,128)} %fusion.106) | copy-start | bytes 196612
  48.9 9.9 %collective-permute-start.2 = (bf16[8,128,128]{2,1,0:T(8,128)(2,1)S(1)}, bf16[8,128,128]{2,1,0:T(8,128)(2,1)S(1)}, u32[]{:S(2)}, u32[]{:S(2)}) collective-permute-start(bf16[8,128,128]{2,1,0:T(8,128)(2,1)S(1)} %get-tuple-element.56), channel_id=1, source_target_pairs={{0,4},{2,6},{4,8},{6,10},{8,12},{10,14},{12,16},{14,18},{16,20},{1... | collective-permute-start | bytes 786440 | tf_op jit(solution)/shard_map/ppermute | solution.py:50
  59.3 10.5 %collective-permute-start.4 = (bf16[8,128,128]{2,1,0:T(8,128)(2,1)S(1)}, bf16[8,128,128]{2,1,0:T(8,128)(2,1)S(1)}, u32[]{:S(2)}, u32[]{:S(2)}) collective-permute-start(bf16[8,128,128]{2,1,0:T(8,128)(2,1)S(1)} %fusion.102), channel_id=1, source_target_pairs={{0,8},{2,10},{4,12},{6,14},{8,16},{10,18},{12,20},{14,22},{16,24},... | collective-permute-start | bytes 786440 | tf_op jit(solution)/shard_map/ppermute | solution.py:50
  60.7 13.2 %collective-permute-start.6 = (bf16[8,128,128]{2,1,0:T(8,128)(2,1)S(1)}, bf16[8,128,128]{2,1,0:T(8,128)(2,1)S(1)}, u32[]{:S(2)}, u32[]{:S(2)}) collective-permute-start(bf16[8,128,128]{2,1,0:T(8,128)(2,1)S(1)} %get-tuple-element.24), channel_id=1, source_target_pairs={{0,8},{2,10},{4,12},{6,14},{8,16},{10,18},{12,20},{14,22},{16,24},... | collective-permute-start | bytes 786440 | tf_op jit(solution)/shard_map/ppermute | solution.py:33
  70.3 3.6 %copy-start.11 = (f32[128,128]{1,0:T(8,128)S(1)}, f32[128,128]{1,0:T(8,128)}, u32[]{:S(2)}) copy-start(f32[128,128]{1,0:T(8,128)} %fusion.105) | copy-start | bytes 196612
  70.5 14.6 %collective-permute-start.7 = (bf16[8,128,128]{2,1,0:T(8,128)(2,1)S(1)}, bf16[8,128,128]{2,1,0:T(8,128)(2,1)S(1)}, u32[]{:S(2)}, u32[]{:S(2)}) collective-permute-start(bf16[8,128,128]{2,1,0:T(8,128)(2,1)S(1)} %fusion.42), channel_id=1, source_target_pairs={{0,16},{2,18},{4,20},{6,22},{8,24},{10,26},{12,28},{14,30},{1,17},... | collective-permute-start | bytes 786440 | tf_op jit(solution)/shard_map/ppermute | solution.py:50
  71.9 13.6 %slice-start.1 = ((f32[2,8,64,128]{3,2,1,0:T(8,128)}), f32[1,8,64,128]{3,2,1,0:T(8,128)S(1)}, s32[]{:S(2)}) async-start(f32[2,8,64,128]{3,2,1,0:T(8,128)} %copy-done.8), calls=%async_computation.1 | async-start | bytes 524288 | tf_op jit(solution)/shard_map/slice | solution.py:251
  71.9 13.6 %slice-start = ((f32[2,8,64,128]{3,2,1,0:T(8,128)}), f32[1,8,64,128]{3,2,1,0:T(8,128)S(1)}, s32[]{:S(2)}) async-start(f32[2,8,64,128]{3,2,1,0:T(8,128)} %copy-done.7), calls=%async_computation | async-start | bytes 524288 | tf_op jit(solution)/shard_map/slice | solution.py:251
  (12 other events, 27.1 us)

commit v15 on v12

--- a/solution.py
+++ b/solution.py
@@ -45,6 +45,7 @@
             inclusive = jnp.where(mine >= span, both[1], inclusive)
     state = jnp.zeros_like(offset)
     carried = offset
+    final_map, final_state = (None, None)
     for step, span in enumerate(spans):
         pairs = [(source, source + span) for source in range(devices - span)]
         earlier = lax.ppermute(carried.astype(jnp.bfloat16), axis, pairs)
@@ -66,8 +67,8 @@
             state = state + both[0]
             carried = both[1] + carried
         else:
-            state = state + product(last_map, earlier)
-    return (state, rider)
+            final_map, final_state = (last_map, earlier)
+    return (state, final_map, final_state, rider)
 
 
 def expand_quantized(raw_rows, scales):
@@ -235,7 +236,7 @@
             "hde,hef->hdf", maps[block][..., :key_width], device_map, precision=HIGHEST
         ).at[..., key_width:].add(maps[block][..., key_width:])
     dev_trans, dev_offset = (device_map[..., :key_width], device_map[..., key_width:])
-    incoming, query_window = scan_states(
+    incoming, final_map, final_state, query_window = scan_states(
         dev_trans, dev_offset, "seq", jnp.concatenate([tail_rows[0], query_deq], axis=0)
     )
     query_conv = causal_filter(query_window, conv_query)
@@ -249,9 +250,13 @@
         read = jnp.einsum("hid,hde->hie", readout[block], maps_before[block], precision=HIGHEST)
         read_maps.append(read[..., :key_width])
         local_outs.append(zero_out[block] + read[..., key_width:])
+    reads = jnp.stack(read_maps)
     outputs = jnp.stack(local_outs) + jnp.einsum(
-        "bhid,hde->bhie", jnp.stack(read_maps), incoming, precision=HIGHEST
-    )
+        "bhid,hde->bhie", reads, incoming, precision=HIGHEST
+    )
+    if final_map is not None:
+        lead = jnp.einsum("bhid,hde->bhie", reads, final_map, precision=HIGHEST)
+        outputs = outputs + jnp.einsum("bhid,hde->bhie", lead, final_state, precision=HIGHEST)
     gated_rows = gated_norm(to_rows(outputs), output_gate, norm_gain)
     return gated_rows
 

time: 90.1 us -> 87.7 us (0.973)
  waiting for transfers between devices: 32.5 us -> 27.9 us
    ppermute x3, waiting for transfers between devices: 5.56 us -> 2.46 us  [scan_states(): earlier = lax.ppermute((inclusive - eye).astype(jnp.bfloat16), axis, pairs)]
    ppermute x4, waiting for transfers between devices: 25.7 us -> 24.1 us  [scan_states(): earlier = lax.ppermute(carried.astype(jnp.bfloat16), axis, pairs)]
    dot_general x1 -> x3, matrix products: 1.87 us -> 2.78 us  [the longest x1 1.63 us: shards(): jnp.einsum('bhid,hde->bhie', reads, incoming, precision=HIGHEST)]
    unnamed x56 -> x50, local copies, waits for them, and re-layouts: 3.4 us -> 4.07 us
    dot_general x4 -> x3, matrix products: 4.25 us -> 3.85 us  [product(): return jnp.einsum('hde,hef->hdf', left, right, precision=HIGHEST)]
  transfers between devices with their start and end apart: 8 -> 8, of which waited for: 7 -> 7; matrix products, arithmetic and copies ran while one was open for 17% -> 23% of each run, Pallas kernels for 0% -> 0%
where the time goes in v15:
time: 87.7 us; the launch traced here: 86.6 us
  waiting for transfers between devices  27.9 us (32%)
  matrix products  23.2 us (26%)
  starting transfers between devices  14.5 us (17%)
  other arithmetic  12.6 us (14%)
  local copies, waits for them, and re-layouts  7.66 us (9%)
    ppermute x4, waiting for transfers between devices, scan_states(): earlier = lax.ppermute(carried.astype(jnp.bfloat16), axis, pairs)  24.1 us
    ppermute x4, starting transfers between devices, scan_states(): earlier = lax.ppermute(carried.astype(jnp.bfloat16), axis, pairs)  6.58 us
    dot_general x4, matrix products, unit_lower_inverse(): jnp.einsum('sbhij,sbhjk->sbhik', jnp.stack([inverse, power]), jnp.stack([...  4.72 us
    ppermute x3, starting transfers between devices, scan_states(): earlier = lax.ppermute((inclusive - eye).astype(jnp.bfloat16), axis, pairs)  4.49 us
    unnamed x50, local copies, waits for them, and re-layouts  4.07 us
    dot_general x3, matrix products, product(): return jnp.einsum('hde,hef->hdf', left, right, precision=HIGHEST)  3.85 us
    ppermute x1, starting transfers between devices, from_behind(): lax.ppermute(value, axis, [(source, source + steps) for source in range(f...  3.4 us
    ppermute x3, waiting for transfers between devices, scan_states(): earlier = lax.ppermute((inclusive - eye).astype(jnp.bfloat16), axis, pairs)  2.46 us
  transfers between devices with their start and end apart: 8, of which 7 were waited for; matrix products, arithmetic and copies ran while one was open for 23% of the time, Pallas kernels for 0%

profile of v15, /device:TPU:28, one launch (start us, length us, event | category | flops | bytes accessed | tf_op | source)
XLA Modules:
  0.0 86.6 jit_solution(14447354033739646765)
XLA Ops:
  5.2 3.4 %collective-permute-start = (f32[3,2048]{1,0:T(4,128)S(1)}, f32[3,2048]{1,0:T(4,128)S(1)}, u32[]{:S(2)}, u32[]{:S(2)}) collective-permute-start(f32[3,2048]{1,0:T(4,128)S(1)} %pad_maximum_fusion.12), channel_id=1, source_target_pairs={{0,2},{2,4},{4,6},{6,8},{8,10},{10,12},{12,14},{14,16},{16,18},{18... | collective-permute-start | bytes 73736 | tf_op jit(solution)/shard_map/ppermute | solution.py:16
  10.6 1.2 %collective-permute-done = f32[3,2048]{1,0:T(4,128)S(1)} collective-permute-done((f32[3,2048]{1,0:T(4,128)S(1)}, f32[3,2048]{1,0:T(4,128)S(1)}, u32[]{:S(2)}, u32[]{:S(2)}) %collective-permute-start) | collective-permute-done | bytes 24608 | tf_op jit(solution)/shard_map/ppermute | solution.py:16
  15.5 1.2 %fusion.5 = f32[2,2,8,64,64]{4,3,2,1,0:T(8,128)S(1)} fusion(f32[1,2,8,64,64]{4,3,2,1,0:T(8,128)S(1)} %bitcast.199, f32[1,2,8,64,64]{4,3,2,1,0:T(8,128)S(1)} %get-tuple-element.38, f32[1,2,8,64,64]{4,3,2,1,0:T(8,128)S(1)} %get-tuple-element.37), kind=kOutput, calls=%fused_computation.21 | convolution fusion | flops 100925440 | bytes 1310720 | tf_op jit(solution)/shard_map/sbhij,sbhjk->sbhik/dot_general | solution.py:117
  16.9 1.2 %fusion.11 = f32[2,2,8,64,64]{4,3,2,1,0:T(8,128)S(1)} fusion(f32[2,2,8,64,64]{4,3,2,1,0:T(8,128)S(1)} %fusion.5, f32[1,2,8,64,64]{4,3,2,1,0:T(8,128)S(1)} %get-tuple-element.32, f32[1,2,8,64,64]{4,3,2,1,0:T(8,128)S(1)} %get-tuple-element.31), kind=kOutput, calls=%fused_computation.29 | convolution fusion | flops 100794368 | bytes 1572864 | tf_op jit(solution)/shard_map/sbhij,sbhjk->sbhik/dot_general | solution.py:117
  18.2 1.2 %fusion.15 = f32[2,2,8,64,64]{4,3,2,1,0:T(8,128)S(1)} fusion(f32[2,2,8,64,64]{4,3,2,1,0:T(8,128)S(1)} %fusion.11, f32[1,2,8,64,64]{4,3,2,1,0:T(8,128)S(1)} %get-tuple-element.30, f32[1,2,8,64,64]{4,3,2,1,0:T(8,128)S(1)} %get-tuple-element.29), kind=kOutput, calls=%fused_computation.33 | convolution fusion | flops 100794368 | bytes 1572864 | tf_op jit(solution)/shard_map/sbhij,sbhjk->sbhik/dot_general | solution.py:117
  19.5 1.2 %fusion.19 = f32[2,2,8,64,64]{4,3,2,1,0:T(8,128)S(1)} fusion(f32[2,2,8,64,64]{4,3,2,1,0:T(8,128)S(1)} %fusion.15, f32[1,2,8,64,64]{4,3,2,1,0:T(8,128)S(1)} %get-tuple-element.28, f32[1,2,8,64,64]{4,3,2,1,0:T(8,128)S(1)} %get-tuple-element.27), kind=kOutput, calls=%fused_computation.37 | convolution fusion | flops 100794368 | bytes 1572864 | tf_op jit(solution)/shard_map/sbhij,sbhjk->sbhik/dot_general | solution.py:117
  23.7 2.3 %fusion.65 = f32[2,8,128,256]{3,2,1,0:T(8,128)S(1)} fusion(f32[2,8,64,256]{3,2,1,0:T(8,128)S(1)} %fusion.23, f32[2,64,8,128]{3,1,0,2:T(8,128)S(1)} %bitcast.202, f32[2,8,64]{2,1,0:T(8,128)S(1)} %get-tuple-element.41), kind=kOutput, calls=%fused_computation.103 | convolution fusion | flops 402784256 | bytes 3674112 | tf_op jit(solution)/shard_map/bhjd,bhje->bhde/dot_general | solution.py:149
  28.3 2.5 %collective-permute-start.1 = (bf16[8,128,128]{2,1,0:T(8,128)(2,1)}, bf16[8,128,128]{2,1,0:T(8,128)(2,1)}, u32[]{:S(2)}, u32[]{:S(2)}) collective-permute-start(bf16[8,128,128]{2,1,0:T(8,128)(2,1)} %get-tuple-element.25), channel_id=1, source_target_pairs={{0,2},{2,4},{4,6},{6,8},{8,10},{10,12},{12,14},{14,16},{16,18},{18... | collective-permute-start | bytes 786440 | tf_op jit(solution)/shard_map/ppermute | solution.py:51
  32.0 1.9 %collective-permute-start.3 = (bf16[8,128,128]{2,1,0:T(8,128)(2,1)}, bf16[8,128,128]{2,1,0:T(8,128)(2,1)}, u32[]{:S(2)}, u32[]{:S(2)}) collective-permute-start(bf16[8,128,128]{2,1,0:T(8,128)(2,1)} %get-tuple-element.26), channel_id=1, source_target_pairs={{0,2},{2,4},{4,6},{6,8},{8,10},{10,12},{12,14},{14,16},{16,18},{18... | collective-permute-start | bytes 786440 | tf_op jit(solution)/shard_map/ppermute | solution.py:33
  34.7 5.7 %collective-permute-done.1 = bf16[8,128,128]{2,1,0:T(8,128)(2,1)} collective-permute-done((bf16[8,128,128]{2,1,0:T(8,128)(2,1)}, bf16[8,128,128]{2,1,0:T(8,128)(2,1)}, u32[]{:S(2)}, u32[]{:S(2)}) %collective-permute-start.1) | collective-permute-done | bytes 262176 | tf_op jit(solution)/shard_map/ppermute | solution.py:51
  40.4 1.5 %multiply_convert_fusion.1 = bf16[128,512]{1,0:T(8,128)(2,1)} fusion(f32[131,512]{1,0:T(8,128)S(1)} %pad_maximum_fusion.10, f32[512]{0:T(512)} %bitcast.224, f32[512]{0:T(512)} %bitcast.225, f32[512]{0:T(512)} %bitcast.223, f32[512]{0:T(512)} %bitcast.222), kind=kLoop, calls=%fused_computation.159 | loop fusion | flops 786432 | bytes 1187840 | tf_op jit(solution)/shard_map/convert_element_type | solution.py:88
  46.3 1.5 %fusion.125 = (bf16[8,128,128]{2,1,0:T(8,128)(2,1)S(1)}, f32[8,128,128]{2,1,0:T(8,128)S(1)}) fusion(f32[8,128,256]{2,1,0:T(8,128)S(1)} %copy-done.6, f32[8,128,256]{2,1,0:T(8,128)S(1)} %fusion.54, bf16[8,128,128]{2,1,0:T(8,128)(2,1)} %collective-permute-done.1), kind=kOutput, calls=%fused_computation.221 | convolution fusion | flops 201719808 | bytes 2621440 | tf_op jit(solution)/shard_map/hde,hef->hdf/dot_general | solution.py:166
  47.8 1.3 %collective-permute-start.2 = (bf16[8,128,128]{2,1,0:T(8,128)(2,1)S(1)}, bf16[8,128,128]{2,1,0:T(8,128)(2,1)S(1)}, u32[]{:S(2)}, u32[]{:S(2)}) collective-permute-start(bf16[8,128,128]{2,1,0:T(8,128)(2,1)S(1)} %get-tuple-element.56), channel_id=1, source_target_pairs={{0,4},{2,6},{4,8},{6,10},{8,12},{10,14},{12,16},{14,18},{16,20},{1... | collective-permute-start | bytes 786440 | tf_op jit(solution)/shard_map/ppermute | solution.py:51
  49.1 1.7 %subtract_convert_fusion.1 = (bf16[8,128,128]{2,1,0:T(8,128)(2,1)S(1)}, f32[8,128,128]{2,1,0:T(8,128)S(1)}) fusion(f32[128,128]{1,0:T(8,128)S(1)} %fusion.107, f32[8,128,256]{2,1,0:T(8,128)S(1)} %fusion.54, bf16[8,128,128]{2,1,0:T(8,128)(2,1)} %collective-permute-done.3, f32[128,128]{1,0:T(8,128)S(1)} %fusion.106, pred[]{:T(512)S(6)} %ge.39), kind=kOutput, calls=%fused_computation.113 | convolution fusion | flops 201981952 | bytes 2228225 | tf_op jit(solution)/shard_map/hde,hef->hdf/dot_general | solution.py:166
  50.8 1.3 %collective-permute-start.5 = (bf16[8,128,128]{2,1,0:T(8,128)(2,1)S(1)}, bf16[8,128,128]{2,1,0:T(8,128)(2,1)S(1)}, u32[]{:S(2)}, u32[]{:S(2)}) collective-permute-start(bf16[8,128,128]{2,1,0:T(8,128)(2,1)S(1)} %get-tuple-element.54), channel_id=1, source_target_pairs={{0,4},{2,6},{4,8},{6,10},{8,12},{10,14},{12,16},{14,18},{16,20},{1... | collective-permute-start | bytes 786440 | tf_op jit(solution)/shard_map/ppermute | solution.py:33
  53.9 3.9 %collective-permute-done.2 = bf16[8,128,128]{2,1,0:T(8,128)(2,1)S(1)} collective-permute-done((bf16[8,128,128]{2,1,0:T(8,128)(2,1)S(1)}, bf16[8,128,128]{2,1,0:T(8,128)(2,1)S(1)}, u32[]{:S(2)}, u32[]{:S(2)}) %collective-permute-start.2) | collective-permute-done | bytes 262176 | tf_op jit(solution)/shard_map/ppermute | solution.py:51
  58.4 1.3 %collective-permute-start.4 = (bf16[8,128,128]{2,1,0:T(8,128)(2,1)S(1)}, bf16[8,128,128]{2,1,0:T(8,128)(2,1)S(1)}, u32[]{:S(2)}, u32[]{:S(2)}) collective-permute-start(bf16[8,128,128]{2,1,0:T(8,128)(2,1)S(1)} %fusion.101), channel_id=1, source_target_pairs={{0,8},{2,10},{4,12},{6,14},{8,16},{10,18},{12,20},{14,22},{16,24},... | collective-permute-start | bytes 786440 | tf_op jit(solution)/shard_map/ppermute | solution.py:51
  60.6 1.0 %convolution_bitcast_fusion.2 = f32[2,8,128,128]{3,2,1,0:T(8,128)S(1)} fusion(f32[1,8,128,128]{3,2,1,0:T(8,128)S(1)} %bitcast.205, f32[1,8,128,128]{3,2,1,0:T(8,128)S(1)} %fusion.72, bf16[8,128,128]{2,1,0:T(8,128)(2,1)S(1)} %collective-permute-done.5, f32[128,128]{1,0:T(8,128)S(1)} %copy-done.9), kind=kOutput, calls=%fused_computation.4 | convolution fusion | flops 403177472 | bytes 2424832 | tf_op jit(solution)/shard_map/shde,hef->shdf/dot_general | solution.py:41
  61.8 1.3 %collective-permute-start.7 = (bf16[8,128,128]{2,1,0:T(8,128)(2,1)S(1)}, bf16[8,128,128]{2,1,0:T(8,128)(2,1)S(1)}, u32[]{:S(2)}, u32[]{:S(2)}) collective-permute-start(bf16[8,128,128]{2,1,0:T(8,128)(2,1)S(1)} %get-tuple-element.23), channel_id=1, source_target_pairs={{0,8},{2,10},{4,12},{6,14},{8,16},{10,18},{12,20},{14,22},{16,24},... | collective-permute-start | bytes 786440 | tf_op jit(solution)/shard_map/ppermute | solution.py:33
  63.1 7.2 %collective-permute-done.4 = bf16[8,128,128]{2,1,0:T(8,128)(2,1)S(1)} collective-permute-done((bf16[8,128,128]{2,1,0:T(8,128)(2,1)S(1)}, bf16[8,128,128]{2,1,0:T(8,128)(2,1)S(1)}, u32[]{:S(2)}, u32[]{:S(2)}) %collective-permute-start.4) | collective-permute-done | bytes 262176 | tf_op jit(solution)/shard_map/ppermute | solution.py:51
  71.0 1.5 %collective-permute-start.6 = (bf16[8,128,128]{2,1,0:T(8,128)(2,1)S(1)}, bf16[8,128,128]{2,1,0:T(8,128)(2,1)S(1)}, u32[]{:S(2)}, u32[]{:S(2)}) collective-permute-start(bf16[8,128,128]{2,1,0:T(8,128)(2,1)S(1)} %fusion.43), channel_id=1, source_target_pairs={{0,16},{2,18},{4,20},{6,22},{8,24},{10,26},{12,28},{14,30},{1,17},... | collective-permute-start | bytes 786440 | tf_op jit(solution)/shard_map/ppermute | solution.py:51
  72.5 1.6 %collective-permute-done.7 = bf16[8,128,128]{2,1,0:T(8,128)(2,1)S(1)} collective-permute-done((bf16[8,128,128]{2,1,0:T(8,128)(2,1)S(1)}, bf16[8,128,128]{2,1,0:T(8,128)(2,1)S(1)}, u32[]{:S(2)}, u32[]{:S(2)}) %collective-permute-start.7) | collective-permute-done | bytes 262176 | tf_op jit(solution)/shard_map/ppermute | solution.py:33
  75.4 1.6 %fusion.2 = f32[2,8,64,128]{3,2,1,0:T(8,128)S(1)} fusion(f32[2,8,128,128]{3,2,1,0:T(8,128)S(1)} %convolution_bitcast_fusion, f32[2,8,128,128]{3,2,1,0:T(8,128)S(1)} %convolution_bitcast_fusion.1, f32[1,8,64,128]{3,2,1,0:T(8,128)S(1)} %get-tuple-element.34, f32[1,8,64,128]{3,2,1,0:T(8,128)S(1)} %slice-done, bf16[8,128,128]{2,1,0:T(8,128)(2,1)} %collective-permute-done.1, ...), kind=kOutput, calls=%fused_computation.17 | convolution fusion | flops 202113024 | bytes 2883584 | tf_op jit(solution)/shard_map/bhid,hde->bhie/dot_general | solution.py:254
  77.1 7.4 %collective-permute-done.6 = bf16[8,128,128]{2,1,0:T(8,128)(2,1)S(1)} collective-permute-done((bf16[8,128,128]{2,1,0:T(8,128)(2,1)S(1)}, bf16[8,128,128]{2,1,0:T(8,128)(2,1)S(1)}, u32[]{:S(2)}, u32[]{:S(2)}) %collective-permute-start.6) | collective-permute-done | bytes 262176 | tf_op jit(solution)/shard_map/ppermute | solution.py:51
  (138 shorter events, 29.9 us)
Async XLA Ops:
  0.0 9.7 %copy-start = (f32[128]{0:T(128)S(1)}, f32[128]{0:T(128)}, u32[]{:S(2)}) copy-start(f32[128]{0:T(128)} %param.31) | copy-start | bytes 1540
  0.0 5.0 %copy-start.8 = (bf16[128,1024]{1,0:T(8,128)(2,1)S(1)}, bf16[128,1024]{1,0:T(8,128)(2,1)}, u32[]{:S(2)}) copy-start(bf16[128,1024]{1,0:T(8,128)(2,1)} %param.19) | copy-start | bytes 786436
  1.6 7.0 %copy-start.21 = (f32[16]{0:T(128)S(1)}, f32[16]{0:T(128)}, u32[]{:S(2)}) copy-start(f32[16]{0:T(128)} %param.28) | copy-start | bytes 196
  1.6 7.1 %copy-start.22 = (f32[16]{0:T(128)S(1)}, f32[16]{0:T(128)}, u32[]{:S(2)}) copy-start(f32[16]{0:T(128)} %param.29) | copy-start | bytes 196
  1.6 7.2 %copy-start.19 = (f32[128,8]{0,1:T(8,128)S(1)}, f32[128,8]{0,1:T(8,128)}, u32[]{:S(2)}) copy-start(f32[128,8]{0,1:T(8,128)} %param.26) | copy-start | bytes 12292
  2.5 7.2 %copy-start.20 = (f32[128,8]{0,1:T(8,128)S(1)}, f32[128,8]{0,1:T(8,128)}, u32[]{:S(2)}) copy-start(f32[128,8]{0,1:T(8,128)} %param.27) | copy-start | bytes 12292
  2.5 7.3 %copy-start.17 = (bf16[4,512]{1,0:T(4,128)(2,1)S(1)}, bf16[4,512]{1,0:T(4,128)(2,1)}, u32[]{:S(2)}) copy-start(bf16[4,512]{1,0:T(4,128)(2,1)} %param.23) | copy-start | bytes 12292
  2.5 7.9 %copy-start.18 = (bf16[4,512]{1,0:T(4,128)(2,1)S(1)}, bf16[4,512]{1,0:T(4,128)(2,1)}, u32[]{:S(2)}) copy-start(bf16[4,512]{1,0:T(4,128)(2,1)} %param.24) | copy-start | bytes 12292
  2.5 7.9 %copy-start.16 = (bf16[4,1024]{1,0:T(4,128)(2,1)S(1)}, bf16[4,1024]{1,0:T(4,128)(2,1)}, u32[]{:S(2)}) copy-start(bf16[4,1024]{1,0:T(4,128)(2,1)} %param.25) | copy-start | bytes 24580
  5.2 6.7 %collective-permute-start = (f32[3,2048]{1,0:T(4,128)S(1)}, f32[3,2048]{1,0:T(4,128)S(1)}, u32[]{:S(2)}, u32[]{:S(2)}) collective-permute-start(f32[3,2048]{1,0:T(4,128)S(1)} %pad_maximum_fusion.12), channel_id=1, source_target_pairs={{0,2},{2,4},{4,6},{6,8},{8,10},{10,12},{12,14},{14,16},{16,18},{18... | collective-permute-start | bytes 73736 | tf_op jit(solution)/shard_map/ppermute | solution.py:16
  8.6 5.2 %copy-start.14 = (pred[64,64]{1,0:T(8,128)(4,1)}, pred[64,64]{1,0:T(8,128)(4,1)S(1)}, u32[]{:S(2)}) copy-start(pred[64,64]{1,0:T(8,128)(4,1)S(1)} %get-tuple-element.61) | copy-start | bytes 12292
  13.8 8.9 %copy-start.3 = (f32[128,4,2,128]{3,0,2,1:T(8,128)}, f32[128,4,2,128]{3,0,2,1:T(8,128)S(1)}, u32[]{:S(2)}) copy-start(f32[128,4,2,128]{3,0,2,1:T(8,128)S(1)} %broadcast_in_dim.31) | copy-start | bytes 1572868
  28.3 12.1 %collective-permute-start.1 = (bf16[8,128,128]{2,1,0:T(8,128)(2,1)}, bf16[8,128,128]{2,1,0:T(8,128)(2,1)}, u32[]{:S(2)}, u32[]{:S(2)}) collective-permute-start(bf16[8,128,128]{2,1,0:T(8,128)(2,1)} %get-tuple-element.25), channel_id=1, source_target_pairs={{0,2},{2,4},{4,6},{6,8},{8,10},{10,12},{12,14},{14,16},{16,18},{18... | collective-permute-start | bytes 786440 | tf_op jit(solution)/shard_map/ppermute | solution.py:51
  32.0 17.1 %collective-permute-start.3 = (bf16[8,128,128]{2,1,0:T(8,128)(2,1)}, bf16[8,128,128]{2,1,0:T(8,128)(2,1)}, u32[]{:S(2)}, u32[]{:S(2)}) collective-permute-start(bf16[8,128,128]{2,1,0:T(8,128)(2,1)} %get-tuple-element.26), channel_id=1, source_target_pairs={{0,2},{2,4},{4,6},{6,8},{8,10},{10,12},{12,14},{14,16},{16,18},{18... | collective-permute-start | bytes 786440 | tf_op jit(solution)/shard_map/ppermute | solution.py:33
  46.2 7.6 %copy-start.7 = (f32[2,8,64,128]{3,2,1,0:T(8,128)}, f32[2,8,64,128]{3,2,1,0:T(8,128)S(1)}, u32[]{:S(2)}) copy-start(f32[2,8,64,128]{3,2,1,0:T(8,128)S(1)} %fusion.52) | copy-start | bytes 1572868
  47.8 9.9 %collective-permute-start.2 = (bf16[8,128,128]{2,1,0:T(8,128)(2,1)S(1)}, bf16[8,128,128]{2,1,0:T(8,128)(2,1)S(1)}, u32[]{:S(2)}, u32[]{:S(2)}) collective-permute-start(bf16[8,128,128]{2,1,0:T(8,128)(2,1)S(1)} %get-tuple-element.56), channel_id=1, source_target_pairs={{0,4},{2,6},{4,8},{6,10},{8,12},{10,14},{12,16},{14,18},{16,20},{1... | collective-permute-start | bytes 786440 | tf_op jit(solution)/shard_map/ppermute | solution.py:51
  50.8 9.8 %collective-permute-start.5 = (bf16[8,128,128]{2,1,0:T(8,128)(2,1)S(1)}, bf16[8,128,128]{2,1,0:T(8,128)(2,1)S(1)}, u32[]{:S(2)}, u32[]{:S(2)}) collective-permute-start(bf16[8,128,128]{2,1,0:T(8,128)(2,1)S(1)} %get-tuple-element.54), channel_id=1, source_target_pairs={{0,4},{2,6},{4,8},{6,10},{8,12},{10,14},{12,16},{14,18},{16,20},{1... | collective-permute-start | bytes 786440 | tf_op jit(solution)/shard_map/ppermute | solution.py:33
  53.9 6.7 %copy-start.9 = (f32[128,128]{1,0:T(8,128)S(1)}, f32[128,128]{1,0:T(8,128)}, u32[]{:S(2)}) copy-start(f32[128,128]{1,0:T(8,128)} %fusion.105) | copy-start | bytes 196612
  58.4 11.8 %collective-permute-start.4 = (bf16[8,128,128]{2,1,0:T(8,128)(2,1)S(1)}, bf16[8,128,128]{2,1,0:T(8,128)(2,1)S(1)}, u32[]{:S(2)}, u32[]{:S(2)}) collective-permute-start(bf16[8,128,128]{2,1,0:T(8,128)(2,1)S(1)} %fusion.101), channel_id=1, source_target_pairs={{0,8},{2,10},{4,12},{6,14},{8,16},{10,18},{12,20},{14,22},{16,24},... | collective-permute-start | bytes 786440 | tf_op jit(solution)/shard_map/ppermute | solution.py:51
  61.8 12.3 %collective-permute-start.7 = (bf16[8,128,128]{2,1,0:T(8,128)(2,1)S(1)}, bf16[8,128,128]{2,1,0:T(8,128)(2,1)S(1)}, u32[]{:S(2)}, u32[]{:S(2)}) collective-permute-start(bf16[8,128,128]{2,1,0:T(8,128)(2,1)S(1)} %get-tuple-element.23), channel_id=1, source_target_pairs={{0,8},{2,10},{4,12},{6,14},{8,16},{10,18},{12,20},{14,22},{16,24},... | collective-permute-start | bytes 786440 | tf_op jit(solution)/shard_map/ppermute | solution.py:33
  70.2 3.9 %copy-start.11 = (f32[128,128]{1,0:T(8,128)S(1)}, f32[128,128]{1,0:T(8,128)}, u32[]{:S(2)}) copy-start(f32[128,128]{1,0:T(8,128)} %fusion.104) | copy-start | bytes 196612
  70.9 4.5 %slice-start = ((f32[2,8,64,128]{3,2,1,0:T(8,128)}), f32[1,8,64,128]{3,2,1,0:T(8,128)S(1)}, s32[]{:S(2)}) async-start(f32[2,8,64,128]{3,2,1,0:T(8,128)} %copy-done.7), calls=%async_computation | async-start | bytes 524288 | tf_op jit(solution)/shard_map/slice | solution.py:248
  71.0 13.5 %collective-permute-start.6 = (bf16[8,128,128]{2,1,0:T(8,128)(2,1)S(1)}, bf16[8,128,128]{2,1,0:T(8,128)(2,1)S(1)}, u32[]{:S(2)}, u32[]{:S(2)}) collective-permute-start(bf16[8,128,128]{2,1,0:T(8,128)(2,1)S(1)} %fusion.43), channel_id=1, source_target_pairs={{0,16},{2,18},{4,20},{6,22},{8,24},{10,26},{12,28},{14,30},{1,17},... | collective-permute-start | bytes 786440 | tf_op jit(solution)/shard_map/ppermute | solution.py:51
  77.0 8.6 %copy-start.10 = (bf16[128,1024]{1,0:T(8,128)(2,1)S(1)}, bf16[128,1024]{1,0:T(8,128)(2,1)}, u32[]{:S(2)}) copy-start(bf16[128,1024]{1,0:T(8,128)(2,1)} %param.30) | copy-start | bytes 786436
  (8 other events, 12.4 us)

commit v16 on v15

--- a/solution.py
+++ b/solution.py
@@ -58,14 +58,8 @@
             if step + 1 < len(spans):
                 carried = product(inclusive_maps[step], earlier) + carried
         elif step + 1 < len(spans):
-            both = jnp.einsum(
-                "shde,hef->shdf",
-                jnp.stack([last_map, inclusive_maps[step]]),
-                earlier,
-                precision=HIGHEST,
-            )
-            state = state + both[0]
-            carried = both[1] + carried
+            carried = product(inclusive_maps[step], earlier) + carried
+            state = state + product(last_map, earlier)
         else:
             final_map, final_state = (last_map, earlier)
     return (state, final_map, final_state, rider)

time: 87.7 us -> 88.1 us (level)
    dot_general x2 -> x0, matrix products: 1.22 us -> none  [scan_states(): jnp.einsum('shde,hef->shdf', jnp.stack([last_map, inclusive_maps[step]]),...]
    unnamed x50 -> x56, local copies, waits for them, and re-layouts: 4.07 us -> 2.89 us
    convert_element_type x3 -> x0, other arithmetic: 1.08 us -> none  [scan_states(): earlier = lax.ppermute(carried.astype(jnp.bfloat16), axis, pairs)]
    reduce_sum x2, other arithmetic: 0.41 us -> 1.42 us  [unit_heads(): jnp.sum(shaped * shaped, axis=-1, keepdims=True) + EPSILON]
    another operation x1, other arithmetic: 0.99 us -> 0.04 us  [scan_states(): jnp.stack([last_map, inclusive])]
    mul x1, other arithmetic: 0.2 us -> 1.15 us  [shards(): query_rows = unit_heads(query_conv, head_width) * head_width ** (-0.5)]
    convert_element_type x1 -> x2, other arithmetic: 0.08 us -> 0.98 us  [scan_states(): earlier = lax.ppermute((inclusive - eye).astype(jnp.bfloat16), axis, pairs)]
    dot_general x3 -> x7, matrix products: 3.85 us -> 4.46 us  [product(): return jnp.einsum('hde,hef->hdf', left, right, precision=HIGHEST)]
  transfers between devices with their start and end apart: 8 -> 8, of which waited for: 7 -> 7; matrix products, arithmetic and copies ran while one was open for 23% -> 24% of each run, Pallas kernels for 0% -> 0%
where the time goes in v16:
time: 88.1 us; the launch traced here: 86.6 us
  waiting for transfers between devices  28.4 us (32%)
  matrix products  22.7 us (26%)
  starting transfers between devices  14.6 us (17%)
  other arithmetic  12.8 us (15%)
  local copies, waits for them, and re-layouts  7.16 us (8%)
  between operations  0.91 us (1%)
    ppermute x4, waiting for transfers between devices, scan_states(): earlier = lax.ppermute(carried.astype(jnp.bfloat16), axis, pairs)  24.5 us
    ppermute x4, starting transfers between devices, scan_states(): earlier = lax.ppermute(carried.astype(jnp.bfloat16), axis, pairs)  6.72 us
    dot_general x4, matrix products, unit_lower_inverse(): jnp.einsum('sbhij,sbhjk->sbhik', jnp.stack([inverse, power]), jnp.stack([...  4.73 us
    ppermute x3, starting transfers between devices, scan_states(): earlier = lax.ppermute((inclusive - eye).astype(jnp.bfloat16), axis, pairs)  4.49 us
    dot_general x7, matrix products, product(): return jnp.einsum('hde,hef->hdf', left, right, precision=HIGHEST)  4.46 us
    ppermute x1, starting transfers between devices, from_behind(): lax.ppermute(value, axis, [(source, source + steps) for source in range(f...  3.4 us
    unnamed x56, local copies, waits for them, and re-layouts  2.89 us
    ppermute x3, waiting for transfers between devices, scan_states(): earlier = lax.ppermute((inclusive - eye).astype(jnp.bfloat16), axis, pairs)  2.71 us
  transfers between devices with their start and end apart: 8, of which 7 were waited for; matrix products, arithmetic and copies ran while one was open for 24% of the time, Pallas kernels for 0%

profile of v16, /device:TPU:28, one launch (start us, length us, event | category | flops | bytes accessed | tf_op | source)
XLA Modules:
  0.0 86.6 jit_solution(6572159850269843431)
XLA Ops:
  3.7 3.4 %collective-permute-start = (f32[3,2048]{1,0:T(4,128)S(1)}, f32[3,2048]{1,0:T(4,128)S(1)}, u32[]{:S(2)}, u32[]{:S(2)}) collective-permute-start(f32[3,2048]{1,0:T(4,128)S(1)} %pad_maximum_fusion.9), channel_id=1, source_target_pairs={{0,2},{2,4},{4,6},{6,8},{8,10},{10,12},{12,14},{14,16},{16,18},{18... | collective-permute-start | bytes 73736 | tf_op jit(solution)/shard_map/ppermute | solution.py:16
  9.2 1.2 %collective-permute-done = f32[3,2048]{1,0:T(4,128)S(1)} collective-permute-done((f32[3,2048]{1,0:T(4,128)S(1)}, f32[3,2048]{1,0:T(4,128)S(1)}, u32[]{:S(2)}, u32[]{:S(2)}) %collective-permute-start) | collective-permute-done | bytes 24608 | tf_op jit(solution)/shard_map/ppermute | solution.py:16
  13.6 1.2 %fusion.6 = f32[2,2,8,64,64]{4,3,2,1,0:T(8,128)S(1)} fusion(f32[1,2,8,64,64]{4,3,2,1,0:T(8,128)S(1)} %bitcast.165, f32[1,2,8,64,64]{4,3,2,1,0:T(8,128)S(1)} %get-tuple-element.36, f32[1,2,8,64,64]{4,3,2,1,0:T(8,128)S(1)} %get-tuple-element.35), kind=kOutput, calls=%fused_computation.22 | convolution fusion | flops 100925440 | bytes 1310720 | tf_op jit(solution)/shard_map/sbhij,sbhjk->sbhik/dot_general | solution.py:111
  14.9 1.2 %fusion.12 = f32[2,2,8,64,64]{4,3,2,1,0:T(8,128)S(1)} fusion(f32[2,2,8,64,64]{4,3,2,1,0:T(8,128)S(1)} %fusion.6, f32[1,2,8,64,64]{4,3,2,1,0:T(8,128)S(1)} %get-tuple-element.30, f32[1,2,8,64,64]{4,3,2,1,0:T(8,128)S(1)} %get-tuple-element.29), kind=kOutput, calls=%fused_computation.30 | convolution fusion | flops 100794368 | bytes 1572864 | tf_op jit(solution)/shard_map/sbhij,sbhjk->sbhik/dot_general | solution.py:111
  16.2 1.2 %fusion.16 = f32[2,2,8,64,64]{4,3,2,1,0:T(8,128)S(1)} fusion(f32[2,2,8,64,64]{4,3,2,1,0:T(8,128)S(1)} %fusion.12, f32[1,2,8,64,64]{4,3,2,1,0:T(8,128)S(1)} %get-tuple-element.28, f32[1,2,8,64,64]{4,3,2,1,0:T(8,128)S(1)} %get-tuple-element.27), kind=kOutput, calls=%fused_computation.34 | convolution fusion | flops 100794368 | bytes 1572864 | tf_op jit(solution)/shard_map/sbhij,sbhjk->sbhik/dot_general | solution.py:111
  17.5 1.2 %fusion.20 = f32[2,2,8,64,64]{4,3,2,1,0:T(8,128)S(1)} fusion(f32[2,2,8,64,64]{4,3,2,1,0:T(8,128)S(1)} %fusion.16, f32[1,2,8,64,64]{4,3,2,1,0:T(8,128)S(1)} %get-tuple-element.26, f32[1,2,8,64,64]{4,3,2,1,0:T(8,128)S(1)} %get-tuple-element.25), kind=kOutput, calls=%fused_computation.38 | convolution fusion | flops 100794368 | bytes 1572864 | tf_op jit(solution)/shard_map/sbhij,sbhjk->sbhik/dot_general | solution.py:111
  21.2 2.3 %fusion.58 = f32[2,8,128,256]{3,2,1,0:T(8,128)S(1)} fusion(f32[2,8,64,256]{3,2,1,0:T(8,128)S(1)} %fusion.24, f32[2,64,8,128]{3,1,0,2:T(8,128)S(1)} %bitcast.168, f32[2,8,64]{2,1,0:T(8,128)S(1)} %get-tuple-element.39), kind=kOutput, calls=%fused_computation.94 | convolution fusion | flops 402784256 | bytes 3674112 | tf_op jit(solution)/shard_map/bhjd,bhje->bhde/dot_general | solution.py:143
  26.8 2.5 %collective-permute-start.1 = (bf16[8,128,128]{2,1,0:T(8,128)(2,1)}, bf16[8,128,128]{2,1,0:T(8,128)(2,1)}, u32[]{:S(2)}, u32[]{:S(2)}) collective-permute-start(bf16[8,128,128]{2,1,0:T(8,128)(2,1)} %get-tuple-element.24), channel_id=1, source_target_pairs={{0,2},{2,4},{4,6},{6,8},{8,10},{10,12},{12,14},{14,16},{16,18},{18... | collective-permute-start | bytes 786440 | tf_op jit(solution)/shard_map/ppermute | solution.py:51
  30.5 1.9 %collective-permute-start.2 = (bf16[8,128,128]{2,1,0:T(8,128)(2,1)}, bf16[8,128,128]{2,1,0:T(8,128)(2,1)S(1)}, u32[]{:S(2)}, u32[]{:S(2)}) collective-permute-start(bf16[8,128,128]{2,1,0:T(8,128)(2,1)} %get-tuple-element.23), channel_id=1, source_target_pairs={{0,2},{2,4},{4,6},{6,8},{8,10},{10,12},{12,14},{14,16},{16,18},{18... | collective-permute-start | bytes 786440 | tf_op jit(solution)/shard_map/ppermute | solution.py:33
  33.4 5.4 %collective-permute-done.1 = bf16[8,128,128]{2,1,0:T(8,128)(2,1)} collective-permute-done((bf16[8,128,128]{2,1,0:T(8,128)(2,1)}, bf16[8,128,128]{2,1,0:T(8,128)(2,1)}, u32[]{:S(2)}, u32[]{:S(2)}) %collective-permute-start.1) | collective-permute-done | bytes 262176 | tf_op jit(solution)/shard_map/ppermute | solution.py:51
  38.8 1.5 %multiply_convert_fusion.1 = bf16[128,512]{1,0:T(8,128)(2,1)} fusion(f32[131,512]{1,0:T(8,128)S(1)} %pad_maximum_fusion.7, f32[512]{0:T(512)} %bitcast.188, f32[512]{0:T(512)} %bitcast.189, f32[512]{0:T(512)} %bitcast.187, f32[512]{0:T(512)} %bitcast.186), kind=kLoop, calls=%fused_computation.153 | loop fusion | flops 786432 | bytes 1187840 | tf_op jit(solution)/shard_map/convert_element_type | solution.py:82
  40.3 1.7 %reshape.175 = f32[128,4,128]{2,1,0:T(4,128)} reshape(bf16[128,512]{1,0:T(8,128)(2,1)} %multiply_convert_fusion.1) | data formatting | bytes 393216 | tf_op jit(solution)/shard_map/reshape | solution.py:87
  42.0 1.2 %multiply_reduce_fusion.1 = f32[128,4]{1,0:T(8,128)S(1)} fusion(f32[128,4,128]{2,1,0:T(4,128)} %reshape.175), kind=kLoop, calls=%fused_computation.152 | loop fusion | flops 130560 | bytes 264192 | tf_op jit(solution)/shard_map/reduce_sum | solution.py:88
  46.2 1.6 %fusion.116 = (bf16[8,128,128]{2,1,0:T(8,128)(2,1)S(1)}, f32[8,128,128]{2,1,0:T(8,128)S(1)}) fusion(f32[8,128,256]{2,1,0:T(8,128)S(1)} %copy-done.6, f32[8,128,256]{2,1,0:T(8,128)S(1)} %copy-done.2, bf16[8,128,128]{2,1,0:T(8,128)(2,1)} %collective-permute-done.1), kind=kOutput, calls=%fused_computation.209 | convolution fusion | flops 201719808 | bytes 2621440 | tf_op jit(solution)/shard_map/hde,hef->hdf/dot_general | solution.py:160
  47.8 1.3 %collective-permute-start.3 = (bf16[8,128,128]{2,1,0:T(8,128)(2,1)S(1)}, bf16[8,128,128]{2,1,0:T(8,128)(2,1)S(1)}, u32[]{:S(2)}, u32[]{:S(2)}) collective-permute-start(bf16[8,128,128]{2,1,0:T(8,128)(2,1)S(1)} %get-tuple-element.52), channel_id=1, source_target_pairs={{0,4},{2,6},{4,8},{6,10},{8,12},{10,14},{12,16},{14,18},{16,20},{1... | collective-permute-start | bytes 786440 | tf_op jit(solution)/shard_map/ppermute | solution.py:51
  50.5 1.3 %collective-permute-start.4 = (bf16[8,128,128]{2,1,0:T(8,128)(2,1)S(1)}, bf16[8,128,128]{2,1,0:T(8,128)(2,1)S(1)}, u32[]{:S(2)}, u32[]{:S(2)}) collective-permute-start(bf16[8,128,128]{2,1,0:T(8,128)(2,1)S(1)} %get-tuple-element.56), channel_id=1, source_target_pairs={{0,4},{2,6},{4,8},{6,10},{8,12},{10,14},{12,16},{14,18},{16,20},{1... | collective-permute-start | bytes 786440 | tf_op jit(solution)/shard_map/ppermute | solution.py:33
  52.7 4.8 %collective-permute-done.3 = bf16[8,128,128]{2,1,0:T(8,128)(2,1)S(1)} collective-permute-done((bf16[8,128,128]{2,1,0:T(8,128)(2,1)S(1)}, bf16[8,128,128]{2,1,0:T(8,128)(2,1)S(1)}, u32[]{:S(2)}, u32[]{:S(2)}) %collective-permute-start.3) | collective-permute-done | bytes 262176 | tf_op jit(solution)/shard_map/ppermute | solution.py:51
  57.9 1.3 %collective-permute-start.5 = (bf16[8,128,128]{2,1,0:T(8,128)(2,1)S(1)}, bf16[8,128,128]{2,1,0:T(8,128)(2,1)S(1)}, u32[]{:S(2)}, u32[]{:S(2)}) collective-permute-start(bf16[8,128,128]{2,1,0:T(8,128)(2,1)S(1)} %get-tuple-element.54), channel_id=1, source_target_pairs={{0,8},{2,10},{4,12},{6,14},{8,16},{10,18},{12,20},{14,22},{16,24},... | collective-permute-start | bytes 786440 | tf_op jit(solution)/shard_map/ppermute | solution.py:51
  61.5 1.3 %collective-permute-start.7 = (bf16[8,128,128]{2,1,0:T(8,128)(2,1)S(1)}, bf16[8,128,128]{2,1,0:T(8,128)(2,1)S(1)}, u32[]{:S(2)}, u32[]{:S(2)}) collective-permute-start(bf16[8,128,128]{2,1,0:T(8,128)(2,1)S(1)} %subtract_convert_fusion), channel_id=1, source_target_pairs={{0,8},{2,10},{4,12},{6,14},{8,16},{10,18},{12,20},{14,22},{16,24},... | collective-permute-start | bytes 786440 | tf_op jit(solution)/shard_map/ppermute | solution.py:33
  63.2 7.2 %collective-permute-done.5 = bf16[8,128,128]{2,1,0:T(8,128)(2,1)S(1)} collective-permute-done((bf16[8,128,128]{2,1,0:T(8,128)(2,1)S(1)}, bf16[8,128,128]{2,1,0:T(8,128)(2,1)S(1)}, u32[]{:S(2)}, u32[]{:S(2)}) %collective-permute-start.5) | collective-permute-done | bytes 262176 | tf_op jit(solution)/shard_map/ppermute | solution.py:51
  70.8 1.6 %collective-permute-start.6 = (bf16[8,128,128]{2,1,0:T(8,128)(2,1)S(1)}, bf16[8,128,128]{2,1,0:T(8,128)(2,1)S(1)}, u32[]{:S(2)}, u32[]{:S(2)}) collective-permute-start(bf16[8,128,128]{2,1,0:T(8,128)(2,1)S(1)} %fusion.5), channel_id=1, source_target_pairs={{0,16},{2,18},{4,20},{6,22},{8,24},{10,26},{12,28},{14,30},{1,17},... | collective-permute-start | bytes 786440 | tf_op jit(solution)/shard_map/ppermute | solution.py:51
  72.4 1.6 %collective-permute-done.7 = bf16[8,128,128]{2,1,0:T(8,128)(2,1)S(1)} collective-permute-done((bf16[8,128,128]{2,1,0:T(8,128)(2,1)S(1)}, bf16[8,128,128]{2,1,0:T(8,128)(2,1)S(1)}, u32[]{:S(2)}, u32[]{:S(2)}) %collective-permute-start.7) | collective-permute-done | bytes 262176 | tf_op jit(solution)/shard_map/ppermute | solution.py:33
  75.7 1.6 %fusion.2 = f32[2,8,64,128]{3,2,1,0:T(8,128)S(1)} fusion(f32[1,8,64,128]{3,2,1,0:T(8,128)S(1)} %get-tuple-element.32, f32[1,8,64,128]{3,2,1,0:T(8,128)S(1)} %slice-done, f32[8,128,128]{2,1,0:T(8,128)S(1)} %fusion.71, f32[8,128,128]{2,1,0:T(8,128)S(1)} %fusion.68, bf16[8,128,128]{2,1,0:T(8,128)(2,1)} %collective-permute-done.1, ...), kind=kOutput, calls=%fused_computation.15 | convolution fusion | flops 202113024 | bytes 2883584 | tf_op jit(solution)/shard_map/bhid,hde->bhie/dot_general | solution.py:248
  77.4 7.1 %collective-permute-done.6 = bf16[8,128,128]{2,1,0:T(8,128)(2,1)S(1)} collective-permute-done((bf16[8,128,128]{2,1,0:T(8,128)(2,1)S(1)}, bf16[8,128,128]{2,1,0:T(8,128)(2,1)S(1)}, u32[]{:S(2)}, u32[]{:S(2)}) %collective-permute-start.6) | collective-permute-done | bytes 262176 | tf_op jit(solution)/shard_map/ppermute | solution.py:51
  (143 shorter events, 29.2 us)
Async XLA Ops:
  0.0 8.9 %copy-start = (f32[128]{0:T(128)S(1)}, f32[128]{0:T(128)}, u32[]{:S(2)}) copy-start(f32[128]{0:T(128)} %param.31) | copy-start | bytes 1540
  0.0 3.6 %copy-start.13 = (bf16[128,512]{1,0:T(8,128)(2,1)S(1)}, bf16[128,512]{1,0:T(8,128)(2,1)}, u32[]{:S(2)}) copy-start(bf16[128,512]{1,0:T(8,128)(2,1)} %param.17) | copy-start | bytes 393220
  1.6 5.5 %copy-start.19 = (bf16[4,512]{1,0:T(4,128)(2,1)S(1)}, bf16[4,512]{1,0:T(4,128)(2,1)}, u32[]{:S(2)}) copy-start(bf16[4,512]{1,0:T(4,128)(2,1)} %param.24) | copy-start | bytes 12292
  1.6 5.6 %copy-start.21 = (f32[128,8]{0,1:T(8,128)S(1)}, f32[128,8]{0,1:T(8,128)}, u32[]{:S(2)}) copy-start(f32[128,8]{0,1:T(8,128)} %param.27) | copy-start | bytes 12292
  1.7 5.6 %copy-start.24 = (f32[16]{0:T(128)S(1)}, f32[16]{0:T(128)}, u32[]{:S(2)}) copy-start(f32[16]{0:T(128)} %param.29) | copy-start | bytes 196
  1.7 5.7 %copy-start.25 = (f32[16]{0:T(128)S(1)}, f32[16]{0:T(128)}, u32[]{:S(2)}) copy-start(f32[16]{0:T(128)} %param.28) | copy-start | bytes 196
  1.7 5.8 %copy-start.22 = (f32[128,8]{0,1:T(8,128)S(1)}, f32[128,8]{0,1:T(8,128)}, u32[]{:S(2)}) copy-start(f32[128,8]{0,1:T(8,128)} %param.26) | copy-start | bytes 12292
  1.7 5.9 %copy-start.18 = (bf16[4,1024]{1,0:T(4,128)(2,1)S(1)}, bf16[4,1024]{1,0:T(4,128)(2,1)}, u32[]{:S(2)}) copy-start(bf16[4,1024]{1,0:T(4,128)(2,1)} %param.25) | copy-start | bytes 24580
  1.7 6.6 %copy-start.20 = (bf16[4,512]{1,0:T(4,128)(2,1)S(1)}, bf16[4,512]{1,0:T(4,128)(2,1)}, u32[]{:S(2)}) copy-start(bf16[4,512]{1,0:T(4,128)(2,1)} %param.23) | copy-start | bytes 12292
  3.7 6.7 %collective-permute-start = (f32[3,2048]{1,0:T(4,128)S(1)}, f32[3,2048]{1,0:T(4,128)S(1)}, u32[]{:S(2)}, u32[]{:S(2)}) collective-permute-start(f32[3,2048]{1,0:T(4,128)S(1)} %pad_maximum_fusion.9), channel_id=1, source_target_pairs={{0,2},{2,4},{4,6},{6,8},{8,10},{10,12},{12,14},{14,16},{16,18},{18... | collective-permute-start | bytes 73736 | tf_op jit(solution)/shard_map/ppermute | solution.py:16
  7.1 5.7 %copy-start.16 = (pred[64,64]{1,0:T(8,128)(4,1)}, pred[64,64]{1,0:T(8,128)(4,1)S(1)}, u32[]{:S(2)}) copy-start(pred[64,64]{1,0:T(8,128)(4,1)S(1)} %get-tuple-element.61) | copy-start | bytes 12292
  11.8 9.4 %copy-start.3 = (f32[128,4,2,128]{3,0,2,1:T(8,128)}, f32[128,4,2,128]{3,0,2,1:T(8,128)S(1)}, u32[]{:S(2)}) copy-start(f32[128,4,2,128]{3,0,2,1:T(8,128)S(1)} %broadcast_in_dim.31) | copy-start | bytes 1572868
  26.8 12.1 %collective-permute-start.1 = (bf16[8,128,128]{2,1,0:T(8,128)(2,1)}, bf16[8,128,128]{2,1,0:T(8,128)(2,1)}, u32[]{:S(2)}, u32[]{:S(2)}) collective-permute-start(bf16[8,128,128]{2,1,0:T(8,128)(2,1)} %get-tuple-element.24), channel_id=1, source_target_pairs={{0,2},{2,4},{4,6},{6,8},{8,10},{10,12},{12,14},{14,16},{16,18},{18... | collective-permute-start | bytes 786440 | tf_op jit(solution)/shard_map/ppermute | solution.py:51
  30.5 19.3 %collective-permute-start.2 = (bf16[8,128,128]{2,1,0:T(8,128)(2,1)}, bf16[8,128,128]{2,1,0:T(8,128)(2,1)S(1)}, u32[]{:S(2)}, u32[]{:S(2)}) collective-permute-start(bf16[8,128,128]{2,1,0:T(8,128)(2,1)} %get-tuple-element.23), channel_id=1, source_target_pairs={{0,2},{2,4},{4,6},{6,8},{8,10},{10,12},{12,14},{14,16},{16,18},{18... | collective-permute-start | bytes 786440 | tf_op jit(solution)/shard_map/ppermute | solution.py:33
  46.2 6.4 %copy-start.7 = (f32[2,8,64,128]{3,2,1,0:T(8,128)}, f32[2,8,64,128]{3,2,1,0:T(8,128)S(1)}, u32[]{:S(2)}) copy-start(f32[2,8,64,128]{3,2,1,0:T(8,128)S(1)} %fusion.45) | copy-start | bytes 1572868
  47.8 9.7 %collective-permute-start.3 = (bf16[8,128,128]{2,1,0:T(8,128)(2,1)S(1)}, bf16[8,128,128]{2,1,0:T(8,128)(2,1)S(1)}, u32[]{:S(2)}, u32[]{:S(2)}) collective-permute-start(bf16[8,128,128]{2,1,0:T(8,128)(2,1)S(1)} %get-tuple-element.52), channel_id=1, source_target_pairs={{0,4},{2,6},{4,8},{6,10},{8,12},{10,14},{12,16},{14,18},{16,20},{1... | collective-permute-start | bytes 786440 | tf_op jit(solution)/shard_map/ppermute | solution.py:51
  50.5 9.8 %collective-permute-start.4 = (bf16[8,128,128]{2,1,0:T(8,128)(2,1)S(1)}, bf16[8,128,128]{2,1,0:T(8,128)(2,1)S(1)}, u32[]{:S(2)}, u32[]{:S(2)}) collective-permute-start(bf16[8,128,128]{2,1,0:T(8,128)(2,1)S(1)} %get-tuple-element.56), channel_id=1, source_target_pairs={{0,4},{2,6},{4,8},{6,10},{8,12},{10,14},{12,16},{14,18},{16,20},{1... | collective-permute-start | bytes 786440 | tf_op jit(solution)/shard_map/ppermute | solution.py:33
  52.6 7.7 %copy-start.9 = (f32[128,128]{1,0:T(8,128)S(1)}, f32[128,128]{1,0:T(8,128)}, u32[]{:S(2)}) copy-start(f32[128,128]{1,0:T(8,128)} %fusion.100) | copy-start | bytes 196612
  57.9 12.4 %collective-permute-start.5 = (bf16[8,128,128]{2,1,0:T(8,128)(2,1)S(1)}, bf16[8,128,128]{2,1,0:T(8,128)(2,1)S(1)}, u32[]{:S(2)}, u32[]{:S(2)}) collective-permute-start(bf16[8,128,128]{2,1,0:T(8,128)(2,1)S(1)} %get-tuple-element.54), channel_id=1, source_target_pairs={{0,8},{2,10},{4,12},{6,14},{8,16},{10,18},{12,20},{14,22},{16,24},... | collective-permute-start | bytes 786440 | tf_op jit(solution)/shard_map/ppermute | solution.py:51
  61.4 12.6 %copy-start.11 = (f32[128,128]{1,0:T(8,128)S(1)}, f32[128,128]{1,0:T(8,128)}, u32[]{:S(2)}) copy-start(f32[128,128]{1,0:T(8,128)} %fusion.99) | copy-start | bytes 196612
  61.5 12.5 %collective-permute-start.7 = (bf16[8,128,128]{2,1,0:T(8,128)(2,1)S(1)}, bf16[8,128,128]{2,1,0:T(8,128)(2,1)S(1)}, u32[]{:S(2)}, u32[]{:S(2)}) collective-permute-start(bf16[8,128,128]{2,1,0:T(8,128)(2,1)S(1)} %subtract_convert_fusion), channel_id=1, source_target_pairs={{0,8},{2,10},{4,12},{6,14},{8,16},{10,18},{12,20},{14,22},{16,24},... | collective-permute-start | bytes 786440 | tf_op jit(solution)/shard_map/ppermute | solution.py:33
  70.7 5.0 %slice-start = ((f32[2,8,64,128]{3,2,1,0:T(8,128)}), f32[1,8,64,128]{3,2,1,0:T(8,128)S(1)}, s32[]{:S(2)}) async-start(f32[2,8,64,128]{3,2,1,0:T(8,128)} %copy-done.7), calls=%async_computation | async-start | bytes 524288 | tf_op jit(solution)/shard_map/slice | solution.py:242
  70.8 13.7 %collective-permute-start.6 = (bf16[8,128,128]{2,1,0:T(8,128)(2,1)S(1)}, bf16[8,128,128]{2,1,0:T(8,128)(2,1)S(1)}, u32[]{:S(2)}, u32[]{:S(2)}) collective-permute-start(bf16[8,128,128]{2,1,0:T(8,128)(2,1)S(1)} %fusion.5), channel_id=1, source_target_pairs={{0,16},{2,18},{4,20},{6,22},{8,24},{10,26},{12,28},{14,30},{1,17},... | collective-permute-start | bytes 786440 | tf_op jit(solution)/shard_map/ppermute | solution.py:51
  77.4 8.2 %copy-start.10 = (bf16[128,1024]{1,0:T(8,128)(2,1)S(1)}, bf16[128,1024]{1,0:T(8,128)(2,1)}, u32[]{:S(2)}) copy-start(bf16[128,1024]{1,0:T(8,128)(2,1)} %param.30) | copy-start | bytes 786436
  (11 other events, 27.9 us)

commit v17 on v15

--- a/solution.py
+++ b/solution.py
@@ -251,12 +251,25 @@
         read_maps.append(read[..., :key_width])
         local_outs.append(zero_out[block] + read[..., key_width:])
     reads = jnp.stack(read_maps)
-    outputs = jnp.stack(local_outs) + jnp.einsum(
-        "bhid,hde->bhie", reads, incoming, precision=HIGHEST
-    )
-    if final_map is not None:
-        lead = jnp.einsum("bhid,hde->bhie", reads, final_map, precision=HIGHEST)
-        outputs = outputs + jnp.einsum("bhid,hde->bhie", lead, final_state, precision=HIGHEST)
+    state_width = incoming.shape[-1]
+    if final_map is None:
+        outputs = jnp.stack(local_outs) + jnp.einsum(
+            "bhid,hde->bhie", reads, incoming, precision=HIGHEST
+        )
+    else:
+        both = jnp.einsum(
+            "bhid,hde->bhie",
+            reads,
+            jnp.concatenate([incoming, final_map], axis=-1),
+            precision=HIGHEST,
+        )
+        outputs = (
+            jnp.stack(local_outs)
+            + both[..., :state_width]
+            + jnp.einsum(
+                "bhid,hde->bhie", both[..., state_width:], final_state, precision=HIGHEST
+            )
+        )
     gated_rows = gated_norm(to_rows(outputs), output_gate, norm_gain)
     return gated_rows
 

time: 87.7 us -> 87.5 us (level)
  other arithmetic: 12.6 us -> 13.7 us
  matrix products: 23.2 us -> 22.1 us
    dot_general x3 -> x2, matrix products: 2.78 us -> 1.66 us  [the longest x1 1.09 us: shards(): jnp.einsum('bhid,hde->bhie', reads, jnp.concatenate([incoming, final_map]...]
    convert_element_type x3, other arithmetic: 1.08 us -> 2.17 us  [scan_states(): earlier = lax.ppermute(carried.astype(jnp.bfloat16), axis, pairs)]
    ppermute x4, waiting for transfers between devices: 24.1 us -> 25.2 us  [scan_states(): earlier = lax.ppermute(carried.astype(jnp.bfloat16), axis, pairs)]
    ppermute x3, waiting for transfers between devices: 2.46 us -> 1.46 us  [scan_states(): earlier = lax.ppermute((inclusive - eye).astype(jnp.bfloat16), axis, pairs)]
    unnamed x50 -> x52, local copies, waits for them, and re-layouts: 4.07 us -> 4.07 us
where the time goes in v17:
time: 87.5 us; the launch traced here: 86.9 us
  waiting for transfers between devices  27.9 us (32%)
  matrix products  22.1 us (25%)
  starting transfers between devices  14.6 us (17%)
  other arithmetic  13.7 us (16%)
  local copies, waits for them, and re-layouts  7.65 us (9%)
  between operations  0.89 us (1%)
    ppermute x4, waiting for transfers between devices, scan_states(): earlier = lax.ppermute(carried.astype(jnp.bfloat16), axis, pairs)  25.2 us
    ppermute x4, starting transfers between devices, scan_states(): earlier = lax.ppermute(carried.astype(jnp.bfloat16), axis, pairs)  6.72 us
    dot_general x4, matrix products, unit_lower_inverse(): jnp.einsum('sbhij,sbhjk->sbhik', jnp.stack([inverse, power]), jnp.stack([...  4.72 us
    ppermute x3, starting transfers between devices, scan_states(): earlier = lax.ppermute((inclusive - eye).astype(jnp.bfloat16), axis, pairs)  4.49 us
    unnamed x52, local copies, waits for them, and re-layouts  4.07 us
    dot_general x3, matrix products, product(): return jnp.einsum('hde,hef->hdf', left, right, precision=HIGHEST)  3.89 us
    ppermute x1, starting transfers between devices, from_behind(): lax.ppermute(value, axis, [(source, source + steps) for source in range(f...  3.4 us
    dot_general x1, matrix products, block_maps(): faded = jnp.einsum('bhjd,bhje->bhde', fading, solved, precision=HIGHEST)  2.3 us
  transfers between devices with their start and end apart: 8, of which 7 were waited for; matrix products, arithmetic and copies ran while one was open for 23% of the time, Pallas kernels for 0%

profile of v17, /device:TPU:28, one launch (start us, length us, event | category | flops | bytes accessed | tf_op | source)
XLA Modules:
  0.0 86.9 jit_solution(8183319269265574766)
XLA Ops:
  5.2 3.4 %collective-permute-start = (f32[3,2048]{1,0:T(4,128)S(1)}, f32[3,2048]{1,0:T(4,128)S(1)}, u32[]{:S(2)}, u32[]{:S(2)}) collective-permute-start(f32[3,2048]{1,0:T(4,128)S(1)} %pad_maximum_fusion.11), channel_id=1, source_target_pairs={{0,2},{2,4},{4,6},{6,8},{8,10},{10,12},{12,14},{14,16},{16,18},{18... | collective-permute-start | bytes 73736 | tf_op jit(solution)/shard_map/ppermute | solution.py:16
  10.6 1.2 %collective-permute-done = f32[3,2048]{1,0:T(4,128)S(1)} collective-permute-done((f32[3,2048]{1,0:T(4,128)S(1)}, f32[3,2048]{1,0:T(4,128)S(1)}, u32[]{:S(2)}, u32[]{:S(2)}) %collective-permute-start) | collective-permute-done | bytes 24608 | tf_op jit(solution)/shard_map/ppermute | solution.py:16
  15.5 1.2 %fusion.4 = f32[2,2,8,64,64]{4,3,2,1,0:T(8,128)S(1)} fusion(f32[1,2,8,64,64]{4,3,2,1,0:T(8,128)S(1)} %bitcast.186, f32[1,2,8,64,64]{4,3,2,1,0:T(8,128)S(1)} %get-tuple-element.40, f32[1,2,8,64,64]{4,3,2,1,0:T(8,128)S(1)} %get-tuple-element.39), kind=kOutput, calls=%fused_computation.18 | convolution fusion | flops 100925440 | bytes 1310720 | tf_op jit(solution)/shard_map/sbhij,sbhjk->sbhik/dot_general | solution.py:117
  16.9 1.2 %fusion.10 = f32[2,2,8,64,64]{4,3,2,1,0:T(8,128)S(1)} fusion(f32[2,2,8,64,64]{4,3,2,1,0:T(8,128)S(1)} %fusion.4, f32[1,2,8,64,64]{4,3,2,1,0:T(8,128)S(1)} %get-tuple-element.34, f32[1,2,8,64,64]{4,3,2,1,0:T(8,128)S(1)} %get-tuple-element.33), kind=kOutput, calls=%fused_computation.26 | convolution fusion | flops 100794368 | bytes 1572864 | tf_op jit(solution)/shard_map/sbhij,sbhjk->sbhik/dot_general | solution.py:117
  18.2 1.2 %fusion.14 = f32[2,2,8,64,64]{4,3,2,1,0:T(8,128)S(1)} fusion(f32[2,2,8,64,64]{4,3,2,1,0:T(8,128)S(1)} %fusion.10, f32[1,2,8,64,64]{4,3,2,1,0:T(8,128)S(1)} %get-tuple-element.32, f32[1,2,8,64,64]{4,3,2,1,0:T(8,128)S(1)} %get-tuple-element.31), kind=kOutput, calls=%fused_computation.30 | convolution fusion | flops 100794368 | bytes 1572864 | tf_op jit(solution)/shard_map/sbhij,sbhjk->sbhik/dot_general | solution.py:117
  19.5 1.2 %fusion.18 = f32[2,2,8,64,64]{4,3,2,1,0:T(8,128)S(1)} fusion(f32[2,2,8,64,64]{4,3,2,1,0:T(8,128)S(1)} %fusion.14, f32[1,2,8,64,64]{4,3,2,1,0:T(8,128)S(1)} %get-tuple-element.30, f32[1,2,8,64,64]{4,3,2,1,0:T(8,128)S(1)} %get-tuple-element.29), kind=kOutput, calls=%fused_computation.34 | convolution fusion | flops 100794368 | bytes 1572864 | tf_op jit(solution)/shard_map/sbhij,sbhjk->sbhik/dot_general | solution.py:117
  23.7 2.3 %fusion.68 = f32[2,8,128,256]{3,2,1,0:T(8,128)S(1)} fusion(f32[2,8,64,256]{3,2,1,0:T(8,128)S(1)} %fusion.22, f32[2,64,8,128]{3,1,0,2:T(8,128)S(1)} %bitcast.189, f32[2,8,64]{2,1,0:T(8,128)S(1)} %get-tuple-element.43), kind=kOutput, calls=%fused_computation.107 | convolution fusion | flops 402784256 | bytes 3674112 | tf_op jit(solution)/shard_map/bhjd,bhje->bhde/dot_general | solution.py:149
  28.2 2.5 %collective-permute-start.1 = (bf16[8,128,128]{2,1,0:T(8,128)(2,1)}, bf16[8,128,128]{2,1,0:T(8,128)(2,1)}, u32[]{:S(2)}, u32[]{:S(2)}) collective-permute-start(bf16[8,128,128]{2,1,0:T(8,128)(2,1)} %get-tuple-element.27), channel_id=1, source_target_pairs={{0,2},{2,4},{4,6},{6,8},{8,10},{10,12},{12,14},{14,16},{16,18},{18... | collective-permute-start | bytes 786440 | tf_op jit(solution)/shard_map/ppermute | solution.py:51
  32.0 1.9 %collective-permute-start.3 = (bf16[8,128,128]{2,1,0:T(8,128)(2,1)}, bf16[8,128,128]{2,1,0:T(8,128)(2,1)}, u32[]{:S(2)}, u32[]{:S(2)}) collective-permute-start(bf16[8,128,128]{2,1,0:T(8,128)(2,1)} %get-tuple-element.28), channel_id=1, source_target_pairs={{0,2},{2,4},{4,6},{6,8},{8,10},{10,12},{12,14},{14,16},{16,18},{18... | collective-permute-start | bytes 786440 | tf_op jit(solution)/shard_map/ppermute | solution.py:33
  34.7 5.7 %collective-permute-done.1 = bf16[8,128,128]{2,1,0:T(8,128)(2,1)} collective-permute-done((bf16[8,128,128]{2,1,0:T(8,128)(2,1)}, bf16[8,128,128]{2,1,0:T(8,128)(2,1)}, u32[]{:S(2)}, u32[]{:S(2)}) %collective-permute-start.1) | collective-permute-done | bytes 262176 | tf_op jit(solution)/shard_map/ppermute | solution.py:51
  40.4 1.5 %multiply_convert_fusion.1 = bf16[128,512]{1,0:T(8,128)(2,1)} fusion(f32[131,512]{1,0:T(8,128)S(1)} %pad_maximum_fusion.9, f32[512]{0:T(512)} %bitcast.211, f32[512]{0:T(512)} %bitcast.212, f32[512]{0:T(512)} %bitcast.210, f32[512]{0:T(512)} %bitcast.209), kind=kLoop, calls=%fused_computation.160 | loop fusion | flops 786432 | bytes 1187840 | tf_op jit(solution)/shard_map/convert_element_type | solution.py:88
  46.3 1.6 %fusion.126 = (bf16[8,128,128]{2,1,0:T(8,128)(2,1)S(1)}, f32[8,128,128]{2,1,0:T(8,128)S(1)}) fusion(f32[8,128,256]{2,1,0:T(8,128)S(1)} %copy-done.6, f32[8,128,256]{2,1,0:T(8,128)S(1)} %fusion.53, bf16[8,128,128]{2,1,0:T(8,128)(2,1)} %collective-permute-done.1), kind=kOutput, calls=%fused_computation.223 | convolution fusion | flops 201719808 | bytes 2621440 | tf_op jit(solution)/shard_map/hde,hef->hdf/dot_general | solution.py:166
  47.8 1.3 %collective-permute-start.2 = (bf16[8,128,128]{2,1,0:T(8,128)(2,1)S(1)}, bf16[8,128,128]{2,1,0:T(8,128)(2,1)S(1)}, u32[]{:S(2)}, u32[]{:S(2)}) collective-permute-start(bf16[8,128,128]{2,1,0:T(8,128)(2,1)S(1)} %get-tuple-element.58), channel_id=1, source_target_pairs={{0,4},{2,6},{4,8},{6,10},{8,12},{10,14},{12,16},{14,18},{16,20},{1... | collective-permute-start | bytes 786440 | tf_op jit(solution)/shard_map/ppermute | solution.py:51
  49.2 1.7 %subtract_convert_fusion.1 = (bf16[8,128,128]{2,1,0:T(8,128)(2,1)S(1)}, f32[8,128,128]{2,1,0:T(8,128)S(1)}) fusion(f32[128,128]{1,0:T(8,128)S(1)} %fusion.107, f32[8,128,256]{2,1,0:T(8,128)S(1)} %fusion.53, bf16[8,128,128]{2,1,0:T(8,128)(2,1)} %collective-permute-done.3, f32[128,128]{1,0:T(8,128)S(1)} %fusion.106, pred[]{:T(512)S(6)} %ge.39), kind=kOutput, calls=%fused_computation.115 | convolution fusion | flops 201981952 | bytes 2228225 | tf_op jit(solution)/shard_map/hde,hef->hdf/dot_general | solution.py:166
  50.8 1.3 %collective-permute-start.5 = (bf16[8,128,128]{2,1,0:T(8,128)(2,1)S(1)}, bf16[8,128,128]{2,1,0:T(8,128)(2,1)S(1)}, u32[]{:S(2)}, u32[]{:S(2)}) collective-permute-start(bf16[8,128,128]{2,1,0:T(8,128)(2,1)S(1)} %get-tuple-element.56), channel_id=1, source_target_pairs={{0,4},{2,6},{4,8},{6,10},{8,12},{10,14},{12,16},{14,18},{16,20},{1... | collective-permute-start | bytes 786440 | tf_op jit(solution)/shard_map/ppermute | solution.py:33
  53.9 3.8 %collective-permute-done.2 = bf16[8,128,128]{2,1,0:T(8,128)(2,1)S(1)} collective-permute-done((bf16[8,128,128]{2,1,0:T(8,128)(2,1)S(1)}, bf16[8,128,128]{2,1,0:T(8,128)(2,1)S(1)}, u32[]{:S(2)}, u32[]{:S(2)}) %collective-permute-start.2) | collective-permute-done | bytes 262176 | tf_op jit(solution)/shard_map/ppermute | solution.py:51
  58.4 1.3 %collective-permute-start.4 = (bf16[8,128,128]{2,1,0:T(8,128)(2,1)S(1)}, bf16[8,128,128]{2,1,0:T(8,128)(2,1)S(1)}, u32[]{:S(2)}, u32[]{:S(2)}) collective-permute-start(bf16[8,128,128]{2,1,0:T(8,128)(2,1)S(1)} %fusion.101), channel_id=1, source_target_pairs={{0,8},{2,10},{4,12},{6,14},{8,16},{10,18},{12,20},{14,22},{16,24},... | collective-permute-start | bytes 786440 | tf_op jit(solution)/shard_map/ppermute | solution.py:51
  60.6 1.0 %convolution_bitcast_fusion.3 = f32[2,8,128,128]{3,2,1,0:T(8,128)S(1)} fusion(f32[1,8,128,128]{3,2,1,0:T(8,128)S(1)} %bitcast.192, f32[1,8,128,128]{3,2,1,0:T(8,128)S(1)} %fusion.73, bf16[8,128,128]{2,1,0:T(8,128)(2,1)S(1)} %collective-permute-done.5, f32[128,128]{1,0:T(8,128)S(1)} %copy-done.10), kind=kOutput, calls=%fused_computation.5 | convolution fusion | flops 403177472 | bytes 2424832 | tf_op jit(solution)/shard_map/shde,hef->shdf/dot_general | solution.py:41
  61.8 1.3 %collective-permute-start.6 = (bf16[8,128,128]{2,1,0:T(8,128)(2,1)S(1)}, bf16[8,128,128]{2,1,0:T(8,128)(2,1)S(1)}, u32[]{:S(2)}, u32[]{:S(2)}) collective-permute-start(bf16[8,128,128]{2,1,0:T(8,128)(2,1)S(1)} %get-tuple-element.26), channel_id=1, source_target_pairs={{0,8},{2,10},{4,12},{6,14},{8,16},{10,18},{12,20},{14,22},{16,24},... | collective-permute-start | bytes 786440 | tf_op jit(solution)/shard_map/ppermute | solution.py:33
  63.1 7.1 %collective-permute-done.4 = bf16[8,128,128]{2,1,0:T(8,128)(2,1)S(1)} collective-permute-done((bf16[8,128,128]{2,1,0:T(8,128)(2,1)S(1)}, bf16[8,128,128]{2,1,0:T(8,128)(2,1)S(1)}, u32[]{:S(2)}, u32[]{:S(2)}) %collective-permute-start.4) | collective-permute-done | bytes 262176 | tf_op jit(solution)/shard_map/ppermute | solution.py:51
  70.8 1.2 %fusion.45 = (bf16[8,128,128]{2,1,0:T(8,128)(2,1)S(1)}, f32[8,128,128]{2,1,0:T(8,128)S(1)}) fusion(f32[2,8,128,128]{3,2,1,0:T(8,128)S(1)} %convolution_bitcast_fusion, f32[8,128,128]{2,1,0:T(8,128)S(1)} %get-tuple-element.59, f32[2,8,128,128]{3,2,1,0:T(8,128)S(1)} %convolution_bitcast_fusion.1, bf16[8,128,128]{2,1,0:T(8,128)(2,1)} %collective-permute-done.1), kind=kLoop, calls=%fused_computation.72 | loop fusion | flops 786432 | bytes 3670016 | tf_op jit(solution)/shard_map/convert_element_type | solution.py:51
  72.0 1.6 %collective-permute-start.7 = (bf16[8,128,128]{2,1,0:T(8,128)(2,1)S(1)}, bf16[8,128,128]{2,1,0:T(8,128)(2,1)S(1)}, u32[]{:S(2)}, u32[]{:S(2)}) collective-permute-start(bf16[8,128,128]{2,1,0:T(8,128)(2,1)S(1)} %get-tuple-element.21), channel_id=1, source_target_pairs={{0,16},{2,18},{4,20},{6,22},{8,24},{10,26},{12,28},{14,30},{1,17},... | collective-permute-start | bytes 786440 | tf_op jit(solution)/shard_map/ppermute | solution.py:51
  75.0 1.1 %convolution_bitcast_fusion.2 = f32[2,8,64,256]{3,2,1,0:T(8,128)S(1)} fusion(f32[8,128,128]{2,1,0:T(8,128)S(1)} %fusion.62, f32[8,128,128]{2,1,0:T(8,128)S(1)} %get-tuple-element.22, f32[1,8,64,128]{3,2,1,0:T(8,128)S(1)} %get-tuple-element.36, f32[1,8,64,128]{3,2,1,0:T(8,128)S(1)} %slice-done.1), kind=kOutput, calls=%fused_computation.4 | convolution fusion | flops 403046400 | bytes 2621440 | tf_op jit(solution)/shard_map/bhid,hde->bhie/dot_general | solution.py:260
  76.1 8.6 %collective-permute-done.7 = bf16[8,128,128]{2,1,0:T(8,128)(2,1)S(1)} collective-permute-done((bf16[8,128,128]{2,1,0:T(8,128)(2,1)S(1)}, bf16[8,128,128]{2,1,0:T(8,128)(2,1)S(1)}, u32[]{:S(2)}, u32[]{:S(2)}) %collective-permute-start.7) | collective-permute-done | bytes 262176 | tf_op jit(solution)/shard_map/ppermute | solution.py:51
  (140 shorter events, 29.8 us)
Async XLA Ops:
  0.0 9.7 %copy-start = (f32[128]{0:T(128)S(1)}, f32[128]{0:T(128)}, u32[]{:S(2)}) copy-start(f32[128]{0:T(128)} %param.31) | copy-start | bytes 1540
  0.0 5.0 %copy-start.9 = (bf16[128,1024]{1,0:T(8,128)(2,1)S(1)}, bf16[128,1024]{1,0:T(8,128)(2,1)}, u32[]{:S(2)}) copy-start(bf16[128,1024]{1,0:T(8,128)(2,1)} %param.19) | copy-start | bytes 786436
  1.6 7.0 %copy-start.22 = (f32[16]{0:T(128)S(1)}, f32[16]{0:T(128)}, u32[]{:S(2)}) copy-start(f32[16]{0:T(128)} %param.28) | copy-start | bytes 196
  1.6 7.1 %copy-start.23 = (f32[16]{0:T(128)S(1)}, f32[16]{0:T(128)}, u32[]{:S(2)}) copy-start(f32[16]{0:T(128)} %param.29) | copy-start | bytes 196
  1.6 7.2 %copy-start.20 = (f32[128,8]{0,1:T(8,128)S(1)}, f32[128,8]{0,1:T(8,128)}, u32[]{:S(2)}) copy-start(f32[128,8]{0,1:T(8,128)} %param.26) | copy-start | bytes 12292
  2.5 7.2 %copy-start.21 = (f32[128,8]{0,1:T(8,128)S(1)}, f32[128,8]{0,1:T(8,128)}, u32[]{:S(2)}) copy-start(f32[128,8]{0,1:T(8,128)} %param.27) | copy-start | bytes 12292
  2.5 7.3 %copy-start.18 = (bf16[4,512]{1,0:T(4,128)(2,1)S(1)}, bf16[4,512]{1,0:T(4,128)(2,1)}, u32[]{:S(2)}) copy-start(bf16[4,512]{1,0:T(4,128)(2,1)} %param.23) | copy-start | bytes 12292
  2.5 7.9 %copy-start.19 = (bf16[4,512]{1,0:T(4,128)(2,1)S(1)}, bf16[4,512]{1,0:T(4,128)(2,1)}, u32[]{:S(2)}) copy-start(bf16[4,512]{1,0:T(4,128)(2,1)} %param.24) | copy-start | bytes 12292
  2.5 7.9 %copy-start.17 = (bf16[4,1024]{1,0:T(4,128)(2,1)S(1)}, bf16[4,1024]{1,0:T(4,128)(2,1)}, u32[]{:S(2)}) copy-start(bf16[4,1024]{1,0:T(4,128)(2,1)} %param.25) | copy-start | bytes 24580
  5.2 6.7 %collective-permute-start = (f32[3,2048]{1,0:T(4,128)S(1)}, f32[3,2048]{1,0:T(4,128)S(1)}, u32[]{:S(2)}, u32[]{:S(2)}) collective-permute-start(f32[3,2048]{1,0:T(4,128)S(1)} %pad_maximum_fusion.11), channel_id=1, source_target_pairs={{0,2},{2,4},{4,6},{6,8},{8,10},{10,12},{12,14},{14,16},{16,18},{18... | collective-permute-start | bytes 73736 | tf_op jit(solution)/shard_map/ppermute | solution.py:16
  8.6 5.2 %copy-start.15 = (pred[64,64]{1,0:T(8,128)(4,1)}, pred[64,64]{1,0:T(8,128)(4,1)S(1)}, u32[]{:S(2)}) copy-start(pred[64,64]{1,0:T(8,128)(4,1)S(1)} %get-tuple-element.63) | copy-start | bytes 12292
  13.8 8.9 %copy-start.3 = (f32[128,4,2,128]{3,0,2,1:T(8,128)}, f32[128,4,2,128]{3,0,2,1:T(8,128)S(1)}, u32[]{:S(2)}) copy-start(f32[128,4,2,128]{3,0,2,1:T(8,128)S(1)} %broadcast_in_dim.31) | copy-start | bytes 1572868
  28.2 12.1 %collective-permute-start.1 = (bf16[8,128,128]{2,1,0:T(8,128)(2,1)}, bf16[8,128,128]{2,1,0:T(8,128)(2,1)}, u32[]{:S(2)}, u32[]{:S(2)}) collective-permute-start(bf16[8,128,128]{2,1,0:T(8,128)(2,1)} %get-tuple-element.27), channel_id=1, source_target_pairs={{0,2},{2,4},{4,6},{6,8},{8,10},{10,12},{12,14},{14,16},{16,18},{18... | collective-permute-start | bytes 786440 | tf_op jit(solution)/shard_map/ppermute | solution.py:51
  32.0 17.1 %collective-permute-start.3 = (bf16[8,128,128]{2,1,0:T(8,128)(2,1)}, bf16[8,128,128]{2,1,0:T(8,128)(2,1)}, u32[]{:S(2)}, u32[]{:S(2)}) collective-permute-start(bf16[8,128,128]{2,1,0:T(8,128)(2,1)} %get-tuple-element.28), channel_id=1, source_target_pairs={{0,2},{2,4},{4,6},{6,8},{8,10},{10,12},{12,14},{14,16},{16,18},{18... | collective-permute-start | bytes 786440 | tf_op jit(solution)/shard_map/ppermute | solution.py:33
  45.6 7.5 %copy-start.8 = (f32[2,8,64,128]{3,2,1,0:T(8,128)}, f32[2,8,64,128]{3,2,1,0:T(8,128)S(1)}, u32[]{:S(2)}) copy-start(f32[2,8,64,128]{3,2,1,0:T(8,128)S(1)} %convolution_subtract_fusion) | copy-start | bytes 1572868
  46.2 7.6 %copy-start.7 = (f32[2,8,64,128]{3,2,1,0:T(8,128)}, f32[2,8,64,128]{3,2,1,0:T(8,128)S(1)}, u32[]{:S(2)}) copy-start(f32[2,8,64,128]{3,2,1,0:T(8,128)S(1)} %fusion.51) | copy-start | bytes 1572868
  47.8 9.9 %collective-permute-start.2 = (bf16[8,128,128]{2,1,0:T(8,128)(2,1)S(1)}, bf16[8,128,128]{2,1,0:T(8,128)(2,1)S(1)}, u32[]{:S(2)}, u32[]{:S(2)}) collective-permute-start(bf16[8,128,128]{2,1,0:T(8,128)(2,1)S(1)} %get-tuple-element.58), channel_id=1, source_target_pairs={{0,4},{2,6},{4,8},{6,10},{8,12},{10,14},{12,16},{14,18},{16,20},{1... | collective-permute-start | bytes 786440 | tf_op jit(solution)/shard_map/ppermute | solution.py:51
  50.8 9.8 %collective-permute-start.5 = (bf16[8,128,128]{2,1,0:T(8,128)(2,1)S(1)}, bf16[8,128,128]{2,1,0:T(8,128)(2,1)S(1)}, u32[]{:S(2)}, u32[]{:S(2)}) collective-permute-start(bf16[8,128,128]{2,1,0:T(8,128)(2,1)S(1)} %get-tuple-element.56), channel_id=1, source_target_pairs={{0,4},{2,6},{4,8},{6,10},{8,12},{10,14},{12,16},{14,18},{16,20},{1... | collective-permute-start | bytes 786440 | tf_op jit(solution)/shard_map/ppermute | solution.py:33
  53.9 6.7 %copy-start.10 = (f32[128,128]{1,0:T(8,128)S(1)}, f32[128,128]{1,0:T(8,128)}, u32[]{:S(2)}) copy-start(f32[128,128]{1,0:T(8,128)} %fusion.105) | copy-start | bytes 196612
  58.4 11.7 %collective-permute-start.4 = (bf16[8,128,128]{2,1,0:T(8,128)(2,1)S(1)}, bf16[8,128,128]{2,1,0:T(8,128)(2,1)S(1)}, u32[]{:S(2)}, u32[]{:S(2)}) collective-permute-start(bf16[8,128,128]{2,1,0:T(8,128)(2,1)S(1)} %fusion.101), channel_id=1, source_target_pairs={{0,8},{2,10},{4,12},{6,14},{8,16},{10,18},{12,20},{14,22},{16,24},... | collective-permute-start | bytes 786440 | tf_op jit(solution)/shard_map/ppermute | solution.py:51
  61.8 12.5 %collective-permute-start.6 = (bf16[8,128,128]{2,1,0:T(8,128)(2,1)S(1)}, bf16[8,128,128]{2,1,0:T(8,128)(2,1)S(1)}, u32[]{:S(2)}, u32[]{:S(2)}) collective-permute-start(bf16[8,128,128]{2,1,0:T(8,128)(2,1)S(1)} %get-tuple-element.26), channel_id=1, source_target_pairs={{0,8},{2,10},{4,12},{6,14},{8,16},{10,18},{12,20},{14,22},{16,24},... | collective-permute-start | bytes 786440 | tf_op jit(solution)/shard_map/ppermute | solution.py:33
  72.0 12.7 %slice-start = ((f32[2,8,64,128]{3,2,1,0:T(8,128)}), f32[1,8,64,128]{3,2,1,0:T(8,128)S(1)}, s32[]{:S(2)}) async-start(f32[2,8,64,128]{3,2,1,0:T(8,128)} %copy-done.7), calls=%async_computation | async-start | bytes 524288 | tf_op jit(solution)/shard_map/slice | solution.py:248
  72.0 12.7 %collective-permute-start.7 = (bf16[8,128,128]{2,1,0:T(8,128)(2,1)S(1)}, bf16[8,128,128]{2,1,0:T(8,128)(2,1)S(1)}, u32[]{:S(2)}, u32[]{:S(2)}) collective-permute-start(bf16[8,128,128]{2,1,0:T(8,128)(2,1)S(1)} %get-tuple-element.21), channel_id=1, source_target_pairs={{0,16},{2,18},{4,20},{6,22},{8,24},{10,26},{12,28},{14,30},{1,17},... | collective-permute-start | bytes 786440 | tf_op jit(solution)/shard_map/ppermute | solution.py:51
  76.1 9.8 %copy-start.11 = (bf16[128,1024]{1,0:T(8,128)(2,1)S(1)}, bf16[128,1024]{1,0:T(8,128)(2,1)}, u32[]{:S(2)}) copy-start(bf16[128,1024]{1,0:T(8,128)(2,1)} %param.30) | copy-start | bytes 786436
  (10 other events, 20.0 us)

commit v18 on v15

--- a/solution.py
+++ b/solution.py
@@ -74,7 +74,9 @@
 def expand_quantized(raw_rows, scales):
     head_count = scales.shape[1]
     width = raw_rows.shape[1] // head_count
-    return raw_rows.astype(jnp.float32) * jnp.repeat(scales, width, axis=1)
+    spread = jnp.arange(raw_rows.shape[1])[None, :] // width == jnp.arange(head_count)[:, None]
+    expanded = jnp.dot(scales, spread.astype(jnp.float32), precision=HIGHEST)
+    return raw_rows.astype(jnp.float32) * expanded
 
 
 def causal_filter(window, weights):

time: 87.7 us -> 92.6 us (1.056)
  the two profiles are of different devices: /device:TPU:28 before, /device:TPU:16 now
where the time goes in v18:
time: 92.6 us; the launch traced here: 91.8 us
  matrix products  27 us (29%)
  starting transfers between devices  25.6 us (28%)
  waiting for transfers between devices  17.2 us (19%)
  other arithmetic  15.1 us (16%)
  local copies, waits for them, and re-layouts  5.93 us (6%)
    ppermute x3, starting transfers between devices, scan_states(): earlier = lax.ppermute((inclusive - eye).astype(jnp.bfloat16), axis, pairs)  11.4 us
    ppermute x4, starting transfers between devices, scan_states(): earlier = lax.ppermute(carried.astype(jnp.bfloat16), axis, pairs)  10.9 us
    ppermute x3, waiting for transfers between devices, scan_states(): earlier = lax.ppermute((inclusive - eye).astype(jnp.bfloat16), axis, pairs)  10.5 us
    ppermute x4, waiting for transfers between devices, scan_states(): earlier = lax.ppermute(carried.astype(jnp.bfloat16), axis, pairs)  6.67 us
    dot_general x4, matrix products, unit_lower_inverse(): jnp.einsum('sbhij,sbhjk->sbhik', jnp.stack([inverse, power]), jnp.stack([...  4.71 us
    dot_general x3, matrix products, expand_quantized(): expanded = jnp.dot(scales, spread.astype(jnp.float32), precision=HIGHEST)  3.87 us
    dot_general x3, matrix products, product(): return jnp.einsum('hde,hef->hdf', left, right, precision=HIGHEST)  3.85 us
    ppermute x1, starting transfers between devices, from_behind(): lax.ppermute(value, axis, [(source, source + steps) for source in range(f...  3.4 us
  transfers between devices with their start and end apart: 8, of which 5 were waited for; matrix products, arithmetic and copies ran while one was open for 28% of the time, Pallas kernels for 0%

profile of v18, /device:TPU:16, one launch (start us, length us, event | category | flops | bytes accessed | tf_op | source)
XLA Modules:
  0.0 91.8 jit_solution(9164776782744159504)
XLA Ops:
  0.0 1.2 %fusion.6 = f32[128,512]{1,0:T(8,128)S(1)} fusion(f32[128,4]{0,1:T(4,128)} %param.21, bf16[128,512]{1,0:T(8,128)(2,1)} %param.18, s32[512]{0:T(512)S(1)} %add_select_fusion.1), kind=kOutput, calls=%fused_computation.24 | convolution fusion | flops 3278848 | bytes 397312 | tf_op jit(solution)/shard_map/dot_general | solution.py:78
  1.3 1.2 %fusion.7 = f32[128,512]{1,0:T(8,128)S(1)} fusion(f32[128,4]{0,1:T(4,128)} %param.20, bf16[128,512]{1,0:T(8,128)(2,1)} %param.17, s32[512]{0:T(512)S(1)} %add_select_fusion.1), kind=kOutput, calls=%fused_computation.26 | convolution fusion | flops 3278848 | bytes 397312 | tf_op jit(solution)/shard_map/dot_general | solution.py:78
  2.6 1.4 %fusion = f32[128,1024]{1,0:T(8,128)S(1)} fusion(f32[128,8]{0,1:T(8,128)S(1)} %copy-done, bf16[128,1024]{1,0:T(8,128)(2,1)} %param.19, s32[1024]{0:T(1024)S(1)} %add_select_fusion), kind=kOutput, calls=%fused_computation.9 | convolution fusion | flops 12853248 | bytes 794624 | tf_op jit(solution)/shard_map/dot_general | solution.py:78
  4.0 3.4 %collective-permute-start = (f32[3,2048]{1,0:T(4,128)S(1)}, f32[3,2048]{1,0:T(4,128)S(1)}, u32[]{:S(2)}, u32[]{:S(2)}) collective-permute-start(f32[3,2048]{1,0:T(4,128)S(1)} %pad_maximum_fusion.12), channel_id=1, source_target_pairs={{0,2},{2,4},{4,6},{6,8},{8,10},{10,12},{12,14},{14,16},{16,18},{18... | collective-permute-start | bytes 73736 | tf_op jit(solution)/shard_map/ppermute | solution.py:16
  11.8 1.4 %slice_convert_fusion.7 = (f32[1,512]{1,0:T(1,128)}, f32[1,512]{1,0:T(1,128)}, f32[1,512]{1,0:T(1,128)}, f32[1,512]{1,0:T(1,128)}) fusion(bf16[4,512]{1,0:T(4,128)(2,1)} %param.23), kind=kLoop, calls=%fused_computation.221 | loop fusion | flops 2048 | bytes 12288 | tf_op jit(solution)/shard_map/mul | solution.py:87
  18.9 1.2 %fusion.8 = f32[2,2,8,64,64]{4,3,2,1,0:T(8,128)S(1)} fusion(f32[1,2,8,64,64]{4,3,2,1,0:T(8,128)S(1)} %bitcast.205, f32[1,2,8,64,64]{4,3,2,1,0:T(8,128)S(1)} %get-tuple-element.38, f32[1,2,8,64,64]{4,3,2,1,0:T(8,128)S(1)} %get-tuple-element.37), kind=kOutput, calls=%fused_computation.27 | convolution fusion | flops 100925440 | bytes 1310720 | tf_op jit(solution)/shard_map/sbhij,sbhjk->sbhik/dot_general | solution.py:119
  20.2 1.2 %fusion.14 = f32[2,2,8,64,64]{4,3,2,1,0:T(8,128)S(1)} fusion(f32[2,2,8,64,64]{4,3,2,1,0:T(8,128)S(1)} %fusion.8, f32[1,2,8,64,64]{4,3,2,1,0:T(8,128)S(1)} %get-tuple-element.32, f32[1,2,8,64,64]{4,3,2,1,0:T(8,128)S(1)} %get-tuple-element.31), kind=kOutput, calls=%fused_computation.35 | convolution fusion | flops 100794368 | bytes 1572864 | tf_op jit(solution)/shard_map/sbhij,sbhjk->sbhik/dot_general | solution.py:119
  27.0 2.3 %fusion.68 = f32[2,8,128,256]{3,2,1,0:T(8,128)S(1)} fusion(f32[2,8,64,256]{3,2,1,0:T(8,128)S(1)} %fusion.26, f32[2,64,8,128]{3,1,0,2:T(8,128)S(1)} %bitcast.208, f32[2,8,64]{2,1,0:T(8,128)S(1)} %get-tuple-element.41), kind=kOutput, calls=%fused_computation.108 | convolution fusion | flops 402784256 | bytes 3674112 | tf_op jit(solution)/shard_map/bhjd,bhje->bhde/dot_general | solution.py:151
  31.6 3.4 %collective-permute-start.1 = (bf16[8,128,128]{2,1,0:T(8,128)(2,1)}, bf16[8,128,128]{2,1,0:T(8,128)(2,1)}, u32[]{:S(2)}, u32[]{:S(2)}) collective-permute-start(bf16[8,128,128]{2,1,0:T(8,128)(2,1)} %get-tuple-element.25), channel_id=1, source_target_pairs={{0,2},{2,4},{4,6},{6,8},{8,10},{10,12},{12,14},{14,16},{16,18},{18... | collective-permute-start | bytes 786440 | tf_op jit(solution)/shard_map/ppermute | solution.py:51
  36.3 3.4 %collective-permute-start.3 = (bf16[8,128,128]{2,1,0:T(8,128)(2,1)}, bf16[8,128,128]{2,1,0:T(8,128)(2,1)}, u32[]{:S(2)}, u32[]{:S(2)}) collective-permute-start(bf16[8,128,128]{2,1,0:T(8,128)(2,1)} %get-tuple-element.26), channel_id=1, source_target_pairs={{0,2},{2,4},{4,6},{6,8},{8,10},{10,12},{12,14},{14,16},{16,18},{18... | collective-permute-start | bytes 786440 | tf_op jit(solution)/shard_map/ppermute | solution.py:33
  40.4 4.1 %collective-permute-done.1 = bf16[8,128,128]{2,1,0:T(8,128)(2,1)} collective-permute-done((bf16[8,128,128]{2,1,0:T(8,128)(2,1)}, bf16[8,128,128]{2,1,0:T(8,128)(2,1)}, u32[]{:S(2)}, u32[]{:S(2)}) %collective-permute-start.1) | collective-permute-done | bytes 262176 | tf_op jit(solution)/shard_map/ppermute | solution.py:51
  44.6 1.5 %multiply_convert_fusion.1 = bf16[128,512]{1,0:T(8,128)(2,1)} fusion(f32[131,512]{1,0:T(8,128)S(1)} %pad_maximum_fusion.10, f32[512]{0:T(512)} %bitcast.227, f32[512]{0:T(512)} %bitcast.228, f32[512]{0:T(512)} %bitcast.226, f32[512]{0:T(512)} %bitcast.225), kind=kLoop, calls=%fused_computation.162 | loop fusion | flops 786432 | bytes 1187840 | tf_op jit(solution)/shard_map/convert_element_type | solution.py:90
  50.5 1.5 %fusion.137 = (bf16[8,128,128]{2,1,0:T(8,128)(2,1)S(1)}, f32[8,128,128]{2,1,0:T(8,128)S(1)}) fusion(f32[8,128,256]{2,1,0:T(8,128)S(1)} %copy-done.6, f32[8,128,256]{2,1,0:T(8,128)S(1)} %fusion.57, bf16[8,128,128]{2,1,0:T(8,128)(2,1)} %collective-permute-done.1), kind=kOutput, calls=%fused_computation.243 | convolution fusion | flops 201719808 | bytes 2621440 | tf_op jit(solution)/shard_map/hde,hef->hdf/dot_general | solution.py:168
  52.0 2.5 %collective-permute-start.2 = (bf16[8,128,128]{2,1,0:T(8,128)(2,1)S(1)}, bf16[8,128,128]{2,1,0:T(8,128)(2,1)S(1)}, u32[]{:S(2)}, u32[]{:S(2)}) collective-permute-start(bf16[8,128,128]{2,1,0:T(8,128)(2,1)S(1)} %get-tuple-element.56), channel_id=1, source_target_pairs={{0,4},{2,6},{4,8},{6,10},{8,12},{10,14},{12,16},{14,18},{16,20},{1... | collective-permute-start | bytes 786440 | tf_op jit(solution)/shard_map/ppermute | solution.py:51
  54.6 1.7 %subtract_convert_fusion.1 = (bf16[8,128,128]{2,1,0:T(8,128)(2,1)S(1)}, f32[8,128,128]{2,1,0:T(8,128)S(1)}) fusion(f32[128,128]{1,0:T(8,128)S(1)} %fusion.110, f32[8,128,256]{2,1,0:T(8,128)S(1)} %fusion.57, bf16[8,128,128]{2,1,0:T(8,128)(2,1)} %collective-permute-done.3, f32[128,128]{1,0:T(8,128)S(1)} %fusion.109, pred[]{:T(512)S(6)} %ge.39), kind=kOutput, calls=%fused_computation.118 | convolution fusion | flops 201981952 | bytes 2228225 | tf_op jit(solution)/shard_map/hde,hef->hdf/dot_general | solution.py:168
  56.2 4.3 %collective-permute-start.5 = (bf16[8,128,128]{2,1,0:T(8,128)(2,1)S(1)}, bf16[8,128,128]{2,1,0:T(8,128)(2,1)S(1)}, u32[]{:S(2)}, u32[]{:S(2)}) collective-permute-start(bf16[8,128,128]{2,1,0:T(8,128)(2,1)S(1)} %get-tuple-element.54), channel_id=1, source_target_pairs={{0,4},{2,6},{4,8},{6,10},{8,12},{10,14},{12,16},{14,18},{16,20},{1... | collective-permute-start | bytes 786440 | tf_op jit(solution)/shard_map/ppermute | solution.py:33
  62.3 1.3 %collective-permute-done.2 = bf16[8,128,128]{2,1,0:T(8,128)(2,1)S(1)} collective-permute-done((bf16[8,128,128]{2,1,0:T(8,128)(2,1)S(1)}, bf16[8,128,128]{2,1,0:T(8,128)(2,1)S(1)}, u32[]{:S(2)}, u32[]{:S(2)}) %collective-permute-start.2) | collective-permute-done | bytes 262176 | tf_op jit(solution)/shard_map/ppermute | solution.py:51
  64.3 3.4 %collective-permute-start.4 = (bf16[8,128,128]{2,1,0:T(8,128)(2,1)S(1)}, bf16[8,128,128]{2,1,0:T(8,128)(2,1)S(1)}, u32[]{:S(2)}, u32[]{:S(2)}) collective-permute-start(bf16[8,128,128]{2,1,0:T(8,128)(2,1)S(1)} %fusion.104), channel_id=1, source_target_pairs={{0,8},{2,10},{4,12},{6,14},{8,16},{10,18},{12,20},{14,22},{16,24},... | collective-permute-start | bytes 786440 | tf_op jit(solution)/shard_map/ppermute | solution.py:51
  67.8 1.3 %collective-permute-done.5 = bf16[8,128,128]{2,1,0:T(8,128)(2,1)S(1)} collective-permute-done((bf16[8,128,128]{2,1,0:T(8,128)(2,1)S(1)}, bf16[8,128,128]{2,1,0:T(8,128)(2,1)S(1)}, u32[]{:S(2)}, u32[]{:S(2)}) %collective-permute-start.5) | collective-permute-done | bytes 262176 | tf_op jit(solution)/shard_map/ppermute | solution.py:33
  70.2 3.7 %collective-permute-start.7 = (bf16[8,128,128]{2,1,0:T(8,128)(2,1)S(1)}, bf16[8,128,128]{2,1,0:T(8,128)(2,1)S(1)}, u32[]{:S(2)}, u32[]{:S(2)}) collective-permute-start(bf16[8,128,128]{2,1,0:T(8,128)(2,1)S(1)} %get-tuple-element.23), channel_id=1, source_target_pairs={{0,8},{2,10},{4,12},{6,14},{8,16},{10,18},{12,20},{14,22},{16,24},... | collective-permute-start | bytes 786440 | tf_op jit(solution)/shard_map/ppermute | solution.py:33
  73.9 1.2 %collective-permute-done.4 = bf16[8,128,128]{2,1,0:T(8,128)(2,1)S(1)} collective-permute-done((bf16[8,128,128]{2,1,0:T(8,128)(2,1)S(1)}, bf16[8,128,128]{2,1,0:T(8,128)(2,1)S(1)}, u32[]{:S(2)}, u32[]{:S(2)}) %collective-permute-start.4) | collective-permute-done | bytes 262176 | tf_op jit(solution)/shard_map/ppermute | solution.py:51
  75.8 1.5 %collective-permute-start.6 = (bf16[8,128,128]{2,1,0:T(8,128)(2,1)S(1)}, bf16[8,128,128]{2,1,0:T(8,128)(2,1)S(1)}, u32[]{:S(2)}, u32[]{:S(2)}) collective-permute-start(bf16[8,128,128]{2,1,0:T(8,128)(2,1)S(1)} %fusion.46), channel_id=1, source_target_pairs={{0,16},{2,18},{4,20},{6,22},{8,24},{10,26},{12,28},{14,30},{1,17},... | collective-permute-start | bytes 786440 | tf_op jit(solution)/shard_map/ppermute | solution.py:51
  77.4 9.3 %collective-permute-done.7 = bf16[8,128,128]{2,1,0:T(8,128)(2,1)S(1)} collective-permute-done((bf16[8,128,128]{2,1,0:T(8,128)(2,1)S(1)}, bf16[8,128,128]{2,1,0:T(8,128)(2,1)S(1)}, u32[]{:S(2)}, u32[]{:S(2)}) %collective-permute-start.7) | collective-permute-done | bytes 262176 | tf_op jit(solution)/shard_map/ppermute | solution.py:33
  87.9 1.6 %fusion.3 = f32[2,8,64,128]{3,2,1,0:T(8,128)S(1)} fusion(f32[2,8,128,128]{3,2,1,0:T(8,128)S(1)} %convolution_bitcast_fusion, f32[2,8,128,128]{3,2,1,0:T(8,128)S(1)} %convolution_bitcast_fusion.1, f32[1,8,64,128]{3,2,1,0:T(8,128)S(1)} %get-tuple-element.34, f32[1,8,64,128]{3,2,1,0:T(8,128)S(1)} %slice-done, bf16[8,128,128]{2,1,0:T(8,128)(2,1)} %collective-permute-done.1, ...), kind=kOutput, calls=%fused_computation.19 | convolution fusion | flops 202113024 | bytes 2883584 | tf_op jit(solution)/shard_map/bhid,hde->bhie/dot_general | solution.py:256
  (118 shorter events, 31.8 us)
Async XLA Ops:
  0.0 2.5 %copy-start = (f32[128,8]{0,1:T(8,128)S(1)}, f32[128,8]{0,1:T(8,128)}, u32[]{:S(2)}) copy-start(f32[128,8]{0,1:T(8,128)} %param.22) | copy-start | bytes 12292
  4.0 11.3 %collective-permute-start = (f32[3,2048]{1,0:T(4,128)S(1)}, f32[3,2048]{1,0:T(4,128)S(1)}, u32[]{:S(2)}, u32[]{:S(2)}) collective-permute-start(f32[3,2048]{1,0:T(4,128)S(1)} %pad_maximum_fusion.12), channel_id=1, source_target_pairs={{0,2},{2,4},{4,6},{6,8},{8,10},{10,12},{12,14},{14,16},{16,18},{18... | collective-permute-start | bytes 73736 | tf_op jit(solution)/shard_map/ppermute | solution.py:16
  7.4 9.7 %copy-start.13 = (pred[64,64]{1,0:T(8,128)(4,1)}, pred[64,64]{1,0:T(8,128)(4,1)S(1)}, u32[]{:S(2)}) copy-start(pred[64,64]{1,0:T(8,128)(4,1)S(1)} %get-tuple-element.61) | copy-start | bytes 12292
  15.1 0.8 copy-start.11
  17.1 8.9 %copy-start.3 = (f32[128,4,2,128]{3,0,2,1:T(8,128)}, f32[128,4,2,128]{3,0,2,1:T(8,128)S(1)}, u32[]{:S(2)}) copy-start(f32[128,4,2,128]{3,0,2,1:T(8,128)S(1)} %broadcast_in_dim.20) | copy-start | bytes 1572868
  26.0 1.0 %copy-start.1 = (f32[2,8,64,256]{3,2,1,0:T(8,128)}, f32[2,8,64,256]{3,2,1,0:T(8,128)S(1)}, u32[]{:S(2)}) copy-start(f32[2,8,64,256]{3,2,1,0:T(8,128)S(1)} %fusion.26) | copy-start | bytes 3145732
  29.6 2.0 %copy-start.5 = (f32[8,128,256]{2,1,0:T(8,128)}, f32[8,128,256]{2,1,0:T(8,128)S(1)}, u32[]{:S(2)}) copy-start(f32[8,128,256]{2,1,0:T(8,128)S(1)} %fusion.10) | copy-start | bytes 3145732
  31.6 12.9 %collective-permute-start.1 = (bf16[8,128,128]{2,1,0:T(8,128)(2,1)}, bf16[8,128,128]{2,1,0:T(8,128)(2,1)}, u32[]{:S(2)}, u32[]{:S(2)}) collective-permute-start(bf16[8,128,128]{2,1,0:T(8,128)(2,1)} %get-tuple-element.25), channel_id=1, source_target_pairs={{0,2},{2,4},{4,6},{6,8},{8,10},{10,12},{12,14},{14,16},{16,18},{18... | collective-permute-start | bytes 786440 | tf_op jit(solution)/shard_map/ppermute | solution.py:51
  36.3 18.3 %collective-permute-start.3 = (bf16[8,128,128]{2,1,0:T(8,128)(2,1)}, bf16[8,128,128]{2,1,0:T(8,128)(2,1)}, u32[]{:S(2)}, u32[]{:S(2)}) collective-permute-start(bf16[8,128,128]{2,1,0:T(8,128)(2,1)} %get-tuple-element.26), channel_id=1, source_target_pairs={{0,2},{2,4},{4,6},{6,8},{8,10},{10,12},{12,14},{14,16},{16,18},{18... | collective-permute-start | bytes 786440 | tf_op jit(solution)/shard_map/ppermute | solution.py:33
  47.1 1.0 %copy-start.4 = (f32[128,4,2,128]{3,0,2,1:T(8,128)S(1)}, f32[128,4,2,128]{3,0,2,1:T(8,128)}, u32[]{:S(2)}) copy-start(f32[128,4,2,128]{3,0,2,1:T(8,128)} %copy-done.3) | copy-start | bytes 1572868
  47.1 1.0 %copy-start.14 = (pred[64,64]{1,0:T(8,128)(4,1)S(1)}, pred[64,64]{1,0:T(8,128)(4,1)}, u32[]{:S(2)}) copy-start(pred[64,64]{1,0:T(8,128)(4,1)} %copy-done.13) | copy-start | bytes 12292
  47.1 2.0 %copy-start.2 = (f32[2,8,64,256]{3,2,1,0:T(8,128)S(1)}, f32[2,8,64,256]{3,2,1,0:T(8,128)}, u32[]{:S(2)}) copy-start(f32[2,8,64,256]{3,2,1,0:T(8,128)} %copy-done.1) | copy-start | bytes 3145732
  47.1 2.0 %copy-start.12 = (f32[2,8,64]{2,1,0:T(8,128)S(1)}, f32[2,8,64]{2,1,0:T(8,128)}, u32[]{:S(2)}) copy-start(f32[2,8,64]{2,1,0:T(8,128)} %copy-done.11) | copy-start | bytes 12292
  49.1 1.4 %copy-start.6 = (f32[8,128,256]{2,1,0:T(8,128)S(1)}, f32[8,128,256]{2,1,0:T(8,128)}, u32[]{:S(2)}) copy-start(f32[8,128,256]{2,1,0:T(8,128)} %copy-done.5) | copy-start | bytes 3145732
  50.4 11.8 %copy-start.7 = (f32[2,8,64,128]{3,2,1,0:T(8,128)}, f32[2,8,64,128]{3,2,1,0:T(8,128)S(1)}, u32[]{:S(2)}) copy-start(f32[2,8,64,128]{3,2,1,0:T(8,128)S(1)} %fusion.55) | copy-start | bytes 1572868
  52.0 11.6 %collective-permute-start.2 = (bf16[8,128,128]{2,1,0:T(8,128)(2,1)S(1)}, bf16[8,128,128]{2,1,0:T(8,128)(2,1)S(1)}, u32[]{:S(2)}, u32[]{:S(2)}) collective-permute-start(bf16[8,128,128]{2,1,0:T(8,128)(2,1)S(1)} %get-tuple-element.56), channel_id=1, source_target_pairs={{0,4},{2,6},{4,8},{6,10},{8,12},{10,14},{12,16},{14,18},{16,20},{1... | collective-permute-start | bytes 786440 | tf_op jit(solution)/shard_map/ppermute | solution.py:51
  56.2 12.8 %collective-permute-start.5 = (bf16[8,128,128]{2,1,0:T(8,128)(2,1)S(1)}, bf16[8,128,128]{2,1,0:T(8,128)(2,1)S(1)}, u32[]{:S(2)}, u32[]{:S(2)}) collective-permute-start(bf16[8,128,128]{2,1,0:T(8,128)(2,1)S(1)} %get-tuple-element.54), channel_id=1, source_target_pairs={{0,4},{2,6},{4,8},{6,10},{8,12},{10,14},{12,16},{14,18},{16,20},{1... | collective-permute-start | bytes 786440 | tf_op jit(solution)/shard_map/ppermute | solution.py:33
  62.3 6.7 %copy-start.8 = (f32[128,128]{1,0:T(8,128)S(1)}, f32[128,128]{1,0:T(8,128)}, u32[]{:S(2)}) copy-start(f32[128,128]{1,0:T(8,128)} %fusion.108) | copy-start | bytes 196612
  64.3 10.8 %collective-permute-start.4 = (bf16[8,128,128]{2,1,0:T(8,128)(2,1)S(1)}, bf16[8,128,128]{2,1,0:T(8,128)(2,1)S(1)}, u32[]{:S(2)}, u32[]{:S(2)}) collective-permute-start(bf16[8,128,128]{2,1,0:T(8,128)(2,1)S(1)} %fusion.104), channel_id=1, source_target_pairs={{0,8},{2,10},{4,12},{6,14},{8,16},{10,18},{12,20},{14,22},{16,24},... | collective-permute-start | bytes 786440 | tf_op jit(solution)/shard_map/ppermute | solution.py:51
  70.2 16.4 %collective-permute-start.7 = (bf16[8,128,128]{2,1,0:T(8,128)(2,1)S(1)}, bf16[8,128,128]{2,1,0:T(8,128)(2,1)S(1)}, u32[]{:S(2)}, u32[]{:S(2)}) collective-permute-start(bf16[8,128,128]{2,1,0:T(8,128)(2,1)S(1)} %get-tuple-element.23), channel_id=1, source_target_pairs={{0,8},{2,10},{4,12},{6,14},{8,16},{10,18},{12,20},{14,22},{16,24},... | collective-permute-start | bytes 786440 | tf_op jit(solution)/shard_map/ppermute | solution.py:33
  75.1 11.5 %copy-start.10 = (f32[128,128]{1,0:T(8,128)S(1)}, f32[128,128]{1,0:T(8,128)}, u32[]{:S(2)}) copy-start(f32[128,128]{1,0:T(8,128)} %fusion.107) | copy-start | bytes 196612
  75.7 12.2 %slice-start = ((f32[2,8,64,128]{3,2,1,0:T(8,128)}), f32[1,8,64,128]{3,2,1,0:T(8,128)S(1)}, s32[]{:S(2)}) async-start(f32[2,8,64,128]{3,2,1,0:T(8,128)} %copy-done.7), calls=%async_computation | async-start | bytes 524288 | tf_op jit(solution)/shard_map/slice | solution.py:250
  75.8 13.7 %collective-permute-start.6 = (bf16[8,128,128]{2,1,0:T(8,128)(2,1)S(1)}, bf16[8,128,128]{2,1,0:T(8,128)(2,1)S(1)}, u32[]{:S(2)}, u32[]{:S(2)}) collective-permute-start(bf16[8,128,128]{2,1,0:T(8,128)(2,1)S(1)} %fusion.46), channel_id=1, source_target_pairs={{0,16},{2,18},{4,20},{6,22},{8,24},{10,26},{12,28},{14,30},{1,17},... | collective-permute-start | bytes 786440 | tf_op jit(solution)/shard_map/ppermute | solution.py:51
  89.6 1.2 %copy-start.9 = (bf16[128,1024]{1,0:T(8,128)(2,1)S(1)}, bf16[128,1024]{1,0:T(8,128)(2,1)}, u32[]{:S(2)}) copy-start(bf16[128,1024]{1,0:T(8,128)(2,1)} %param.30) | copy-start | bytes 786436
